TPU v7x, 128 devices: a whole 4x4x4 slice. The times are simulated.
128 devices in a mesh: seq: 16 (over z, x_hi, core), head: 8 (over y, x_lo).
Axes of the slice: x: 4 (x_hi: 2, x_lo: 2; x = x_hi * 2 + x_lo), y: 4, z: 4, core: 2. Of those that a mesh axis runs over, the one named last changes fastest.
Arguments:
- queries: bfloat16 [16384, 4096], P('seq', 'head'), may hold values from -6 to 6
- key_rows: bfloat16 [16384, 4096], P('seq', 'head'), may hold values from -6 to 6
- value_rows: bfloat16 [16384, 4096], P('seq', 'head'), may hold values from -6 to 6
- out_weight: bfloat16 [4096, 4096], P('head'), may hold values from -0.375 to 0.375
- cotangent: bfloat16 [16384, 4096], P('seq', 'head'), may hold values from -1.5 to 1.5
- pattern: int32 [128, 7], P('seq'), may hold values 0 or 1
Outputs:
- output: bfloat16 [16384, 4096], P('seq', 'head')
- grad_query: bfloat16 [16384, 4096], P('seq', 'head')
- grad_keys: bfloat16 [16384, 4096], P('seq', 'head')
- grad_values: bfloat16 [16384, 4096], P('seq', 'head')
- grad_weight: float32 [4096, 4096], P('seq', 'head')
All inputs are finite; a program needn't handle non-finite values. No bound on the sum of `pattern` on one device may be relied on, other than what follows from the above.
Results may differ from a plain program's by a relative error of at most 0.0076.
Values may be sent and summed in bfloat16 or wider, within the bound.
No kernel may reach another device: no remote copies, remote signals or barrier semaphores. Data moves between devices by JAX's collectives and lax.ppermute only.
A program may use at most 256 MiB of HBM per device.

v0:
```python
import math

import jax
import jax.numpy as jnp
from jax import lax
from jax.sharding import PartitionSpec as P

DH = 128
BLK = 128


LOG_TWO = math.log(2.0)


def swapped(value, axis, bit):
    mask = 2**bit
    pairs = [(source, source ^ mask) for source in range(lax.axis_size(axis))]
    return lax.ppermute(value, axis, pairs)


def pair_mean(tensor):
    shape_in = tensor.shape
    paired = tensor.reshape(shape_in[:-2] + (shape_in[-2] // 2, 2, shape_in[-1]))
    return jnp.sum(paired, axis=-2) * 0.5


def spread_rows(grads, factor):
    shape_in = grads.shape
    wide = jnp.broadcast_to(grads[..., :, None, :], shape_in[:-1] + (factor, shape_in[-1])) * (
        1.0 / factor
    )
    return wide.reshape(shape_in[:-2] + (shape_in[-2] * factor, shape_in[-1]))


def body(queries, key_rows, value_rows, out_weight, cotangent, pattern):
    row_count, features = queries.shape
    blocks = row_count // BLK
    local_levels = blocks.bit_length() - 1
    seq_count = lax.axis_size("seq")
    cross_levels = seq_count.bit_length() - 1
    level_count = local_levels + cross_levels
    head_count = features // DH
    keys_all = (1 + level_count) * BLK
    score_scale = DH ** (-0.5)
    where_seq = lax.axis_index("seq")
    stacked = jnp.stack([key_rows, value_rows])
    coarse_base = (
        stacked.reshape(2, BLK, row_count // BLK, features).astype(jnp.float32).mean(axis=2)
    )
    siblings = []
    current = coarse_base
    for level_idx in range(cross_levels):
        received = swapped(current, "seq", level_idx)
        siblings.append(received)
        if level_idx + 1 < cross_levels:
            upper_half = jnp.right_shift(where_seq, level_idx) & 1 == 1
            joined = jnp.where(
                upper_half,
                jnp.concatenate([received, current], axis=1),
                jnp.concatenate([current, received], axis=1),
            )
            current = pair_mean(joined)
    segments = [stacked.reshape(2, blocks, BLK, features)]
    for level_idx in range(local_levels):
        factor = 2**level_idx
        group_count = blocks >> level_idx
        if level_idx == 0:
            pooled = stacked
        else:
            pooled = (
                stacked.reshape(2, row_count // factor, factor, features)
                .astype(jnp.float32)
                .mean(axis=2)
                .astype(jnp.bfloat16)
            )
        sibling = pooled.reshape(2, group_count // 2, 2, BLK, features)[:, :, ::-1].reshape(
            2, group_count, BLK, features
        )
        segments.append(
            jnp.broadcast_to(sibling[:, :, None], (2, group_count, factor, BLK, features)).reshape(
                2, blocks, BLK, features
            )
        )
    for level_idx in range(cross_levels):
        segments.append(
            jnp.broadcast_to(
                siblings[level_idx].astype(jnp.bfloat16)[:, None], (2, blocks, BLK, features)
            )
        )
    key_set = jnp.concatenate(segments, axis=2)
    key_bias = jnp.concatenate(
        [jnp.zeros((BLK,), jnp.float32)]
        + [jnp.full((BLK,), level_idx * LOG_TWO, jnp.float32) for level_idx in range(level_count)]
    )
    level_flags = pattern == 1
    kept_mask = jnp.concatenate(
        [
            jnp.ones((blocks, BLK), bool),
            jnp.broadcast_to(level_flags[:, :, None], (blocks, level_count, BLK)).reshape(
                blocks, level_count * BLK
            ),
        ],
        axis=1,
    )
    query_heads = queries.reshape(blocks, BLK, head_count, DH)
    key_heads = key_set[0].reshape(blocks, keys_all, head_count, DH)
    value_heads = key_set[1].reshape(blocks, keys_all, head_count, DH)
    scores = (
        jnp.einsum("bqhd,bkhd->bhqk", query_heads, key_heads, preferred_element_type=jnp.float32)
        * score_scale
        + key_bias
    )
    scores = jnp.where(kept_mask[:, None, None, :], scores, -jnp.inf)
    row_max = jnp.max(scores, axis=-1, keepdims=True)
    weights_raw = jnp.exp(scores - row_max)
    attn_prob = weights_raw / jnp.sum(weights_raw, axis=-1, keepdims=True)
    prob_low = attn_prob.astype(jnp.bfloat16)
    mixed = jnp.einsum("bhqk,bkhd->bqhd", prob_low, value_heads, preferred_element_type=jnp.float32)
    attended = mixed.astype(jnp.bfloat16).reshape(row_count, features)
    partial_out = jnp.dot(attended, out_weight, preferred_element_type=jnp.float32)
    output = lax.psum_scatter(partial_out, "head", scatter_dimension=1, tiled=True).astype(
        jnp.bfloat16
    )
    grads_full = lax.all_gather(cotangent, "head", axis=1, tiled=True)
    grad_attn = lax.dot_general(
        grads_full, out_weight, (((1,), (1,)), ((), ())), preferred_element_type=jnp.float32
    ).astype(jnp.bfloat16)
    grad_weight = lax.psum_scatter(
        lax.dot_general(
            grads_full, attended, (((0,), (0,)), ((), ())), preferred_element_type=jnp.float32
        ),
        "seq",
        scatter_dimension=0,
        tiled=True,
    )
    grad_heads = grad_attn.reshape(blocks, BLK, head_count, DH)
    grad_prob = jnp.einsum(
        "bqhd,bkhd->bhqk", grad_heads, value_heads, preferred_element_type=jnp.float32
    )
    row_delta = jnp.sum(attn_prob * grad_prob, axis=-1, keepdims=True)
    grad_score = (attn_prob * (grad_prob - row_delta)).astype(jnp.bfloat16)
    grad_query = (
        (
            jnp.einsum("bhqk,bkhd->bqhd", grad_score, key_heads, preferred_element_type=jnp.float32)
            * score_scale
        )
        .astype(jnp.bfloat16)
        .reshape(row_count, features)
    )
    grad_keyset = (
        jnp.einsum("bhqk,bqhd->bkhd", grad_score, query_heads, preferred_element_type=jnp.float32)
        * score_scale
    )
    grad_valset = jnp.einsum(
        "bhqk,bqhd->bkhd", prob_low, grad_heads, preferred_element_type=jnp.float32
    )
    grad_sets = jnp.stack([grad_keyset, grad_valset]).reshape(2, blocks, keys_all, features)
    token_grad = grad_sets[:, :, :BLK].reshape(2, row_count, features)
    for level_idx in range(local_levels):
        factor = 2**level_idx
        group_count = blocks >> level_idx
        lower = (level_idx + 1) * BLK
        segment = (
            grad_sets[:, :, lower : lower + BLK]
            .reshape(2, group_count, factor, BLK, features)
            .sum(axis=2)
        )
        restored = segment.reshape(2, group_count // 2, 2, BLK, features)[:, :, ::-1].reshape(
            2, group_count * BLK, features
        )
        token_grad = token_grad + spread_rows(restored, factor)
    sibling_grads = []
    for level_idx in range(cross_levels):
        lower = (local_levels + 1 + level_idx) * BLK
        sibling_grads.append(jnp.sum(grad_sets[:, :, lower : lower + BLK], axis=1))
    carried = jnp.zeros((2, BLK, features), jnp.float32)
    for level_idx in reversed(range(cross_levels)):
        outgoing = sibling_grads[level_idx]
        if level_idx + 1 < cross_levels:
            halves = spread_rows(carried, 2)
            lower_part = halves[:, :BLK]
            upper_part = halves[:, BLK:]
            upper_half = jnp.right_shift(where_seq, level_idx) & 1 == 1
            own_part = jnp.where(upper_half, upper_part, lower_part)
            outgoing = outgoing + jnp.where(upper_half, lower_part, upper_part)
        else:
            own_part = jnp.zeros_like(outgoing)
        carried = own_part + swapped(outgoing, "seq", level_idx)
    token_grad = token_grad + spread_rows(carried, 2**local_levels)
    grad_keys = token_grad[0].astype(jnp.bfloat16)
    grad_values = token_grad[1].astype(jnp.bfloat16)
    return (output, grad_query, grad_keys, grad_values, grad_weight)


def solution(mesh):
    placed = (
        P("seq", "head"),
        P("seq", "head"),
        P("seq", "head"),
        P("head", None),
        P("seq", "head"),
        P("seq", None),
    )
    return jax.shard_map(
        body,
        mesh=mesh,
        in_specs=placed,
        out_specs=(
            P("seq", "head"),
            P("seq", "head"),
            P("seq", "head"),
            P("seq", "head"),
            P("seq", "head"),
        ),
        check_vma=False,
    )
```

profile of v0, /device:TPU:0, one launch (start us, length us, event | category | flops | bytes accessed | tf_op | source)
XLA Modules:
  0.0 653.6 jit_solution(3892878592659367330)
XLA Ops:
  55.0 8.0 %collective-permute-done.1 = f32[2,128,512]{2,0,1:T(2,128)} collective-permute-done((f32[2,128,512]{2,0,1:T(2,128)}, f32[2,128,512]{2,0,1:T(2,128)}, u32[]{:S(2)}, u32[]{:S(2)}) %collective-permute-start.1) | collective-permute-done | bytes 524320 | tf_op jit(solution)/shard_map/ppermute | solution.py:18
  72.5 7.7 %collective-permute-done.2 = f32[2,128,512]{2,0,1:T(2,128)S(1)} collective-permute-done((f32[2,128,512]{2,0,1:T(2,128)S(1)}, f32[2,128,512]{2,0,1:T(2,128)S(1)}, u32[]{:S(2)}, u32[]{:S(2)}) %collective-permute-start.2) | collective-permute-done | bytes 524320 | tf_op jit(solution)/shard_map/ppermute | solution.py:18
  92.4 11.4 %fusion.43 = (bf16[1,8,1024,512]{3,2,1,0:T(8,128)(2,1)}, bf16[1,8,1024,512]{3,2,1,0:T(8,128)(2,1)}) fusion(bf16[2,8,1024,512]{3,2,1,0:T(8,128)(2,1)} %broadcast_dynamic-update-slice_fusion), kind=kLoop, calls=%fused_computation.102 | loop fusion | bytes 33554432 | tf_op jit(solution)/shard_map/slice | solution.py:106
  103.8 11.4 %copy.175 = bf16[1,8,1024,512]{2,3,1,0:T(8,128)(2,1)} copy(bf16[1,8,1024,512]{3,2,1,0:T(8,128)(2,1)} %get-tuple-element.43) | data formatting | bytes 16777216 | tf_op jit(solution)/shard_map/slice | solution.py:106
  115.2 11.5 %copy.173 = bf16[1,8,1024,512]{2,3,1,0:T(8,128)(2,1)} copy(bf16[1,8,1024,512]{3,2,1,0:T(8,128)(2,1)} %get-tuple-element.44) | data formatting | bytes 16777216 | tf_op jit(solution)/shard_map/slice | solution.py:107
  126.8 12.9 %fusion.45 = (f32[8,4,128]{2,1,0:T(4,128)S(1)}, f32[8,4,128,1024]{2,3,1,0:T(8,128)}) fusion(f32[1024]{0:T(1024)S(1)} %copy-done.10, pred[8,1024]{1,0:T(8,128)(4,1)S(1)} %concatenate.37, bf16[8,1024,4,128]{1,3,2,0:T(8,128)(2,1)} %bitcast.122, bf16[8,128,4,128]{1,3,2,0:T(8,128)(2,1)S(1)} %copy.187), kind=kOutput, calls=%fused_computation.104 | convolution fusion | flops 1094714368 | bytes 26243072 | tf_op jit(solution)/shard_map/sub | solution.py:115
  139.6 10.7 %fusion.30 = bf16[8,128,4,128]{1,3,2,0:T(8,128)(2,1)S(1)} fusion(bf16[8,1024,4,128]{1,3,2,0:T(8,128)(2,1)} %bitcast.124, f32[8,4,128,1024]{2,3,1,0:T(8,128)} %get-tuple-element.50, f32[8,4,128]{2,1,0:T(4,128)S(1)} %get-tuple-element.49), kind=kOutput, calls=%fused_computation.60 | convolution fusion | flops 1082654720 | bytes 26230784 | tf_op jit(solution)/shard_map/bhqk,bkhd->bqhd/dot_general | solution.py:118
  151.0 40.7 %all-gather.2.cloned.1.call-done = bf16[1024,4096]{1,0:T(8,128)(2,1)} async-done(((bf16[1024,512]{1,0:T(8,128)(2,1)}), bf16[1024,4096]{1,0:T(8,128)(2,1)}) %all-gather.2.cloned.1.call-update) | async-done | bytes 8388624 | tf_op jit(solution)/shard_map/all_gather | solution.py:124
  191.7 10.0 %convolution_bitcast_fusion = f32[4096,512]{0,1:T(8,128)} fusion(bf16[1024,4096]{1,0:T(8,128)(2,1)} %all-gather.2.cloned.1.call-done, bf16[64,8,8,128]{3,2,1,0:T(8,128)(2,1)S(1)} %bitcast.133), kind=kOutput, calls=%fused_computation.28 | convolution fusion | flops 4294967296 | bytes 17825792 | tf_op jit(solution)/shard_map/dot_general | solution.py:129
  201.8 10.8 %fusion.35 = f32[1024,4096]{1,0:T(8,128)} fusion(bf16[512,4096]{1,0:T(8,128)(2,1)} %param.9, bf16[64,8,8,128]{3,2,1,0:T(8,128)(2,1)S(1)} %bitcast.134), kind=kOutput, calls=%fused_computation.64 | convolution fusion | flops 4294967296 | bytes 22020096 | tf_op jit(solution)/shard_map/dot_general | solution.py:120
  212.6 10.3 %convolution_convert_fusion = bf16[1024,512]{1,0:T(8,128)(2,1)S(1)} fusion(bf16[1024,4096]{1,0:T(8,128)(2,1)} %all-gather.2.cloned.1.call-done, bf16[512,4096]{1,0:T(8,128)(2,1)} %param.9), kind=kOutput, calls=%fused_computation.58 | convolution fusion | flops 4295491584 | bytes 13631488 | tf_op jit(solution)/shard_map/dot_general | solution.py:125
  223.9 16.4 %multiply_reduce_fusion = (f32[8,4,128]{2,1,0:T(4,128)S(1)}, f32[8,4,128,1024]{2,3,1,0:T(8,128)}) fusion(f32[8,4,128,1024]{2,3,1,0:T(8,128)} %get-tuple-element.50, f32[8,4,128]{2,1,0:T(4,128)S(1)} %get-tuple-element.49, bf16[8,128,4,128]{1,3,2,0:T(8,128)(2,1)S(1)} %copy.190, bf16[8,1024,4,128]{1,3,2,0:T(8,128)(2,1)} %bitcast.125), kind=kOutput, calls=%fused_computation.21 | convolution fusion | flops 1086320640 | bytes 43024384 | tf_op jit(solution)/shard_map/bqhd,bkhd->bhqk/dot_general | solution.py:137
  240.2 11.5 %multiply_convert_fusion = bf16[8,4,128,1024]{2,3,1,0:T(8,128)(2,1)S(1)} fusion(f32[8,4,128,1024]{2,3,1,0:T(8,128)} %get-tuple-element.52, f32[8,4,128]{2,1,0:T(4,128)S(1)} %get-tuple-element.51, f32[8,4,128,1024]{2,3,1,0:T(8,128)} %get-tuple-element.50, f32[8,4,128]{2,1,0:T(4,128)S(1)} %get-tuple-element.49), kind=kLoop, calls=%fused_computation.20 | loop fusion | flops 16777216 | bytes 41975808 | tf_op jit(solution)/shard_map/convert_element_type | solution.py:141
  255.0 7.1 %multiply_bitcast_fusion = f32[8,1024,4,128]{3,1,2,0:T(8,128)} fusion(bf16[8,4,128,1024]{2,3,1,0:T(8,128)(2,1)S(1)} %multiply_convert_fusion, bf16[8,128,4,128]{1,3,2,0:T(8,128)(2,1)S(1)} %copy.187), kind=kOutput, calls=%fused_computation.19 | convolution fusion | flops 1077936128 | bytes 26214400 | tf_op jit(solution)/shard_map/bhqk,bqhd->bkhd/dot_general | solution.py:151
  262.1 16.7 %copy.189 = f32[8,1024,4,128]{1,3,2,0:T(8,128)} copy(f32[8,1024,4,128]{3,1,2,0:T(8,128)} %multiply_bitcast_fusion) | data formatting | bytes 33554432 | tf_op jit(solution)/shard_map/mul | solution.py:151
  278.8 13.8 %fusion.20 = f32[8,4,128,1024]{3,2,1,0:T(8,128)} fusion(bf16[8,128,4,128]{1,3,2,0:T(8,128)(2,1)S(1)} %copy.190, f32[8,4,128,1024]{2,3,1,0:T(8,128)} %get-tuple-element.50, f32[8,4,128]{2,1,0:T(4,128)S(1)} %get-tuple-element.49), kind=kOutput, calls=%fused_computation.43 | convolution fusion | flops 1082130432 | bytes 34619392 | tf_op jit(solution)/shard_map/bhqk,bqhd->bkhd/dot_general | solution.py:154
  292.7 19.0 %fusion.25 = (f32[2,128,512]{1,2,0:T(8,128)S(1)}, f32[2,128,512]{1,2,0:T(8,128)S(1)}, f32[2,128,512]{1,2,0:T(8,128)S(1)}, f32[2,128,512]{1,2,0:T(8,128)S(1)}, f3...) fusion(f32[1,8,1024,512]{2,3,1,0:T(8,128)} %bitcast.111, ...), kind=kLoop, calls=%fused_computation.51 | loop fusion | flops 12058624 | bytes 52428800 | tf_op jit(solution)/shard_map/reduce_sum | solution.py:175
  315.6 11.9 %collective-permute-done.4 = f32[2,128,512]{2,0,1:T(2,128)S(1)} collective-permute-done((f32[2,128,512]{2,0,1:T(2,128)S(1)}, f32[2,128,512]{2,0,1:T(2,128)S(1)}, u32[]{:S(2)}, u32[]{:S(2)}) %collective-permute-start.4) | collective-permute-done | bytes 524320 | tf_op jit(solution)/shard_map/ppermute | solution.py:18
  330.9 11.7 %collective-permute-done.5 = f32[2,128,512]{2,0,1:T(2,128)S(1)} collective-permute-done((f32[2,128,512]{2,0,1:T(2,128)}, f32[2,128,512]{2,0,1:T(2,128)S(1)}, u32[]{:S(2)}, u32[]{:S(2)}) %collective-permute-start.5) | collective-permute-done | bytes 524320 | tf_op jit(solution)/shard_map/ppermute | solution.py:18
  346.6 24.0 %collective-permute-done.6 = f32[2,128,512]{2,0,1:T(2,128)S(1)} collective-permute-done((f32[2,128,512]{2,0,1:T(2,128)S(1)}, f32[2,128,512]{2,0,1:T(2,128)S(1)}, u32[]{:S(2)}, u32[]{:S(2)}) %collective-permute-start.6) | collective-permute-done | bytes 524320 | tf_op jit(solution)/shard_map/ppermute | solution.py:18
  372.7 8.2 %fusion.33 = bf16[8,128,4,128]{1,3,2,0:T(8,128)(2,1)S(1)} fusion(bf16[8,1024,4,128]{1,3,2,0:T(8,128)(2,1)} %bitcast.123, bf16[8,4,128,1024]{2,3,1,0:T(8,128)(2,1)} %copy-done), kind=kOutput, calls=%fused_computation.61 | convolution fusion | flops 1074790400 | bytes 17825792 | tf_op jit(solution)/shard_map/bhqk,bkhd->bqhd/dot_general | solution.py:144
  397.9 6.0 reshape.172
  428.6 7.8 %fusion.17 = bf16[2,1024,512]{2,1,0:T(8,128)(2,1)S(1)} fusion(f32[2,1024,512]{2,1,0:T(8,128)} %reshape.174, f32[2,1024,512]{2,1,0:T(8,128)} %reshape.172, f32[2,4,2,128,512]{4,3,2,1,0:T(8,128)} %copy.193, f32[2,8,128,512]{3,2,1,0:T(8,128)} %copy.192, f32[2,128,512]{2,1,0:T(8,128)S(1)} %add_multiply_fusion), kind=kLoop, calls=%fused_computation.39 | loop fusion | flops 5242880 | bytes 19398656 | tf_op jit(solution)/shard_map/convert.1
  439.9 204.1 %reduce-scatter.3.cloned.1.call-done = f32[1024,512]{1,0:T(8,128)} async-done(((f32[1024,4096]{1,0:T(8,128)}), f32[1024,512]{1,0:T(8,128)}) %reduce-scatter.3.cloned.1.call-update) | async-done | bytes 2097168 | tf_op jit(solution)/shard_map/reduce_scatter | solution.py:121
  (118 shorter events, 135.5 us)
Async XLA Ops:
  7.2 10.8 %copy-start.2 = (bf16[1024,512]{1,0:T(8,128)(2,1)S(1)}, bf16[1024,512]{1,0:T(8,128)(2,1)}, u32[]{:S(2)}) copy-start(bf16[1024,512]{1,0:T(8,128)(2,1)} %param.7) | copy-start | bytes 3145732
  7.2 8.2 %copy-start.1 = (bf16[1024,512]{1,0:T(8,128)(2,1)S(1)}, bf16[1024,512]{1,0:T(8,128)(2,1)}, u32[]{:S(2)}) copy-start(bf16[1024,512]{1,0:T(8,128)(2,1)} %param.8) | copy-start | bytes 3145732
  7.2 10.7 %copy-start.9 = (s32[8,7]{1,0:T(8,128)S(1)}, s32[8,7]{1,0:T(8,128)}, u32[]{:S(2)}) copy-start(s32[8,7]{1,0:T(8,128)} %param.11) | copy-start | bytes 676
  7.2 184.5 %all-gather.2.cloned.1.call-start = ((), (), s32[]{:S(2)}) async-start(), calls=%async_computation.3 | async-start | bytes 9437184 | tf_op jit(solution)/shard_map/all_gather | solution.py:124
  7.9 429.9 %reduce-scatter.5.cloned.1.call-start = ((), (), s32[]{:S(2)}) async-start(), calls=%async_computation.4 | async-start | bytes 8912896 | tf_op jit(solution)/shard_map/reduce_scatter | solution.py:128
  11.8 19.4 %collective-permute-start = (f32[2,128,512]{2,1,0:T(8,128)}, f32[2,128,512]{2,1,0:T(8,128)}, u32[]{:S(2)}, u32[]{:S(2)}) collective-permute-start(f32[2,128,512]{2,1,0:T(8,128)} %broadcast_multiply_fusion.4), channel_id=1, source_target_pairs={{0,8},{8,0},{16,24},{24,16},{32,40},{40,32},{48,56},{56,48},{64,72... | collective-permute-start | bytes 1572872 | tf_op jit(solution)/shard_map/ppermute | solution.py:18
  18.0 3.0 copy-start.4
  18.0 6.0 copy-start.5
  18.0 6.0 copy-start.6
  23.9 15.3 %copy-start.8 = (bf16[1024,512]{1,0:T(8,128)(2,1)S(1)}, bf16[1024,512]{1,0:T(8,128)(2,1)}, u32[]{:S(2)}) copy-start(bf16[1024,512]{1,0:T(8,128)(2,1)} %param.6) | copy-start | bytes 3145732
  29.9 14.8 %copy-start.3 = (bf16[2,4,2,128,512]{4,3,2,1,0:T(8,128)(2,1)S(1)}, bf16[2,4,2,128,512]{4,3,2,1,0:T(8,128)(2,1)}, u32[]{:S(2)}) copy-start(bf16[2,4,2,128,512]{4,3,2,1,0:T(8,128)(2,1)} %pad_maximum_fusion.1) | copy-start | bytes 6291460
  35.2 27.7 %collective-permute-start.1 = (f32[2,128,512]{2,0,1:T(2,128)}, f32[2,128,512]{2,0,1:T(2,128)}, u32[]{:S(2)}, u32[]{:S(2)}) collective-permute-start(f32[2,128,512]{2,0,1:T(2,128)} %broadcast_multiply_fusion.3), channel_id=1, source_target_pairs={{0,16},{8,24},{16,0},{24,8},{32,48},{40,56},{48,32},{56,40},{64,80... | collective-permute-start | bytes 1572872 | tf_op jit(solution)/shard_map/ppermute | solution.py:18
  46.2 6.1 copy-start.7
  66.2 14.0 %collective-permute-start.2 = (f32[2,128,512]{2,0,1:T(2,128)S(1)}, f32[2,128,512]{2,0,1:T(2,128)S(1)}, u32[]{:S(2)}, u32[]{:S(2)}) collective-permute-start(f32[2,128,512]{2,0,1:T(2,128)S(1)} %broadcast_multiply_fusion.2), channel_id=1, source_target_pairs={{0,32},{8,40},{16,48},{24,56},{32,0},{40,8},{48,16},{56,24},{64,96... | collective-permute-start | bytes 1572872 | tf_op jit(solution)/shard_map/ppermute | solution.py:18
  81.7 9.2 %collective-permute-start.3 = (bf16[2,128,512]{2,0,1:T(2,128)(2,1)S(1)}, bf16[2,128,512]{2,0,1:T(2,128)(2,1)S(1)}, u32[]{:S(2)}, u32[]{:S(2)}) collective-permute-start(bf16[2,128,512]{2,0,1:T(2,128)(2,1)S(1)} %broadcast_multiply_fusion.1), channel_id=1, source_target_pairs={{0,64},{8,72},{16,80},{24,88},{32,96},{40,104},{48,112},{56,120},{... | collective-permute-start | bytes 786440 | tf_op jit(solution)/shard_map/ppermute | solution.py:18
  115.2 11.5 %copy-start.10 = (f32[1024]{0:T(1024)S(1)}, f32[1024]{0:T(1024)}, u32[]{:S(2)}) copy-start(f32[1024]{0:T(1024)} %constant.9.clone.1) | copy-start | bytes 12292
  201.7 442.3 %reduce-scatter.3.cloned.1.call-start = ((), (), s32[]{:S(2)}) async-start(), calls=%async_computation.2 | async-start | bytes 18874368 | tf_op jit(solution)/shard_map/reduce_scatter | solution.py:121
  251.8 3.2 copy-start
  311.9 15.6 %collective-permute-start.4 = (f32[2,128,512]{2,0,1:T(2,128)S(1)}, f32[2,128,512]{2,0,1:T(2,128)S(1)}, u32[]{:S(2)}, u32[]{:S(2)}) collective-permute-start(f32[2,128,512]{2,0,1:T(2,128)S(1)} %copy.196), channel_id=1, source_target_pairs={{0,64},{8,72},{16,80},{24,88},{32,96},{40,104},{48,112},{56,120},{... | collective-permute-start | bytes 1572872 | tf_op jit(solution)/shard_map/ppermute | solution.py:18
  329.1 13.5 %collective-permute-start.5 = (f32[2,128,512]{2,0,1:T(2,128)}, f32[2,128,512]{2,0,1:T(2,128)S(1)}, u32[]{:S(2)}, u32[]{:S(2)}) collective-permute-start(f32[2,128,512]{2,0,1:T(2,128)} %select_add_fusion.2), channel_id=1, source_target_pairs={{0,32},{8,40},{16,48},{24,56},{32,0},{40,8},{48,16},{56,24},{64,96... | collective-permute-start | bytes 1572872 | tf_op jit(solution)/shard_map/ppermute | solution.py:18
  343.7 26.9 %collective-permute-start.6 = (f32[2,128,512]{2,0,1:T(2,128)S(1)}, f32[2,128,512]{2,0,1:T(2,128)S(1)}, u32[]{:S(2)}, u32[]{:S(2)}) collective-permute-start(f32[2,128,512]{2,0,1:T(2,128)S(1)} %select_add_fusion.1), channel_id=1, source_target_pairs={{0,16},{8,24},{16,0},{24,8},{32,48},{40,56},{48,32},{56,40},{64,80... | collective-permute-start | bytes 1572872 | tf_op jit(solution)/shard_map/ppermute | solution.py:18
  372.7 54.6 %collective-permute-start.7 = (f32[2,128,512]{2,1,0:T(8,128)}, f32[2,128,512]{2,1,0:T(8,128)}, u32[]{:S(2)}, u32[]{:S(2)}) collective-permute-start(f32[2,128,512]{2,1,0:T(8,128)} %select_add_fusion), channel_id=1, source_target_pairs={{0,8},{8,0},{16,24},{24,16},{32,40},{40,32},{48,56},{56,48},{64,72... | collective-permute-start | bytes 1572872 | tf_op jit(solution)/shard_map/ppermute | solution.py:18
Sparse Core Ops, SparseCore 0:
  9.7 181.9 all-gather.1
  201.8 103.2 reduce-scatter.4
  307.6 336.4 reduce-scatter.2
where the time goes:
time: 659 us; the launch traced here: 654 us
  waiting for transfers between devices  313 us (47%)
  local copies, waits for them, and re-layouts  126 us (19%)
  matrix products  100 us (15%)
  other arithmetic  83.2 us (13%)
  starting transfers between devices  16.8 us (3%)
  between operations  14.4 us (2%)
    reduce_scatter x1, waiting for transfers between devices, body(): lax.psum_scatter(partial_out, 'head', scatter_dimension=1, tiled=True)  204 us
    ppermute x8, waiting for transfers between devices, swapped(): return lax.ppermute(value, axis, pairs)  67.2 us
    all_gather x1, waiting for transfers between devices, body(): grads_full = lax.all_gather(cotangent, 'head', axis=1, tiled=True)  40.7 us
    slice x2, local copies, waits for them, and re-layouts, body(): key_heads = key_set[0].reshape(blocks, keys_all, head_count, DH)  22.8 us
    reduce_sum x1, other arithmetic, body(): sibling_grads.append(jnp.sum(grad_sets[:, :, lower:lower + BLK], axis=1))  19 us
    unnamed x31, local copies, waits for them, and re-layouts  17.9 us
    mul x1, local copies, waits for them, and re-layouts, body(): jnp.einsum('bhqk,bqhd->bkhd', grad_score, query_heads, preferred_element_...  16.7 us
    ppermute x8, starting transfers between devices, swapped(): return lax.ppermute(value, axis, pairs)  16.7 us
  transfers between devices with their start and end apart: 11, of which 8 were waited for; matrix products, arithmetic and copies ran while one was open for 45% of the time, Pallas kernels for 0%

commit v1 on v0

--- a/solution.py
+++ b/solution.py
@@ -30,6 +30,56 @@
         1.0 / factor
     )
     return wide.reshape(shape_in[:-2] + (shape_in[-2] * factor, shape_in[-1]))
+
+
+def head_ring_gather(value):
+    count = lax.axis_size("head")
+    rings = count // 2
+    width = value.shape[-1]
+    where_head = lax.axis_index("head")
+    ring_pos = where_head // 2
+    partner = lax.ppermute(value, "head", [(src, src ^ 1) for src in range(count)])
+    low_first = where_head % 2 == 0
+    pair_block = jnp.concatenate(
+        [jnp.where(low_first, value, partner), jnp.where(low_first, partner, value)], axis=-1
+    )
+    upward = [(src, ((src // 2 + 1) % rings) * 2 + src % 2) for src in range(count)]
+    downward = [(src, ((src // 2 - 1) % rings) * 2 + src % 2) for src in range(count)]
+    from_below = lax.ppermute(pair_block, "head", upward)
+    from_above = lax.ppermute(pair_block, "head", downward)
+    blocks = [pair_block, from_above]
+    if rings == 4:
+        far = jnp.concatenate(
+            [
+                lax.ppermute(from_below[..., :width], "head", upward),
+                lax.ppermute(from_above[..., width:], "head", downward),
+            ],
+            axis=-1,
+        )
+        blocks = [pair_block, from_above, far, from_below]
+    stacked = jnp.stack(blocks)
+    order = (jnp.arange(rings) - ring_pos) % rings
+    placed = stacked[order]
+    return jnp.moveaxis(placed, 0, -2).reshape(value.shape[:-1] + (rings * 2 * width,))
+
+
+def weight_columns(out_weight):
+    count = lax.axis_size("head")
+    where_head = lax.axis_index("head")
+    rows, cols = out_weight.shape
+    width = cols // count
+    pieces = [lax.dynamic_slice_in_dim(out_weight, where_head * width, width, axis=1)]
+    for shift in range(1, count):
+        outgoing = lax.dynamic_slice_in_dim(
+            out_weight, ((where_head + shift) % count) * width, width, axis=1
+        )
+        pieces.append(
+            lax.ppermute(outgoing, "head", [(src, (src + shift) % count) for src in range(count)])
+        )
+    stacked = jnp.stack(pieces)
+    order = (where_head - jnp.arange(count)) % count
+    placed = jnp.zeros_like(stacked).at[order].set(stacked)
+    return placed.reshape(count * rows, width)
 
 
 def body(queries, key_rows, value_rows, out_weight, cotangent, pattern):
@@ -117,10 +167,10 @@
     prob_low = attn_prob.astype(jnp.bfloat16)
     mixed = jnp.einsum("bhqk,bkhd->bqhd", prob_low, value_heads, preferred_element_type=jnp.float32)
     attended = mixed.astype(jnp.bfloat16).reshape(row_count, features)
-    partial_out = jnp.dot(attended, out_weight, preferred_element_type=jnp.float32)
-    output = lax.psum_scatter(partial_out, "head", scatter_dimension=1, tiled=True).astype(
-        jnp.bfloat16
-    )
+    attended_full = head_ring_gather(attended)
+    output = jnp.dot(
+        attended_full, weight_columns(out_weight), preferred_element_type=jnp.float32
+    ).astype(jnp.bfloat16)
     grads_full = lax.all_gather(cotangent, "head", axis=1, tiled=True)
     grad_attn = lax.dot_general(
         grads_full, out_weight, (((1,), (1,)), ((), ())), preferred_element_type=jnp.float32

time: 659 us -> 598 us (0.907)
  the two profiles are of different devices: /device:TPU:0 before, /device:TPU:15 now
where the time goes in v1:
time: 598 us; the launch traced here: 593 us
  local copies, waits for them, and re-layouts  176 us (29%)
  waiting for transfers between devices  163 us (27%)
  other arithmetic  102 us (17%)
  matrix products  96.2 us (16%)
  starting transfers between devices  41.7 us (7%)
  between operations  15 us (3%)
    ppermute x7, waiting for transfers between devices, weight_columns(): lax.ppermute(outgoing, 'head', [(src, (src + shift) % count) for src in r...  75.9 us
    ppermute x1, waiting for transfers between devices, head_ring_gather(): lax.ppermute(value, 'head', [(src, src ^ 1) for src in range(count)])  46.6 us
    ppermute x8, waiting for transfers between devices, swapped(): return lax.ppermute(value, axis, pairs)  31.9 us
    unnamed x49, local copies, waits for them, and re-layouts  28.3 us
    ppermute x7, starting transfers between devices, weight_columns(): lax.ppermute(outgoing, 'head', [(src, (src + shift) % count) for src in r...  27.8 us
    slice x2, local copies, waits for them, and re-layouts, body(): key_heads = key_set[0].reshape(blocks, keys_all, head_count, DH)  22.9 us
    reduce_sum x1, other arithmetic, body(): sibling_grads.append(jnp.sum(grad_sets[:, :, lower:lower + BLK], axis=1))  19.2 us
    mul x1, local copies, waits for them, and re-layouts, body(): jnp.einsum('bhqk,bqhd->bkhd', grad_score, query_heads, preferred_element_...  16.9 us
  transfers between devices with their start and end apart: 22, of which 11 were waited for; matrix products, arithmetic and copies ran while one was open for 59% of the time, Pallas kernels for 0%

profile of v1, /device:TPU:15, one launch (start us, length us, event | category | flops | bytes accessed | tf_op | source)
XLA Modules:
  0.0 592.7 jit_solution(5698508017065120775)
XLA Ops:
  53.5 8.8 %collective-permute-done.1 = f32[2,128,512]{2,0,1:T(2,128)} collective-permute-done((f32[2,128,512]{2,0,1:T(2,128)}, f32[2,128,512]{2,0,1:T(2,128)}, u32[]{:S(2)}, u32[]{:S(2)}) %collective-permute-start.1) | collective-permute-done | bytes 524320 | tf_op jit(solution)/shard_map/ppermute | solution.py:18
  90.4 11.4 %fusion.43 = (bf16[1,8,1024,512]{3,2,1,0:T(8,128)(2,1)}, bf16[1,8,1024,512]{3,2,1,0:T(8,128)(2,1)}) fusion(bf16[2,8,1024,512]{3,2,1,0:T(8,128)(2,1)} %broadcast_dynamic-update-slice_fusion), kind=kLoop, calls=%fused_computation.137 | loop fusion | bytes 33554432 | tf_op jit(solution)/shard_map/slice | solution.py:156
  101.8 11.5 %copy.175 = bf16[1,8,1024,512]{2,3,1,0:T(8,128)(2,1)} copy(bf16[1,8,1024,512]{3,2,1,0:T(8,128)(2,1)} %get-tuple-element.43) | data formatting | bytes 16777216 | tf_op jit(solution)/shard_map/slice | solution.py:156
  113.3 11.5 %copy.173 = bf16[1,8,1024,512]{2,3,1,0:T(8,128)(2,1)} copy(bf16[1,8,1024,512]{3,2,1,0:T(8,128)(2,1)} %get-tuple-element.44) | data formatting | bytes 16777216 | tf_op jit(solution)/shard_map/slice | solution.py:157
  124.8 12.9 %fusion.46 = (f32[8,4,128]{2,1,0:T(4,128)S(1)}, f32[8,4,128,1024]{2,3,1,0:T(8,128)}) fusion(f32[1024]{0:T(1024)S(1)} %copy-done.15, pred[8,1024]{1,0:T(8,128)(4,1)S(1)} %concatenate.43, bf16[8,1024,4,128]{1,3,2,0:T(8,128)(2,1)} %bitcast.161, bf16[8,128,4,128]{1,3,2,0:T(8,128)(2,1)S(1)} %copy.187), kind=kOutput, calls=%fused_computation.140 | convolution fusion | flops 1094714368 | bytes 26243072 | tf_op jit(solution)/shard_map/sub | solution.py:165
  137.7 10.7 %fusion.30 = bf16[8,128,4,128]{1,3,2,0:T(8,128)(2,1)S(1)} fusion(bf16[8,1024,4,128]{1,3,2,0:T(8,128)(2,1)} %bitcast.163, f32[8,4,128,1024]{2,3,1,0:T(8,128)} %get-tuple-element.63, f32[8,4,128]{2,1,0:T(4,128)S(1)} %get-tuple-element.62), kind=kOutput, calls=%fused_computation.68 | convolution fusion | flops 1082654720 | bytes 26230784 | tf_op jit(solution)/shard_map/bhqk,bkhd->bqhd/dot_general | solution.py:168
  149.9 46.6 %collective-permute-done.4 = bf16[1024,512]{0,1:T(8,128)(2,1)S(1)} collective-permute-done((bf16[1024,512]{0,1:T(8,128)(2,1)S(1)}, bf16[1024,512]{0,1:T(8,128)(2,1)S(1)}, u32[]{:S(2)}, u32[]{:S(2)}) %collective-permute-start.4) | collective-permute-done | bytes 1048608 | tf_op jit(solution)/shard_map/ppermute | solution.py:41
  210.5 12.7 %collective-permute-done.9 = bf16[512,512]{1,0:T(8,128)(2,1)} collective-permute-done((bf16[512,512]{1,0:T(8,128)(2,1)}, bf16[512,512]{1,0:T(8,128)(2,1)}, u32[]{:S(2)}, u32[]{:S(2)}) %collective-permute-start.9) | collective-permute-done | bytes 524320 | tf_op jit(solution)/shard_map/ppermute | solution.py:77
  226.9 40.5 %collective-permute-done.10 = bf16[512,512]{1,0:T(8,128)(2,1)} collective-permute-done((bf16[512,512]{1,0:T(8,128)(2,1)}, bf16[512,512]{1,0:T(8,128)(2,1)}, u32[]{:S(2)}, u32[]{:S(2)}) %collective-permute-start.10) | collective-permute-done | bytes 524320 | tf_op jit(solution)/shard_map/ppermute | solution.py:77
  267.5 20.0 %collective-permute-start.13 = (bf16[512,512]{1,0:T(8,128)(2,1)}, bf16[512,512]{1,0:T(8,128)(2,1)S(1)}, u32[]{:S(2)}, u32[]{:S(2)}) collective-permute-start(bf16[512,512]{1,0:T(8,128)(2,1)} %get-tuple-element.49), channel_id=1, source_target_pairs={{0,5},{1,6},{2,7},{3,0},{4,1},{5,2},{6,3},{7,4},{8,13},{9,14},{10,... | collective-permute-start | bytes 1572872 | tf_op jit(solution)/shard_map/ppermute | solution.py:77
  300.4 22.7 %collective-permute-done.14 = bf16[512,512]{1,0:T(8,128)(2,1)S(1)} collective-permute-done((bf16[512,512]{1,0:T(8,128)(2,1)}, bf16[512,512]{1,0:T(8,128)(2,1)S(1)}, u32[]{:S(2)}, u32[]{:S(2)}) %collective-permute-start.14) | collective-permute-done | bytes 524320 | tf_op jit(solution)/shard_map/ppermute | solution.py:77
  327.0 11.0 %scatter_fusion = bf16[8,512,512]{2,1,0:T(8,128)(2,1)} fusion(bf16[8,512,512]{2,1,0:T(8,128)(2,1)} %broadcast_in_dim.55, s32[8]{0:T(128)S(1)} %fusion.39, bf16[8,512,512]{2,1,0:T(8,128)(2,1)} %bitcast_dynamic-update-slice_fusion), kind=kCustom, calls=%fused_computation.2 | custom fusion | bytes 12582944 | tf_op jit(solution)/shard_map/scatter | solution.py:81
  338.0 7.6 %collective-permute-done.8 = bf16[1024,512]{0,1:T(8,128)(2,1)} collective-permute-done((bf16[1024,512]{0,1:T(8,128)(2,1)}, bf16[1024,512]{0,1:T(8,128)(2,1)}, u32[]{:S(2)}, u32[]{:S(2)}) %collective-permute-start.8) | collective-permute-done | bytes 1048608 | tf_op jit(solution)/shard_map/ppermute | solution.py:55
  353.4 9.1 %convolution_convert_fusion = bf16[1024,512]{1,0:T(8,128)(2,1)S(1)} fusion(bf16[1024,4096]{1,0:T(8,128)(2,1)} %all-gather.2.cloned.1.call-done, bf16[512,4096]{1,0:T(8,128)(2,1)} %param.9), kind=kOutput, calls=%fused_computation.65 | convolution fusion | flops 4295491584 | bytes 13631488 | tf_op jit(solution)/shard_map/dot_general | solution.py:175
  363.5 10.0 %convolution_bitcast_fusion = f32[4096,512]{0,1:T(8,128)} fusion(bf16[1024,4096]{1,0:T(8,128)(2,1)} %all-gather.2.cloned.1.call-done, bf16[64,8,8,128]{3,2,1,0:T(8,128)(2,1)S(1)} %bitcast.153), kind=kOutput, calls=%fused_computation.33 | convolution fusion | flops 4294967296 | bytes 17825792 | tf_op jit(solution)/shard_map/dot_general | solution.py:179
  373.6 15.7 %multiply_reduce_fusion = (f32[8,4,128]{2,1,0:T(4,128)S(1)}, f32[8,4,128,1024]{2,3,1,0:T(8,128)}) fusion(f32[8,4,128,1024]{2,3,1,0:T(8,128)} %get-tuple-element.63, f32[8,4,128]{2,1,0:T(4,128)S(1)} %get-tuple-element.62, bf16[8,128,4,128]{1,3,2,0:T(8,128)(2,1)S(1)} %copy.190, bf16[8,1024,4,128]{1,3,2,0:T(8,128)(2,1)} %bitcast.164), kind=kOutput, calls=%fused_computation.24 | convolution fusion | flops 1086320640 | bytes 43024384 | tf_op jit(solution)/shard_map/bqhd,bkhd->bhqk/dot_general | solution.py:187
  389.3 13.7 %multiply_convert_fusion = bf16[8,4,128,1024]{2,3,1,0:T(8,128)(2,1)S(1)} fusion(f32[8,4,128,1024]{2,3,1,0:T(8,128)} %get-tuple-element.65, f32[8,4,128]{2,1,0:T(4,128)S(1)} %get-tuple-element.64, f32[8,4,128,1024]{2,3,1,0:T(8,128)} %get-tuple-element.63, f32[8,4,128]{2,1,0:T(4,128)S(1)} %get-tuple-element.62), kind=kLoop, calls=%fused_computation.23 | loop fusion | flops 16777216 | bytes 41975808 | tf_op jit(solution)/shard_map/convert_element_type | solution.py:191
  413.5 16.9 %copy.189 = f32[8,1024,4,128]{1,3,2,0:T(8,128)} copy(f32[8,1024,4,128]{3,1,2,0:T(8,128)} %multiply_bitcast_fusion) | data formatting | bytes 33554432 | tf_op jit(solution)/shard_map/mul | solution.py:201
  430.4 14.2 %fusion.20 = f32[8,4,128,1024]{3,2,1,0:T(8,128)} fusion(bf16[8,128,4,128]{1,3,2,0:T(8,128)(2,1)S(1)} %copy.190, f32[8,4,128,1024]{2,3,1,0:T(8,128)} %get-tuple-element.63, f32[8,4,128]{2,1,0:T(4,128)S(1)} %get-tuple-element.62), kind=kOutput, calls=%fused_computation.48 | convolution fusion | flops 1082130432 | bytes 34619392 | tf_op jit(solution)/shard_map/bhqk,bqhd->bkhd/dot_general | solution.py:204
  444.6 19.2 %fusion.25 = (f32[2,128,512]{1,2,0:T(8,128)S(1)}, f32[2,128,512]{1,2,0:T(8,128)S(1)}, f32[2,128,512]{1,2,0:T(8,128)S(1)}, f32[2,128,512]{1,2,0:T(8,128)S(1)}, f3...) fusion(f32[1,8,1024,512]{2,3,1,0:T(8,128)} %bitcast.146, ...), kind=kLoop, calls=%fused_computation.56 | loop fusion | flops 12058624 | bytes 52428800 | tf_op jit(solution)/shard_map/reduce_sum | solution.py:225
  484.7 7.8 %pad_maximum_fusion.1 = bf16[4,1024,1024]{1,2,0:T(8,128)(2,1)} fusion(bf16[4,512,1024]{1,2,0:T(8,128)(2,1)} %gather_fusion.1, bf16[4,512,1024]{1,2,0:T(8,128)(2,1)} %gather_fusion), kind=kLoop, calls=%fused_computation.27 | loop fusion | flops 16777216 | bytes 16777216
  498.8 8.1 %convolution_convert_fusion.1 = bf16[1024,512]{1,0:T(8,128)(2,1)} fusion(bf16[1024,4096]{0,1:T(8,128)(2,1)} %bitcast.165, bf16[4096,512]{1,0:T(8,128)(2,1)S(1)} %bitcast.150), kind=kOutput, calls=%fused_computation.66 | convolution fusion | flops 4295491584 | bytes 13631488 | tf_op jit(solution)/shard_map/dot_general | solution.py:171
  517.0 8.1 %fusion.33 = bf16[8,128,4,128]{1,3,2,0:T(8,128)(2,1)S(1)} fusion(bf16[8,1024,4,128]{1,3,2,0:T(8,128)(2,1)} %bitcast.162, bf16[8,4,128,1024]{2,3,1,0:T(8,128)(2,1)} %copy-done), kind=kOutput, calls=%fused_computation.69 | convolution fusion | flops 1074790400 | bytes 17825792 | tf_op jit(solution)/shard_map/bhqk,bkhd->bqhd/dot_general | solution.py:194
  574.2 7.8 %fusion.17 = bf16[2,1024,512]{2,1,0:T(8,128)(2,1)S(1)} fusion(f32[2,1024,512]{2,1,0:T(8,128)} %reshape.280, f32[2,1024,512]{2,1,0:T(8,128)} %reshape.278, f32[2,4,2,128,512]{4,3,2,1,0:T(8,128)} %copy.193, f32[2,8,128,512]{3,2,1,0:T(8,128)} %copy.192, f32[2,128,512]{2,1,0:T(8,128)S(1)} %add_multiply_fusion), kind=kLoop, calls=%fused_computation.44 | loop fusion | flops 5242880 | bytes 19398656 | tf_op jit(solution)/shard_map/convert.1
  (173 shorter events, 219.2 us)
Async XLA Ops:
  7.2 346.2 %all-gather.2.cloned.1.call-start = ((), (), s32[]{:S(2)}) async-start(), calls=%async_computation.1 | async-start | bytes 9437184 | tf_op jit(solution)/shard_map/all_gather | solution.py:174
  7.9 575.5 %reduce-scatter.2.cloned.1.call-start = ((), (), s32[]{:S(2)}) async-start(), calls=%async_computation.2 | async-start | bytes 8912896 | tf_op jit(solution)/shard_map/reduce_scatter | solution.py:178
  11.8 19.5 %collective-permute-start = (f32[2,128,512]{2,1,0:T(8,128)}, f32[2,128,512]{2,1,0:T(8,128)}, u32[]{:S(2)}, u32[]{:S(2)}) collective-permute-start(f32[2,128,512]{2,1,0:T(8,128)} %broadcast_multiply_fusion.4), channel_id=1, source_target_pairs={{0,8},{8,0},{16,24},{24,16},{32,40},{40,32},{48,56},{56,48},{64,72... | collective-permute-start | bytes 1572872 | tf_op jit(solution)/shard_map/ppermute | solution.py:18
  35.3 27.0 %collective-permute-start.1 = (f32[2,128,512]{2,0,1:T(2,128)}, f32[2,128,512]{2,0,1:T(2,128)}, u32[]{:S(2)}, u32[]{:S(2)}) collective-permute-start(f32[2,128,512]{2,0,1:T(2,128)} %broadcast_multiply_fusion.3), channel_id=1, source_target_pairs={{0,16},{8,24},{16,0},{24,8},{32,48},{40,56},{48,32},{56,40},{64,80... | collective-permute-start | bytes 1572872 | tf_op jit(solution)/shard_map/ppermute | solution.py:18
  41.5 83.3 %copy-start.6 = (bf16[8,128,4,128]{1,3,2,0:T(8,128)(2,1)}, bf16[8,128,4,128]{1,3,2,0:T(8,128)(2,1)S(1)}, u32[]{:S(2)}) copy-start(bf16[8,128,4,128]{1,3,2,0:T(8,128)(2,1)S(1)} %copy.187) | copy-start | bytes 3145732
  65.6 13.3 %collective-permute-start.2 = (f32[2,128,512]{2,0,1:T(2,128)S(1)}, f32[2,128,512]{2,0,1:T(2,128)S(1)}, u32[]{:S(2)}, u32[]{:S(2)}) collective-permute-start(f32[2,128,512]{2,0,1:T(2,128)S(1)} %broadcast_multiply_fusion.2), channel_id=1, source_target_pairs={{0,32},{8,40},{16,48},{24,56},{32,0},{40,8},{48,16},{56,24},{64,96... | collective-permute-start | bytes 1572872 | tf_op jit(solution)/shard_map/ppermute | solution.py:18
  80.3 8.5 %collective-permute-start.3 = (bf16[2,128,512]{2,0,1:T(2,128)(2,1)S(1)}, bf16[2,128,512]{2,0,1:T(2,128)(2,1)S(1)}, u32[]{:S(2)}, u32[]{:S(2)}) collective-permute-start(bf16[2,128,512]{2,0,1:T(2,128)(2,1)S(1)} %broadcast_multiply_fusion.1), channel_id=1, source_target_pairs={{0,64},{8,72},{16,80},{24,88},{32,96},{40,104},{48,112},{56,120},{... | collective-permute-start | bytes 786440 | tf_op jit(solution)/shard_map/ppermute | solution.py:18
  149.4 47.2 %collective-permute-start.4 = (bf16[1024,512]{0,1:T(8,128)(2,1)S(1)}, bf16[1024,512]{0,1:T(8,128)(2,1)S(1)}, u32[]{:S(2)}, u32[]{:S(2)}) collective-permute-start(bf16[1024,512]{0,1:T(8,128)(2,1)S(1)} %bitcast.175), channel_id=1, source_target_pairs={{0,1},{1,0},{2,3},{3,2},{4,5},{5,4},{6,7},{7,6},{8,9},{9,8},{10,11... | collective-permute-start | bytes 3145736 | tf_op jit(solution)/shard_map/ppermute | solution.py:41
  198.6 90.7 %collective-permute-start.5 = (bf16[1024,1024]{0,1:T(8,128)(2,1)}, bf16[1024,1024]{0,1:T(8,128)(2,1)}, u32[]{:S(2)}, u32[]{:S(2)}) collective-permute-start(bf16[1024,1024]{0,1:T(8,128)(2,1)} %get-tuple-element.57), channel_id=1, source_target_pairs={{0,6},{1,7},{2,0},{3,1},{4,2},{5,3},{6,4},{7,5},{8,14},{9,15},{10,... | collective-permute-start | bytes 6291464 | tf_op jit(solution)/shard_map/ppermute | solution.py:49
  198.7 94.2 %collective-permute-start.6 = (bf16[1024,1024]{0,1:T(8,128)(2,1)}, bf16[1024,1024]{0,1:T(8,128)(2,1)}, u32[]{:S(2)}, u32[]{:S(2)}) collective-permute-start(bf16[1024,1024]{0,1:T(8,128)(2,1)} %get-tuple-element.57), channel_id=1, source_target_pairs={{0,2},{1,3},{2,4},{3,5},{4,6},{5,7},{6,0},{7,1},{8,10},{9,11},{10,... | collective-permute-start | bytes 6291464 | tf_op jit(solution)/shard_map/ppermute | solution.py:48
  203.9 19.2 %collective-permute-start.9 = (bf16[512,512]{1,0:T(8,128)(2,1)}, bf16[512,512]{1,0:T(8,128)(2,1)}, u32[]{:S(2)}, u32[]{:S(2)}) collective-permute-start(bf16[512,512]{1,0:T(8,128)(2,1)} %get-tuple-element.53), channel_id=1, source_target_pairs={{0,1},{1,2},{2,3},{3,4},{4,5},{5,6},{6,7},{7,0},{8,9},{9,10},{10,1... | collective-permute-start | bytes 1572872 | tf_op jit(solution)/shard_map/ppermute | solution.py:77
  205.5 90.0 %collective-permute-start.11 = (bf16[512,512]{1,0:T(8,128)(2,1)}, bf16[512,512]{1,0:T(8,128)(2,1)}, u32[]{:S(2)}, u32[]{:S(2)}) collective-permute-start(bf16[512,512]{1,0:T(8,128)(2,1)} %get-tuple-element.51), channel_id=1, source_target_pairs={{0,3},{1,4},{2,5},{3,6},{4,7},{5,0},{6,1},{7,2},{8,11},{9,12},{10,... | collective-permute-start | bytes 1572872 | tf_op jit(solution)/shard_map/ppermute | solution.py:77
  208.4 59.1 %collective-permute-start.10 = (bf16[512,512]{1,0:T(8,128)(2,1)}, bf16[512,512]{1,0:T(8,128)(2,1)}, u32[]{:S(2)}, u32[]{:S(2)}) collective-permute-start(bf16[512,512]{1,0:T(8,128)(2,1)} %get-tuple-element.52), channel_id=1, source_target_pairs={{0,2},{1,3},{2,4},{3,5},{4,6},{5,7},{6,0},{7,1},{8,10},{9,11},{10,... | collective-permute-start | bytes 1572872 | tf_op jit(solution)/shard_map/ppermute | solution.py:77
  208.5 90.0 %copy-start.13 = (bf16[512,512]{1,0:T(8,128)(2,1)S(1)}, bf16[512,512]{1,0:T(8,128)(2,1)}, u32[]{:S(2)}) copy-start(bf16[512,512]{1,0:T(8,128)(2,1)} %get-tuple-element.47) | copy-start | bytes 1572868
  223.2 75.3 %collective-permute-start.12 = (bf16[512,512]{1,0:T(8,128)(2,1)}, bf16[512,512]{1,0:T(8,128)(2,1)S(1)}, u32[]{:S(2)}, u32[]{:S(2)}) collective-permute-start(bf16[512,512]{1,0:T(8,128)(2,1)} %get-tuple-element.50), channel_id=1, source_target_pairs={{0,4},{1,5},{2,6},{3,7},{4,0},{5,1},{6,2},{7,3},{8,12},{9,13},{10,... | collective-permute-start | bytes 1572872 | tf_op jit(solution)/shard_map/ppermute | solution.py:77
  267.5 32.0 %collective-permute-start.13 = (bf16[512,512]{1,0:T(8,128)(2,1)}, bf16[512,512]{1,0:T(8,128)(2,1)S(1)}, u32[]{:S(2)}, u32[]{:S(2)}) collective-permute-start(bf16[512,512]{1,0:T(8,128)(2,1)} %get-tuple-element.49), channel_id=1, source_target_pairs={{0,5},{1,6},{2,7},{3,0},{4,1},{5,2},{6,3},{7,4},{8,13},{9,14},{10,... | collective-permute-start | bytes 1572872 | tf_op jit(solution)/shard_map/ppermute | solution.py:77
  289.3 33.7 %collective-permute-start.14 = (bf16[512,512]{1,0:T(8,128)(2,1)}, bf16[512,512]{1,0:T(8,128)(2,1)S(1)}, u32[]{:S(2)}, u32[]{:S(2)}) collective-permute-start(bf16[512,512]{1,0:T(8,128)(2,1)} %get-tuple-element.48), channel_id=1, source_target_pairs={{0,6},{1,7},{2,0},{3,1},{4,2},{5,3},{6,4},{7,5},{8,14},{9,15},{10,... | collective-permute-start | bytes 1572872 | tf_op jit(solution)/shard_map/ppermute | solution.py:77
  292.9 52.7 %collective-permute-start.8 = (bf16[1024,512]{0,1:T(8,128)(2,1)}, bf16[1024,512]{0,1:T(8,128)(2,1)}, u32[]{:S(2)}, u32[]{:S(2)}) collective-permute-start(bf16[1024,512]{0,1:T(8,128)(2,1)} %slice.89), channel_id=1, source_target_pairs={{0,6},{1,7},{2,0},{3,1},{4,2},{5,3},{6,4},{7,5},{8,14},{9,15},{10,... | collective-permute-start | bytes 3145736 | tf_op jit(solution)/shard_map/ppermute | solution.py:55
  295.5 50.1 %collective-permute-start.7 = (bf16[1024,512]{0,1:T(8,128)(2,1)}, bf16[1024,512]{0,1:T(8,128)(2,1)}, u32[]{:S(2)}, u32[]{:S(2)}) collective-permute-start(bf16[1024,512]{0,1:T(8,128)(2,1)} %slice.88), channel_id=1, source_target_pairs={{0,2},{1,3},{2,4},{3,5},{4,6},{5,7},{6,0},{7,1},{8,10},{9,11},{10,... | collective-permute-start | bytes 3145736 | tf_op jit(solution)/shard_map/ppermute | solution.py:54
  298.5 25.4 %collective-permute-start.15 = (bf16[512,512]{1,0:T(8,128)(2,1)S(1)}, bf16[512,512]{1,0:T(8,128)(2,1)S(1)}, u32[]{:S(2)}, u32[]{:S(2)}) collective-permute-start(bf16[512,512]{1,0:T(8,128)(2,1)S(1)} %copy-done.13), channel_id=1, source_target_pairs={{0,7},{1,0},{2,1},{3,2},{4,3},{5,4},{6,5},{7,6},{8,15},{9,8},{10,9... | collective-permute-start | bytes 1572872 | tf_op jit(solution)/shard_map/ppermute | solution.py:77
  464.0 19.0 %collective-permute-start.16 = (f32[2,128,512]{2,0,1:T(2,128)S(1)}, f32[2,128,512]{2,0,1:T(2,128)S(1)}, u32[]{:S(2)}, u32[]{:S(2)}) collective-permute-start(f32[2,128,512]{2,0,1:T(2,128)S(1)} %copy.196), channel_id=1, source_target_pairs={{0,64},{8,72},{16,80},{24,88},{32,96},{40,104},{48,112},{56,120},{... | collective-permute-start | bytes 1572872 | tf_op jit(solution)/shard_map/ppermute | solution.py:18
  484.7 12.9 %collective-permute-start.17 = (f32[2,128,512]{2,0,1:T(2,128)}, f32[2,128,512]{2,0,1:T(2,128)S(1)}, u32[]{:S(2)}, u32[]{:S(2)}) collective-permute-start(f32[2,128,512]{2,0,1:T(2,128)} %select_add_fusion.2), channel_id=1, source_target_pairs={{0,32},{8,40},{16,48},{24,56},{32,0},{40,8},{48,16},{56,24},{64,96... | collective-permute-start | bytes 1572872 | tf_op jit(solution)/shard_map/ppermute | solution.py:18
  498.7 13.4 %collective-permute-start.18 = (f32[2,128,512]{2,0,1:T(2,128)S(1)}, f32[2,128,512]{2,0,1:T(2,128)S(1)}, u32[]{:S(2)}, u32[]{:S(2)}) collective-permute-start(f32[2,128,512]{2,0,1:T(2,128)S(1)} %select_add_fusion.1), channel_id=1, source_target_pairs={{0,16},{8,24},{16,0},{24,8},{32,48},{40,56},{48,32},{56,40},{64,80... | collective-permute-start | bytes 1572872 | tf_op jit(solution)/shard_map/ppermute | solution.py:18
  514.3 58.6 %collective-permute-start.19 = (f32[2,128,512]{2,1,0:T(8,128)}, f32[2,128,512]{2,1,0:T(8,128)}, u32[]{:S(2)}, u32[]{:S(2)}) collective-permute-start(f32[2,128,512]{2,1,0:T(8,128)} %select_add_fusion), channel_id=1, source_target_pairs={{0,8},{8,0},{16,24},{24,16},{32,40},{40,32},{48,56},{56,48},{64,72... | collective-permute-start | bytes 1572872 | tf_op jit(solution)/shard_map/ppermute | solution.py:18
  (14 other events, 88.8 us)
Sparse Core Ops, SparseCore 0:
  9.6 208.8 all-gather.1
  373.7 101.9 reduce-scatter.1

commit v2 on v1

--- a/solution.py
+++ b/solution.py
@@ -167,13 +167,23 @@
     prob_low = attn_prob.astype(jnp.bfloat16)
     mixed = jnp.einsum("bhqk,bkhd->bqhd", prob_low, value_heads, preferred_element_type=jnp.float32)
     attended = mixed.astype(jnp.bfloat16).reshape(row_count, features)
-    attended_full = head_ring_gather(attended)
-    output = jnp.dot(
-        attended_full, weight_columns(out_weight), preferred_element_type=jnp.float32
-    ).astype(jnp.bfloat16)
-    grads_full = lax.all_gather(cotangent, "head", axis=1, tiled=True)
+    half_rows = row_count // 2
+    grads_full = jnp.concatenate(
+        [
+            lax.all_gather(cotangent[:half_rows], "head", axis=1, tiled=True),
+            head_ring_gather(cotangent[half_rows:]),
+        ],
+        axis=0,
+    )
     grad_attn = lax.dot_general(
         grads_full, out_weight, (((1,), (1,)), ((), ())), preferred_element_type=jnp.float32
+    ).astype(jnp.bfloat16)
+    late_attended, late_weight, grad_attn = lax.optimization_barrier(
+        (attended, out_weight, grad_attn)
+    )
+    attended_full = head_ring_gather(late_attended)
+    output = jnp.dot(
+        attended_full, weight_columns(late_weight), preferred_element_type=jnp.float32
     ).astype(jnp.bfloat16)
     grad_weight = lax.psum_scatter(
         lax.dot_general(

time: 598 us -> 576 us (0.963)
  the two profiles are of different devices: /device:TPU:15 before, /device:TPU:0 now
where the time goes in v2:
time: 576 us; the launch traced here: 566 us
  local copies, waits for them, and re-layouts  196 us (34%)
  other arithmetic  108 us (19%)
  waiting for transfers between devices  103 us (18%)
  matrix products  102 us (18%)
  starting transfers between devices  42.3 us (7%)
  between operations  14.9 us (3%)
    ppermute x7, waiting for transfers between devices, weight_columns(): lax.ppermute(outgoing, 'head', [(src, (src + shift) % count) for src in r...  64 us
    unnamed x69, local copies, waits for them, and re-layouts  29.5 us
    slice x2, local copies, waits for them, and re-layouts, body(): key_heads = key_set[0].reshape(blocks, keys_all, head_count, DH)  23.1 us
    reduce_sum x1, other arithmetic, body(): sibling_grads.append(jnp.sum(grad_sets[:, :, lower:lower + BLK], axis=1))  20.3 us
    ppermute x8, waiting for transfers between devices, swapped(): return lax.ppermute(value, axis, pairs)  20.2 us
    gather x4, local copies, waits for them, and re-layouts, head_ring_gather(): placed = stacked[order]  18.9 us
    mul x1, local copies, waits for them, and re-layouts, body(): jnp.einsum('bhqk,bqhd->bkhd', grad_score, query_heads, preferred_element_...  16.8 us
    dot_general x1, matrix products, body(): jnp.einsum('bqhd,bkhd->bhqk', grad_heads, value_heads, preferred_element_...  15.7 us
  transfers between devices with their start and end apart: 27, of which 10 were waited for; matrix products, arithmetic and copies ran while one was open for 61% of the time, Pallas kernels for 0%

profile of v2, /device:TPU:0, one launch (start us, length us, event | category | flops | bytes accessed | tf_op | source)
XLA Modules:
  0.0 566.3 jit_solution(6713058488973735782)
XLA Ops:
  18.8 7.7 %convert_reduce_fusion.2 = f32[2,512,512]{2,1,0:T(8,128)S(1)} fusion(bf16[1,512,2,512]{3,2,1,0:T(2,128)(2,1)} %stack.106, bf16[1,512,2,512]{3,2,1,0:T(2,128)(2,1)} %stack.105), kind=kLoop, calls=%fused_computation.58 | loop fusion | flops 2621440 | bytes 4194304 | tf_op jit(solution)/shard_map/reduce_sum | solution.py:123
  77.5 7.4 %collective-permute-done.2 = f32[2,128,512]{2,0,1:T(2,128)S(1)} collective-permute-done((f32[2,128,512]{2,0,1:T(2,128)S(1)}, f32[2,128,512]{2,0,1:T(2,128)S(1)}, u32[]{:S(2)}, u32[]{:S(2)}) %collective-permute-start.2) | collective-permute-done | bytes 524320 | tf_op jit(solution)/shard_map/ppermute | solution.py:18
  105.3 11.6 %fusion.49 = (bf16[1,8,1024,512]{3,2,1,0:T(8,128)(2,1)}, bf16[1,8,1024,512]{3,2,1,0:T(8,128)(2,1)}) fusion(bf16[2,8,1024,512]{3,2,1,0:T(8,128)(2,1)} %broadcast_dynamic-update-slice_fusion), kind=kLoop, calls=%fused_computation.148 | loop fusion | bytes 33554432 | tf_op jit(solution)/shard_map/slice | solution.py:156
  117.0 11.5 %copy.177 = bf16[1,8,1024,512]{2,3,1,0:T(8,128)(2,1)} copy(bf16[1,8,1024,512]{3,2,1,0:T(8,128)(2,1)} %get-tuple-element.44) | data formatting | bytes 16777216 | tf_op jit(solution)/shard_map/slice | solution.py:156
  128.5 11.5 %copy.175 = bf16[1,8,1024,512]{2,3,1,0:T(8,128)(2,1)} copy(bf16[1,8,1024,512]{3,2,1,0:T(8,128)(2,1)} %get-tuple-element.45) | data formatting | bytes 16777216 | tf_op jit(solution)/shard_map/slice | solution.py:157
  140.0 12.9 %fusion.52 = (f32[8,4,128]{2,1,0:T(4,128)S(1)}, f32[8,4,128,1024]{2,3,1,0:T(8,128)}) fusion(f32[1024]{0:T(1024)S(1)} %copy-done.25, pred[8,1024]{1,0:T(8,128)(4,1)S(1)} %concatenate.52, bf16[8,1024,4,128]{1,3,2,0:T(8,128)(2,1)} %bitcast.159, bf16[8,128,4,128]{1,3,2,0:T(8,128)(2,1)S(1)} %copy.191), kind=kOutput, calls=%fused_computation.151 | convolution fusion | flops 1094714368 | bytes 26243072 | tf_op jit(solution)/shard_map/sub | solution.py:165
  152.8 10.6 %fusion.33 = bf16[8,128,4,128]{1,3,2,0:T(8,128)(2,1)S(1)} fusion(bf16[8,1024,4,128]{1,3,2,0:T(8,128)(2,1)} %bitcast.161, f32[8,4,128,1024]{2,3,1,0:T(8,128)} %get-tuple-element.69, f32[8,4,128]{2,1,0:T(4,128)S(1)} %get-tuple-element.68), kind=kOutput, calls=%fused_computation.72 | convolution fusion | flops 1082654720 | bytes 26230784 | tf_op jit(solution)/shard_map/bhqk,bkhd->bqhd/dot_general | solution.py:168
  181.6 10.2 %fusion.29 = bf16[1024,512]{1,0:T(8,128)(2,1)} fusion(bf16[512,4096]{1,0:T(8,128)(2,1)} %param.9, bf16[512,4096]{0,1:T(8,128)(2,1)} %bitcast.169, bf16[512,4096]{0,1:T(8,128)(2,1)} %all-gather.2.cloned.1.call-done), kind=kOutput, calls=%fused_computation.69 | convolution fusion | flops 4312268800 | bytes 13631488 | tf_op jit(solution)/shard_map/dot_general | solution.py:178
  194.5 15.7 %multiply_reduce_fusion = (f32[8,4,128]{2,1,0:T(4,128)S(1)}, f32[8,4,128,1024]{2,3,1,0:T(8,128)}) fusion(f32[8,4,128,1024]{2,3,1,0:T(8,128)} %get-tuple-element.69, f32[8,4,128]{2,1,0:T(4,128)S(1)} %get-tuple-element.68, bf16[8,128,4,128]{1,3,2,0:T(8,128)(2,1)} %copy.194, bf16[8,1024,4,128]{1,3,2,0:T(8,128)(2,1)} %bitcast.162), kind=kOutput, calls=%fused_computation.25 | convolution fusion | flops 1086320640 | bytes 43024384 | tf_op jit(solution)/shard_map/bqhd,bkhd->bhqk/dot_general | solution.py:197
  210.2 13.9 %fusion.22 = f32[8,4,128,1024]{3,2,1,0:T(8,128)} fusion(bf16[8,128,4,128]{1,3,2,0:T(8,128)(2,1)S(1)} %copy-done.17, f32[8,4,128,1024]{2,3,1,0:T(8,128)} %get-tuple-element.69, f32[8,4,128]{2,1,0:T(4,128)S(1)} %get-tuple-element.68), kind=kOutput, calls=%fused_computation.52 | convolution fusion | flops 1082130432 | bytes 34619392 | tf_op jit(solution)/shard_map/bhqk,bqhd->bkhd/dot_general | solution.py:214
  224.1 11.3 %fusion.9 = f32[4096,512]{1,0:T(8,128)} fusion(bf16[512,4096]{0,1:T(8,128)(2,1)} %bitcast.170, bf16[512,4096]{0,1:T(8,128)(2,1)} %all-gather.2.cloned.1.call-done, bf16[64,8,8,128]{3,2,1,0:T(8,128)(2,1)S(1)} %bitcast.172), kind=kOutput, calls=%fused_computation.35 | convolution fusion | flops 4311744512 | bytes 17825792 | tf_op jit(solution)/shard_map/dot_general | solution.py:189
  235.5 12.1 %multiply_convert_fusion = bf16[8,4,128,1024]{2,3,1,0:T(8,128)(2,1)S(1)} fusion(f32[8,4,128,1024]{2,3,1,0:T(8,128)} %get-tuple-element.71, f32[8,4,128]{2,1,0:T(4,128)S(1)} %get-tuple-element.70, f32[8,4,128,1024]{2,3,1,0:T(8,128)} %get-tuple-element.69, f32[8,4,128]{2,1,0:T(4,128)S(1)} %get-tuple-element.68), kind=kLoop, calls=%fused_computation.24 | loop fusion | flops 16777216 | bytes 41975808 | tf_op jit(solution)/shard_map/convert_element_type | solution.py:201
  251.3 8.3 %multiply_bitcast_fusion = f32[8,1024,4,128]{3,1,2,0:T(8,128)} fusion(bf16[8,4,128,1024]{2,3,1,0:T(8,128)(2,1)S(1)} %multiply_convert_fusion, bf16[8,128,4,128]{1,3,2,0:T(8,128)(2,1)S(1)} %copy.191), kind=kOutput, calls=%fused_computation.23 | convolution fusion | flops 1077936128 | bytes 26214400 | tf_op jit(solution)/shard_map/bhqk,bqhd->bkhd/dot_general | solution.py:211
  259.6 16.8 %copy.193 = f32[8,1024,4,128]{1,3,2,0:T(8,128)} copy(f32[8,1024,4,128]{3,1,2,0:T(8,128)} %multiply_bitcast_fusion) | data formatting | bytes 33554432 | tf_op jit(solution)/shard_map/mul | solution.py:211
  276.4 20.3 %fusion.27 = (f32[2,128,512]{1,2,0:T(8,128)S(1)}, f32[2,128,512]{1,2,0:T(8,128)}, f32[2,128,512]{1,2,0:T(8,128)}, f32[2,128,512]{1,2,0:T(8,128)}, f32[2,8,128,51...) fusion(f32[1,8,1024,512]{2,3,1,0:T(8,128)} %bitcast.146, ...), kind=kLoop, calls=%fused_computation.60 | loop fusion | flops 12058624 | bytes 52428800 | tf_op jit(solution)/shard_map/reduce_sum | solution.py:235
  302.5 9.1 %fusion.36 = bf16[8,128,4,128]{1,3,2,0:T(8,128)(2,1)} fusion(bf16[8,1024,4,128]{1,3,2,0:T(8,128)(2,1)} %bitcast.160, bf16[8,4,128,1024]{2,3,1,0:T(8,128)(2,1)} %copy-done), kind=kOutput, calls=%fused_computation.73 | convolution fusion | flops 1074790400 | bytes 17825792 | tf_op jit(solution)/shard_map/bhqk,bkhd->bqhd/dot_general | solution.py:204
  381.8 14.3 %collective-permute-done.15 = bf16[512,512]{1,0:T(8,128)(2,1)S(1)} collective-permute-done((bf16[512,512]{1,0:T(8,128)(2,1)S(1)}, bf16[512,512]{1,0:T(8,128)(2,1)S(1)}, u32[]{:S(2)}, u32[]{:S(2)}) %collective-permute-start.15) | collective-permute-done | bytes 524320 | tf_op jit(solution)/shard_map/ppermute | solution.py:77
  425.9 7.4 %collective-permute-done.18 = bf16[512,512]{1,0:T(8,128)(2,1)S(1)} collective-permute-done((bf16[512,512]{1,0:T(8,128)(2,1)S(1)}, bf16[512,512]{1,0:T(8,128)(2,1)S(1)}, u32[]{:S(2)}, u32[]{:S(2)}) %collective-permute-start.18) | collective-permute-done | bytes 524320 | tf_op jit(solution)/shard_map/ppermute | solution.py:77
  434.1 42.3 %collective-permute-done.19 = bf16[512,512]{1,0:T(8,128)(2,1)S(1)} collective-permute-done((bf16[512,512]{1,0:T(8,128)(2,1)S(1)}, bf16[512,512]{1,0:T(8,128)(2,1)S(1)}, u32[]{:S(2)}, u32[]{:S(2)}) %collective-permute-start.19) | collective-permute-done | bytes 524320 | tf_op jit(solution)/shard_map/ppermute | solution.py:77
  481.5 10.9 %scatter_fusion = bf16[8,512,512]{2,1,0:T(8,128)(2,1)} fusion(bf16[8,512,512]{2,1,0:T(8,128)(2,1)} %broadcast_in_dim.55, s32[8]{0:T(128)S(1)} %copy-done.24, bf16[8,512,512]{2,1,0:T(8,128)(2,1)} %bitcast_dynamic-update-slice_fusion), kind=kCustom, calls=%fused_computation.3 | custom fusion | bytes 12582944 | tf_op jit(solution)/shard_map/scatter | solution.py:81
  501.5 6.7 %fusion.19 = bf16[2,1024,512]{2,1,0:T(8,128)(2,1)S(1)} fusion(f32[2,1024,512]{2,1,0:T(8,128)} %reshape.284, f32[2,1024,512]{2,1,0:T(8,128)S(1)} %copy-done.3, f32[2,4,2,128,512]{4,3,2,1,0:T(8,128)} %copy.197, f32[2,8,128,512]{3,2,1,0:T(8,128)} %copy.196, f32[2,128,512]{2,1,0:T(8,128)S(1)} %copy-done.11), kind=kLoop, calls=%fused_computation.48 | loop fusion | flops 5242880 | bytes 19398656 | tf_op jit(solution)/shard_map/convert.1
  509.7 8.0 %collective-permute-done.13 = bf16[1024,512]{0,1:T(8,128)(2,1)} collective-permute-done((bf16[1024,512]{0,1:T(8,128)(2,1)}, bf16[1024,512]{0,1:T(8,128)(2,1)}, u32[]{:S(2)}, u32[]{:S(2)}) %collective-permute-start.13) | collective-permute-done | bytes 1048608 | tf_op jit(solution)/shard_map/ppermute | solution.py:55
  541.4 7.8 %pad_maximum_fusion.2 = bf16[4,1024,1024]{1,2,0:T(8,128)(2,1)} fusion(bf16[4,512,1024]{1,2,0:T(8,128)(2,1)} %gather_fusion.2, bf16[4,512,1024]{1,2,0:T(8,128)(2,1)} %gather_fusion.1), kind=kLoop, calls=%fused_computation.29 | loop fusion | flops 16777216 | bytes 16777216
  549.2 10.1 %convolution_convert_fusion = bf16[1024,512]{1,0:T(8,128)(2,1)} fusion(bf16[1024,4096]{0,1:T(8,128)(2,1)} %bitcast.163, bf16[4096,512]{1,0:T(8,128)(2,1)} %bitcast.150), kind=kOutput, calls=%fused_computation.70 | convolution fusion | flops 4295491584 | bytes 13631488 | tf_op jit(solution)/shard_map/dot_general | solution.py:185
  (212 shorter events, 253.1 us)
Async XLA Ops:
  7.2 174.4 %all-gather.2.cloned.1.call-start = ((), (), s32[]{:S(2)}) async-start(), calls=%async_computation.1 | async-start | bytes 4718592 | tf_op jit(solution)/shard_map/all_gather | solution.py:173
  9.2 46.2 %collective-permute-start.4 = (bf16[512,512]{1,0:T(8,128)(2,1)}, bf16[512,512]{1,0:T(8,128)(2,1)}, u32[]{:S(2)}, u32[]{:S(2)}) collective-permute-start(bf16[512,512]{1,0:T(8,128)(2,1)} %slice.77), channel_id=1, source_target_pairs={{0,1},{1,0},{2,3},{3,2},{4,5},{5,4},{6,7},{7,6},{8,9},{9,8},{10,11... | collective-permute-start | bytes 1572872 | tf_op jit(solution)/shard_map/ppermute | solution.py:41
  14.6 33.5 %collective-permute-start = (f32[2,128,512]{2,1,0:T(8,128)}, f32[2,128,512]{2,1,0:T(8,128)}, u32[]{:S(2)}, u32[]{:S(2)}) collective-permute-start(f32[2,128,512]{2,1,0:T(8,128)} %broadcast_multiply_fusion.4), channel_id=1, source_target_pairs={{0,8},{8,0},{16,24},{24,16},{32,40},{40,32},{48,56},{56,48},{64,72... | collective-permute-start | bytes 1572872 | tf_op jit(solution)/shard_map/ppermute | solution.py:18
  52.1 16.1 %collective-permute-start.1 = (f32[2,128,512]{2,0,1:T(2,128)}, f32[2,128,512]{2,0,1:T(2,128)}, u32[]{:S(2)}, u32[]{:S(2)}) collective-permute-start(f32[2,128,512]{2,0,1:T(2,128)} %broadcast_multiply_fusion.3), channel_id=1, source_target_pairs={{0,16},{8,24},{16,0},{24,8},{32,48},{40,56},{48,32},{56,40},{64,80... | collective-permute-start | bytes 1572872 | tf_op jit(solution)/shard_map/ppermute | solution.py:18
  58.6 31.6 %collective-permute-start.5 = (bf16[512,1024]{1,0:T(8,128)(2,1)}, bf16[512,1024]{1,0:T(8,128)(2,1)S(1)}, u32[]{:S(2)}, u32[]{:S(2)}) collective-permute-start(bf16[512,1024]{1,0:T(8,128)(2,1)} %get-tuple-element.67), channel_id=1, source_target_pairs={{0,6},{1,7},{2,0},{3,1},{4,2},{5,3},{6,4},{7,5},{8,14},{9,15},{10,... | collective-permute-start | bytes 3145736 | tf_op jit(solution)/shard_map/ppermute | solution.py:49
  61.6 38.8 %collective-permute-start.6 = (bf16[512,1024]{1,0:T(8,128)(2,1)}, bf16[512,1024]{1,0:T(8,128)(2,1)}, u32[]{:S(2)}, u32[]{:S(2)}) collective-permute-start(bf16[512,1024]{1,0:T(8,128)(2,1)} %get-tuple-element.67), channel_id=1, source_target_pairs={{0,2},{1,3},{2,4},{3,5},{4,6},{5,7},{6,0},{7,1},{8,10},{9,11},{10,... | collective-permute-start | bytes 3145736 | tf_op jit(solution)/shard_map/ppermute | solution.py:48
  63.7 495.6 %reduce-scatter.2.cloned.1.call-start = ((), (), s32[]{:S(2)}) async-start(), calls=%async_computation.2 | async-start | bytes 8912896 | tf_op jit(solution)/shard_map/reduce_scatter | solution.py:188
  71.3 13.7 %collective-permute-start.2 = (f32[2,128,512]{2,0,1:T(2,128)S(1)}, f32[2,128,512]{2,0,1:T(2,128)S(1)}, u32[]{:S(2)}, u32[]{:S(2)}) collective-permute-start(f32[2,128,512]{2,0,1:T(2,128)S(1)} %broadcast_multiply_fusion.2), channel_id=1, source_target_pairs={{0,32},{8,40},{16,48},{24,56},{32,0},{40,8},{48,16},{56,24},{64,96... | collective-permute-start | bytes 1572872 | tf_op jit(solution)/shard_map/ppermute | solution.py:18
  86.4 17.4 %collective-permute-start.3 = (bf16[2,128,512]{2,0,1:T(2,128)(2,1)S(1)}, bf16[2,128,512]{2,0,1:T(2,128)(2,1)S(1)}, u32[]{:S(2)}, u32[]{:S(2)}) collective-permute-start(bf16[2,128,512]{2,0,1:T(2,128)(2,1)S(1)} %broadcast_multiply_fusion.1), channel_id=1, source_target_pairs={{0,64},{8,72},{16,80},{24,88},{32,96},{40,104},{48,112},{56,120},{... | collective-permute-start | bytes 786440 | tf_op jit(solution)/shard_map/ppermute | solution.py:18
  91.1 74.3 %collective-permute-start.8 = (bf16[512,512]{1,0:T(8,128)(2,1)}, bf16[512,512]{1,0:T(8,128)(2,1)}, u32[]{:S(2)}, u32[]{:S(2)}) collective-permute-start(bf16[512,512]{1,0:T(8,128)(2,1)} %slice.107), channel_id=1, source_target_pairs={{0,6},{1,7},{2,0},{3,1},{4,2},{5,3},{6,4},{7,5},{8,14},{9,15},{10,... | collective-permute-start | bytes 1572872 | tf_op jit(solution)/shard_map/ppermute | solution.py:55
  102.3 63.1 %collective-permute-start.7 = (bf16[512,512]{1,0:T(8,128)(2,1)}, bf16[512,512]{1,0:T(8,128)(2,1)}, u32[]{:S(2)}, u32[]{:S(2)}) collective-permute-start(bf16[512,512]{1,0:T(8,128)(2,1)} %slice.106), channel_id=1, source_target_pairs={{0,2},{1,3},{2,4},{3,5},{4,6},{5,7},{6,0},{7,1},{8,10},{9,11},{10,... | collective-permute-start | bytes 1572872 | tf_op jit(solution)/shard_map/ppermute | solution.py:54
  235.4 163.5 %collective-permute-start.9 = (bf16[1024,512]{0,1:T(8,128)(2,1)}, bf16[1024,512]{0,1:T(8,128)(2,1)}, u32[]{:S(2)}, u32[]{:S(2)}) collective-permute-start(bf16[1024,512]{0,1:T(8,128)(2,1)} %bitcast.137), channel_id=1, source_target_pairs={{0,1},{1,0},{2,3},{3,2},{4,5},{5,4},{6,7},{7,6},{8,9},{9,8},{10,11... | collective-permute-start | bytes 3145736 | tf_op jit(solution)/shard_map/ppermute | solution.py:41
  297.6 75.7 %collective-permute-start.21 = (f32[2,128,512]{2,0,1:T(2,128)}, f32[2,128,512]{2,0,1:T(2,128)}, u32[]{:S(2)}, u32[]{:S(2)}) collective-permute-start(f32[2,128,512]{2,0,1:T(2,128)} %copy.200), channel_id=1, source_target_pairs={{0,64},{8,72},{16,80},{24,88},{32,96},{40,104},{48,112},{56,120},{... | collective-permute-start | bytes 1572872 | tf_op jit(solution)/shard_map/ppermute | solution.py:18
  313.5 163.8 %collective-permute-start.20 = (bf16[512,512]{1,0:T(8,128)(2,1)}, bf16[512,512]{1,0:T(8,128)(2,1)}, u32[]{:S(2)}, u32[]{:S(2)}) collective-permute-start(bf16[512,512]{1,0:T(8,128)(2,1)} %get-tuple-element.48), channel_id=1, source_target_pairs={{0,7},{1,0},{2,1},{3,2},{4,3},{5,4},{6,5},{7,6},{8,15},{9,8},{10,9... | collective-permute-start | bytes 1572872 | tf_op jit(solution)/shard_map/ppermute | solution.py:77
  317.8 95.2 %collective-permute-start.17 = (bf16[512,512]{1,0:T(8,128)(2,1)}, bf16[512,512]{1,0:T(8,128)(2,1)}, u32[]{:S(2)}, u32[]{:S(2)}) collective-permute-start(bf16[512,512]{1,0:T(8,128)(2,1)} %get-tuple-element.51), channel_id=1, source_target_pairs={{0,4},{1,5},{2,6},{3,7},{4,0},{5,1},{6,2},{7,3},{8,12},{9,13},{10,... | collective-permute-start | bytes 1572872 | tf_op jit(solution)/shard_map/ppermute | solution.py:77
  317.8 58.4 %collective-permute-start.14 = (bf16[512,512]{1,0:T(8,128)(2,1)}, bf16[512,512]{1,0:T(8,128)(2,1)}, u32[]{:S(2)}, u32[]{:S(2)}) collective-permute-start(bf16[512,512]{1,0:T(8,128)(2,1)} %get-tuple-element.54), channel_id=1, source_target_pairs={{0,1},{1,2},{2,3},{3,4},{4,5},{5,6},{6,7},{7,0},{8,9},{9,10},{10,1... | collective-permute-start | bytes 1572872 | tf_op jit(solution)/shard_map/ppermute | solution.py:77
  373.3 22.8 %collective-permute-start.15 = (bf16[512,512]{1,0:T(8,128)(2,1)S(1)}, bf16[512,512]{1,0:T(8,128)(2,1)S(1)}, u32[]{:S(2)}, u32[]{:S(2)}) collective-permute-start(bf16[512,512]{1,0:T(8,128)(2,1)S(1)} %copy-done.21), channel_id=1, source_target_pairs={{0,2},{1,3},{2,4},{3,5},{4,6},{5,7},{6,0},{7,1},{8,10},{9,11},{10,... | collective-permute-start | bytes 1572872 | tf_op jit(solution)/shard_map/ppermute | solution.py:77
  376.2 34.4 %collective-permute-start.16 = (bf16[512,512]{1,0:T(8,128)(2,1)S(1)}, bf16[512,512]{1,0:T(8,128)(2,1)S(1)}, u32[]{:S(2)}, u32[]{:S(2)}) collective-permute-start(bf16[512,512]{1,0:T(8,128)(2,1)S(1)} %copy-done.20), channel_id=1, source_target_pairs={{0,3},{1,4},{2,5},{3,6},{4,7},{5,0},{6,1},{7,2},{8,11},{9,12},{10,... | collective-permute-start | bytes 1572872 | tf_op jit(solution)/shard_map/ppermute | solution.py:77
  410.1 84.6 %collective-permute-start.10 = (bf16[1024,1024]{0,1:T(8,128)(2,1)}, bf16[1024,1024]{0,1:T(8,128)(2,1)}, u32[]{:S(2)}, u32[]{:S(2)}) collective-permute-start(bf16[1024,1024]{0,1:T(8,128)(2,1)} %get-tuple-element.58), channel_id=1, source_target_pairs={{0,6},{1,7},{2,0},{3,1},{4,2},{5,3},{6,4},{7,5},{8,14},{9,15},{10,... | collective-permute-start | bytes 6291464 | tf_op jit(solution)/shard_map/ppermute | solution.py:49
  410.6 87.9 %collective-permute-start.11 = (bf16[1024,1024]{0,1:T(8,128)(2,1)}, bf16[1024,1024]{0,1:T(8,128)(2,1)}, u32[]{:S(2)}, u32[]{:S(2)}) collective-permute-start(bf16[1024,1024]{0,1:T(8,128)(2,1)} %get-tuple-element.58), channel_id=1, source_target_pairs={{0,2},{1,3},{2,4},{3,5},{4,6},{5,7},{6,0},{7,1},{8,10},{9,11},{10,... | collective-permute-start | bytes 6291464 | tf_op jit(solution)/shard_map/ppermute | solution.py:48
  413.0 63.5 %collective-permute-start.19 = (bf16[512,512]{1,0:T(8,128)(2,1)S(1)}, bf16[512,512]{1,0:T(8,128)(2,1)S(1)}, u32[]{:S(2)}, u32[]{:S(2)}) collective-permute-start(bf16[512,512]{1,0:T(8,128)(2,1)S(1)} %copy-done.18), channel_id=1, source_target_pairs={{0,6},{1,7},{2,0},{3,1},{4,2},{5,3},{6,4},{7,5},{8,14},{9,15},{10,... | collective-permute-start | bytes 1572872 | tf_op jit(solution)/shard_map/ppermute | solution.py:77
  433.3 59.1 %collective-permute-start.24 = (f32[2,128,512]{2,1,0:T(8,128)}, f32[2,128,512]{2,1,0:T(8,128)}, u32[]{:S(2)}, u32[]{:S(2)}) collective-permute-start(f32[2,128,512]{2,1,0:T(8,128)} %select_add_fusion), channel_id=1, source_target_pairs={{0,8},{8,0},{16,24},{24,16},{32,40},{40,32},{48,56},{56,48},{64,72... | collective-permute-start | bytes 1572872 | tf_op jit(solution)/shard_map/ppermute | solution.py:18
  497.0 20.7 %collective-permute-start.13 = (bf16[1024,512]{0,1:T(8,128)(2,1)}, bf16[1024,512]{0,1:T(8,128)(2,1)}, u32[]{:S(2)}, u32[]{:S(2)}) collective-permute-start(bf16[1024,512]{0,1:T(8,128)(2,1)} %slice.109), channel_id=1, source_target_pairs={{0,6},{1,7},{2,0},{3,1},{4,2},{5,3},{6,4},{7,5},{8,14},{9,15},{10,... | collective-permute-start | bytes 3145736 | tf_op jit(solution)/shard_map/ppermute | solution.py:55
  500.8 21.6 %collective-permute-start.12 = (bf16[1024,512]{0,1:T(8,128)(2,1)}, bf16[1024,512]{0,1:T(8,128)(2,1)}, u32[]{:S(2)}, u32[]{:S(2)}) collective-permute-start(bf16[1024,512]{0,1:T(8,128)(2,1)} %slice.108), channel_id=1, source_target_pairs={{0,2},{1,3},{2,4},{3,5},{4,6},{5,7},{6,0},{7,1},{8,10},{9,11},{10,... | collective-permute-start | bytes 3145736 | tf_op jit(solution)/shard_map/ppermute | solution.py:54
  (29 other events, 434.4 us)
Sparse Core Ops, SparseCore 0:
  63.8 91.0 all-gather.1
  235.5 108.4 reduce-scatter.1

commit v3 on v2

--- a/solution.py
+++ b/solution.py
@@ -65,22 +65,38 @@
 
 def weight_columns(out_weight):
     count = lax.axis_size("head")
+    seq_count = lax.axis_size("seq")
     where_head = lax.axis_index("head")
+    core = lax.axis_index("seq") % 2
     rows, cols = out_weight.shape
     width = cols // count
-    pieces = [lax.dynamic_slice_in_dim(out_weight, where_head * width, width, axis=1)]
-    for shift in range(1, count):
+    own = lax.dynamic_slice_in_dim(out_weight, where_head * width, width, axis=1)
+    fetched = []
+    for step in range(count // 2):
+        shift_low, shift_high = 2 * step + 1, 2 * step + 2
+        pairs = []
+        for seq_idx in range(seq_count):
+            shift = shift_low if seq_idx % 2 == 0 else shift_high
+            if shift % count == 0:
+                continue
+            for src in range(count):
+                pairs.append((seq_idx * count + src, seq_idx * count + (src + shift) % count))
+        shift = jnp.where(core == 0, shift_low, shift_high)
         outgoing = lax.dynamic_slice_in_dim(
             out_weight, ((where_head + shift) % count) * width, width, axis=1
         )
-        pieces.append(
-            lax.ppermute(outgoing, "head", [(src, (src + shift) % count) for src in range(count)])
-        )
-    stacked = jnp.stack(pieces)
+        fetched.append(lax.ppermute(outgoing, ("seq", "head"), pairs))
+    mine = jnp.stack(fetched)
+    theirs = lax.ppermute(mine, "seq", [(src, src ^ 1) for src in range(seq_count)])
+    odd = jnp.where(core == 0, mine, theirs)
+    even = jnp.where(core == 0, theirs, mine)
+    by_shift = [own]
+    for shift in range(1, count):
+        by_shift.append(odd[(shift - 1) // 2] if shift % 2 else even[shift // 2 - 1])
+    stacked = jnp.stack(by_shift)
     order = (where_head - jnp.arange(count)) % count
     placed = jnp.zeros_like(stacked).at[order].set(stacked)
     return placed.reshape(count * rows, width)
-
 
 def body(queries, key_rows, value_rows, out_weight, cotangent, pattern):
     row_count, features = queries.shape
@@ -167,6 +183,7 @@
     prob_low = attn_prob.astype(jnp.bfloat16)
     mixed = jnp.einsum("bhqk,bkhd->bqhd", prob_low, value_heads, preferred_element_type=jnp.float32)
     attended = mixed.astype(jnp.bfloat16).reshape(row_count, features)
+    attended, weight_cols = lax.optimization_barrier((attended, weight_columns(out_weight)))
     half_rows = row_count // 2
     grads_full = jnp.concatenate(
         [
@@ -178,13 +195,11 @@
     grad_attn = lax.dot_general(
         grads_full, out_weight, (((1,), (1,)), ((), ())), preferred_element_type=jnp.float32
     ).astype(jnp.bfloat16)
-    late_attended, late_weight, grad_attn = lax.optimization_barrier(
-        (attended, out_weight, grad_attn)
-    )
+    late_attended, grad_attn = lax.optimization_barrier((attended, grad_attn))
     attended_full = head_ring_gather(late_attended)
-    output = jnp.dot(
-        attended_full, weight_columns(late_weight), preferred_element_type=jnp.float32
-    ).astype(jnp.bfloat16)
+    output = jnp.dot(attended_full, weight_cols, preferred_element_type=jnp.float32).astype(
+        jnp.bfloat16
+    )
     grad_weight = lax.psum_scatter(
         lax.dot_general(
             grads_full, attended, (((0,), (0,)), ((), ())), preferred_element_type=jnp.float32

time: 576 us -> 525 us (0.911)
  waiting for transfers between devices: 103 us -> 64.6 us
  local copies, waits for them, and re-layouts: 196 us -> 187 us
  other arithmetic: 108 us -> 115 us
    ppermute x7 -> x5, waiting for transfers between devices: 64 us -> 0.01 us  [the longest x4 0.01 us: weight_columns(): fetched.append(lax.ppermute(outgoing, ('seq', 'head'), pairs))]
    ppermute x8, waiting for transfers between devices: 20.2 us -> 39 us  [swapped(): return lax.ppermute(value, axis, pairs)]
    ppermute x2, waiting for transfers between devices: 0.01 us -> 7.12 us  [head_ring_gather(): lax.ppermute(value, 'head', [(src, src ^ 1) for src in range(count)])]
    ppermute x2, waiting for transfers between devices: 6.33 us -> 0.01 us  [head_ring_gather(): from_below = lax.ppermute(pair_block, 'head', upward)]
    ppermute x7 -> x5, starting transfers between devices: 14.7 us -> 10.9 us  [the longest x4 10.9 us: weight_columns(): fetched.append(lax.ppermute(outgoing, ('seq', 'head'), pairs))]
    unnamed x69 -> x65, local copies, waits for them, and re-layouts: 29.5 us -> 26.3 us
  transfers between devices with their start and end apart: 27 -> 25, of which waited for: 10 -> 8; matrix products, arithmetic and copies ran while one was open for 61% -> 71% of each run, Pallas kernels for 0% -> 0%
where the time goes in v3:
time: 525 us; the launch traced here: 519 us
  local copies, waits for them, and re-layouts  187 us (36%)
  other arithmetic  115 us (22%)
  matrix products  97.9 us (19%)
  waiting for transfers between devices  64.6 us (12%)
  starting transfers between devices  39.9 us (8%)
  between operations  14.9 us (3%)
    ppermute x8, waiting for transfers between devices, swapped(): return lax.ppermute(value, axis, pairs)  39 us
    unnamed x65, local copies, waits for them, and re-layouts  26.3 us
    slice x2, local copies, waits for them, and re-layouts, body(): key_heads = key_set[0].reshape(blocks, keys_all, head_count, DH)  23.1 us
    reduce_sum x1, other arithmetic, body(): sibling_grads.append(jnp.sum(grad_sets[:, :, lower:lower + BLK], axis=1))  19.3 us
    gather x4, local copies, waits for them, and re-layouts, head_ring_gather(): placed = stacked[order]  19 us
    ppermute x8, starting transfers between devices, swapped(): return lax.ppermute(value, axis, pairs)  17.8 us
    mul x1, local copies, waits for them, and re-layouts, body(): jnp.einsum('bhqk,bqhd->bkhd', grad_score, query_heads, preferred_element_...  16.5 us
    dot_general x1, matrix products, body(): jnp.einsum('bqhd,bkhd->bhqk', grad_heads, value_heads, preferred_element_...  15.7 us
  transfers between devices with their start and end apart: 25, of which 8 were waited for; matrix products, arithmetic and copies ran while one was open for 71% of the time, Pallas kernels for 0%

profile of v3, /device:TPU:0, one launch (start us, length us, event | category | flops | bytes accessed | tf_op | source)
XLA Modules:
  0.0 518.9 jit_solution(10203941278556518998)
XLA Ops:
  27.5 7.7 %convert_reduce_fusion.2 = f32[2,512,512]{2,1,0:T(8,128)S(1)} fusion(bf16[1,512,2,512]{3,2,1,0:T(2,128)(2,1)} %stack.100, bf16[1,512,2,512]{3,2,1,0:T(2,128)(2,1)} %stack.99), kind=kLoop, calls=%fused_computation.58 | loop fusion | flops 2621440 | bytes 4194304 | tf_op jit(solution)/shard_map/reduce_sum | solution.py:139
  79.1 7.7 %collective-permute-done.1 = f32[2,128,512]{2,0,1:T(2,128)} collective-permute-done((f32[2,128,512]{2,0,1:T(2,128)}, f32[2,128,512]{2,0,1:T(2,128)}, u32[]{:S(2)}, u32[]{:S(2)}) %collective-permute-start.1) | collective-permute-done | bytes 524320 | tf_op jit(solution)/shard_map/ppermute | solution.py:18
  117.0 11.6 %fusion.49 = (bf16[1,8,1024,512]{3,2,1,0:T(8,128)(2,1)}, bf16[1,8,1024,512]{3,2,1,0:T(8,128)(2,1)}) fusion(bf16[2,8,1024,512]{3,2,1,0:T(8,128)(2,1)} %broadcast_dynamic-update-slice_fusion), kind=kLoop, calls=%fused_computation.148 | loop fusion | bytes 33554432 | tf_op jit(solution)/shard_map/slice | solution.py:172
  128.6 11.5 %copy.177 = bf16[1,8,1024,512]{2,3,1,0:T(8,128)(2,1)} copy(bf16[1,8,1024,512]{3,2,1,0:T(8,128)(2,1)} %get-tuple-element.46) | data formatting | bytes 16777216 | tf_op jit(solution)/shard_map/slice | solution.py:172
  140.1 11.5 %copy.175 = bf16[1,8,1024,512]{2,3,1,0:T(8,128)(2,1)} copy(bf16[1,8,1024,512]{3,2,1,0:T(8,128)(2,1)} %get-tuple-element.47) | data formatting | bytes 16777216 | tf_op jit(solution)/shard_map/slice | solution.py:173
  151.6 12.9 %fusion.52 = (f32[8,4,128]{2,1,0:T(4,128)S(1)}, f32[8,4,128,1024]{2,3,1,0:T(8,128)}) fusion(f32[1024]{0:T(1024)S(1)} %copy-done.21, pred[8,1024]{1,0:T(8,128)(4,1)S(1)} %concatenate.52, bf16[8,1024,4,128]{1,3,2,0:T(8,128)(2,1)} %bitcast.151, bf16[8,128,4,128]{1,3,2,0:T(8,128)(2,1)S(1)} %copy.191), kind=kOutput, calls=%fused_computation.151 | convolution fusion | flops 1094714368 | bytes 26243072 | tf_op jit(solution)/shard_map/sub | solution.py:181
  164.5 10.6 %fusion.33 = bf16[8,128,4,128]{1,3,2,0:T(8,128)(2,1)S(1)} fusion(bf16[8,1024,4,128]{1,3,2,0:T(8,128)(2,1)} %bitcast.153, f32[8,4,128,1024]{2,3,1,0:T(8,128)} %get-tuple-element.70, f32[8,4,128]{2,1,0:T(4,128)S(1)} %get-tuple-element.69), kind=kOutput, calls=%fused_computation.75 | convolution fusion | flops 1082654720 | bytes 26230784 | tf_op jit(solution)/shard_map/bhqk,bkhd->bqhd/dot_general | solution.py:184
  184.8 6.2 %copy.183 = bf16[512,4,1024]{0,2,1:T(8,128)(2,1)} copy(bf16[512,4,1024]{2,0,1:T(8,128)(2,1)} %bitcast.143) | data formatting | bytes 8388608 | tf_op jit(solution)/shard_map/transpose | solution.py:63
  201.6 11.3 %scatter_fusion = bf16[8,512,512]{2,1,0:T(8,128)(2,1)} fusion(bf16[8,512,512]{2,1,0:T(8,128)(2,1)} %broadcast_in_dim.55, s32[8]{0:T(128)S(1)} %fusion.41, bf16[8,512,512]{2,1,0:T(8,128)(2,1)} %slice_dynamic-update-slice_fusion), kind=kCustom, calls=%fused_computation.3 | custom fusion | bytes 12582944 | tf_op jit(solution)/shard_map/scatter | solution.py:98
  212.9 10.2 %fusion.29 = bf16[1024,512]{1,0:T(8,128)(2,1)} fusion(bf16[512,4096]{1,0:T(8,128)(2,1)} %param.9, bf16[512,4096]{0,1:T(8,128)(2,1)} %bitcast.164, bf16[512,4096]{0,1:T(8,128)(2,1)} %all-gather.2.cloned.1.call-done), kind=kOutput, calls=%fused_computation.72 | convolution fusion | flops 4312268800 | bytes 13631488 | tf_op jit(solution)/shard_map/dot_general | solution.py:195
  225.8 11.3 %fusion.9 = f32[4096,512]{1,0:T(8,128)} fusion(bf16[1024,512]{0,1:T(8,128)(2,1)S(1)} %bitcast.158, bf16[512,4096]{0,1:T(8,128)(2,1)} %bitcast.165, bf16[512,4096]{0,1:T(8,128)(2,1)} %all-gather.2.cloned.1.call-done), kind=kOutput, calls=%fused_computation.35 | convolution fusion | flops 4311744512 | bytes 17825792 | tf_op jit(solution)/shard_map/dot_general | solution.py:204
  238.3 15.7 %multiply_reduce_fusion = (f32[8,4,128]{2,1,0:T(4,128)S(1)}, f32[8,4,128,1024]{2,3,1,0:T(8,128)}) fusion(f32[8,4,128,1024]{2,3,1,0:T(8,128)} %get-tuple-element.70, f32[8,4,128]{2,1,0:T(4,128)S(1)} %get-tuple-element.69, bf16[8,128,4,128]{1,3,2,0:T(8,128)(2,1)S(1)} %copy-done.18, bf16[8,1024,4,128]{1,3,2,0:T(8,128)(2,1)} %bitcast.154), kind=kOutput, calls=%fused_computation.25 | convolution fusion | flops 1086320640 | bytes 43024384 | tf_op jit(solution)/shard_map/bqhd,bkhd->bhqk/dot_general | solution.py:212
  254.0 13.8 %multiply_convert_fusion = bf16[8,4,128,1024]{2,3,1,0:T(8,128)(2,1)S(1)} fusion(f32[8,4,128,1024]{2,3,1,0:T(8,128)} %get-tuple-element.72, f32[8,4,128]{2,1,0:T(4,128)S(1)} %get-tuple-element.71, f32[8,4,128,1024]{2,3,1,0:T(8,128)} %get-tuple-element.70, f32[8,4,128]{2,1,0:T(4,128)S(1)} %get-tuple-element.69), kind=kLoop, calls=%fused_computation.24 | loop fusion | flops 16777216 | bytes 41975808 | tf_op jit(solution)/shard_map/convert_element_type | solution.py:216
  271.0 7.3 %multiply_bitcast_fusion = f32[8,1024,4,128]{3,1,2,0:T(8,128)} fusion(bf16[8,4,128,1024]{2,3,1,0:T(8,128)(2,1)S(1)} %multiply_convert_fusion, bf16[8,128,4,128]{1,3,2,0:T(8,128)(2,1)S(1)} %copy.191), kind=kOutput, calls=%fused_computation.23 | convolution fusion | flops 1077936128 | bytes 26214400 | tf_op jit(solution)/shard_map/bhqk,bqhd->bkhd/dot_general | solution.py:226
  278.3 16.5 %copy.193 = f32[8,1024,4,128]{1,3,2,0:T(8,128)} copy(f32[8,1024,4,128]{3,1,2,0:T(8,128)} %multiply_bitcast_fusion) | data formatting | bytes 33554432 | tf_op jit(solution)/shard_map/mul | solution.py:226
  294.8 14.1 %fusion.22 = f32[8,4,128,1024]{3,2,1,0:T(8,128)} fusion(bf16[8,128,4,128]{1,3,2,0:T(8,128)(2,1)S(1)} %copy-done.18, f32[8,4,128,1024]{2,3,1,0:T(8,128)} %get-tuple-element.70, f32[8,4,128]{2,1,0:T(4,128)S(1)} %get-tuple-element.69), kind=kOutput, calls=%fused_computation.52 | convolution fusion | flops 1082130432 | bytes 34619392 | tf_op jit(solution)/shard_map/bhqk,bqhd->bkhd/dot_general | solution.py:229
  308.9 19.3 %fusion.27 = (f32[2,128,512]{1,2,0:T(8,128)S(1)}, f32[2,128,512]{1,2,0:T(8,128)S(1)}, f32[2,128,512]{1,2,0:T(8,128)S(1)}, f32[2,128,512]{1,2,0:T(8,128)S(1)}, f3...) fusion(f32[1,8,1024,512]{2,3,1,0:T(8,128)} %bitcast.138, ...), kind=kLoop, calls=%fused_computation.60 | loop fusion | flops 12058624 | bytes 52428800 | tf_op jit(solution)/shard_map/reduce_sum | solution.py:250
  335.7 14.1 %collective-permute-done.19 = f32[2,128,512]{2,0,1:T(2,128)S(1)} collective-permute-done((f32[2,128,512]{2,0,1:T(2,128)}, f32[2,128,512]{2,0,1:T(2,128)S(1)}, u32[]{:S(2)}, u32[]{:S(2)}) %collective-permute-start.19) | collective-permute-done | bytes 524320 | tf_op jit(solution)/shard_map/ppermute | solution.py:18
  354.0 7.9 %collective-permute-done.20 = f32[2,128,512]{2,0,1:T(2,128)} collective-permute-done((f32[2,128,512]{2,0,1:T(2,128)}, f32[2,128,512]{2,0,1:T(2,128)}, u32[]{:S(2)}, u32[]{:S(2)}) %collective-permute-start.20) | collective-permute-done | bytes 524320 | tf_op jit(solution)/shard_map/ppermute | solution.py:18
  367.2 7.1 %collective-permute-done.14 = bf16[1024,512]{0,1:T(8,128)(2,1)} collective-permute-done((bf16[1024,512]{0,1:T(8,128)(2,1)S(1)}, bf16[1024,512]{0,1:T(8,128)(2,1)}, u32[]{:S(2)}, u32[]{:S(2)}) %collective-permute-start.14) | collective-permute-done | bytes 1048608 | tf_op jit(solution)/shard_map/ppermute | solution.py:41
  448.4 6.7 %fusion.19 = bf16[2,1024,512]{2,1,0:T(8,128)(2,1)S(1)} fusion(f32[2,1024,512]{2,1,0:T(8,128)} %reshape.284, f32[2,1024,512]{2,1,0:T(8,128)S(1)} %copy-done.3, f32[2,4,2,128,512]{4,3,2,1,0:T(8,128)} %copy.197, f32[2,8,128,512]{3,2,1,0:T(8,128)} %copy.196, f32[2,128,512]{2,1,0:T(8,128)S(1)} %add_multiply_fusion), kind=kLoop, calls=%fused_computation.48 | loop fusion | flops 5242880 | bytes 19398656 | tf_op jit(solution)/shard_map/convert.1
  456.6 13.2 %collective-permute-done.18 = bf16[1024,512]{0,1:T(8,128)(2,1)} collective-permute-done((bf16[1024,512]{0,1:T(8,128)(2,1)S(1)}, bf16[1024,512]{0,1:T(8,128)(2,1)}, u32[]{:S(2)}, u32[]{:S(2)}) %collective-permute-start.18) | collective-permute-done | bytes 1048608 | tf_op jit(solution)/shard_map/ppermute | solution.py:55
  493.9 7.8 %pad_maximum_fusion.2 = bf16[4,1024,1024]{1,2,0:T(8,128)(2,1)} fusion(bf16[4,512,1024]{1,2,0:T(8,128)(2,1)} %gather_fusion.2, bf16[4,512,1024]{1,2,0:T(8,128)(2,1)} %gather_fusion.1), kind=kLoop, calls=%fused_computation.29 | loop fusion | flops 16777216 | bytes 16777216
  501.8 10.1 %convolution_convert_fusion = bf16[1024,512]{1,0:T(8,128)(2,1)} fusion(bf16[1024,4096]{0,1:T(8,128)(2,1)} %bitcast.155, bf16[4096,512]{1,0:T(8,128)(2,1)} %bitcast.142), kind=kOutput, calls=%fused_computation.73 | convolution fusion | flops 4295491584 | bytes 13631488 | tf_op jit(solution)/shard_map/dot_general | solution.py:200
  (207 shorter events, 237.9 us)
Async XLA Ops:
  7.2 205.8 %all-gather.2.cloned.1.call-start = ((), (), s32[]{:S(2)}) async-start(), calls=%async_computation.1 | async-start | bytes 4718592 | tf_op jit(solution)/shard_map/all_gather | solution.py:190
  9.1 58.5 %collective-permute-start.9 = (bf16[512,512]{1,0:T(8,128)(2,1)}, bf16[512,512]{1,0:T(8,128)(2,1)}, u32[]{:S(2)}, u32[]{:S(2)}) collective-permute-start(bf16[512,512]{1,0:T(8,128)(2,1)} %slice.105), channel_id=1, source_target_pairs={{0,1},{1,0},{2,3},{3,2},{4,5},{5,4},{6,7},{7,6},{8,9},{9,8},{10,11... | collective-permute-start | bytes 1572872 | tf_op jit(solution)/shard_map/ppermute | solution.py:41
  14.5 44.0 %collective-permute-start = (f32[2,128,512]{2,1,0:T(8,128)}, f32[2,128,512]{2,1,0:T(8,128)}, u32[]{:S(2)}, u32[]{:S(2)}) collective-permute-start(f32[2,128,512]{2,1,0:T(8,128)} %broadcast_multiply_fusion.4), channel_id=1, source_target_pairs={{0,8},{8,0},{16,24},{24,16},{32,40},{40,32},{48,56},{56,48},{64,72... | collective-permute-start | bytes 1572872 | tf_op jit(solution)/shard_map/ppermute | solution.py:18
  17.5 55.2 %collective-permute-start.4 = (bf16[512,512]{1,0:T(8,128)(2,1)}, bf16[512,512]{1,0:T(8,128)(2,1)}, u32[]{:S(2)}, u32[]{:S(2)}) collective-permute-start(bf16[512,512]{1,0:T(8,128)(2,1)} %get-tuple-element.52), channel_id=1, source_target_pairs={{0,1},{1,2},{2,3},{3,4},{4,5},{5,6},{6,7},{7,0},{8,10},{9,11},{10,... | collective-permute-start | bytes 1572872 | tf_op jit(solution)/shard_map/ppermute | solution.py:88
  17.9 56.7 %collective-permute-start.6 = (bf16[512,512]{1,0:T(8,128)(2,1)}, bf16[512,512]{1,0:T(8,128)(2,1)}, u32[]{:S(2)}, u32[]{:S(2)}) collective-permute-start(bf16[512,512]{1,0:T(8,128)(2,1)} %get-tuple-element.53), channel_id=1, source_target_pairs={{0,5},{1,6},{2,7},{3,0},{4,1},{5,2},{6,3},{7,4},{8,14},{9,15},{10,... | collective-permute-start | bytes 1572872 | tf_op jit(solution)/shard_map/ppermute | solution.py:88
  22.9 52.0 %collective-permute-start.5 = (bf16[512,512]{1,0:T(8,128)(2,1)}, bf16[512,512]{1,0:T(8,128)(2,1)}, u32[]{:S(2)}, u32[]{:S(2)}) collective-permute-start(bf16[512,512]{1,0:T(8,128)(2,1)} %get-tuple-element.54), channel_id=1, source_target_pairs={{0,3},{1,4},{2,5},{3,6},{4,7},{5,0},{6,1},{7,2},{8,12},{9,13},{10,... | collective-permute-start | bytes 1572872 | tf_op jit(solution)/shard_map/ppermute | solution.py:88
  58.5 16.3 %collective-permute-start.7 = (bf16[512,512]{1,0:T(8,128)(2,1)}, bf16[512,512]{1,0:T(8,128)(2,1)}, u32[]{:S(2)}, u32[]{:S(2)}) collective-permute-start(bf16[512,512]{1,0:T(8,128)(2,1)} %get-tuple-element.55), channel_id=1, source_target_pairs={{0,7},{1,0},{2,1},{3,2},{4,3},{5,4},{6,5},{7,6},{16,23},{17,16},{1... | collective-permute-start | bytes 1572872 | tf_op jit(solution)/shard_map/ppermute | solution.py:88
  67.6 19.2 %collective-permute-start.1 = (f32[2,128,512]{2,0,1:T(2,128)}, f32[2,128,512]{2,0,1:T(2,128)}, u32[]{:S(2)}, u32[]{:S(2)}) collective-permute-start(f32[2,128,512]{2,0,1:T(2,128)} %broadcast_multiply_fusion.3), channel_id=1, source_target_pairs={{0,16},{8,24},{16,0},{24,8},{32,48},{40,56},{48,32},{56,40},{64,80... | collective-permute-start | bytes 1572872 | tf_op jit(solution)/shard_map/ppermute | solution.py:18
  72.5 439.3 %reduce-scatter.2.cloned.1.call-start = ((), (), s32[]{:S(2)}) async-start(), calls=%async_computation.2 | async-start | bytes 8912896 | tf_op jit(solution)/shard_map/reduce_scatter | solution.py:203
  72.7 36.5 %collective-permute-start.10 = (bf16[512,1024]{1,0:T(8,128)(2,1)S(1)}, bf16[512,1024]{1,0:T(8,128)(2,1)S(1)}, u32[]{:S(2)}, u32[]{:S(2)}) collective-permute-start(bf16[512,1024]{1,0:T(8,128)(2,1)S(1)} %get-tuple-element.68), channel_id=1, source_target_pairs={{0,6},{1,7},{2,0},{3,1},{4,2},{5,3},{6,4},{7,5},{8,14},{9,15},{10,... | collective-permute-start | bytes 3145736 | tf_op jit(solution)/shard_map/ppermute | solution.py:49
  74.6 35.5 %collective-permute-start.11 = (bf16[512,1024]{1,0:T(8,128)(2,1)S(1)}, bf16[512,1024]{1,0:T(8,128)(2,1)S(1)}, u32[]{:S(2)}, u32[]{:S(2)}) collective-permute-start(bf16[512,1024]{1,0:T(8,128)(2,1)S(1)} %get-tuple-element.68), channel_id=1, source_target_pairs={{0,2},{1,3},{2,4},{3,5},{4,6},{5,7},{6,0},{7,1},{8,10},{9,11},{10,... | collective-permute-start | bytes 3145736 | tf_op jit(solution)/shard_map/ppermute | solution.py:48
  78.0 113.0 %collective-permute-start.8 = (bf16[4,512,512]{2,1,0:T(8,128)(2,1)}, bf16[4,512,512]{2,1,0:T(8,128)(2,1)}, u32[]{:S(2)}, u32[]{:S(2)}) collective-permute-start(bf16[4,512,512]{2,1,0:T(8,128)(2,1)} %pad_maximum_fusion.8), channel_id=1, source_target_pairs={{0,8},{8,0},{16,24},{24,16},{32,40},{40,32},{48,56},{56,48},{64,72... | collective-permute-start | bytes 6291464 | tf_op jit(solution)/shard_map/ppermute | solution.py:90
  90.0 12.1 %collective-permute-start.2 = (f32[2,128,512]{2,0,1:T(2,128)S(1)}, f32[2,128,512]{2,0,1:T(2,128)S(1)}, u32[]{:S(2)}, u32[]{:S(2)}) collective-permute-start(f32[2,128,512]{2,0,1:T(2,128)S(1)} %broadcast_multiply_fusion.2), channel_id=1, source_target_pairs={{0,32},{8,40},{16,48},{24,56},{32,0},{40,8},{48,16},{56,24},{64,96... | collective-permute-start | bytes 1572872 | tf_op jit(solution)/shard_map/ppermute | solution.py:18
  103.5 12.0 %collective-permute-start.3 = (bf16[2,128,512]{2,0,1:T(2,128)(2,1)S(1)}, bf16[2,128,512]{2,0,1:T(2,128)(2,1)S(1)}, u32[]{:S(2)}, u32[]{:S(2)}) collective-permute-start(bf16[2,128,512]{2,0,1:T(2,128)(2,1)S(1)} %broadcast_multiply_fusion.1), channel_id=1, source_target_pairs={{0,64},{8,72},{16,80},{24,88},{32,96},{40,104},{48,112},{56,120},{... | collective-permute-start | bytes 786440 | tf_op jit(solution)/shard_map/ppermute | solution.py:18
  110.1 66.0 %collective-permute-start.13 = (bf16[512,512]{1,0:T(8,128)(2,1)}, bf16[512,512]{1,0:T(8,128)(2,1)}, u32[]{:S(2)}, u32[]{:S(2)}) collective-permute-start(bf16[512,512]{1,0:T(8,128)(2,1)} %slice.142), channel_id=1, source_target_pairs={{0,6},{1,7},{2,0},{3,1},{4,2},{5,3},{6,4},{7,5},{8,14},{9,15},{10,... | collective-permute-start | bytes 1572872 | tf_op jit(solution)/shard_map/ppermute | solution.py:55
  111.9 64.2 %collective-permute-start.12 = (bf16[512,512]{1,0:T(8,128)(2,1)}, bf16[512,512]{1,0:T(8,128)(2,1)}, u32[]{:S(2)}, u32[]{:S(2)}) collective-permute-start(bf16[512,512]{1,0:T(8,128)(2,1)} %slice.141), channel_id=1, source_target_pairs={{0,2},{1,3},{2,4},{3,5},{4,6},{5,7},{6,0},{7,1},{8,10},{9,11},{10,... | collective-permute-start | bytes 1572872 | tf_op jit(solution)/shard_map/ppermute | solution.py:54
  329.2 20.5 %collective-permute-start.19 = (f32[2,128,512]{2,0,1:T(2,128)}, f32[2,128,512]{2,0,1:T(2,128)S(1)}, u32[]{:S(2)}, u32[]{:S(2)}) collective-permute-start(f32[2,128,512]{2,0,1:T(2,128)} %copy.200), channel_id=1, source_target_pairs={{0,64},{8,72},{16,80},{24,88},{32,96},{40,104},{48,112},{56,120},{... | collective-permute-start | bytes 1572872 | tf_op jit(solution)/shard_map/ppermute | solution.py:18
  353.0 21.3 %collective-permute-start.14 = (bf16[1024,512]{0,1:T(8,128)(2,1)S(1)}, bf16[1024,512]{0,1:T(8,128)(2,1)}, u32[]{:S(2)}, u32[]{:S(2)}) collective-permute-start(bf16[1024,512]{0,1:T(8,128)(2,1)S(1)} %bitcast.159), channel_id=1, source_target_pairs={{0,1},{1,0},{2,3},{3,2},{4,5},{5,4},{6,7},{7,6},{8,9},{9,8},{10,11... | collective-permute-start | bytes 3145736 | tf_op jit(solution)/shard_map/ppermute | solution.py:41
  365.9 19.0 %collective-permute-start.21 = (f32[2,128,512]{2,0,1:T(2,128)}, f32[2,128,512]{2,0,1:T(2,128)S(1)}, u32[]{:S(2)}, u32[]{:S(2)}) collective-permute-start(f32[2,128,512]{2,0,1:T(2,128)} %select_add_fusion.1), channel_id=1, source_target_pairs={{0,16},{8,24},{16,0},{24,8},{32,48},{40,56},{48,32},{56,40},{64,80... | collective-permute-start | bytes 1572872 | tf_op jit(solution)/shard_map/ppermute | solution.py:18
  378.6 63.9 %collective-permute-start.15 = (bf16[1024,1024]{0,1:T(8,128)(2,1)}, bf16[1024,1024]{0,1:T(8,128)(2,1)}, u32[]{:S(2)}, u32[]{:S(2)}) collective-permute-start(bf16[1024,1024]{0,1:T(8,128)(2,1)} %get-tuple-element.59), channel_id=1, source_target_pairs={{0,6},{1,7},{2,0},{3,1},{4,2},{5,3},{6,4},{7,5},{8,14},{9,15},{10,... | collective-permute-start | bytes 6291464 | tf_op jit(solution)/shard_map/ppermute | solution.py:49
  380.7 66.0 %collective-permute-start.16 = (bf16[1024,1024]{0,1:T(8,128)(2,1)}, bf16[1024,1024]{0,1:T(8,128)(2,1)}, u32[]{:S(2)}, u32[]{:S(2)}) collective-permute-start(bf16[1024,1024]{0,1:T(8,128)(2,1)} %get-tuple-element.59), channel_id=1, source_target_pairs={{0,2},{1,3},{2,4},{3,5},{4,6},{5,7},{6,0},{7,1},{8,10},{9,11},{10,... | collective-permute-start | bytes 6291464 | tf_op jit(solution)/shard_map/ppermute | solution.py:48
  387.1 53.9 %collective-permute-start.22 = (f32[2,128,512]{2,1,0:T(8,128)}, f32[2,128,512]{2,1,0:T(8,128)}, u32[]{:S(2)}, u32[]{:S(2)}) collective-permute-start(f32[2,128,512]{2,1,0:T(8,128)} %select_add_fusion), channel_id=1, source_target_pairs={{0,8},{8,0},{16,24},{24,16},{32,40},{40,32},{48,56},{56,48},{64,72... | collective-permute-start | bytes 1572872 | tf_op jit(solution)/shard_map/ppermute | solution.py:18
  443.8 26.0 %collective-permute-start.18 = (bf16[1024,512]{0,1:T(8,128)(2,1)S(1)}, bf16[1024,512]{0,1:T(8,128)(2,1)}, u32[]{:S(2)}, u32[]{:S(2)}) collective-permute-start(bf16[1024,512]{0,1:T(8,128)(2,1)S(1)} %slice.144), channel_id=1, source_target_pairs={{0,6},{1,7},{2,0},{3,1},{4,2},{5,3},{6,4},{7,5},{8,14},{9,15},{10,... | collective-permute-start | bytes 3145736 | tf_op jit(solution)/shard_map/ppermute | solution.py:55
  448.0 26.9 %collective-permute-start.17 = (bf16[1024,512]{0,1:T(8,128)(2,1)S(1)}, bf16[1024,512]{0,1:T(8,128)(2,1)}, u32[]{:S(2)}, u32[]{:S(2)}) collective-permute-start(bf16[1024,512]{0,1:T(8,128)(2,1)S(1)} %slice.143), channel_id=1, source_target_pairs={{0,2},{1,3},{2,4},{3,5},{4,6},{5,7},{6,0},{7,1},{8,10},{9,11},{10,... | collective-permute-start | bytes 3145736 | tf_op jit(solution)/shard_map/ppermute | solution.py:54
  (25 other events, 338.7 us)
Sparse Core Ops, SparseCore 0:
  72.6 89.7 all-gather.1
  237.2 103.8 reduce-scatter.1

commit v4 on v3

--- a/solution.py
+++ b/solution.py
@@ -32,7 +32,7 @@
     return wide.reshape(shape_in[:-2] + (shape_in[-2] * factor, shape_in[-1]))
 
 
-def head_ring_gather(value):
+def head_ring_gather(value, relative=False):
     count = lax.axis_size("head")
     rings = count // 2
     width = value.shape[-1]
@@ -57,6 +57,8 @@
             axis=-1,
         )
         blocks = [pair_block, from_above, far, from_below]
+    if relative:
+        return blocks
     stacked = jnp.stack(blocks)
     order = (jnp.arange(rings) - ring_pos) % rings
     placed = stacked[order]
@@ -93,10 +95,21 @@
     by_shift = [own]
     for shift in range(1, count):
         by_shift.append(odd[(shift - 1) // 2] if shift % 2 else even[shift // 2 - 1])
-    stacked = jnp.stack(by_shift)
-    order = (where_head - jnp.arange(count)) % count
-    placed = jnp.zeros_like(stacked).at[order].set(stacked)
-    return placed.reshape(count * rows, width)
+    low_first = where_head % 2 == 0
+    ring_blocks = []
+    for dist in range(count // 2):
+        ring_blocks.append(
+            jnp.where(
+                low_first,
+                jnp.concatenate(
+                    [by_shift[(-2 * dist) % count], by_shift[(-1 - 2 * dist) % count]], axis=0
+                ),
+                jnp.concatenate(
+                    [by_shift[(1 - 2 * dist) % count], by_shift[(-2 * dist) % count]], axis=0
+                ),
+            )
+        )
+    return ring_blocks
 
 def body(queries, key_rows, value_rows, out_weight, cotangent, pattern):
     row_count, features = queries.shape
@@ -196,10 +209,13 @@
         grads_full, out_weight, (((1,), (1,)), ((), ())), preferred_element_type=jnp.float32
     ).astype(jnp.bfloat16)
     late_attended, grad_attn = lax.optimization_barrier((attended, grad_attn))
-    attended_full = head_ring_gather(late_attended)
-    output = jnp.dot(attended_full, weight_cols, preferred_element_type=jnp.float32).astype(
-        jnp.bfloat16
-    )
+    attended_blocks = head_ring_gather(late_attended, relative=True)
+    output_sum = jnp.dot(attended_blocks[0], weight_cols[0], preferred_element_type=jnp.float32)
+    for dist in range(1, len(attended_blocks)):
+        output_sum = output_sum + jnp.dot(
+            attended_blocks[dist], weight_cols[dist], preferred_element_type=jnp.float32
+        )
+    output = output_sum.astype(jnp.bfloat16)
     grad_weight = lax.psum_scatter(
         lax.dot_general(
             grads_full, attended, (((0,), (0,)), ((), ())), preferred_element_type=jnp.float32
@@ -231,6 +247,7 @@
     )
     grad_sets = jnp.stack([grad_keyset, grad_valset]).reshape(2, blocks, keys_all, features)
     token_grad = grad_sets[:, :, :BLK].reshape(2, row_count, features)
+    level_grads = []
     for level_idx in range(local_levels):
         factor = 2**level_idx
         group_count = blocks >> level_idx
@@ -243,7 +260,7 @@
         restored = segment.reshape(2, group_count // 2, 2, BLK, features)[:, :, ::-1].reshape(
             2, group_count * BLK, features
         )
-        token_grad = token_grad + spread_rows(restored, factor)
+        level_grads.append(restored)
     sibling_grads = []
     for level_idx in range(cross_levels):
         lower = (local_levels + 1 + level_idx) * BLK
@@ -261,7 +278,10 @@
         else:
             own_part = jnp.zeros_like(outgoing)
         carried = own_part + swapped(outgoing, "seq", level_idx)
-    token_grad = token_grad + spread_rows(carried, 2**local_levels)
+    pooled_grad = carried
+    for level_idx in reversed(range(local_levels)):
+        pooled_grad = level_grads[level_idx] + spread_rows(pooled_grad, 2)
+    token_grad = token_grad + pooled_grad
     grad_keys = token_grad[0].astype(jnp.bfloat16)
     grad_values = token_grad[1].astype(jnp.bfloat16)
     return (output, grad_query, grad_keys, grad_values, grad_weight)

time: 525 us -> 498 us (0.949)
  local copies, waits for them, and re-layouts: 187 us -> 165 us
  other arithmetic: 115 us -> 103 us
  matrix products: 97.9 us -> 104 us
    reduce_sum x1 -> x0, other arithmetic: 19.3 us -> none  [body(): sibling_grads.append(jnp.sum(grad_sets[:, :, lower:lower + BLK], axis=1))]
    another operation x1 -> x2, other arithmetic: 6.72 us -> 24.7 us  [the longest x1 18.8 us: body(): jnp.stack([grad_keyset, grad_valset]).reshape(2, blocks, keys_all, features)]
    gather x4 -> x1, local copies, waits for them, and re-layouts: 19 us -> 5.04 us  [head_ring_gather(): placed = stacked[order]]
    scatter x1 -> x0, local copies, waits for them, and re-layouts: 11.3 us -> none  [weight_columns(): placed = jnp.zeros_like(stacked).at[order].set(stacked)]
    unnamed x3 -> x1, other arithmetic: 9.37 us -> 1.51 us
    another operation x6 -> x3, other arithmetic: 11.4 us -> 3.72 us  [head_ring_gather(): stacked = jnp.stack(blocks)]
    ppermute x2, waiting for transfers between devices: 7.12 us -> 13.1 us  [head_ring_gather(): lax.ppermute(value, 'head', [(src, src ^ 1) for src in range(count)])]
    dot_general x1 -> x4, matrix products: 10.1 us -> 12.7 us  [the longest x3 8.19 us: body(): jnp.dot(attended_blocks[dist], weight_cols[dist], preferred_element_type=...]
  transfers between devices with their start and end apart: 25 -> 25, of which waited for: 8 -> 9; matrix products, arithmetic and copies ran while one was open for 71% -> 69% of each run, Pallas kernels for 0% -> 0%
where the time goes in v4:
time: 498 us; the launch traced here: 491 us
  local copies, waits for them, and re-layouts  165 us (33%)
  matrix products  104 us (21%)
  other arithmetic  103 us (21%)
  waiting for transfers between devices  64.2 us (13%)
  starting transfers between devices  39.4 us (8%)
  between operations  14.8 us (3%)
    ppermute x8, waiting for transfers between devices, swapped(): return lax.ppermute(value, axis, pairs)  35.1 us
    unnamed x61, local copies, waits for them, and re-layouts  28.3 us
    slice x2, local copies, waits for them, and re-layouts, body(): key_heads = key_set[0].reshape(blocks, keys_all, head_count, DH)  23.3 us
    another operation x1, other arithmetic, body(): jnp.stack([grad_keyset, grad_valset]).reshape(2, blocks, keys_all, features)  18.8 us
    ppermute x8, starting transfers between devices, swapped(): return lax.ppermute(value, axis, pairs)  18.3 us
    dot_general x1, matrix products, body(): jnp.einsum('bqhd,bkhd->bhqk', grad_heads, value_heads, preferred_element_...  17.3 us
    mul x1, local copies, waits for them, and re-layouts, body(): jnp.einsum('bhqk,bqhd->bkhd', grad_score, query_heads, preferred_element_...  16.5 us
    dot_general x1, matrix products, body(): jnp.einsum('bhqk,bqhd->bkhd', prob_low, grad_heads, preferred_element_typ...  14.4 us
  transfers between devices with their start and end apart: 25, of which 9 were waited for; matrix products, arithmetic and copies ran while one was open for 69% of the time, Pallas kernels for 0%

profile of v4, /device:TPU:0, one launch (start us, length us, event | category | flops | bytes accessed | tf_op | source)
XLA Modules:
  0.0 491.3 jit_solution(17120386292860499754)
XLA Ops:
  32.3 7.7 %convert_reduce_fusion.2 = f32[2,512,512]{2,1,0:T(8,128)S(1)} fusion(bf16[1,512,2,512]{3,2,1,0:T(2,128)(2,1)} %stack.79, bf16[1,512,2,512]{3,2,1,0:T(2,128)(2,1)} %stack.78), kind=kLoop, calls=%fused_computation.51 | loop fusion | flops 2621440 | bytes 4194304 | tf_op jit(solution)/shard_map/reduce_sum | solution.py:152
  84.3 8.3 %collective-permute-done.1 = f32[2,128,512]{2,0,1:T(2,128)} collective-permute-done((f32[2,128,512]{2,0,1:T(2,128)}, f32[2,128,512]{2,0,1:T(2,128)}, u32[]{:S(2)}, u32[]{:S(2)}) %collective-permute-start.1) | collective-permute-done | bytes 524320 | tf_op jit(solution)/shard_map/ppermute | solution.py:18
  108.7 6.3 %collective-permute-start.3 = (bf16[2,128,512]{2,0,1:T(2,128)(2,1)S(1)}, bf16[2,128,512]{2,0,1:T(2,128)(2,1)S(1)}, u32[]{:S(2)}, u32[]{:S(2)}) collective-permute-start(bf16[2,128,512]{2,0,1:T(2,128)(2,1)S(1)} %broadcast_multiply_fusion.1), channel_id=1, source_target_pairs={{0,64},{8,72},{16,80},{24,88},{32,96},{40,104},{48,112},{56,120},{... | collective-permute-start | bytes 786440 | tf_op jit(solution)/shard_map/ppermute | solution.py:18
  123.9 11.8 %fusion.53 = (bf16[1,8,1024,512]{3,2,1,0:T(8,128)(2,1)}, bf16[1,8,1024,512]{3,2,1,0:T(8,128)(2,1)}) fusion(bf16[2,8,1024,512]{3,2,1,0:T(8,128)(2,1)} %broadcast_dynamic-update-slice_fusion), kind=kLoop, calls=%fused_computation.145 | loop fusion | bytes 33554432 | tf_op jit(solution)/shard_map/slice | solution.py:185
  135.7 11.5 %copy.198 = bf16[1,8,1024,512]{2,3,1,0:T(8,128)(2,1)} copy(bf16[1,8,1024,512]{3,2,1,0:T(8,128)(2,1)} %get-tuple-element.56) | data formatting | bytes 16777216 | tf_op jit(solution)/shard_map/slice | solution.py:185
  147.2 11.5 %copy.196 = bf16[1,8,1024,512]{2,3,1,0:T(8,128)(2,1)} copy(bf16[1,8,1024,512]{3,2,1,0:T(8,128)(2,1)} %get-tuple-element.57) | data formatting | bytes 16777216 | tf_op jit(solution)/shard_map/slice | solution.py:186
  158.7 12.9 %fusion.54 = (f32[8,4,128]{2,1,0:T(4,128)S(1)}, f32[8,4,128,1024]{2,3,1,0:T(8,128)}) fusion(f32[1024]{0:T(1024)S(1)} %copy-done.22, pred[8,1024]{1,0:T(8,128)(4,1)S(1)} %concatenate.76, bf16[8,1024,4,128]{1,3,2,0:T(8,128)(2,1)} %bitcast.152, bf16[8,128,4,128]{1,3,2,0:T(8,128)(2,1)S(1)} %copy.217), kind=kOutput, calls=%fused_computation.146 | convolution fusion | flops 1094714368 | bytes 26243072 | tf_op jit(solution)/shard_map/sub | solution.py:194
  171.6 10.6 %fusion.37 = bf16[8,128,4,128]{1,3,2,0:T(8,128)(2,1)S(1)} fusion(bf16[8,1024,4,128]{1,3,2,0:T(8,128)(2,1)} %bitcast.154, f32[8,4,128,1024]{2,3,1,0:T(8,128)} %get-tuple-element.86, f32[8,4,128]{2,1,0:T(4,128)S(1)} %get-tuple-element.85), kind=kOutput, calls=%fused_computation.72 | convolution fusion | flops 1082654720 | bytes 26230784 | tf_op jit(solution)/shard_map/bhqk,bkhd->bqhd/dot_general | solution.py:197
  191.8 6.2 %copy.209 = bf16[512,4,1024]{0,2,1:T(8,128)(2,1)} copy(bf16[512,4,1024]{2,0,1:T(8,128)(2,1)} %bitcast.143) | data formatting | bytes 8388608 | tf_op jit(solution)/shard_map/transpose | solution.py:65
  204.1 10.2 %fusion.33 = bf16[1024,512]{1,0:T(8,128)(2,1)} fusion(bf16[512,4096]{1,0:T(8,128)(2,1)} %param.9, bf16[512,4096]{0,1:T(8,128)(2,1)} %bitcast.163, bf16[512,4096]{0,1:T(8,128)(2,1)} %all-gather.2.cloned.1.call-done), kind=kOutput, calls=%fused_computation.70 | convolution fusion | flops 4312268800 | bytes 13631488 | tf_op jit(solution)/shard_map/dot_general | solution.py:208
  216.9 11.3 %fusion.9 = f32[4096,512]{1,0:T(8,128)} fusion(bf16[1024,512]{0,1:T(8,128)(2,1)S(1)} %bitcast.158, bf16[512,4096]{0,1:T(8,128)(2,1)} %bitcast.164, bf16[512,4096]{0,1:T(8,128)(2,1)} %all-gather.2.cloned.1.call-done), kind=kOutput, calls=%fused_computation.30 | convolution fusion | flops 4311744512 | bytes 17825792 | tf_op jit(solution)/shard_map/dot_general | solution.py:220
  229.4 17.3 %multiply_reduce_fusion = (f32[8,4,128]{2,1,0:T(4,128)S(1)}, f32[8,4,128,1024]{2,3,1,0:T(8,128)}) fusion(f32[8,4,128,1024]{2,3,1,0:T(8,128)} %get-tuple-element.86, f32[8,4,128]{2,1,0:T(4,128)S(1)} %get-tuple-element.85, bf16[8,128,4,128]{1,3,2,0:T(8,128)(2,1)S(1)} %copy-done.20, bf16[8,1024,4,128]{1,3,2,0:T(8,128)(2,1)} %bitcast.155), kind=kOutput, calls=%fused_computation.22 | convolution fusion | flops 1086320640 | bytes 43024384 | tf_op jit(solution)/shard_map/bqhd,bkhd->bhqk/dot_general | solution.py:228
  246.7 13.0 %multiply_convert_fusion = bf16[8,4,128,1024]{2,3,1,0:T(8,128)(2,1)S(1)} fusion(f32[8,4,128,1024]{2,3,1,0:T(8,128)} %get-tuple-element.88, f32[8,4,128]{2,1,0:T(4,128)S(1)} %get-tuple-element.87, f32[8,4,128,1024]{2,3,1,0:T(8,128)} %get-tuple-element.86, f32[8,4,128]{2,1,0:T(4,128)S(1)} %get-tuple-element.85), kind=kLoop, calls=%fused_computation.21 | loop fusion | flops 16777216 | bytes 41975808 | tf_op jit(solution)/shard_map/convert_element_type | solution.py:232
  262.9 7.0 %multiply_bitcast_fusion = f32[8,1024,4,128]{3,1,2,0:T(8,128)} fusion(bf16[8,4,128,1024]{2,3,1,0:T(8,128)(2,1)S(1)} %multiply_convert_fusion, bf16[8,128,4,128]{1,3,2,0:T(8,128)(2,1)S(1)} %copy.217), kind=kOutput, calls=%fused_computation.20 | convolution fusion | flops 1077936128 | bytes 26214400 | tf_op jit(solution)/shard_map/bhqk,bqhd->bkhd/dot_general | solution.py:242
  269.9 16.5 %copy.219 = f32[8,1024,4,128]{1,3,2,0:T(8,128)} copy(f32[8,1024,4,128]{3,1,2,0:T(8,128)} %multiply_bitcast_fusion) | data formatting | bytes 33554432 | tf_op jit(solution)/shard_map/mul | solution.py:242
  286.4 14.4 %fusion.21 = f32[8,4,128,1024]{3,2,1,0:T(8,128)} fusion(bf16[8,128,4,128]{1,3,2,0:T(8,128)(2,1)S(1)} %copy-done.20, f32[8,4,128,1024]{2,3,1,0:T(8,128)} %get-tuple-element.86, f32[8,4,128]{2,1,0:T(4,128)S(1)} %get-tuple-element.85), kind=kOutput, calls=%fused_computation.45 | convolution fusion | flops 1082130432 | bytes 34619392 | tf_op jit(solution)/shard_map/bhqk,bqhd->bkhd/dot_general | solution.py:245
  300.8 18.8 %fusion.12 = (f32[2,8,128,512]{2,3,1,0:T(8,128)}, f32[2,8,128,512]{2,3,1,0:T(8,128)}, f32[2,128,512]{1,2,0:T(8,128)S(1)}, f32[2,128,512]{1,2,0:T(8,128)S(1)}, f3...) fusion(f32[1,8,1024,512]{2,3,1,0:T(8,128)} %bitcast.132, ...), kind=kLoop, calls=%fused_computation.33 | loop fusion | flops 12058624 | bytes 52428800 | tf_op jit(solution)/shard_map/stack | solution.py:248
  325.1 11.2 %collective-permute-done.19 = f32[2,128,512]{2,0,1:T(2,128)S(1)} collective-permute-done((f32[2,128,512]{2,0,1:T(2,128)}, f32[2,128,512]{2,0,1:T(2,128)S(1)}, u32[]{:S(2)}, u32[]{:S(2)}) %collective-permute-start.19) | collective-permute-done | bytes 524320 | tf_op jit(solution)/shard_map/ppermute | solution.py:18
  342.4 6.1 %collective-permute-done.20 = f32[2,128,512]{2,0,1:T(2,128)} collective-permute-done((f32[2,128,512]{2,0,1:T(2,128)}, f32[2,128,512]{2,0,1:T(2,128)}, u32[]{:S(2)}, u32[]{:S(2)}) %collective-permute-start.20) | collective-permute-done | bytes 524320 | tf_op jit(solution)/shard_map/ppermute | solution.py:18
  353.7 13.1 %collective-permute-done.14 = bf16[1024,512]{0,1:T(8,128)(2,1)} collective-permute-done((bf16[1024,512]{0,1:T(8,128)(2,1)S(1)}, bf16[1024,512]{0,1:T(8,128)(2,1)}, u32[]{:S(2)}, u32[]{:S(2)}) %collective-permute-start.14) | collective-permute-done | bytes 1048608 | tf_op jit(solution)/shard_map/ppermute | solution.py:41
  380.0 8.1 %fusion.40 = bf16[8,128,4,128]{1,3,2,0:T(8,128)(2,1)S(1)} fusion(bf16[8,1024,4,128]{1,3,2,0:T(8,128)(2,1)} %bitcast.153, bf16[8,4,128,1024]{2,3,1,0:T(8,128)(2,1)} %copy-done), kind=kOutput, calls=%fused_computation.73 | convolution fusion | flops 1074790400 | bytes 17825792 | tf_op jit(solution)/shard_map/bhqk,bkhd->bqhd/dot_general | solution.py:235
  442.0 6.1 %reshape.255 = f32[2,1024,512]{2,1,0:T(8,128)} reshape(f32[2,512,2,512]{3,2,1,0:T(2,128)} %broadcast_in_dim.58) | data formatting | bytes 8388608 | tf_op jit(solution)/shard_map/reshape | solution.py:32
  453.1 5.9 %fusion.20 = bf16[2,1024,512]{2,1,0:T(8,128)(2,1)S(1)} fusion(f32[2,1024,512]{2,1,0:T(8,128)} %reshape.255, f32[2,4,2,128,512]{4,3,2,1,0:T(8,128)} %copy.223, f32[2,8,128,512]{3,2,1,0:T(8,128)} %copy.222), kind=kLoop, calls=%fused_computation.44 | loop fusion | flops 3145728 | bytes 14680064 | tf_op jit(solution)/shard_map/convert.1
  463.6 11.4 %collective-permute-done.18 = bf16[1024,512]{0,1:T(8,128)(2,1)S(1)} collective-permute-done((bf16[1024,512]{0,1:T(8,128)(2,1)S(1)}, bf16[1024,512]{0,1:T(8,128)(2,1)S(1)}, u32[]{:S(2)}, u32[]{:S(2)}) %collective-permute-start.18) | collective-permute-done | bytes 1048608 | tf_op jit(solution)/shard_map/ppermute | solution.py:55
  (201 shorter events, 219.5 us)
Async XLA Ops:
  7.2 196.9 %all-gather.2.cloned.1.call-start = ((), (), s32[]{:S(2)}) async-start(), calls=%async_computation.1 | async-start | bytes 4718592 | tf_op jit(solution)/shard_map/all_gather | solution.py:203
  9.1 63.4 %collective-permute-start.9 = (bf16[512,512]{1,0:T(8,128)(2,1)}, bf16[512,512]{1,0:T(8,128)(2,1)}, u32[]{:S(2)}, u32[]{:S(2)}) collective-permute-start(bf16[512,512]{1,0:T(8,128)(2,1)} %slice.105), channel_id=1, source_target_pairs={{0,1},{1,0},{2,3},{3,2},{4,5},{5,4},{6,7},{7,6},{8,9},{9,8},{10,11... | collective-permute-start | bytes 1572872 | tf_op jit(solution)/shard_map/ppermute | solution.py:41
  14.6 50.9 %collective-permute-start = (f32[2,128,512]{2,1,0:T(8,128)}, f32[2,128,512]{2,1,0:T(8,128)}, u32[]{:S(2)}, u32[]{:S(2)}) collective-permute-start(f32[2,128,512]{2,1,0:T(8,128)} %broadcast_multiply_fusion.4), channel_id=1, source_target_pairs={{0,8},{8,0},{16,24},{24,16},{32,40},{40,32},{48,56},{56,48},{64,72... | collective-permute-start | bytes 1572872 | tf_op jit(solution)/shard_map/ppermute | solution.py:18
  19.7 58.2 %collective-permute-start.7 = (bf16[512,512]{0,1:T(8,128)(2,1)}, bf16[512,512]{0,1:T(8,128)(2,1)}, u32[]{:S(2)}, u32[]{:S(2)}) collective-permute-start(bf16[512,512]{0,1:T(8,128)(2,1)} %copy.246), channel_id=1, source_target_pairs={{0,7},{1,0},{2,1},{3,2},{4,3},{5,4},{6,5},{7,6},{16,23},{17,16},{1... | collective-permute-start | bytes 1572872 | tf_op jit(solution)/shard_map/ppermute | solution.py:90
  25.6 54.2 %collective-permute-start.4 = (bf16[512,512]{0,1:T(8,128)(2,1)}, bf16[512,512]{0,1:T(8,128)(2,1)}, u32[]{:S(2)}, u32[]{:S(2)}) collective-permute-start(bf16[512,512]{0,1:T(8,128)(2,1)} %copy.243), channel_id=1, source_target_pairs={{0,1},{1,2},{2,3},{3,4},{4,5},{5,6},{6,7},{7,0},{8,10},{9,11},{10,... | collective-permute-start | bytes 1572872 | tf_op jit(solution)/shard_map/ppermute | solution.py:90
  26.6 53.4 %collective-permute-start.5 = (bf16[512,512]{0,1:T(8,128)(2,1)}, bf16[512,512]{0,1:T(8,128)(2,1)}, u32[]{:S(2)}, u32[]{:S(2)}) collective-permute-start(bf16[512,512]{0,1:T(8,128)(2,1)} %copy.244), channel_id=1, source_target_pairs={{0,3},{1,4},{2,5},{3,6},{4,7},{5,0},{6,1},{7,2},{8,12},{9,13},{10,... | collective-permute-start | bytes 1572872 | tf_op jit(solution)/shard_map/ppermute | solution.py:90
  65.5 14.5 %collective-permute-start.6 = (bf16[512,512]{0,1:T(8,128)(2,1)}, bf16[512,512]{0,1:T(8,128)(2,1)}, u32[]{:S(2)}, u32[]{:S(2)}) collective-permute-start(bf16[512,512]{0,1:T(8,128)(2,1)} %copy.245), channel_id=1, source_target_pairs={{0,5},{1,6},{2,7},{3,0},{4,1},{5,2},{6,3},{7,4},{8,14},{9,15},{10,... | collective-permute-start | bytes 1572872 | tf_op jit(solution)/shard_map/ppermute | solution.py:90
  72.5 20.1 %collective-permute-start.1 = (f32[2,128,512]{2,0,1:T(2,128)}, f32[2,128,512]{2,0,1:T(2,128)}, u32[]{:S(2)}, u32[]{:S(2)}) collective-permute-start(f32[2,128,512]{2,0,1:T(2,128)} %broadcast_multiply_fusion.3), channel_id=1, source_target_pairs={{0,16},{8,24},{16,0},{24,8},{32,48},{40,56},{48,32},{56,40},{64,80... | collective-permute-start | bytes 1572872 | tf_op jit(solution)/shard_map/ppermute | solution.py:18
  77.7 406.5 %reduce-scatter.2.cloned.1.call-start = ((), (), s32[]{:S(2)}) async-start(), calls=%async_computation.2 | async-start | bytes 8912896 | tf_op jit(solution)/shard_map/reduce_scatter | solution.py:219
  77.9 37.0 %collective-permute-start.10 = (bf16[512,1024]{1,0:T(8,128)(2,1)S(1)}, bf16[512,1024]{1,0:T(8,128)(2,1)S(1)}, u32[]{:S(2)}, u32[]{:S(2)}) collective-permute-start(bf16[512,1024]{1,0:T(8,128)(2,1)S(1)} %get-tuple-element.80), channel_id=1, source_target_pairs={{0,6},{1,7},{2,0},{3,1},{4,2},{5,3},{6,4},{7,5},{8,14},{9,15},{10,... | collective-permute-start | bytes 3145736 | tf_op jit(solution)/shard_map/ppermute | solution.py:49
  79.8 36.7 %collective-permute-start.11 = (bf16[512,1024]{1,0:T(8,128)(2,1)S(1)}, bf16[512,1024]{1,0:T(8,128)(2,1)S(1)}, u32[]{:S(2)}, u32[]{:S(2)}) collective-permute-start(bf16[512,1024]{1,0:T(8,128)(2,1)S(1)} %get-tuple-element.80), channel_id=1, source_target_pairs={{0,2},{1,3},{2,4},{3,5},{4,6},{5,7},{6,0},{7,1},{8,10},{9,11},{10,... | collective-permute-start | bytes 3145736 | tf_op jit(solution)/shard_map/ppermute | solution.py:48
  83.2 114.8 %collective-permute-start.8 = (bf16[4,512,512]{1,2,0:T(8,128)(2,1)}, bf16[4,512,512]{1,2,0:T(8,128)(2,1)}, u32[]{:S(2)}, u32[]{:S(2)}) collective-permute-start(bf16[4,512,512]{1,2,0:T(8,128)(2,1)} %pad_maximum_fusion.6), channel_id=1, source_target_pairs={{0,8},{8,0},{16,24},{24,16},{32,40},{40,32},{48,56},{56,48},{64,72... | collective-permute-start | bytes 6291464 | tf_op jit(solution)/shard_map/ppermute | solution.py:92
  95.7 11.6 %collective-permute-start.2 = (f32[2,128,512]{2,0,1:T(2,128)S(1)}, f32[2,128,512]{2,0,1:T(2,128)S(1)}, u32[]{:S(2)}, u32[]{:S(2)}) collective-permute-start(f32[2,128,512]{2,0,1:T(2,128)S(1)} %broadcast_multiply_fusion.2), channel_id=1, source_target_pairs={{0,32},{8,40},{16,48},{24,56},{32,0},{40,8},{48,16},{56,24},{64,96... | collective-permute-start | bytes 1572872 | tf_op jit(solution)/shard_map/ppermute | solution.py:18
  108.7 13.6 %collective-permute-start.3 = (bf16[2,128,512]{2,0,1:T(2,128)(2,1)S(1)}, bf16[2,128,512]{2,0,1:T(2,128)(2,1)S(1)}, u32[]{:S(2)}, u32[]{:S(2)}) collective-permute-start(bf16[2,128,512]{2,0,1:T(2,128)(2,1)S(1)} %broadcast_multiply_fusion.1), channel_id=1, source_target_pairs={{0,64},{8,72},{16,80},{24,88},{32,96},{40,104},{48,112},{56,120},{... | collective-permute-start | bytes 786440 | tf_op jit(solution)/shard_map/ppermute | solution.py:18
  115.9 67.3 %collective-permute-start.13 = (bf16[512,512]{1,0:T(8,128)(2,1)}, bf16[512,512]{1,0:T(8,128)(2,1)}, u32[]{:S(2)}, u32[]{:S(2)}) collective-permute-start(bf16[512,512]{1,0:T(8,128)(2,1)} %slice.138), channel_id=1, source_target_pairs={{0,6},{1,7},{2,0},{3,1},{4,2},{5,3},{6,4},{7,5},{8,14},{9,15},{10,... | collective-permute-start | bytes 1572872 | tf_op jit(solution)/shard_map/ppermute | solution.py:55
  118.2 64.9 %collective-permute-start.12 = (bf16[512,512]{1,0:T(8,128)(2,1)}, bf16[512,512]{1,0:T(8,128)(2,1)}, u32[]{:S(2)}, u32[]{:S(2)}) collective-permute-start(bf16[512,512]{1,0:T(8,128)(2,1)} %slice.137), channel_id=1, source_target_pairs={{0,2},{1,3},{2,4},{3,5},{4,6},{5,7},{6,0},{7,1},{8,10},{9,11},{10,... | collective-permute-start | bytes 1572872 | tf_op jit(solution)/shard_map/ppermute | solution.py:54
  320.6 15.7 %collective-permute-start.19 = (f32[2,128,512]{2,0,1:T(2,128)}, f32[2,128,512]{2,0,1:T(2,128)S(1)}, u32[]{:S(2)}, u32[]{:S(2)}) collective-permute-start(f32[2,128,512]{2,0,1:T(2,128)} %copy.226), channel_id=1, source_target_pairs={{0,64},{8,72},{16,80},{24,88},{32,96},{40,104},{48,112},{56,120},{... | collective-permute-start | bytes 1572872 | tf_op jit(solution)/shard_map/ppermute | solution.py:18
  340.7 26.1 %collective-permute-start.14 = (bf16[1024,512]{0,1:T(8,128)(2,1)S(1)}, bf16[1024,512]{0,1:T(8,128)(2,1)}, u32[]{:S(2)}, u32[]{:S(2)}) collective-permute-start(bf16[1024,512]{0,1:T(8,128)(2,1)S(1)} %bitcast.159), channel_id=1, source_target_pairs={{0,1},{1,0},{2,3},{3,2},{4,5},{5,4},{6,7},{7,6},{8,9},{9,8},{10,11... | collective-permute-start | bytes 3145736 | tf_op jit(solution)/shard_map/ppermute | solution.py:41
  352.5 24.4 %collective-permute-start.21 = (f32[2,128,512]{2,0,1:T(2,128)}, f32[2,128,512]{2,0,1:T(2,128)}, u32[]{:S(2)}, u32[]{:S(2)}) collective-permute-start(f32[2,128,512]{2,0,1:T(2,128)} %select_add_fusion.1), channel_id=1, source_target_pairs={{0,16},{8,24},{16,0},{24,8},{32,48},{40,56},{48,32},{56,40},{64,80... | collective-permute-start | bytes 1572872 | tf_op jit(solution)/shard_map/ppermute | solution.py:18
  369.9 78.2 %collective-permute-start.15 = (bf16[1024,1024]{0,1:T(8,128)(2,1)}, bf16[1024,1024]{0,1:T(8,128)(2,1)}, u32[]{:S(2)}, u32[]{:S(2)}) collective-permute-start(bf16[1024,1024]{0,1:T(8,128)(2,1)} %pad_maximum_fusion.7), channel_id=1, source_target_pairs={{0,6},{1,7},{2,0},{3,1},{4,2},{5,3},{6,4},{7,5},{8,14},{9,15},{10,... | collective-permute-start | bytes 6291464 | tf_op jit(solution)/shard_map/ppermute | solution.py:49
  369.9 81.0 %collective-permute-start.16 = (bf16[1024,1024]{0,1:T(8,128)(2,1)}, bf16[1024,1024]{0,1:T(8,128)(2,1)}, u32[]{:S(2)}, u32[]{:S(2)}) collective-permute-start(bf16[1024,1024]{0,1:T(8,128)(2,1)} %pad_maximum_fusion.7), channel_id=1, source_target_pairs={{0,2},{1,3},{2,4},{3,5},{4,6},{5,7},{6,0},{7,1},{8,10},{9,11},{10,... | collective-permute-start | bytes 6291464 | tf_op jit(solution)/shard_map/ppermute | solution.py:48
  379.8 44.8 %collective-permute-start.22 = (f32[2,128,512]{2,0,1:T(2,128)}, f32[2,128,512]{2,0,1:T(2,128)}, u32[]{:S(2)}, u32[]{:S(2)}) collective-permute-start(f32[2,128,512]{2,0,1:T(2,128)} %select_add_fusion), channel_id=1, source_target_pairs={{0,8},{8,0},{16,24},{24,16},{32,40},{40,32},{48,56},{56,48},{64,72... | collective-permute-start | bytes 1572872 | tf_op jit(solution)/shard_map/ppermute | solution.py:18
  449.4 25.6 %collective-permute-start.18 = (bf16[1024,512]{0,1:T(8,128)(2,1)S(1)}, bf16[1024,512]{0,1:T(8,128)(2,1)S(1)}, u32[]{:S(2)}, u32[]{:S(2)}) collective-permute-start(bf16[1024,512]{0,1:T(8,128)(2,1)S(1)} %slice.140), channel_id=1, source_target_pairs={{0,6},{1,7},{2,0},{3,1},{4,2},{5,3},{6,4},{7,5},{8,14},{9,15},{10,... | collective-permute-start | bytes 3145736 | tf_op jit(solution)/shard_map/ppermute | solution.py:55
  452.2 26.8 %collective-permute-start.17 = (bf16[1024,512]{0,1:T(8,128)(2,1)S(1)}, bf16[1024,512]{0,1:T(8,128)(2,1)S(1)}, u32[]{:S(2)}, u32[]{:S(2)}) collective-permute-start(bf16[1024,512]{0,1:T(8,128)(2,1)S(1)} %slice.139), channel_id=1, source_target_pairs={{0,2},{1,3},{2,4},{3,5},{4,6},{5,7},{6,0},{7,1},{8,10},{9,11},{10,... | collective-permute-start | bytes 3145736 | tf_op jit(solution)/shard_map/ppermute | solution.py:54
  (24 other events, 197.0 us)
Sparse Core Ops, SparseCore 0:
  77.8 90.4 all-gather.1
  228.3 102.4 reduce-scatter.1

commit v5 on v4

--- a/solution.py
+++ b/solution.py
@@ -266,18 +266,22 @@
         lower = (local_levels + 1 + level_idx) * BLK
         sibling_grads.append(jnp.sum(grad_sets[:, :, lower : lower + BLK], axis=1))
     carried = jnp.zeros((2, BLK, features), jnp.float32)
-    for level_idx in reversed(range(cross_levels)):
-        outgoing = sibling_grads[level_idx]
-        if level_idx + 1 < cross_levels:
-            halves = spread_rows(carried, 2)
-            lower_part = halves[:, :BLK]
-            upper_part = halves[:, BLK:]
-            upper_half = jnp.right_shift(where_seq, level_idx) & 1 == 1
-            own_part = jnp.where(upper_half, upper_part, lower_part)
-            outgoing = outgoing + jnp.where(upper_half, lower_part, upper_part)
-        else:
-            own_part = jnp.zeros_like(outgoing)
-        carried = own_part + swapped(outgoing, "seq", level_idx)
+    for level_idx in range(cross_levels):
+        group = 2**level_idx
+        chunk_rows = BLK // group
+        position = where_seq & (group - 1)
+        received = None
+        for offset in range(group):
+            pairs = [
+                (src, (((src >> level_idx) ^ 1) << level_idx) + ((src & (group - 1)) ^ offset))
+                for src in range(seq_count)
+            ]
+            piece = lax.dynamic_slice_in_dim(
+                sibling_grads[level_idx], (position ^ offset) * chunk_rows, chunk_rows, axis=1
+            )
+            arrived = lax.ppermute(piece, "seq", pairs)
+            received = arrived if received is None else received + arrived
+        carried = carried + spread_rows(received, group)
     pooled_grad = carried
     for level_idx in reversed(range(local_levels)):
         pooled_grad = level_grads[level_idx] + spread_rows(pooled_grad, 2)

time: 498 us -> 588 us (1.18)
  waiting for transfers between devices: 64.2 us -> 134 us
  starting transfers between devices: 39.4 us -> 58 us
  local copies, waits for them, and re-layouts: 165 us -> 173 us
    ppermute x0 -> x15, waiting for transfers between devices: none -> 106 us  [body(): arrived = lax.ppermute(piece, 'seq', pairs)]
    ppermute x8 -> x4, waiting for transfers between devices: 35.1 us -> 9.15 us  [swapped(): return lax.ppermute(value, axis, pairs)]
    ppermute x0 -> x15, starting transfers between devices: none -> 20.5 us  [body(): arrived = lax.ppermute(piece, 'seq', pairs)]
    ppermute x2, waiting for transfers between devices: 13.1 us -> 0.01 us  [head_ring_gather(): lax.ppermute(value, 'head', [(src, src ^ 1) for src in range(count)])]
    ppermute x2, waiting for transfers between devices: 0.57 us -> 6.82 us  [head_ring_gather(): from_below = lax.ppermute(pair_block, 'head', upward)]
    ppermute x8 -> x4, starting transfers between devices: 18.3 us -> 13.7 us  [swapped(): return lax.ppermute(value, axis, pairs)]
    reshape x3 -> x4, local copies, waits for them, and re-layouts: 11.7 us -> 13.6 us  [spread_rows(): return wide.reshape(shape_in[:-2] + (shape_in[-2] * factor, shape_in[-1]))]
    unnamed x61 -> x81, local copies, waits for them, and re-layouts: 28.3 us -> 29.4 us
  transfers between devices with their start and end apart: 25 -> 36, of which waited for: 9 -> 12; matrix products, arithmetic and copies ran while one was open for 69% -> 59% of each run, Pallas kernels for 0% -> 0%
where the time goes in v5:
time: 588 us; the launch traced here: 582 us
  local copies, waits for them, and re-layouts  173 us (29%)
  waiting for transfers between devices  134 us (23%)
  matrix products  102 us (17%)
  other arithmetic  99.3 us (17%)
  starting transfers between devices  58 us (10%)
  between operations  14.9 us (3%)
    ppermute x15, waiting for transfers between devices, body(): arrived = lax.ppermute(piece, 'seq', pairs)  106 us
    unnamed x81, local copies, waits for them, and re-layouts  29.4 us
    slice x2, local copies, waits for them, and re-layouts, body(): key_heads = key_set[0].reshape(blocks, keys_all, head_count, DH)  23.4 us
    ppermute x15, starting transfers between devices, body(): arrived = lax.ppermute(piece, 'seq', pairs)  20.5 us
    another operation x1, other arithmetic, body(): jnp.stack([grad_keyset, grad_valset]).reshape(2, blocks, keys_all, features)  19.6 us
    dot_general x1, matrix products, body(): jnp.einsum('bqhd,bkhd->bhqk', grad_heads, value_heads, preferred_element_...  18.2 us
    mul x1, local copies, waits for them, and re-layouts, body(): jnp.einsum('bhqk,bqhd->bkhd', grad_score, query_heads, preferred_element_...  16.5 us
    dot_general x1, matrix products, body(): jnp.einsum('bhqk,bqhd->bkhd', prob_low, grad_heads, preferred_element_typ...  14.4 us
  transfers between devices with their start and end apart: 36, of which 12 were waited for; matrix products, arithmetic and copies ran while one was open for 59% of the time, Pallas kernels for 0%

profile of v5, /device:TPU:0, one launch (start us, length us, event | category | flops | bytes accessed | tf_op | source)
XLA Modules:
  0.0 581.9 jit_solution(18143548244726757916)
XLA Ops:
  32.3 7.7 %convert_reduce_fusion.2 = f32[2,512,512]{2,1,0:T(8,128)S(1)} fusion(bf16[1,512,2,512]{3,2,1,0:T(2,128)(2,1)} %stack.79, bf16[1,512,2,512]{3,2,1,0:T(2,128)(2,1)} %stack.78), kind=kLoop, calls=%fused_computation.51 | loop fusion | flops 2621440 | bytes 4194304 | tf_op jit(solution)/shard_map/reduce_sum | solution.py:152
  104.5 7.9 %collective-permute-start.3 = (bf16[2,128,512]{2,0,1:T(2,128)(2,1)S(1)}, bf16[2,128,512]{2,0,1:T(2,128)(2,1)S(1)}, u32[]{:S(2)}, u32[]{:S(2)}) collective-permute-start(bf16[2,128,512]{2,0,1:T(2,128)(2,1)S(1)} %broadcast_multiply_fusion), channel_id=1, source_target_pairs={{0,64},{8,72},{16,80},{24,88},{32,96},{40,104},{48,112},{56,120},{... | collective-permute-start | bytes 786440 | tf_op jit(solution)/shard_map/ppermute | solution.py:18
  114.3 6.8 %collective-permute-done.11 = bf16[512,1024]{1,0:T(8,128)(2,1)S(1)} collective-permute-done((bf16[512,1024]{1,0:T(8,128)(2,1)S(1)}, bf16[512,1024]{1,0:T(8,128)(2,1)S(1)}, u32[]{:S(2)}, u32[]{:S(2)}) %collective-permute-start.11) | collective-permute-done | bytes 1048608 | tf_op jit(solution)/shard_map/ppermute | solution.py:48
  129.6 11.9 %fusion.55 = (bf16[1,8,1024,512]{3,2,1,0:T(8,128)(2,1)}, bf16[1,8,1024,512]{3,2,1,0:T(8,128)(2,1)}) fusion(bf16[2,8,1024,512]{3,2,1,0:T(8,128)(2,1)} %broadcast_dynamic-update-slice_fusion), kind=kLoop, calls=%fused_computation.160 | loop fusion | bytes 33554432 | tf_op jit(solution)/shard_map/slice | solution.py:185
  141.5 11.5 %copy.194 = bf16[1,8,1024,512]{2,3,1,0:T(8,128)(2,1)} copy(bf16[1,8,1024,512]{3,2,1,0:T(8,128)(2,1)} %get-tuple-element.56) | data formatting | bytes 16777216 | tf_op jit(solution)/shard_map/slice | solution.py:185
  153.0 11.5 %copy.192 = bf16[1,8,1024,512]{2,3,1,0:T(8,128)(2,1)} copy(bf16[1,8,1024,512]{3,2,1,0:T(8,128)(2,1)} %get-tuple-element.57) | data formatting | bytes 16777216 | tf_op jit(solution)/shard_map/slice | solution.py:186
  164.5 12.9 %fusion.56 = (f32[8,4,128]{2,1,0:T(4,128)S(1)}, f32[8,4,128,1024]{2,3,1,0:T(8,128)}) fusion(f32[1024]{0:T(1024)S(1)} %copy-done.32, pred[8,1024]{1,0:T(8,128)(4,1)S(1)} %concatenate.76, bf16[8,1024,4,128]{1,3,2,0:T(8,128)(2,1)} %bitcast.155, bf16[8,128,4,128]{1,3,2,0:T(8,128)(2,1)S(1)} %copy.213), kind=kOutput, calls=%fused_computation.161 | convolution fusion | flops 1094714368 | bytes 26243072 | tf_op jit(solution)/shard_map/sub | solution.py:194
  177.4 10.6 %fusion.37 = bf16[8,128,4,128]{1,3,2,0:T(8,128)(2,1)S(1)} fusion(bf16[8,1024,4,128]{1,3,2,0:T(8,128)(2,1)} %bitcast.157, f32[8,4,128,1024]{2,3,1,0:T(8,128)} %get-tuple-element.100, f32[8,4,128]{2,1,0:T(4,128)S(1)} %get-tuple-element.99), kind=kOutput, calls=%fused_computation.72 | convolution fusion | flops 1082654720 | bytes 26230784 | tf_op jit(solution)/shard_map/bhqk,bkhd->bqhd/dot_general | solution.py:197
  209.9 10.2 %fusion.33 = bf16[1024,512]{1,0:T(8,128)(2,1)} fusion(bf16[512,4096]{1,0:T(8,128)(2,1)} %param.9, bf16[512,4096]{0,1:T(8,128)(2,1)} %bitcast.166, bf16[512,4096]{0,1:T(8,128)(2,1)} %all-gather.2.cloned.1.call-done), kind=kOutput, calls=%fused_computation.70 | convolution fusion | flops 4312268800 | bytes 13631488 | tf_op jit(solution)/shard_map/dot_general | solution.py:208
  222.7 11.3 %fusion.9 = f32[4096,512]{1,0:T(8,128)} fusion(bf16[1024,512]{0,1:T(8,128)(2,1)S(1)} %bitcast.161, bf16[512,4096]{0,1:T(8,128)(2,1)} %bitcast.167, bf16[512,4096]{0,1:T(8,128)(2,1)} %all-gather.2.cloned.1.call-done), kind=kOutput, calls=%fused_computation.30 | convolution fusion | flops 4311744512 | bytes 17825792 | tf_op jit(solution)/shard_map/dot_general | solution.py:220
  234.1 18.2 %multiply_reduce_fusion = (f32[8,4,128]{2,1,0:T(4,128)S(1)}, f32[8,4,128,1024]{2,3,1,0:T(8,128)}) fusion(f32[8,4,128,1024]{2,3,1,0:T(8,128)} %get-tuple-element.100, f32[8,4,128]{2,1,0:T(4,128)S(1)} %get-tuple-element.99, bf16[8,128,4,128]{1,3,2,0:T(8,128)(2,1)} %copy.216, bf16[8,1024,4,128]{1,3,2,0:T(8,128)(2,1)} %bitcast.158), kind=kOutput, calls=%fused_computation.22 | convolution fusion | flops 1086320640 | bytes 43024384 | tf_op jit(solution)/shard_map/bqhd,bkhd->bhqk/dot_general | solution.py:228
  252.3 12.4 %multiply_convert_fusion = bf16[8,4,128,1024]{2,3,1,0:T(8,128)(2,1)S(1)} fusion(f32[8,4,128,1024]{2,3,1,0:T(8,128)} %get-tuple-element.102, f32[8,4,128]{2,1,0:T(4,128)S(1)} %get-tuple-element.101, f32[8,4,128,1024]{2,3,1,0:T(8,128)} %get-tuple-element.100, f32[8,4,128]{2,1,0:T(4,128)S(1)} %get-tuple-element.99), kind=kLoop, calls=%fused_computation.21 | loop fusion | flops 16777216 | bytes 41975808 | tf_op jit(solution)/shard_map/convert_element_type | solution.py:232
  268.0 7.0 %multiply_bitcast_fusion = f32[8,1024,4,128]{3,1,2,0:T(8,128)} fusion(bf16[8,4,128,1024]{2,3,1,0:T(8,128)(2,1)S(1)} %multiply_convert_fusion, bf16[8,128,4,128]{1,3,2,0:T(8,128)(2,1)S(1)} %copy.213), kind=kOutput, calls=%fused_computation.20 | convolution fusion | flops 1077936128 | bytes 26214400 | tf_op jit(solution)/shard_map/bhqk,bqhd->bkhd/dot_general | solution.py:242
  275.0 16.5 %copy.215 = f32[8,1024,4,128]{1,3,2,0:T(8,128)} copy(f32[8,1024,4,128]{3,1,2,0:T(8,128)} %multiply_bitcast_fusion) | data formatting | bytes 33554432 | tf_op jit(solution)/shard_map/mul | solution.py:242
  291.6 14.4 %fusion.21 = f32[8,4,128,1024]{3,2,1,0:T(8,128)} fusion(bf16[8,128,4,128]{1,3,2,0:T(8,128)(2,1)S(1)} %copy-done.25, f32[8,4,128,1024]{2,3,1,0:T(8,128)} %get-tuple-element.100, f32[8,4,128]{2,1,0:T(4,128)S(1)} %get-tuple-element.99), kind=kOutput, calls=%fused_computation.45 | convolution fusion | flops 1082130432 | bytes 34619392 | tf_op jit(solution)/shard_map/bhqk,bqhd->bkhd/dot_general | solution.py:245
  305.9 19.6 %fusion.12 = (f32[2,8,128,512]{2,3,1,0:T(8,128)}, f32[2,8,128,512]{2,3,1,0:T(8,128)}, f32[2,128,512]{1,2,0:T(8,128)S(1)}, f32[2,128,512]{1,2,0:T(8,128)S(1)}, f3...) fusion(f32[1,8,1024,512]{2,3,1,0:T(8,128)} %bitcast.141, ...), kind=kLoop, calls=%fused_computation.33 | loop fusion | flops 12058624 | bytes 52428800 | tf_op jit(solution)/shard_map/stack | solution.py:248
  337.6 8.1 %fusion.40 = bf16[8,128,4,128]{1,3,2,0:T(8,128)(2,1)S(1)} fusion(bf16[8,1024,4,128]{1,3,2,0:T(8,128)(2,1)} %bitcast.156, bf16[8,4,128,1024]{2,3,1,0:T(8,128)(2,1)} %copy-done), kind=kOutput, calls=%fused_computation.73 | convolution fusion | flops 1074790400 | bytes 17825792 | tf_op jit(solution)/shard_map/bhqk,bkhd->bqhd/dot_general | solution.py:235
  348.0 9.1 %collective-permute-done.27 = f32[2,16,512]{1,2,0:T(8,128)S(1)} collective-permute-done((f32[2,16,512]{1,2,0:T(8,128)S(1)}, f32[2,16,512]{1,2,0:T(8,128)S(1)}, u32[]{:S(2)}, u32[]{:S(2)}) %collective-permute-start.27) | collective-permute-done | bytes 65568 | tf_op jit(solution)/shard_map/ppermute | solution.py:282
  367.1 21.9 %collective-permute-done.31 = f32[2,16,512]{1,2,0:T(8,128)S(1)} collective-permute-done((f32[2,16,512]{1,2,0:T(8,128)S(1)}, f32[2,16,512]{1,2,0:T(8,128)S(1)}, u32[]{:S(2)}, u32[]{:S(2)}) %collective-permute-start.31) | collective-permute-done | bytes 65568 | tf_op jit(solution)/shard_map/ppermute | solution.py:282
  390.1 21.3 %collective-permute-done.30 = f32[2,16,512]{1,2,0:T(8,128)S(1)} collective-permute-done((f32[2,16,512]{1,2,0:T(8,128)S(1)}, f32[2,16,512]{1,2,0:T(8,128)S(1)}, u32[]{:S(2)}, u32[]{:S(2)}) %collective-permute-start.30) | collective-permute-done | bytes 65568 | tf_op jit(solution)/shard_map/ppermute | solution.py:282
  454.6 27.4 %collective-permute-done.23 = f32[2,32,512]{1,2,0:T(8,128)} collective-permute-done((f32[2,32,512]{1,2,0:T(8,128)}, f32[2,32,512]{1,2,0:T(8,128)}, u32[]{:S(2)}, u32[]{:S(2)}) %collective-permute-start.23) | collective-permute-done | bytes 131104 | tf_op jit(solution)/shard_map/ppermute | solution.py:282
  484.4 11.8 %collective-permute-done.22 = f32[2,32,512]{1,2,0:T(8,128)S(1)} collective-permute-done((f32[2,32,512]{1,2,0:T(8,128)}, f32[2,32,512]{1,2,0:T(8,128)S(1)}, u32[]{:S(2)}, u32[]{:S(2)}) %collective-permute-start.22) | collective-permute-done | bytes 131104 | tf_op jit(solution)/shard_map/ppermute | solution.py:282
  500.2 11.2 %collective-permute-done.20 = f32[2,64,512]{1,2,0:T(8,128)} collective-permute-done((f32[2,64,512]{1,2,0:T(8,128)}, f32[2,64,512]{1,2,0:T(8,128)}, u32[]{:S(2)}, u32[]{:S(2)}) %collective-permute-start.20) | collective-permute-done | bytes 262176 | tf_op jit(solution)/shard_map/ppermute | solution.py:282
  557.3 7.3 %collective-permute-done.18 = bf16[1024,512]{0,1:T(8,128)(2,1)S(1)} collective-permute-done((bf16[1024,512]{0,1:T(8,128)(2,1)S(1)}, bf16[1024,512]{0,1:T(8,128)(2,1)S(1)}, u32[]{:S(2)}, u32[]{:S(2)}) %collective-permute-start.18) | collective-permute-done | bytes 1048608 | tf_op jit(solution)/shard_map/ppermute | solution.py:55
  (241 shorter events, 258.5 us)
Async XLA Ops:
  7.2 202.7 %all-gather.2.cloned.1.call-start = ((), (), s32[]{:S(2)}) async-start(), calls=%async_computation.1 | async-start | bytes 4718592 | tf_op jit(solution)/shard_map/all_gather | solution.py:203
  9.1 62.8 %collective-permute-start.9 = (bf16[512,512]{1,0:T(8,128)(2,1)}, bf16[512,512]{1,0:T(8,128)(2,1)}, u32[]{:S(2)}, u32[]{:S(2)}) collective-permute-start(bf16[512,512]{1,0:T(8,128)(2,1)} %slice.87), channel_id=1, source_target_pairs={{0,1},{1,0},{2,3},{3,2},{4,5},{5,4},{6,7},{7,6},{8,9},{9,8},{10,11... | collective-permute-start | bytes 1572872 | tf_op jit(solution)/shard_map/ppermute | solution.py:41
  14.5 51.1 %collective-permute-start = (f32[2,128,512]{2,1,0:T(8,128)}, f32[2,128,512]{2,1,0:T(8,128)}, u32[]{:S(2)}, u32[]{:S(2)}) collective-permute-start(f32[2,128,512]{2,1,0:T(8,128)} %broadcast_multiply_fusion.3), channel_id=1, source_target_pairs={{0,8},{8,0},{16,24},{24,16},{32,40},{40,32},{48,56},{56,48},{64,72... | collective-permute-start | bytes 1572872 | tf_op jit(solution)/shard_map/ppermute | solution.py:18
  19.6 60.8 %collective-permute-start.7 = (bf16[512,512]{0,1:T(8,128)(2,1)}, bf16[512,512]{0,1:T(8,128)(2,1)}, u32[]{:S(2)}, u32[]{:S(2)}) collective-permute-start(bf16[512,512]{0,1:T(8,128)(2,1)} %copy.243), channel_id=1, source_target_pairs={{0,7},{1,0},{2,1},{3,2},{4,3},{5,4},{6,5},{7,6},{16,23},{17,16},{1... | collective-permute-start | bytes 1572872 | tf_op jit(solution)/shard_map/ppermute | solution.py:90
  25.6 56.7 %collective-permute-start.4 = (bf16[512,512]{0,1:T(8,128)(2,1)}, bf16[512,512]{0,1:T(8,128)(2,1)}, u32[]{:S(2)}, u32[]{:S(2)}) collective-permute-start(bf16[512,512]{0,1:T(8,128)(2,1)} %copy.240), channel_id=1, source_target_pairs={{0,1},{1,2},{2,3},{3,4},{4,5},{5,6},{6,7},{7,0},{8,10},{9,11},{10,... | collective-permute-start | bytes 1572872 | tf_op jit(solution)/shard_map/ppermute | solution.py:90
  26.6 55.9 %collective-permute-start.5 = (bf16[512,512]{0,1:T(8,128)(2,1)}, bf16[512,512]{0,1:T(8,128)(2,1)}, u32[]{:S(2)}, u32[]{:S(2)}) collective-permute-start(bf16[512,512]{0,1:T(8,128)(2,1)} %copy.241), channel_id=1, source_target_pairs={{0,3},{1,4},{2,5},{3,6},{4,7},{5,0},{6,1},{7,2},{8,12},{9,13},{10,... | collective-permute-start | bytes 1572872 | tf_op jit(solution)/shard_map/ppermute | solution.py:90
  78.1 496.7 %reduce-scatter.2.cloned.1.call-start = ((), (), s32[]{:S(2)}) async-start(), calls=%async_computation.2 | async-start | bytes 8912896 | tf_op jit(solution)/shard_map/reduce_scatter | solution.py:219
  82.3 38.8 %collective-permute-start.11 = (bf16[512,1024]{1,0:T(8,128)(2,1)S(1)}, bf16[512,1024]{1,0:T(8,128)(2,1)S(1)}, u32[]{:S(2)}, u32[]{:S(2)}) collective-permute-start(bf16[512,1024]{1,0:T(8,128)(2,1)S(1)} %get-tuple-element.80), channel_id=1, source_target_pairs={{0,2},{1,3},{2,4},{3,5},{4,6},{5,7},{6,0},{7,1},{8,10},{9,11},{10,... | collective-permute-start | bytes 3145736 | tf_op jit(solution)/shard_map/ppermute | solution.py:48
  85.7 118.3 %collective-permute-start.8 = (bf16[4,512,512]{1,2,0:T(8,128)(2,1)}, bf16[4,512,512]{1,2,0:T(8,128)(2,1)}, u32[]{:S(2)}, u32[]{:S(2)}) collective-permute-start(bf16[4,512,512]{1,2,0:T(8,128)(2,1)} %pad_maximum_fusion.6), channel_id=1, source_target_pairs={{0,8},{8,0},{16,24},{24,16},{32,40},{40,32},{48,56},{56,48},{64,72... | collective-permute-start | bytes 6291464 | tf_op jit(solution)/shard_map/ppermute | solution.py:92
  114.3 74.7 %collective-permute-start.13 = (bf16[512,512]{1,0:T(8,128)(2,1)}, bf16[512,512]{1,0:T(8,128)(2,1)}, u32[]{:S(2)}, u32[]{:S(2)}) collective-permute-start(bf16[512,512]{1,0:T(8,128)(2,1)} %slice.114), channel_id=1, source_target_pairs={{0,6},{1,7},{2,0},{3,1},{4,2},{5,3},{6,4},{7,5},{8,14},{9,15},{10,... | collective-permute-start | bytes 1572872 | tf_op jit(solution)/shard_map/ppermute | solution.py:55
  122.9 66.1 %collective-permute-start.12 = (bf16[512,512]{1,0:T(8,128)(2,1)}, bf16[512,512]{1,0:T(8,128)(2,1)}, u32[]{:S(2)}, u32[]{:S(2)}) collective-permute-start(bf16[512,512]{1,0:T(8,128)(2,1)} %slice.113), channel_id=1, source_target_pairs={{0,2},{1,3},{2,4},{3,5},{4,6},{5,7},{6,0},{7,1},{8,10},{9,11},{10,... | collective-permute-start | bytes 1572872 | tf_op jit(solution)/shard_map/ppermute | solution.py:54
  234.0 111.7 %collective-permute-start.14 = (bf16[1024,512]{0,1:T(8,128)(2,1)S(1)}, bf16[1024,512]{0,1:T(8,128)(2,1)S(1)}, u32[]{:S(2)}, u32[]{:S(2)}) collective-permute-start(bf16[1024,512]{0,1:T(8,128)(2,1)S(1)} %bitcast.162), channel_id=1, source_target_pairs={{0,1},{1,0},{2,3},{3,2},{4,5},{5,4},{6,7},{7,6},{8,9},{9,8},{10,11... | collective-permute-start | bytes 3145736 | tf_op jit(solution)/shard_map/ppermute | solution.py:41
  327.8 33.6 %collective-permute-start.33 = (f32[2,16,512]{1,2,0:T(8,128)S(1)}, f32[2,16,512]{1,2,0:T(8,128)S(1)}, u32[]{:S(2)}, u32[]{:S(2)}) collective-permute-start(f32[2,16,512]{1,2,0:T(8,128)S(1)} %get-tuple-element.88), channel_id=1, source_target_pairs={{0,120},{8,112},{16,104},{24,96},{32,88},{40,80},{48,72},{56,64},{... | collective-permute-start | bytes 196616 | tf_op jit(solution)/shard_map/ppermute | solution.py:282
  331.2 35.4 %collective-permute-start.32 = (f32[2,16,512]{1,2,0:T(8,128)S(1)}, f32[2,16,512]{1,2,0:T(8,128)S(1)}, u32[]{:S(2)}, u32[]{:S(2)}) collective-permute-start(f32[2,16,512]{1,2,0:T(8,128)S(1)} %get-tuple-element.89), channel_id=1, source_target_pairs={{0,112},{8,120},{16,96},{24,104},{32,80},{40,88},{48,64},{56,72},{... | collective-permute-start | bytes 196616 | tf_op jit(solution)/shard_map/ppermute | solution.py:282
  337.6 51.4 %collective-permute-start.31 = (f32[2,16,512]{1,2,0:T(8,128)S(1)}, f32[2,16,512]{1,2,0:T(8,128)S(1)}, u32[]{:S(2)}, u32[]{:S(2)}) collective-permute-start(f32[2,16,512]{1,2,0:T(8,128)S(1)} %get-tuple-element.90), channel_id=1, source_target_pairs={{0,104},{8,96},{16,120},{24,112},{32,72},{40,64},{48,88},{56,80},{... | collective-permute-start | bytes 196616 | tf_op jit(solution)/shard_map/ppermute | solution.py:282
  345.7 65.8 %collective-permute-start.30 = (f32[2,16,512]{1,2,0:T(8,128)S(1)}, f32[2,16,512]{1,2,0:T(8,128)S(1)}, u32[]{:S(2)}, u32[]{:S(2)}) collective-permute-start(f32[2,16,512]{1,2,0:T(8,128)S(1)} %get-tuple-element.91), channel_id=1, source_target_pairs={{0,96},{8,104},{16,112},{24,120},{32,64},{40,72},{48,80},{56,88},{... | collective-permute-start | bytes 196616 | tf_op jit(solution)/shard_map/ppermute | solution.py:282
  357.1 182.2 %collective-permute-start.15 = (bf16[1024,1024]{0,1:T(8,128)(2,1)}, bf16[1024,1024]{0,1:T(8,128)(2,1)}, u32[]{:S(2)}, u32[]{:S(2)}) collective-permute-start(bf16[1024,1024]{0,1:T(8,128)(2,1)} %pad_maximum_fusion.7), channel_id=1, source_target_pairs={{0,6},{1,7},{2,0},{3,1},{4,2},{5,3},{6,4},{7,5},{8,14},{9,15},{10,... | collective-permute-start | bytes 6291464 | tf_op jit(solution)/shard_map/ppermute | solution.py:49
  361.4 181.5 %collective-permute-start.16 = (bf16[1024,1024]{0,1:T(8,128)(2,1)}, bf16[1024,1024]{0,1:T(8,128)(2,1)}, u32[]{:S(2)}, u32[]{:S(2)}) collective-permute-start(bf16[1024,1024]{0,1:T(8,128)(2,1)} %pad_maximum_fusion.7), channel_id=1, source_target_pairs={{0,2},{1,3},{2,4},{3,5},{4,6},{5,7},{6,0},{7,1},{8,10},{9,11},{10,... | collective-permute-start | bytes 6291464 | tf_op jit(solution)/shard_map/ppermute | solution.py:48
  366.5 78.5 %collective-permute-start.29 = (f32[2,16,512]{1,2,0:T(8,128)}, f32[2,16,512]{1,2,0:T(8,128)}, u32[]{:S(2)}, u32[]{:S(2)}) collective-permute-start(f32[2,16,512]{1,2,0:T(8,128)} %get-tuple-element.92), channel_id=1, source_target_pairs={{0,88},{8,80},{16,72},{24,64},{32,120},{40,112},{48,104},{56,96},{... | collective-permute-start | bytes 196616 | tf_op jit(solution)/shard_map/ppermute | solution.py:282
  389.0 56.5 %collective-permute-start.28 = (f32[2,16,512]{1,2,0:T(8,128)}, f32[2,16,512]{1,2,0:T(8,128)}, u32[]{:S(2)}, u32[]{:S(2)}) collective-permute-start(f32[2,16,512]{1,2,0:T(8,128)} %get-tuple-element.93), channel_id=1, source_target_pairs={{0,80},{8,88},{16,64},{24,72},{32,112},{40,120},{48,96},{56,104},{... | collective-permute-start | bytes 196616 | tf_op jit(solution)/shard_map/ppermute | solution.py:282
  411.5 35.1 %collective-permute-start.26 = (f32[2,16,512]{1,2,0:T(8,128)}, f32[2,16,512]{1,2,0:T(8,128)}, u32[]{:S(2)}, u32[]{:S(2)}) collective-permute-start(f32[2,16,512]{1,2,0:T(8,128)} %get-tuple-element.94), channel_id=1, source_target_pairs={{0,64},{8,72},{16,80},{24,88},{32,96},{40,104},{48,112},{56,120},{... | collective-permute-start | bytes 196616 | tf_op jit(solution)/shard_map/ppermute | solution.py:282
  445.0 37.0 %collective-permute-start.23 = (f32[2,32,512]{1,2,0:T(8,128)}, f32[2,32,512]{1,2,0:T(8,128)}, u32[]{:S(2)}, u32[]{:S(2)}) collective-permute-start(f32[2,32,512]{1,2,0:T(8,128)} %get-tuple-element.83), channel_id=1, source_target_pairs={{0,40},{8,32},{16,56},{24,48},{32,8},{40,0},{48,24},{56,16},{64,10... | collective-permute-start | bytes 393224 | tf_op jit(solution)/shard_map/ppermute | solution.py:282
  445.5 38.4 %collective-permute-start.25 = (f32[2,32,512]{1,2,0:T(8,128)}, f32[2,32,512]{1,2,0:T(8,128)}, u32[]{:S(2)}, u32[]{:S(2)}) collective-permute-start(f32[2,32,512]{1,2,0:T(8,128)} %get-tuple-element.84), channel_id=1, source_target_pairs={{0,56},{8,48},{16,40},{24,32},{32,24},{40,16},{48,8},{56,0},{64,12... | collective-permute-start | bytes 393224 | tf_op jit(solution)/shard_map/ppermute | solution.py:282
  446.5 37.4 %collective-permute-start.24 = (f32[2,32,512]{1,2,0:T(8,128)}, f32[2,32,512]{1,2,0:T(8,128)}, u32[]{:S(2)}, u32[]{:S(2)}) collective-permute-start(f32[2,32,512]{1,2,0:T(8,128)} %get-tuple-element.85), channel_id=1, source_target_pairs={{0,48},{8,56},{16,32},{24,40},{32,16},{40,24},{48,0},{56,8},{64,11... | collective-permute-start | bytes 393224 | tf_op jit(solution)/shard_map/ppermute | solution.py:282
  (45 other events, 636.3 us)
Sparse Core Ops, SparseCore 0:
  78.3 89.8 all-gather.1
  234.2 131.4 reduce-scatter.1

commit v6 on v4

--- a/solution.py
+++ b/solution.py
@@ -210,12 +210,6 @@
     ).astype(jnp.bfloat16)
     late_attended, grad_attn = lax.optimization_barrier((attended, grad_attn))
     attended_blocks = head_ring_gather(late_attended, relative=True)
-    output_sum = jnp.dot(attended_blocks[0], weight_cols[0], preferred_element_type=jnp.float32)
-    for dist in range(1, len(attended_blocks)):
-        output_sum = output_sum + jnp.dot(
-            attended_blocks[dist], weight_cols[dist], preferred_element_type=jnp.float32
-        )
-    output = output_sum.astype(jnp.bfloat16)
     grad_weight = lax.psum_scatter(
         lax.dot_general(
             grads_full, attended, (((0,), (0,)), ((), ())), preferred_element_type=jnp.float32
@@ -278,6 +272,13 @@
         else:
             own_part = jnp.zeros_like(outgoing)
         carried = own_part + swapped(outgoing, "seq", level_idx)
+    attended_blocks, carried = lax.optimization_barrier((attended_blocks, carried))
+    output_sum = jnp.dot(attended_blocks[0], weight_cols[0], preferred_element_type=jnp.float32)
+    for dist in range(1, len(attended_blocks)):
+        output_sum = output_sum + jnp.dot(
+            attended_blocks[dist], weight_cols[dist], preferred_element_type=jnp.float32
+        )
+    output = output_sum.astype(jnp.bfloat16)
     pooled_grad = carried
     for level_idx in reversed(range(local_levels)):
         pooled_grad = level_grads[level_idx] + spread_rows(pooled_grad, 2)

time: 498 us -> 499 us (level)
  waiting for transfers between devices: 64.2 us -> 51.8 us
  local copies, waits for them, and re-layouts: 165 us -> 172 us
    reduce_sum x0 -> x1, other arithmetic: none -> 19.8 us  [body(): sibling_grads.append(jnp.sum(grad_sets[:, :, lower:lower + BLK], axis=1))]
    another operation x2 -> x1, other arithmetic: 24.7 us -> 5.89 us  [the longest x1 18.8 us: body(): jnp.stack([grad_keyset, grad_valset]).reshape(2, blocks, keys_all, features)]
    ppermute x2, waiting for transfers between devices: 0.57 us -> 16.6 us  [head_ring_gather(): from_below = lax.ppermute(pair_block, 'head', upward)]
    ppermute x2, waiting for transfers between devices: 13.1 us -> 0.01 us  [head_ring_gather(): lax.ppermute(value, 'head', [(src, src ^ 1) for src in range(count)])]
    ppermute x2, waiting for transfers between devices: 11.4 us -> 0.01 us  [head_ring_gather(): lax.ppermute(from_above[..., width:], 'head', downward)]
    unnamed x61 -> x65, local copies, waits for them, and re-layouts: 28.3 us -> 31.7 us
  transfers between devices with their start and end apart: 25 -> 25, of which waited for: 9 -> 7; matrix products, arithmetic and copies ran while one was open for 69% -> 71% of each run, Pallas kernels for 0% -> 0%
where the time goes in v6:
time: 499 us; the launch traced here: 491 us
  local copies, waits for them, and re-layouts  172 us (34%)
  other arithmetic  107 us (21%)
  matrix products  103 us (21%)
  waiting for transfers between devices  51.8 us (10%)
  starting transfers between devices  42.7 us (9%)
  between operations  14.9 us (3%)
    ppermute x8, waiting for transfers between devices, swapped(): return lax.ppermute(value, axis, pairs)  35.1 us
    unnamed x65, local copies, waits for them, and re-layouts  31.7 us
    slice x2, local copies, waits for them, and re-layouts, body(): key_heads = key_set[0].reshape(blocks, keys_all, head_count, DH)  23.3 us
    ppermute x8, starting transfers between devices, swapped(): return lax.ppermute(value, axis, pairs)  20.3 us
    reduce_sum x1, other arithmetic, body(): sibling_grads.append(jnp.sum(grad_sets[:, :, lower:lower + BLK], axis=1))  19.8 us
    dot_general x1, matrix products, body(): jnp.einsum('bqhd,bkhd->bhqk', grad_heads, value_heads, preferred_element_...  18 us
    ppermute x2, waiting for transfers between devices, head_ring_gather(): from_below = lax.ppermute(pair_block, 'head', upward)  16.6 us
    mul x1, local copies, waits for them, and re-layouts, body(): jnp.einsum('bhqk,bqhd->bkhd', grad_score, query_heads, preferred_element_...  16.5 us
  transfers between devices with their start and end apart: 25, of which 7 were waited for; matrix products, arithmetic and copies ran while one was open for 71% of the time, Pallas kernels for 0%

profile of v6, /device:TPU:0, one launch (start us, length us, event | category | flops | bytes accessed | tf_op | source)
XLA Modules:
  0.0 491.0 jit_solution(17339775070296203423)
XLA Ops:
  32.2 7.7 %convert_reduce_fusion.2 = f32[2,512,512]{2,1,0:T(8,128)S(1)} fusion(bf16[1,512,2,512]{3,2,1,0:T(2,128)(2,1)} %stack.79, bf16[1,512,2,512]{3,2,1,0:T(2,128)(2,1)} %stack.78), kind=kLoop, calls=%fused_computation.50 | loop fusion | flops 2621440 | bytes 4194304 | tf_op jit(solution)/shard_map/reduce_sum | solution.py:152
  84.2 8.4 %collective-permute-done.1 = f32[2,128,512]{2,0,1:T(2,128)} collective-permute-done((f32[2,128,512]{2,0,1:T(2,128)}, f32[2,128,512]{2,0,1:T(2,128)}, u32[]{:S(2)}, u32[]{:S(2)}) %collective-permute-start.1) | collective-permute-done | bytes 524320 | tf_op jit(solution)/shard_map/ppermute | solution.py:18
  109.0 6.1 %collective-permute-start.3 = (bf16[2,128,512]{2,0,1:T(2,128)(2,1)S(1)}, bf16[2,128,512]{2,0,1:T(2,128)(2,1)S(1)}, u32[]{:S(2)}, u32[]{:S(2)}) collective-permute-start(bf16[2,128,512]{2,0,1:T(2,128)(2,1)S(1)} %broadcast_multiply_fusion.2), channel_id=1, source_target_pairs={{0,64},{8,72},{16,80},{24,88},{32,96},{40,104},{48,112},{56,120},{... | collective-permute-start | bytes 786440 | tf_op jit(solution)/shard_map/ppermute | solution.py:18
  123.9 11.8 %fusion.47 = (bf16[1,8,1024,512]{3,2,1,0:T(8,128)(2,1)}, bf16[1,8,1024,512]{3,2,1,0:T(8,128)(2,1)}) fusion(bf16[2,8,1024,512]{3,2,1,0:T(8,128)(2,1)} %broadcast_dynamic-update-slice_fusion), kind=kLoop, calls=%fused_computation.141 | loop fusion | bytes 33554432 | tf_op jit(solution)/shard_map/slice | solution.py:185
  135.7 11.5 %copy.198 = bf16[1,8,1024,512]{2,3,1,0:T(8,128)(2,1)} copy(bf16[1,8,1024,512]{3,2,1,0:T(8,128)(2,1)} %get-tuple-element.62) | data formatting | bytes 16777216 | tf_op jit(solution)/shard_map/slice | solution.py:185
  147.2 11.5 %copy.196 = bf16[1,8,1024,512]{2,3,1,0:T(8,128)(2,1)} copy(bf16[1,8,1024,512]{3,2,1,0:T(8,128)(2,1)} %get-tuple-element.63) | data formatting | bytes 16777216 | tf_op jit(solution)/shard_map/slice | solution.py:186
  158.7 12.8 %fusion.48 = (f32[8,4,128]{2,1,0:T(4,128)S(1)}, f32[8,4,128,1024]{2,3,1,0:T(8,128)}) fusion(f32[1024]{0:T(1024)S(1)} %copy-done.24, pred[8,1024]{1,0:T(8,128)(4,1)S(1)} %concatenate.76, bf16[8,1024,4,128]{1,3,2,0:T(8,128)(2,1)} %bitcast.154, bf16[8,128,4,128]{1,3,2,0:T(8,128)(2,1)S(1)} %copy.215), kind=kOutput, calls=%fused_computation.142 | convolution fusion | flops 1094714368 | bytes 26243072 | tf_op jit(solution)/shard_map/sub | solution.py:194
  171.5 10.6 %fusion.33 = bf16[8,128,4,128]{1,3,2,0:T(8,128)(2,1)S(1)} fusion(bf16[8,1024,4,128]{1,3,2,0:T(8,128)(2,1)} %bitcast.156, f32[8,4,128,1024]{2,3,1,0:T(8,128)} %get-tuple-element.92, f32[8,4,128]{2,1,0:T(4,128)S(1)} %get-tuple-element.91), kind=kOutput, calls=%fused_computation.69 | convolution fusion | flops 1082654720 | bytes 26230784 | tf_op jit(solution)/shard_map/bhqk,bkhd->bqhd/dot_general | solution.py:197
  191.8 6.3 %copy.209 = bf16[512,4,1024]{0,2,1:T(8,128)(2,1)} copy(bf16[512,4,1024]{2,0,1:T(8,128)(2,1)} %bitcast.145) | data formatting | bytes 8388608 | tf_op jit(solution)/shard_map/transpose | solution.py:65
  204.1 10.2 %fusion.29 = bf16[1024,512]{1,0:T(8,128)(2,1)} fusion(bf16[512,4096]{1,0:T(8,128)(2,1)} %param.9, bf16[512,4096]{0,1:T(8,128)(2,1)} %bitcast.165, bf16[512,4096]{0,1:T(8,128)(2,1)} %all-gather.2.cloned.1.call-done), kind=kOutput, calls=%fused_computation.67 | convolution fusion | flops 4312268800 | bytes 13631488 | tf_op jit(solution)/shard_map/dot_general | solution.py:208
  216.9 11.3 %fusion.9 = f32[4096,512]{1,0:T(8,128)} fusion(bf16[1024,512]{0,1:T(8,128)(2,1)S(1)} %bitcast.160, bf16[512,4096]{0,1:T(8,128)(2,1)} %bitcast.166, bf16[512,4096]{0,1:T(8,128)(2,1)} %all-gather.2.cloned.1.call-done), kind=kOutput, calls=%fused_computation.30 | convolution fusion | flops 4311744512 | bytes 17825792 | tf_op jit(solution)/shard_map/dot_general | solution.py:214
  229.4 18.0 %multiply_reduce_fusion = (f32[8,4,128]{2,1,0:T(4,128)S(1)}, f32[8,4,128,1024]{2,3,1,0:T(8,128)}) fusion(f32[8,4,128,1024]{2,3,1,0:T(8,128)} %get-tuple-element.92, f32[8,4,128]{2,1,0:T(4,128)S(1)} %get-tuple-element.91, bf16[8,128,4,128]{1,3,2,0:T(8,128)(2,1)S(1)} %copy-done.22, bf16[8,1024,4,128]{1,3,2,0:T(8,128)(2,1)} %bitcast.157), kind=kOutput, calls=%fused_computation.22 | convolution fusion | flops 1086320640 | bytes 43024384 | tf_op jit(solution)/shard_map/bqhd,bkhd->bhqk/dot_general | solution.py:222
  247.4 12.5 %multiply_convert_fusion = bf16[8,4,128,1024]{2,3,1,0:T(8,128)(2,1)S(1)} fusion(f32[8,4,128,1024]{2,3,1,0:T(8,128)} %get-tuple-element.94, f32[8,4,128]{2,1,0:T(4,128)S(1)} %get-tuple-element.93, f32[8,4,128,1024]{2,3,1,0:T(8,128)} %get-tuple-element.92, f32[8,4,128]{2,1,0:T(4,128)S(1)} %get-tuple-element.91), kind=kLoop, calls=%fused_computation.21 | loop fusion | flops 16777216 | bytes 41975808 | tf_op jit(solution)/shard_map/convert_element_type | solution.py:226
  263.2 7.0 %multiply_bitcast_fusion = f32[8,1024,4,128]{3,1,2,0:T(8,128)} fusion(bf16[8,4,128,1024]{2,3,1,0:T(8,128)(2,1)S(1)} %multiply_convert_fusion, bf16[8,128,4,128]{1,3,2,0:T(8,128)(2,1)S(1)} %copy.215), kind=kOutput, calls=%fused_computation.20 | convolution fusion | flops 1077936128 | bytes 26214400 | tf_op jit(solution)/shard_map/bhqk,bqhd->bkhd/dot_general | solution.py:236
  270.2 16.5 %copy.217 = f32[8,1024,4,128]{1,3,2,0:T(8,128)} copy(f32[8,1024,4,128]{3,1,2,0:T(8,128)} %multiply_bitcast_fusion) | data formatting | bytes 33554432 | tf_op jit(solution)/shard_map/mul | solution.py:236
  286.6 14.4 %fusion.20 = f32[8,4,128,1024]{3,2,1,0:T(8,128)} fusion(bf16[8,128,4,128]{1,3,2,0:T(8,128)(2,1)S(1)} %copy-done.22, f32[8,4,128,1024]{2,3,1,0:T(8,128)} %get-tuple-element.92, f32[8,4,128]{2,1,0:T(4,128)S(1)} %get-tuple-element.91), kind=kOutput, calls=%fused_computation.44 | convolution fusion | flops 1082130432 | bytes 34619392 | tf_op jit(solution)/shard_map/bhqk,bqhd->bkhd/dot_general | solution.py:239
  301.0 19.8 %fusion.27 = (f32[2,128,512]{1,2,0:T(8,128)S(1)}, f32[2,128,512]{1,2,0:T(8,128)S(1)}, f32[2,128,512]{1,2,0:T(8,128)}, f32[2,128,512]{1,2,0:T(8,128)}, f32[2,8,12...) fusion(f32[1,8,1024,512]{2,3,1,0:T(8,128)} %bitcast.141, ...), kind=kLoop, calls=%fused_computation.54 | loop fusion | flops 12058624 | bytes 52428800 | tf_op jit(solution)/shard_map/reduce_sum | solution.py:261
  324.7 11.8 %collective-permute-done.19 = f32[2,128,512]{2,0,1:T(2,128)S(1)} collective-permute-done((f32[2,128,512]{2,0,1:T(2,128)S(1)}, f32[2,128,512]{2,0,1:T(2,128)S(1)}, u32[]{:S(2)}, u32[]{:S(2)}) %collective-permute-start.19) | collective-permute-done | bytes 524320 | tf_op jit(solution)/shard_map/ppermute | solution.py:18
  359.4 8.1 %collective-permute-done.21 = f32[2,128,512]{2,0,1:T(2,128)} collective-permute-done((f32[2,128,512]{2,0,1:T(2,128)}, f32[2,128,512]{2,0,1:T(2,128)}, u32[]{:S(2)}, u32[]{:S(2)}) %collective-permute-start.21) | collective-permute-done | bytes 524320 | tf_op jit(solution)/shard_map/ppermute | solution.py:18
  371.5 16.2 %collective-permute-done.16 = bf16[1024,1024]{0,1:T(8,128)(2,1)S(1)} collective-permute-done((bf16[1024,1024]{0,1:T(8,128)(2,1)}, bf16[1024,1024]{0,1:T(8,128)(2,1)S(1)}, u32[]{:S(2)}, u32[]{:S(2)}) %collective-permute-start.16) | collective-permute-done | bytes 2097184 | tf_op jit(solution)/shard_map/ppermute | solution.py:48
  394.3 9.1 %fusion.36 = bf16[8,128,4,128]{1,3,2,0:T(8,128)(2,1)} fusion(bf16[8,1024,4,128]{1,3,2,0:T(8,128)(2,1)} %bitcast.155, bf16[8,4,128,1024]{2,3,1,0:T(8,128)(2,1)} %copy-done), kind=kOutput, calls=%fused_computation.70 | convolution fusion | flops 1074790400 | bytes 17825792 | tf_op jit(solution)/shard_map/bhqk,bkhd->bqhd/dot_general | solution.py:229
  423.1 5.4 %copy.226 = f32[2,8,128,512]{3,2,1,0:T(8,128)} copy(f32[2,8,128,512]{2,3,1,0:T(8,128)} %get-tuple-element.58) | data formatting | bytes 8388608 | tf_op jit(solution)/shard_map/slice | solution.py:243
  459.9 6.3 %reshape.255 = f32[2,1024,512]{2,1,0:T(8,128)} reshape(f32[2,512,2,512]{3,2,1,0:T(2,128)} %broadcast_in_dim.58) | data formatting | bytes 8388608 | tf_op jit(solution)/shard_map/reshape | solution.py:32
  466.2 5.9 %fusion.19 = bf16[2,1024,512]{2,1,0:T(8,128)(2,1)S(1)} fusion(f32[2,1024,512]{2,1,0:T(8,128)} %reshape.255, f32[2,4,2,128,512]{4,3,2,1,0:T(8,128)} %copy.227, f32[2,8,128,512]{3,2,1,0:T(8,128)} %copy.226), kind=kLoop, calls=%fused_computation.43 | loop fusion | flops 3145728 | bytes 14680064 | tf_op jit(solution)/shard_map/convert.1
  (207 shorter events, 217.0 us)
Async XLA Ops:
  7.2 196.9 %all-gather.2.cloned.1.call-start = ((), (), s32[]{:S(2)}) async-start(), calls=%async_computation.1 | async-start | bytes 4718592 | tf_op jit(solution)/shard_map/all_gather | solution.py:203
  9.1 63.3 %collective-permute-start.9 = (bf16[512,512]{1,0:T(8,128)(2,1)}, bf16[512,512]{1,0:T(8,128)(2,1)}, u32[]{:S(2)}, u32[]{:S(2)}) collective-permute-start(bf16[512,512]{1,0:T(8,128)(2,1)} %slice.105), channel_id=1, source_target_pairs={{0,1},{1,0},{2,3},{3,2},{4,5},{5,4},{6,7},{7,6},{8,9},{9,8},{10,11... | collective-permute-start | bytes 1572872 | tf_op jit(solution)/shard_map/ppermute | solution.py:41
  14.5 51.0 %collective-permute-start = (f32[2,128,512]{2,1,0:T(8,128)}, f32[2,128,512]{2,1,0:T(8,128)}, u32[]{:S(2)}, u32[]{:S(2)}) collective-permute-start(f32[2,128,512]{2,1,0:T(8,128)} %broadcast_multiply_fusion.5), channel_id=1, source_target_pairs={{0,8},{8,0},{16,24},{24,16},{32,40},{40,32},{48,56},{56,48},{64,72... | collective-permute-start | bytes 1572872 | tf_op jit(solution)/shard_map/ppermute | solution.py:18
  19.6 58.2 %collective-permute-start.7 = (bf16[512,512]{0,1:T(8,128)(2,1)}, bf16[512,512]{0,1:T(8,128)(2,1)}, u32[]{:S(2)}, u32[]{:S(2)}) collective-permute-start(bf16[512,512]{0,1:T(8,128)(2,1)} %copy.246), channel_id=1, source_target_pairs={{0,7},{1,0},{2,1},{3,2},{4,3},{5,4},{6,5},{7,6},{16,23},{17,16},{1... | collective-permute-start | bytes 1572872 | tf_op jit(solution)/shard_map/ppermute | solution.py:90
  25.5 54.2 %collective-permute-start.4 = (bf16[512,512]{0,1:T(8,128)(2,1)}, bf16[512,512]{0,1:T(8,128)(2,1)}, u32[]{:S(2)}, u32[]{:S(2)}) collective-permute-start(bf16[512,512]{0,1:T(8,128)(2,1)} %copy.243), channel_id=1, source_target_pairs={{0,1},{1,2},{2,3},{3,4},{4,5},{5,6},{6,7},{7,0},{8,10},{9,11},{10,... | collective-permute-start | bytes 1572872 | tf_op jit(solution)/shard_map/ppermute | solution.py:90
  26.5 53.5 %collective-permute-start.5 = (bf16[512,512]{0,1:T(8,128)(2,1)}, bf16[512,512]{0,1:T(8,128)(2,1)}, u32[]{:S(2)}, u32[]{:S(2)}) collective-permute-start(bf16[512,512]{0,1:T(8,128)(2,1)} %copy.244), channel_id=1, source_target_pairs={{0,3},{1,4},{2,5},{3,6},{4,7},{5,0},{6,1},{7,2},{8,12},{9,13},{10,... | collective-permute-start | bytes 1572872 | tf_op jit(solution)/shard_map/ppermute | solution.py:90
  65.5 14.5 %collective-permute-start.6 = (bf16[512,512]{0,1:T(8,128)(2,1)}, bf16[512,512]{0,1:T(8,128)(2,1)}, u32[]{:S(2)}, u32[]{:S(2)}) collective-permute-start(bf16[512,512]{0,1:T(8,128)(2,1)} %copy.245), channel_id=1, source_target_pairs={{0,5},{1,6},{2,7},{3,0},{4,1},{5,2},{6,3},{7,4},{8,14},{9,15},{10,... | collective-permute-start | bytes 1572872 | tf_op jit(solution)/shard_map/ppermute | solution.py:90
  72.4 20.2 %collective-permute-start.1 = (f32[2,128,512]{2,0,1:T(2,128)}, f32[2,128,512]{2,0,1:T(2,128)}, u32[]{:S(2)}, u32[]{:S(2)}) collective-permute-start(f32[2,128,512]{2,0,1:T(2,128)} %broadcast_multiply_fusion.4), channel_id=1, source_target_pairs={{0,16},{8,24},{16,0},{24,8},{32,48},{40,56},{48,32},{56,40},{64,80... | collective-permute-start | bytes 1572872 | tf_op jit(solution)/shard_map/ppermute | solution.py:18
  77.7 406.2 %reduce-scatter.2.cloned.1.call-start = ((), (), s32[]{:S(2)}) async-start(), calls=%async_computation.2 | async-start | bytes 8912896 | tf_op jit(solution)/shard_map/reduce_scatter | solution.py:213
  77.9 37.2 %collective-permute-start.10 = (bf16[512,1024]{1,0:T(8,128)(2,1)S(1)}, bf16[512,1024]{1,0:T(8,128)(2,1)S(1)}, u32[]{:S(2)}, u32[]{:S(2)}) collective-permute-start(bf16[512,1024]{1,0:T(8,128)(2,1)S(1)} %get-tuple-element.86), channel_id=1, source_target_pairs={{0,6},{1,7},{2,0},{3,1},{4,2},{5,3},{6,4},{7,5},{8,14},{9,15},{10,... | collective-permute-start | bytes 3145736 | tf_op jit(solution)/shard_map/ppermute | solution.py:49
  79.7 36.7 %collective-permute-start.11 = (bf16[512,1024]{1,0:T(8,128)(2,1)S(1)}, bf16[512,1024]{1,0:T(8,128)(2,1)S(1)}, u32[]{:S(2)}, u32[]{:S(2)}) collective-permute-start(bf16[512,1024]{1,0:T(8,128)(2,1)S(1)} %get-tuple-element.86), channel_id=1, source_target_pairs={{0,2},{1,3},{2,4},{3,5},{4,6},{5,7},{6,0},{7,1},{8,10},{9,11},{10,... | collective-permute-start | bytes 3145736 | tf_op jit(solution)/shard_map/ppermute | solution.py:48
  83.1 114.9 %collective-permute-start.8 = (bf16[4,512,512]{1,2,0:T(8,128)(2,1)}, bf16[4,512,512]{1,2,0:T(8,128)(2,1)}, u32[]{:S(2)}, u32[]{:S(2)}) collective-permute-start(bf16[4,512,512]{1,2,0:T(8,128)(2,1)} %pad_maximum_fusion.6), channel_id=1, source_target_pairs={{0,8},{8,0},{16,24},{24,16},{32,40},{40,32},{48,56},{56,48},{64,72... | collective-permute-start | bytes 6291464 | tf_op jit(solution)/shard_map/ppermute | solution.py:92
  95.8 11.7 %collective-permute-start.2 = (f32[2,128,512]{2,0,1:T(2,128)S(1)}, f32[2,128,512]{2,0,1:T(2,128)S(1)}, u32[]{:S(2)}, u32[]{:S(2)}) collective-permute-start(f32[2,128,512]{2,0,1:T(2,128)S(1)} %broadcast_multiply_fusion.3), channel_id=1, source_target_pairs={{0,32},{8,40},{16,48},{24,56},{32,0},{40,8},{48,16},{56,24},{64,96... | collective-permute-start | bytes 1572872 | tf_op jit(solution)/shard_map/ppermute | solution.py:18
  109.0 13.3 %collective-permute-start.3 = (bf16[2,128,512]{2,0,1:T(2,128)(2,1)S(1)}, bf16[2,128,512]{2,0,1:T(2,128)(2,1)S(1)}, u32[]{:S(2)}, u32[]{:S(2)}) collective-permute-start(bf16[2,128,512]{2,0,1:T(2,128)(2,1)S(1)} %broadcast_multiply_fusion.2), channel_id=1, source_target_pairs={{0,64},{8,72},{16,80},{24,88},{32,96},{40,104},{48,112},{56,120},{... | collective-permute-start | bytes 786440 | tf_op jit(solution)/shard_map/ppermute | solution.py:18
  116.0 67.2 %collective-permute-start.13 = (bf16[512,512]{1,0:T(8,128)(2,1)}, bf16[512,512]{1,0:T(8,128)(2,1)}, u32[]{:S(2)}, u32[]{:S(2)}) collective-permute-start(bf16[512,512]{1,0:T(8,128)(2,1)} %slice.138), channel_id=1, source_target_pairs={{0,6},{1,7},{2,0},{3,1},{4,2},{5,3},{6,4},{7,5},{8,14},{9,15},{10,... | collective-permute-start | bytes 1572872 | tf_op jit(solution)/shard_map/ppermute | solution.py:55
  118.2 64.9 %collective-permute-start.12 = (bf16[512,512]{1,0:T(8,128)(2,1)}, bf16[512,512]{1,0:T(8,128)(2,1)}, u32[]{:S(2)}, u32[]{:S(2)}) collective-permute-start(bf16[512,512]{1,0:T(8,128)(2,1)} %slice.137), channel_id=1, source_target_pairs={{0,2},{1,3},{2,4},{3,5},{4,6},{5,7},{6,0},{7,1},{8,10},{9,11},{10,... | collective-permute-start | bytes 1572872 | tf_op jit(solution)/shard_map/ppermute | solution.py:54
  228.2 111.0 %collective-permute-start.14 = (bf16[1024,512]{0,1:T(8,128)(2,1)S(1)}, bf16[1024,512]{0,1:T(8,128)(2,1)}, u32[]{:S(2)}, u32[]{:S(2)}) collective-permute-start(bf16[1024,512]{0,1:T(8,128)(2,1)S(1)} %bitcast.161), channel_id=1, source_target_pairs={{0,1},{1,0},{2,3},{3,2},{4,5},{5,4},{6,7},{7,6},{8,9},{9,8},{10,11... | collective-permute-start | bytes 3145736 | tf_op jit(solution)/shard_map/ppermute | solution.py:41
  321.1 15.5 %collective-permute-start.19 = (f32[2,128,512]{2,0,1:T(2,128)S(1)}, f32[2,128,512]{2,0,1:T(2,128)S(1)}, u32[]{:S(2)}, u32[]{:S(2)}) collective-permute-start(f32[2,128,512]{2,0,1:T(2,128)S(1)} %copy.220), channel_id=1, source_target_pairs={{0,64},{8,72},{16,80},{24,88},{32,96},{40,104},{48,112},{56,120},{... | collective-permute-start | bytes 1572872 | tf_op jit(solution)/shard_map/ppermute | solution.py:18
  342.1 45.7 %collective-permute-start.16 = (bf16[1024,1024]{0,1:T(8,128)(2,1)}, bf16[1024,1024]{0,1:T(8,128)(2,1)S(1)}, u32[]{:S(2)}, u32[]{:S(2)}) collective-permute-start(bf16[1024,1024]{0,1:T(8,128)(2,1)} %pad_maximum_fusion.7), channel_id=1, source_target_pairs={{0,2},{1,3},{2,4},{3,5},{4,6},{5,7},{6,0},{7,1},{8,10},{9,11},{10,... | collective-permute-start | bytes 6291464 | tf_op jit(solution)/shard_map/ppermute | solution.py:48
  343.8 46.1 %collective-permute-start.15 = (bf16[1024,1024]{0,1:T(8,128)(2,1)}, bf16[1024,1024]{0,1:T(8,128)(2,1)}, u32[]{:S(2)}, u32[]{:S(2)}) collective-permute-start(bf16[1024,1024]{0,1:T(8,128)(2,1)} %pad_maximum_fusion.7), channel_id=1, source_target_pairs={{0,6},{1,7},{2,0},{3,1},{4,2},{5,3},{6,4},{7,5},{8,14},{9,15},{10,... | collective-permute-start | bytes 6291464 | tf_op jit(solution)/shard_map/ppermute | solution.py:49
  353.3 14.3 %collective-permute-start.21 = (f32[2,128,512]{2,0,1:T(2,128)}, f32[2,128,512]{2,0,1:T(2,128)}, u32[]{:S(2)}, u32[]{:S(2)}) collective-permute-start(f32[2,128,512]{2,0,1:T(2,128)} %select_add_fusion.2), channel_id=1, source_target_pairs={{0,16},{8,24},{16,0},{24,8},{32,48},{40,56},{48,32},{56,40},{64,80... | collective-permute-start | bytes 1572872 | tf_op jit(solution)/shard_map/ppermute | solution.py:18
  371.5 66.8 %collective-permute-start.22 = (f32[2,128,512]{2,0,1:T(2,128)}, f32[2,128,512]{2,0,1:T(2,128)}, u32[]{:S(2)}, u32[]{:S(2)}) collective-permute-start(f32[2,128,512]{2,0,1:T(2,128)} %select_add_fusion), channel_id=1, source_target_pairs={{0,8},{8,0},{16,24},{24,16},{32,40},{40,32},{48,56},{56,48},{64,72... | collective-permute-start | bytes 1572872 | tf_op jit(solution)/shard_map/ppermute | solution.py:18
  388.8 50.8 %collective-permute-start.17 = (bf16[1024,512]{0,1:T(8,128)(2,1)}, bf16[1024,512]{0,1:T(8,128)(2,1)}, u32[]{:S(2)}, u32[]{:S(2)}) collective-permute-start(bf16[1024,512]{0,1:T(8,128)(2,1)} %slice.139), channel_id=1, source_target_pairs={{0,2},{1,3},{2,4},{3,5},{4,6},{5,7},{6,0},{7,1},{8,10},{9,11},{10,... | collective-permute-start | bytes 3145736 | tf_op jit(solution)/shard_map/ppermute | solution.py:54
  392.2 47.5 %collective-permute-start.18 = (bf16[1024,512]{0,1:T(8,128)(2,1)}, bf16[1024,512]{0,1:T(8,128)(2,1)}, u32[]{:S(2)}, u32[]{:S(2)}) collective-permute-start(bf16[1024,512]{0,1:T(8,128)(2,1)} %slice.140), channel_id=1, source_target_pairs={{0,6},{1,7},{2,0},{3,1},{4,2},{5,3},{6,4},{7,5},{8,14},{9,15},{10,... | collective-permute-start | bytes 3145736 | tf_op jit(solution)/shard_map/ppermute | solution.py:55
  (26 other events, 159.4 us)
Sparse Core Ops, SparseCore 0:
  77.8 90.4 all-gather.1
  228.3 103.8 reduce-scatter.1

commit v7 on v6

--- a/solution.py
+++ b/solution.py
@@ -160,13 +160,12 @@
                 2, blocks, BLK, features
             )
         )
-    for level_idx in range(cross_levels):
-        segments.append(
-            jnp.broadcast_to(
-                siblings[level_idx].astype(jnp.bfloat16)[:, None], (2, blocks, BLK, features)
-            )
-        )
     key_set = jnp.concatenate(segments, axis=2)
+    far_set = jnp.concatenate(
+        [siblings[level_idx].astype(jnp.bfloat16) for level_idx in range(cross_levels)], axis=1
+    )
+    near_keys = (1 + local_levels) * BLK
+    far_keys = cross_levels * BLK
     key_bias = jnp.concatenate(
         [jnp.zeros((BLK,), jnp.float32)]
         + [jnp.full((BLK,), level_idx * LOG_TWO, jnp.float32) for level_idx in range(level_count)]
@@ -182,10 +181,22 @@
         axis=1,
     )
     query_heads = queries.reshape(blocks, BLK, head_count, DH)
-    key_heads = key_set[0].reshape(blocks, keys_all, head_count, DH)
-    value_heads = key_set[1].reshape(blocks, keys_all, head_count, DH)
+    key_heads = key_set[0].reshape(blocks, near_keys, head_count, DH)
+    value_heads = key_set[1].reshape(blocks, near_keys, head_count, DH)
+    far_key_heads = far_set[0].reshape(far_keys, head_count, DH)
+    far_value_heads = far_set[1].reshape(far_keys, head_count, DH)
     scores = (
-        jnp.einsum("bqhd,bkhd->bhqk", query_heads, key_heads, preferred_element_type=jnp.float32)
+        jnp.concatenate(
+            [
+                jnp.einsum(
+                    "bqhd,bkhd->bhqk", query_heads, key_heads, preferred_element_type=jnp.float32
+                ),
+                jnp.einsum(
+                    "bqhd,khd->bhqk", query_heads, far_key_heads, preferred_element_type=jnp.float32
+                ),
+            ],
+            axis=-1,
+        )
         * score_scale
         + key_bias
     )
@@ -194,7 +205,10 @@
     weights_raw = jnp.exp(scores - row_max)
     attn_prob = weights_raw / jnp.sum(weights_raw, axis=-1, keepdims=True)
     prob_low = attn_prob.astype(jnp.bfloat16)
-    mixed = jnp.einsum("bhqk,bkhd->bqhd", prob_low, value_heads, preferred_element_type=jnp.float32)
+    near_prob, far_prob = prob_low[..., :near_keys], prob_low[..., near_keys:]
+    mixed = jnp.einsum(
+        "bhqk,bkhd->bqhd", near_prob, value_heads, preferred_element_type=jnp.float32
+    ) + jnp.einsum("bhqk,khd->bqhd", far_prob, far_value_heads, preferred_element_type=jnp.float32)
     attended = mixed.astype(jnp.bfloat16).reshape(row_count, features)
     attended, weight_cols = lax.optimization_barrier((attended, weight_columns(out_weight)))
     half_rows = row_count // 2
@@ -219,27 +233,51 @@
         tiled=True,
     )
     grad_heads = grad_attn.reshape(blocks, BLK, head_count, DH)
-    grad_prob = jnp.einsum(
-        "bqhd,bkhd->bhqk", grad_heads, value_heads, preferred_element_type=jnp.float32
+    grad_prob = jnp.concatenate(
+        [
+            jnp.einsum(
+                "bqhd,bkhd->bhqk", grad_heads, value_heads, preferred_element_type=jnp.float32
+            ),
+            jnp.einsum(
+                "bqhd,khd->bhqk", grad_heads, far_value_heads, preferred_element_type=jnp.float32
+            ),
+        ],
+        axis=-1,
     )
     row_delta = jnp.sum(attn_prob * grad_prob, axis=-1, keepdims=True)
     grad_score = (attn_prob * (grad_prob - row_delta)).astype(jnp.bfloat16)
+    near_score, far_score = grad_score[..., :near_keys], grad_score[..., near_keys:]
     grad_query = (
         (
-            jnp.einsum("bhqk,bkhd->bqhd", grad_score, key_heads, preferred_element_type=jnp.float32)
+            (
+                jnp.einsum(
+                    "bhqk,bkhd->bqhd", near_score, key_heads, preferred_element_type=jnp.float32
+                )
+                + jnp.einsum(
+                    "bhqk,khd->bqhd", far_score, far_key_heads, preferred_element_type=jnp.float32
+                )
+            )
             * score_scale
         )
         .astype(jnp.bfloat16)
         .reshape(row_count, features)
     )
     grad_keyset = (
-        jnp.einsum("bhqk,bqhd->bkhd", grad_score, query_heads, preferred_element_type=jnp.float32)
+        jnp.einsum("bhqk,bqhd->bkhd", near_score, query_heads, preferred_element_type=jnp.float32)
         * score_scale
     )
     grad_valset = jnp.einsum(
-        "bhqk,bqhd->bkhd", prob_low, grad_heads, preferred_element_type=jnp.float32
-    )
-    grad_sets = jnp.stack([grad_keyset, grad_valset]).reshape(2, blocks, keys_all, features)
+        "bhqk,bqhd->bkhd", near_prob, grad_heads, preferred_element_type=jnp.float32
+    )
+    grad_sets = jnp.stack([grad_keyset, grad_valset]).reshape(2, blocks, near_keys, features)
+    far_grad_keys = (
+        jnp.einsum("bhqk,bqhd->khd", far_score, query_heads, preferred_element_type=jnp.float32)
+        * score_scale
+    )
+    far_grad_values = jnp.einsum(
+        "bhqk,bqhd->khd", far_prob, grad_heads, preferred_element_type=jnp.float32
+    )
+    far_grads = jnp.stack([far_grad_keys, far_grad_values]).reshape(2, far_keys, features)
     token_grad = grad_sets[:, :, :BLK].reshape(2, row_count, features)
     level_grads = []
     for level_idx in range(local_levels):
@@ -257,8 +295,7 @@
         level_grads.append(restored)
     sibling_grads = []
     for level_idx in range(cross_levels):
-        lower = (local_levels + 1 + level_idx) * BLK
-        sibling_grads.append(jnp.sum(grad_sets[:, :, lower : lower + BLK], axis=1))
+        sibling_grads.append(far_grads[:, level_idx * BLK : (level_idx + 1) * BLK])
     carried = jnp.zeros((2, BLK, features), jnp.float32)
     for level_idx in reversed(range(cross_levels)):
         outgoing = sibling_grads[level_idx]

time: 499 us -> 473 us (0.948)
  local copies, waits for them, and re-layouts: 172 us -> 137 us
  matrix products: 103 us -> 76.2 us
  other arithmetic: 107 us -> 123 us
  waiting for transfers between devices: 51.8 us -> 62.8 us
  starting transfers between devices: 42.7 us -> 52.5 us
    sub x0 -> x2, other arithmetic: none -> 37.7 us  [the longest x1 29.8 us: body(): grad_score = (attn_prob * (grad_prob - row_delta)).astype(jnp.bfloat16)]
    reduce_sum x1 -> x0, other arithmetic: 19.8 us -> none  [body(): sibling_grads.append(jnp.sum(grad_sets[:, :, lower:lower + BLK], axis=1))]
    mul x1 -> x0, local copies, waits for them, and re-layouts: 16.5 us -> none  [body(): jnp.einsum('bhqk,bqhd->bkhd', grad_score, query_heads, preferred_element_...]
    slice x3 -> x9, local copies, waits for them, and re-layouts: 34.8 us -> 20.2 us  [the longest x2 10 us: body(): value_heads = key_set[1].reshape(blocks, near_keys, head_count, DH)]
    dot_general x1, matrix products: 18 us -> 4.59 us  [body(): jnp.einsum('bqhd,bkhd->bhqk', grad_heads, value_heads, preferred_element_...]
    ppermute x1, starting transfers between devices: 0.01 us -> 13.2 us  [weight_columns(): lax.ppermute(mine, 'seq', [(src, src ^ 1) for src in range(seq_count)])]
    sub x1 -> x0, matrix products: 12.8 us -> none  [body(): weights_raw = jnp.exp(scores - row_max)]
    all_gather x1, waiting for transfers between devices: 0.02 us -> 10.9 us  [body(): lax.all_gather(cotangent[:half_rows], 'head', axis=1, tiled=True)]
  transfers between devices with their start and end apart: 25 -> 25, of which waited for: 7 -> 6; matrix products, arithmetic and copies ran while one was open for 71% -> 62% of each run, Pallas kernels for 0% -> 0%
where the time goes in v7:
time: 473 us; the launch traced here: 466 us
  local copies, waits for them, and re-layouts  137 us (29%)
  other arithmetic  123 us (26%)
  matrix products  76.2 us (16%)
  waiting for transfers between devices  62.8 us (13%)
  starting transfers between devices  52.5 us (11%)
  between operations  15.2 us (3%)
    ppermute x8, waiting for transfers between devices, swapped(): return lax.ppermute(value, axis, pairs)  33.3 us
    sub x1, other arithmetic, body(): grad_score = (attn_prob * (grad_prob - row_delta)).astype(jnp.bfloat16)  29.8 us
    unnamed x99, local copies, waits for them, and re-layouts  24.8 us
    ppermute x8, starting transfers between devices, swapped(): return lax.ppermute(value, axis, pairs)  16.8 us
    ppermute x2, waiting for transfers between devices, head_ring_gather(): from_below = lax.ppermute(pair_block, 'head', upward)  14.2 us
    ppermute x1, starting transfers between devices, weight_columns(): lax.ppermute(mine, 'seq', [(src, src ^ 1) for src in range(seq_count)])  13.2 us
    reshape x3, local copies, waits for them, and re-layouts, spread_rows(): return wide.reshape(shape_in[:-2] + (shape_in[-2] * factor, shape_in[-1]))  12.9 us
    reduce_sum x2, other arithmetic, body(): pooled = stacked.reshape(2, row_count // factor, factor, features).astype...  12.1 us
  transfers between devices with their start and end apart: 25, of which 6 were waited for; matrix products, arithmetic and copies ran while one was open for 62% of the time, Pallas kernels for 0%

profile of v7, /device:TPU:0, one launch (start us, length us, event | category | flops | bytes accessed | tf_op | source)
XLA Modules:
  0.0 466.4 jit_solution(15084327549146137877)
XLA Ops:
  18.5 4.9 %collective-permute-start.7 = (bf16[512,512]{0,1:T(8,128)(2,1)}, bf16[512,512]{0,1:T(8,128)(2,1)}, u32[]{:S(2)}, u32[]{:S(2)}) collective-permute-start(bf16[512,512]{0,1:T(8,128)(2,1)} %copy.282), channel_id=1, source_target_pairs={{0,7},{1,0},{2,1},{3,2},{4,3},{5,4},{6,5},{7,6},{16,23},{17,16},{1... | collective-permute-start | bytes 1572872 | tf_op jit(solution)/shard_map/ppermute | solution.py:90
  32.0 7.6 %convert_reduce_fusion.2 = f32[2,512,512]{2,1,0:T(8,128)S(1)} fusion(bf16[1,512,2,512]{3,2,1,0:T(2,128)(2,1)} %stack.88, bf16[1,512,2,512]{3,2,1,0:T(2,128)(2,1)} %stack.87), kind=kLoop, calls=%fused_computation.40 | loop fusion | flops 2621440 | bytes 4194304 | tf_op jit(solution)/shard_map/reduce_sum | solution.py:152
  60.4 6.7 %copy.204 = bf16[1,8,512,512]{2,3,1,0:T(8,128)(2,1)} copy(bf16[1,8,512,512]{3,2,1,0:T(8,128)(2,1)} %get-tuple-element.54) | data formatting | bytes 8388608 | tf_op jit(solution)/shard_map/slice | solution.py:184
  78.1 6.1 %collective-permute-done.1 = f32[2,128,512]{2,1,0:T(8,128)S(1)} collective-permute-done((f32[2,128,512]{2,1,0:T(8,128)S(1)}, f32[2,128,512]{2,1,0:T(8,128)S(1)}, u32[]{:S(2)}, u32[]{:S(2)}) %collective-permute-start.1) | collective-permute-done | bytes 524320 | tf_op jit(solution)/shard_map/ppermute | solution.py:18
  94.0 6.5 %copy.202 = bf16[1,8,512,512]{2,3,1,0:T(8,128)(2,1)} copy(bf16[1,8,512,512]{3,2,1,0:T(8,128)(2,1)} %get-tuple-element.53) | data formatting | bytes 8388608 | tf_op jit(solution)/shard_map/slice | solution.py:185
  127.7 13.2 %collective-permute-start.8 = (bf16[4,512,512]{1,2,0:T(8,128)(2,1)}, bf16[4,512,512]{1,2,0:T(8,128)(2,1)}, u32[]{:S(2)}, u32[]{:S(2)}) collective-permute-start(bf16[4,512,512]{1,2,0:T(8,128)(2,1)} %pad_maximum_fusion.9), channel_id=1, source_target_pairs={{0,8},{8,0},{16,24},{24,16},{32,40},{40,32},{48,56},{56,48},{64,72... | collective-permute-start | bytes 6291464 | tf_op jit(solution)/shard_map/ppermute | solution.py:92
  152.1 7.8 %fusion.75 = (f32[8,4,128]{2,1,0:T(4,128)S(1)}, f32[8,4,128,1024]{2,3,1,0:T(8,128)S(1)}) fusion(f32[8,4,128,512]{2,3,1,0:T(8,128)S(1)} %convolution_bitcast_fusion.1, f32[8,4,128,512]{2,3,1,0:T(8,128)} %convolution_bitcast_fusion.2, f32[1024]{0:T(1024)S(1)} %copy-done.38, pred[8,1024]{1,0:T(8,128)(4,1)S(1)} %concatenate.80), kind=kOutput, calls=%fused_computation.157 | output fusion | flops 25166848 | bytes 33583104 | tf_op jit(solution)/shard_map/sub | solution.py:205
  181.2 5.0 %gather_fusion = bf16[4,512,1024]{2,1,0:T(8,128)(2,1)} fusion(bf16[4,512,1024]{2,1,0:T(8,128)(2,1)} %pad_maximum_fusion.7, s32[1024]{0:T(1024)S(1)} %pad_clamp_fusion), kind=kCustom, calls=%fused_computation | custom fusion | bytes 8388624 | tf_op jit(solution)/shard_map/gather | solution.py:64
  186.2 6.3 %copy.226 = bf16[512,4,1024]{0,2,1:T(8,128)(2,1)} copy(bf16[512,4,1024]{2,0,1:T(8,128)(2,1)} %bitcast.181) | data formatting | bytes 8388608 | tf_op jit(solution)/shard_map/transpose | solution.py:65
  198.6 10.9 %all-gather.2.cloned.1.call-done = bf16[512,4096]{0,1:T(8,128)(2,1)} async-done(((bf16[512,512]{0,1:T(8,128)(2,1)}), bf16[512,4096]{0,1:T(8,128)(2,1)}) %all-gather.2.cloned.1.call-update) | async-done | bytes 4194320 | tf_op jit(solution)/shard_map/all_gather | solution.py:217
  209.4 9.2 %fusion.44 = bf16[1024,512]{1,0:T(8,128)(2,1)S(1)} fusion(bf16[512,4096]{1,0:T(8,128)(2,1)} %param.9, bf16[512,4096]{0,1:T(8,128)(2,1)} %bitcast.195, bf16[512,4096]{0,1:T(8,128)(2,1)} %all-gather.2.cloned.1.call-done), kind=kOutput, calls=%fused_computation.77 | convolution fusion | flops 4312268800 | bytes 13631488 | tf_op jit(solution)/shard_map/dot_general | solution.py:222
  221.4 5.4 %fusion.20 = f32[4,128,512,1]{2,1,3,0:T(8,128)} fusion(bf16[8,128,4,128]{3,2,1,0:T(4,128)(2,1)} %reshape.241, bf16[8,4,128,1024]{2,3,1,0:T(8,128)(2,1)} %fusion.69), kind=kOutput, calls=%fused_computation.35 | convolution fusion | flops 536870912 | bytes 6291456 | tf_op jit(solution)/shard_map/bhqk,bqhd->khd/dot_general | solution.py:277
  231.4 5.5 %convolution_bitcast_fusion = f32[8,4,128,512]{2,3,1,0:T(8,128)} fusion(bf16[512,4,128,1]{0,2,1,3:T(8,128)(2,1)S(1)} %bitcast.190, bf16[8,128,4,128]{1,3,2,0:T(8,128)(2,1)S(1)} %copy.252), kind=kOutput, calls=%fused_computation.53 | convolution fusion | flops 536870912 | bytes 9961472 | tf_op jit(solution)/shard_map/bqhd,khd->bhqk/dot_general | solution.py:241
  237.7 8.3 %fusion.13 = f32[4096,512]{1,0:T(8,128)} fusion(bf16[1024,512]{0,1:T(8,128)(2,1)} %bitcast.162, bf16[512,4096]{0,1:T(8,128)(2,1)S(1)} %bitcast.196, bf16[512,4096]{0,1:T(8,128)(2,1)S(1)} %copy-done.37), kind=kOutput, calls=%fused_computation.25 | convolution fusion | flops 4311744512 | bytes 17825792 | tf_op jit(solution)/shard_map/dot_general | solution.py:228
  248.0 29.8 %multiply_convert_fusion = bf16[8,4,128,1024]{2,3,1,0:T(8,128)(2,1)} fusion(f32[8,4,128,512]{2,3,1,0:T(8,128)} %convolution_bitcast_fusion, f32[8,4,128,512]{2,3,1,0:T(8,128)} %fusion.76, f32[8,4,128,1024]{2,3,1,0:T(8,128)} %copy-done.7, f32[8,4,128]{2,1,0:T(4,128)S(1)} %get-tuple-element.90), kind=kOutput, calls=%fused_computation.13 | output fusion | flops 33559552 | bytes 41959424 | tf_op jit(solution)/shard_map/sub | solution.py:248
  296.9 14.6 %collective-permute-done.19 = f32[2,128,512]{2,1,0:T(8,128)S(1)} collective-permute-done((f32[2,128,512]{2,1,0:T(8,128)S(1)}, f32[2,128,512]{2,1,0:T(8,128)S(1)}, u32[]{:S(2)}, u32[]{:S(2)}) %collective-permute-start.19) | collective-permute-done | bytes 524320 | tf_op jit(solution)/shard_map/ppermute | solution.py:18
  339.0 12.6 %collective-permute-done.21 = f32[2,128,512]{2,1,0:T(8,128)S(1)} collective-permute-done((f32[2,128,512]{2,1,0:T(8,128)S(1)}, f32[2,128,512]{2,1,0:T(8,128)S(1)}, u32[]{:S(2)}, u32[]{:S(2)}) %collective-permute-start.21) | collective-permute-done | bytes 524320 | tf_op jit(solution)/shard_map/ppermute | solution.py:18
  352.9 14.2 %collective-permute-done.16 = bf16[1024,1024]{0,1:T(8,128)(2,1)} collective-permute-done((bf16[1024,1024]{0,1:T(8,128)(2,1)}, bf16[1024,1024]{0,1:T(8,128)(2,1)}, u32[]{:S(2)}, u32[]{:S(2)}) %collective-permute-start.16) | collective-permute-done | bytes 2097184 | tf_op jit(solution)/shard_map/ppermute | solution.py:48
  375.9 7.0 %fusion.16 = (f32[2,8,128,512]{2,3,1,0:T(8,128)}, f32[2,8,128,512]{2,3,1,0:T(8,128)}, f32[2,8,128,512]{2,3,1,0:T(8,128)}, f32[2,8,128,512]{2,3,1,0:T(8,128)}) fusion(f32[1,8,512,512]{2,3,1,0:T(8,128)S(1)} %bitcast.172, f32[1,8,512,512]{2,3,1,0:T(8,128)S(1)} %bitcast.171), kind=kLoop, calls=%fused_computation.28 | loop fusion | flops 4194304 | bytes 33554432 | tf_op jit(solution)/shard_map/stack | solution.py:272
  382.9 5.4 %copy.254 = f32[2,8,128,512]{3,2,1,0:T(8,128)} copy(f32[2,8,128,512]{2,3,1,0:T(8,128)} %get-tuple-element.49) | data formatting | bytes 8388608 | tf_op jit(solution)/shard_map/slice | solution.py:281
  388.3 5.3 %copy.255 = f32[2,4,2,128,512]{4,3,2,1,0:T(8,128)} copy(f32[2,4,2,128,512]{3,4,2,1,0:T(8,128)} %bitcast.184) | data formatting | bytes 8388608 | tf_op jit(solution)/shard_map/reshape | solution.py:292
  393.6 4.8 %rev.19 = f32[2,4,2,128,512]{4,3,2,1,0:T(8,128)} reverse(f32[2,4,2,128,512]{4,3,2,1,0:T(8,128)} %copy.255), dimensions={2} | reverse | bytes 8388608 | tf_op jit(solution)/shard_map/rev | solution.py:292
  434.3 6.3 %reshape.256 = f32[2,1024,512]{2,1,0:T(8,128)} reshape(f32[2,512,2,512]{3,2,1,0:T(2,128)} %broadcast_in_dim.46) | data formatting | bytes 8388608 | tf_op jit(solution)/shard_map/reshape | solution.py:32
  440.6 5.9 %fusion.19 = bf16[2,1024,512]{2,1,0:T(8,128)(2,1)S(1)} fusion(f32[2,1024,512]{2,1,0:T(8,128)} %reshape.256, f32[2,4,2,128,512]{4,3,2,1,0:T(8,128)} %rev.19, f32[2,8,128,512]{3,2,1,0:T(8,128)} %copy.254), kind=kLoop, calls=%fused_computation.34 | loop fusion | flops 3145728 | bytes 14680064 | tf_op jit(solution)/shard_map/convert.1
  (257 shorter events, 242.2 us)
Async XLA Ops:
  7.2 202.3 %all-gather.2.cloned.1.call-start = ((), (), s32[]{:S(2)}) async-start(), calls=%async_computation.1 | async-start | bytes 4718592 | tf_op jit(solution)/shard_map/all_gather | solution.py:217
  9.1 79.2 %collective-permute-start.9 = (bf16[512,512]{1,0:T(8,128)(2,1)}, bf16[512,512]{1,0:T(8,128)(2,1)}, u32[]{:S(2)}, u32[]{:S(2)}) collective-permute-start(bf16[512,512]{1,0:T(8,128)(2,1)} %slice.127), channel_id=1, source_target_pairs={{0,1},{1,0},{2,3},{3,2},{4,5},{5,4},{6,7},{7,6},{8,9},{9,8},{10,11... | collective-permute-start | bytes 1572872 | tf_op jit(solution)/shard_map/ppermute | solution.py:41
  14.5 52.6 %collective-permute-start = (f32[2,128,512]{2,1,0:T(8,128)}, f32[2,128,512]{2,1,0:T(8,128)}, u32[]{:S(2)}, u32[]{:S(2)}) collective-permute-start(f32[2,128,512]{2,1,0:T(8,128)} %broadcast_multiply_fusion.3), channel_id=1, source_target_pairs={{0,8},{8,0},{16,24},{24,16},{32,40},{40,32},{48,56},{56,48},{64,72... | collective-permute-start | bytes 1572872 | tf_op jit(solution)/shard_map/ppermute | solution.py:18
  18.5 91.6 %collective-permute-start.7 = (bf16[512,512]{0,1:T(8,128)(2,1)}, bf16[512,512]{0,1:T(8,128)(2,1)}, u32[]{:S(2)}, u32[]{:S(2)}) collective-permute-start(bf16[512,512]{0,1:T(8,128)(2,1)} %copy.282), channel_id=1, source_target_pairs={{0,7},{1,0},{2,1},{3,2},{4,3},{5,4},{6,5},{7,6},{16,23},{17,16},{1... | collective-permute-start | bytes 1572872 | tf_op jit(solution)/shard_map/ppermute | solution.py:90
  24.4 90.0 %collective-permute-start.4 = (bf16[512,512]{0,1:T(8,128)(2,1)}, bf16[512,512]{0,1:T(8,128)(2,1)}, u32[]{:S(2)}, u32[]{:S(2)}) collective-permute-start(bf16[512,512]{0,1:T(8,128)(2,1)} %copy.279), channel_id=1, source_target_pairs={{0,1},{1,2},{2,3},{3,4},{4,5},{5,6},{6,7},{7,0},{8,10},{9,11},{10,... | collective-permute-start | bytes 1572872 | tf_op jit(solution)/shard_map/ppermute | solution.py:90
  70.3 13.8 %collective-permute-start.1 = (f32[2,128,512]{2,1,0:T(8,128)S(1)}, f32[2,128,512]{2,1,0:T(8,128)S(1)}, u32[]{:S(2)}, u32[]{:S(2)}) collective-permute-start(f32[2,128,512]{2,1,0:T(8,128)S(1)} %copy_multiply_fusion.2), channel_id=1, source_target_pairs={{0,16},{8,24},{16,0},{24,8},{32,48},{40,56},{48,32},{56,40},{64,80... | collective-permute-start | bytes 1572872 | tf_op jit(solution)/shard_map/ppermute | solution.py:18
  86.4 20.2 %collective-permute-start.2 = (f32[2,128,512]{2,1,0:T(8,128)}, f32[2,128,512]{2,1,0:T(8,128)}, u32[]{:S(2)}, u32[]{:S(2)}) collective-permute-start(f32[2,128,512]{2,1,0:T(8,128)} %copy_multiply_fusion.1), channel_id=1, source_target_pairs={{0,32},{8,40},{16,48},{24,56},{32,0},{40,8},{48,16},{56,24},{64,96... | collective-permute-start | bytes 1572872 | tf_op jit(solution)/shard_map/ppermute | solution.py:18
  91.9 50.2 %collective-permute-start.10 = (bf16[512,1024]{1,0:T(8,128)(2,1)}, bf16[512,1024]{1,0:T(8,128)(2,1)S(1)}, u32[]{:S(2)}, u32[]{:S(2)}) collective-permute-start(bf16[512,1024]{1,0:T(8,128)(2,1)} %get-tuple-element.83), channel_id=1, source_target_pairs={{0,6},{1,7},{2,0},{3,1},{4,2},{5,3},{6,4},{7,5},{8,14},{9,15},{10,... | collective-permute-start | bytes 3145736 | tf_op jit(solution)/shard_map/ppermute | solution.py:49
  93.6 51.3 %collective-permute-start.11 = (bf16[512,1024]{1,0:T(8,128)(2,1)}, bf16[512,1024]{1,0:T(8,128)(2,1)S(1)}, u32[]{:S(2)}, u32[]{:S(2)}) collective-permute-start(bf16[512,1024]{1,0:T(8,128)(2,1)} %get-tuple-element.83), channel_id=1, source_target_pairs={{0,2},{1,3},{2,4},{3,5},{4,6},{5,7},{6,0},{7,1},{8,10},{9,11},{10,... | collective-permute-start | bytes 3145736 | tf_op jit(solution)/shard_map/ppermute | solution.py:48
  110.1 14.5 %collective-permute-start.6 = (bf16[512,512]{0,1:T(8,128)(2,1)}, bf16[512,512]{0,1:T(8,128)(2,1)}, u32[]{:S(2)}, u32[]{:S(2)}) collective-permute-start(bf16[512,512]{0,1:T(8,128)(2,1)} %copy.281), channel_id=1, source_target_pairs={{0,5},{1,6},{2,7},{3,0},{4,1},{5,2},{6,3},{7,4},{8,14},{9,15},{10,... | collective-permute-start | bytes 1572872 | tf_op jit(solution)/shard_map/ppermute | solution.py:90
  114.4 33.0 %collective-permute-start.3 = (bf16[2,128,512]{2,1,0:T(8,128)(2,1)S(1)}, bf16[2,128,512]{2,1,0:T(8,128)(2,1)}, u32[]{:S(2)}, u32[]{:S(2)}) collective-permute-start(bf16[2,128,512]{2,1,0:T(8,128)(2,1)S(1)} %copy_multiply_fusion), channel_id=1, source_target_pairs={{0,64},{8,72},{16,80},{24,88},{32,96},{40,104},{48,112},{56,120},{... | collective-permute-start | bytes 786440 | tf_op jit(solution)/shard_map/ppermute | solution.py:18
  120.2 339.2 %reduce-scatter.2.cloned.1.call-start = ((), (), s32[]{:S(2)}) async-start(), calls=%async_computation.2 | async-start | bytes 8912896 | tf_op jit(solution)/shard_map/reduce_scatter | solution.py:227
  127.7 64.8 %collective-permute-start.8 = (bf16[4,512,512]{1,2,0:T(8,128)(2,1)}, bf16[4,512,512]{1,2,0:T(8,128)(2,1)}, u32[]{:S(2)}, u32[]{:S(2)}) collective-permute-start(bf16[4,512,512]{1,2,0:T(8,128)(2,1)} %pad_maximum_fusion.9), channel_id=1, source_target_pairs={{0,8},{8,0},{16,24},{24,16},{32,40},{40,32},{48,56},{56,48},{64,72... | collective-permute-start | bytes 6291464 | tf_op jit(solution)/shard_map/ppermute | solution.py:92
  143.0 34.5 %collective-permute-start.13 = (bf16[512,512]{1,0:T(8,128)(2,1)}, bf16[512,512]{1,0:T(8,128)(2,1)}, u32[]{:S(2)}, u32[]{:S(2)}) collective-permute-start(bf16[512,512]{1,0:T(8,128)(2,1)} %slice.166), channel_id=1, source_target_pairs={{0,6},{1,7},{2,0},{3,1},{4,2},{5,3},{6,4},{7,5},{8,14},{9,15},{10,... | collective-permute-start | bytes 1572872 | tf_op jit(solution)/shard_map/ppermute | solution.py:55
  145.8 31.7 %collective-permute-start.12 = (bf16[512,512]{1,0:T(8,128)(2,1)}, bf16[512,512]{1,0:T(8,128)(2,1)}, u32[]{:S(2)}, u32[]{:S(2)}) collective-permute-start(bf16[512,512]{1,0:T(8,128)(2,1)} %slice.165), channel_id=1, source_target_pairs={{0,2},{1,3},{2,4},{3,5},{4,6},{5,7},{6,0},{7,1},{8,10},{9,11},{10,... | collective-permute-start | bytes 1572872 | tf_op jit(solution)/shard_map/ppermute | solution.py:54
  247.6 68.4 %collective-permute-start.14 = (bf16[1024,512]{0,1:T(8,128)(2,1)}, bf16[1024,512]{0,1:T(8,128)(2,1)}, u32[]{:S(2)}, u32[]{:S(2)}) collective-permute-start(bf16[1024,512]{0,1:T(8,128)(2,1)} %bitcast.162), channel_id=1, source_target_pairs={{0,1},{1,0},{2,3},{3,2},{4,5},{5,4},{6,7},{7,6},{8,9},{9,8},{10,11... | collective-permute-start | bytes 3145736 | tf_op jit(solution)/shard_map/ppermute | solution.py:41
  284.2 27.2 %collective-permute-start.19 = (f32[2,128,512]{2,1,0:T(8,128)S(1)}, f32[2,128,512]{2,1,0:T(8,128)S(1)}, u32[]{:S(2)}, u32[]{:S(2)}) collective-permute-start(f32[2,128,512]{2,1,0:T(8,128)S(1)} %fusion.55), channel_id=1, source_target_pairs={{0,64},{8,72},{16,80},{24,88},{32,96},{40,104},{48,112},{56,120},{... | collective-permute-start | bytes 1572872 | tf_op jit(solution)/shard_map/ppermute | solution.py:18
  314.4 14.8 %collective-permute-start.20 = (f32[2,128,512]{2,1,0:T(8,128)}, f32[2,128,512]{2,1,0:T(8,128)}, u32[]{:S(2)}, u32[]{:S(2)}) collective-permute-start(f32[2,128,512]{2,1,0:T(8,128)} %fusion.57), channel_id=1, source_target_pairs={{0,32},{8,40},{16,48},{24,56},{32,0},{40,8},{48,16},{56,24},{64,96... | collective-permute-start | bytes 1572872 | tf_op jit(solution)/shard_map/ppermute | solution.py:18
  319.2 47.9 %collective-permute-start.16 = (bf16[1024,1024]{0,1:T(8,128)(2,1)}, bf16[1024,1024]{0,1:T(8,128)(2,1)}, u32[]{:S(2)}, u32[]{:S(2)}) collective-permute-start(bf16[1024,1024]{0,1:T(8,128)(2,1)} %pad_maximum_fusion.10), channel_id=1, source_target_pairs={{0,2},{1,3},{2,4},{3,5},{4,6},{5,7},{6,0},{7,1},{8,10},{9,11},{10,... | collective-permute-start | bytes 6291464 | tf_op jit(solution)/shard_map/ppermute | solution.py:48
  320.7 48.9 %collective-permute-start.15 = (bf16[1024,1024]{0,1:T(8,128)(2,1)}, bf16[1024,1024]{0,1:T(8,128)(2,1)}, u32[]{:S(2)}, u32[]{:S(2)}) collective-permute-start(bf16[1024,1024]{0,1:T(8,128)(2,1)} %pad_maximum_fusion.10), channel_id=1, source_target_pairs={{0,6},{1,7},{2,0},{3,1},{4,2},{5,3},{6,4},{7,5},{8,14},{9,15},{10,... | collective-permute-start | bytes 6291464 | tf_op jit(solution)/shard_map/ppermute | solution.py:49
  332.1 19.5 %collective-permute-start.21 = (f32[2,128,512]{2,1,0:T(8,128)S(1)}, f32[2,128,512]{2,1,0:T(8,128)S(1)}, u32[]{:S(2)}, u32[]{:S(2)}) collective-permute-start(f32[2,128,512]{2,1,0:T(8,128)S(1)} %fusion.54), channel_id=1, source_target_pairs={{0,16},{8,24},{16,0},{24,8},{32,48},{40,56},{48,32},{56,40},{64,80... | collective-permute-start | bytes 1572872 | tf_op jit(solution)/shard_map/ppermute | solution.py:18
  369.4 45.1 %collective-permute-start.17 = (bf16[1024,512]{0,1:T(8,128)(2,1)}, bf16[1024,512]{0,1:T(8,128)(2,1)}, u32[]{:S(2)}, u32[]{:S(2)}) collective-permute-start(bf16[1024,512]{0,1:T(8,128)(2,1)} %slice.167), channel_id=1, source_target_pairs={{0,2},{1,3},{2,4},{3,5},{4,6},{5,7},{6,0},{7,1},{8,10},{9,11},{10,... | collective-permute-start | bytes 3145736 | tf_op jit(solution)/shard_map/ppermute | solution.py:54
  371.8 42.6 %collective-permute-start.18 = (bf16[1024,512]{0,1:T(8,128)(2,1)}, bf16[1024,512]{0,1:T(8,128)(2,1)}, u32[]{:S(2)}, u32[]{:S(2)}) collective-permute-start(bf16[1024,512]{0,1:T(8,128)(2,1)} %slice.168), channel_id=1, source_target_pairs={{0,6},{1,7},{2,0},{3,1},{4,2},{5,3},{6,4},{7,5},{8,14},{9,15},{10,... | collective-permute-start | bytes 3145736 | tf_op jit(solution)/shard_map/ppermute | solution.py:55
  375.9 37.2 %collective-permute-start.22 = (f32[2,128,512]{2,1,0:T(8,128)}, f32[2,128,512]{2,1,0:T(8,128)}, u32[]{:S(2)}, u32[]{:S(2)}) collective-permute-start(f32[2,128,512]{2,1,0:T(8,128)} %fusion.58), channel_id=1, source_target_pairs={{0,8},{8,0},{16,24},{24,16},{32,40},{40,32},{48,56},{56,48},{64,72... | collective-permute-start | bytes 1572872 | tf_op jit(solution)/shard_map/ppermute | solution.py:18
  (46 other events, 393.3 us)
Sparse Core Ops, SparseCore 0:
  120.3 89.1 all-gather.1
  246.2 112.8 reduce-scatter.1

commit v8 on v6

--- a/solution.py
+++ b/solution.py
@@ -139,7 +139,8 @@
                 jnp.concatenate([current, received], axis=1),
             )
             current = pair_mean(joined)
-    segments = [stacked.reshape(2, blocks, BLK, features)]
+    per_block = [stacked.reshape(2, blocks, BLK, features)]
+    groups = []
     for level_idx in range(local_levels):
         factor = 2**level_idx
         group_count = blocks >> level_idx
@@ -155,18 +156,72 @@
         sibling = pooled.reshape(2, group_count // 2, 2, BLK, features)[:, :, ::-1].reshape(
             2, group_count, BLK, features
         )
-        segments.append(
-            jnp.broadcast_to(sibling[:, :, None], (2, group_count, factor, BLK, features)).reshape(
-                2, blocks, BLK, features
-            )
-        )
-    for level_idx in range(cross_levels):
-        segments.append(
-            jnp.broadcast_to(
-                siblings[level_idx].astype(jnp.bfloat16)[:, None], (2, blocks, BLK, features)
-            )
-        )
-    key_set = jnp.concatenate(segments, axis=2)
+        if factor == 1:
+            per_block.append(sibling)
+        else:
+            groups.append((sibling, factor))
+    groups.insert(0, (jnp.concatenate(per_block, axis=2), 1))
+    if cross_levels:
+        far_set = jnp.concatenate(
+            [siblings[level_idx].astype(jnp.bfloat16) for level_idx in range(cross_levels)], axis=1
+        )
+        groups.append((far_set[:, None], blocks))
+    key_groups = [
+        (
+            rows[0].reshape(rows.shape[1], rows.shape[2], head_count, DH),
+            rows[1].reshape(rows.shape[1], rows.shape[2], head_count, DH),
+            factor,
+        )
+        for rows, factor in groups
+    ]
+    widths = [rows.shape[2] for rows, _ in groups]
+    bounds = [sum(widths[:idx]) for idx in range(len(widths) + 1)]
+
+    def by_block(tensor, factor):
+        return tensor.reshape((blocks // factor, factor) + tensor.shape[1:])
+
+    def split_keys(tensor):
+        return [tensor[..., bounds[idx] : bounds[idx + 1]] for idx in range(len(widths))]
+
+    def against_keys(rows_heads, which):
+        parts = []
+        for group_keys, group_values, factor in key_groups:
+            operand = group_keys if which == 0 else group_values
+            part = jnp.einsum(
+                "gfqhd,gkhd->gfhqk",
+                by_block(rows_heads, factor),
+                operand,
+                preferred_element_type=jnp.float32,
+            )
+            parts.append(part.reshape((blocks,) + part.shape[2:]))
+        return jnp.concatenate(parts, axis=-1)
+
+    def mix_keys(weights, which):
+        total = None
+        for (group_keys, group_values, factor), piece in zip(key_groups, split_keys(weights)):
+            operand = group_keys if which == 0 else group_values
+            part = jnp.einsum(
+                "gfhqk,gkhd->gfqhd",
+                by_block(piece, factor),
+                operand,
+                preferred_element_type=jnp.float32,
+            ).reshape(blocks, BLK, head_count, DH)
+            total = part if total is None else total + part
+        return total
+
+    def key_grads(weights, rows_heads):
+        out = []
+        for (_, _, factor), piece in zip(key_groups, split_keys(weights)):
+            out.append(
+                jnp.einsum(
+                    "gfhqk,gfqhd->gkhd",
+                    by_block(piece, factor),
+                    by_block(rows_heads, factor),
+                    preferred_element_type=jnp.float32,
+                )
+            )
+        return out
+
     key_bias = jnp.concatenate(
         [jnp.zeros((BLK,), jnp.float32)]
         + [jnp.full((BLK,), level_idx * LOG_TWO, jnp.float32) for level_idx in range(level_count)]
@@ -182,19 +237,13 @@
         axis=1,
     )
     query_heads = queries.reshape(blocks, BLK, head_count, DH)
-    key_heads = key_set[0].reshape(blocks, keys_all, head_count, DH)
-    value_heads = key_set[1].reshape(blocks, keys_all, head_count, DH)
-    scores = (
-        jnp.einsum("bqhd,bkhd->bhqk", query_heads, key_heads, preferred_element_type=jnp.float32)
-        * score_scale
-        + key_bias
-    )
+    scores = against_keys(query_heads, 0) * score_scale + key_bias
     scores = jnp.where(kept_mask[:, None, None, :], scores, -jnp.inf)
     row_max = jnp.max(scores, axis=-1, keepdims=True)
     weights_raw = jnp.exp(scores - row_max)
     attn_prob = weights_raw / jnp.sum(weights_raw, axis=-1, keepdims=True)
     prob_low = attn_prob.astype(jnp.bfloat16)
-    mixed = jnp.einsum("bhqk,bkhd->bqhd", prob_low, value_heads, preferred_element_type=jnp.float32)
+    mixed = mix_keys(prob_low, 1)
     attended = mixed.astype(jnp.bfloat16).reshape(row_count, features)
     attended, weight_cols = lax.optimization_barrier((attended, weight_columns(out_weight)))
     half_rows = row_count // 2
@@ -219,46 +268,38 @@
         tiled=True,
     )
     grad_heads = grad_attn.reshape(blocks, BLK, head_count, DH)
-    grad_prob = jnp.einsum(
-        "bqhd,bkhd->bhqk", grad_heads, value_heads, preferred_element_type=jnp.float32
-    )
+    grad_prob = against_keys(grad_heads, 1)
     row_delta = jnp.sum(attn_prob * grad_prob, axis=-1, keepdims=True)
     grad_score = (attn_prob * (grad_prob - row_delta)).astype(jnp.bfloat16)
     grad_query = (
-        (
-            jnp.einsum("bhqk,bkhd->bqhd", grad_score, key_heads, preferred_element_type=jnp.float32)
-            * score_scale
-        )
-        .astype(jnp.bfloat16)
-        .reshape(row_count, features)
-    )
-    grad_keyset = (
-        jnp.einsum("bhqk,bqhd->bkhd", grad_score, query_heads, preferred_element_type=jnp.float32)
-        * score_scale
-    )
-    grad_valset = jnp.einsum(
-        "bhqk,bqhd->bkhd", prob_low, grad_heads, preferred_element_type=jnp.float32
-    )
-    grad_sets = jnp.stack([grad_keyset, grad_valset]).reshape(2, blocks, keys_all, features)
-    token_grad = grad_sets[:, :, :BLK].reshape(2, row_count, features)
+        (mix_keys(grad_score, 0) * score_scale).astype(jnp.bfloat16).reshape(row_count, features)
+    )
+    grad_groups = [
+        jnp.stack([keys_part * score_scale, values_part]).reshape(
+            (2,) + keys_part.shape[:2] + (features,)
+        )
+        for keys_part, values_part in zip(
+            key_grads(grad_score, query_heads), key_grads(prob_low, grad_heads)
+        )
+    ]
+    near = grad_groups[0]
+    token_grad = near[:, :, :BLK].reshape(2, row_count, features)
     level_grads = []
     for level_idx in range(local_levels):
-        factor = 2**level_idx
         group_count = blocks >> level_idx
-        lower = (level_idx + 1) * BLK
-        segment = (
-            grad_sets[:, :, lower : lower + BLK]
-            .reshape(2, group_count, factor, BLK, features)
-            .sum(axis=2)
-        )
+        if level_idx == 0:
+            segment = near[:, :, BLK : 2 * BLK]
+        else:
+            segment = grad_groups[level_idx][:, :, :BLK]
         restored = segment.reshape(2, group_count // 2, 2, BLK, features)[:, :, ::-1].reshape(
             2, group_count * BLK, features
         )
         level_grads.append(restored)
     sibling_grads = []
-    for level_idx in range(cross_levels):
-        lower = (local_levels + 1 + level_idx) * BLK
-        sibling_grads.append(jnp.sum(grad_sets[:, :, lower : lower + BLK], axis=1))
+    if cross_levels:
+        far_grads = grad_groups[-1][:, 0]
+        for level_idx in range(cross_levels):
+            sibling_grads.append(far_grads[:, level_idx * BLK : (level_idx + 1) * BLK])
     carried = jnp.zeros((2, BLK, features), jnp.float32)
     for level_idx in reversed(range(cross_levels)):
         outgoing = sibling_grads[level_idx]

time: 499 us -> 531 us (1.064)
  local copies, waits for them, and re-layouts: 172 us -> 212 us
  matrix products: 103 us -> 83 us
  other arithmetic: 107 us -> 125 us
  waiting for transfers between devices: 51.8 us -> 43.2 us
    sub x0 -> x2, other arithmetic: none -> 37.2 us  [the longest x1 28.8 us: body(): grad_score = (attn_prob * (grad_prob - row_delta)).astype(jnp.bfloat16)]
    reshape x4 -> x13, local copies, waits for them, and re-layouts: 5.62 us -> 39.5 us  [the longest x8 30.2 us: mix_keys(): part = jnp.einsum('gfhqk,gkhd->gfqhd', by_block(piece, factor), operand,...]
    reduce_sum x3 -> x0, other arithmetic: 26 us -> none  [the longest x1 19.8 us: body(): sibling_grads.append(jnp.sum(grad_sets[:, :, lower:lower + BLK], axis=1))]
    another operation x2 -> x20, local copies, waits for them, and re-layouts: 4.92 us -> 28.8 us  [the longest x8 11 us: by_block(): return tensor.reshape((blocks // factor, factor) + tensor.shape[1:])]
    transpose x0 -> x8, local copies, waits for them, and re-layouts: none -> 17.1 us  [the longest x4 10.3 us: mix_keys(): jnp.einsum('gfhqk,gkhd->gfqhd', by_block(piece, factor), operand, preferr...]
    mul x1 -> x0, local copies, waits for them, and re-layouts: 16.5 us -> none  [body(): jnp.einsum('bhqk,bqhd->bkhd', grad_score, query_heads, preferred_element_...]
    sub x1 -> x0, matrix products: 12.8 us -> none  [body(): weights_raw = jnp.exp(scores - row_max)]
    ppermute x8, waiting for transfers between devices: 35.1 us -> 25.2 us  [swapped(): return lax.ppermute(value, axis, pairs)]
  transfers between devices with their start and end apart: 25 -> 25, of which waited for: 7 -> 5; matrix products, arithmetic and copies ran while one was open for 71% -> 68% of each run, Pallas kernels for 0% -> 0%
where the time goes in v8:
time: 531 us; the launch traced here: 522 us
  local copies, waits for them, and re-layouts  212 us (40%)
  other arithmetic  125 us (24%)
  matrix products  83 us (16%)
  starting transfers between devices  43.5 us (8%)
  waiting for transfers between devices  43.2 us (8%)
  between operations  15.2 us (3%)
    reshape x8, local copies, waits for them, and re-layouts, mix_keys(): part = jnp.einsum('gfhqk,gkhd->gfqhd', by_block(piece, factor), operand,...  30.2 us
    sub x1, other arithmetic, body(): grad_score = (attn_prob * (grad_prob - row_delta)).astype(jnp.bfloat16)  28.8 us
    unnamed x133, local copies, waits for them, and re-layouts  28.2 us
    ppermute x8, waiting for transfers between devices, swapped(): return lax.ppermute(value, axis, pairs)  25.2 us
    dot_general x8, matrix products, against_keys(): jnp.einsum('gfqhd,gkhd->gfhqk', by_block(rows_heads, factor), operand, pr...  22.4 us
    dot_general x8, matrix products, key_grads(): jnp.einsum('gfhqk,gfqhd->gkhd', by_block(piece, factor), by_block(rows_he...  22.2 us
    ppermute x8, starting transfers between devices, swapped(): return lax.ppermute(value, axis, pairs)  15.5 us
    slice x9, local copies, waits for them, and re-layouts, body(): rows[1].reshape(rows.shape[1], rows.shape[2], head_count, DH)  14.9 us
  transfers between devices with their start and end apart: 25, of which 5 were waited for; matrix products, arithmetic and copies ran while one was open for 68% of the time, Pallas kernels for 0%

profile of v8, /device:TPU:0, one launch (start us, length us, event | category | flops | bytes accessed | tf_op | source)
XLA Modules:
  0.0 522.1 jit_solution(14304161914479463246)
XLA Ops:
  18.4 4.9 collective-permute-start.7
  35.1 7.8 %convert_reduce_fusion.2 = f32[2,512,512]{2,1,0:T(8,128)S(1)} fusion(bf16[1,512,2,512]{3,2,1,0:T(2,128)(2,1)} %stack.106, bf16[1,512,2,512]{3,2,1,0:T(2,128)(2,1)} %stack.105), kind=kLoop, calls=%fused_computation.26 | loop fusion | flops 2621440 | bytes 4194304 | tf_op jit(solution)/shard_map/reduce_sum | solution.py:153
  50.1 4.5 convert_reduce_fusion.1
  147.9 5.5 %collective-permute-start.8 = (bf16[4,512,512]{1,2,0:T(8,128)(2,1)}, bf16[4,512,512]{1,2,0:T(8,128)(2,1)}, u32[]{:S(2)}, u32[]{:S(2)}) collective-permute-start(bf16[4,512,512]{1,2,0:T(8,128)(2,1)} %pad_maximum_fusion.9), channel_id=1, source_target_pairs={{0,8},{8,0},{16,24},{24,16},{32,40},{40,32},{48,56},{56,48},{64,72... | collective-permute-start | bytes 6291464 | tf_op jit(solution)/shard_map/ppermute | solution.py:92
  168.4 8.4 %fusion.92 = (f32[8,4,128]{2,0,1:T(8,128)S(1)}, f32[8,4,128,1024]{2,3,0,1:T(8,128)S(1)}) fusion(f32[8,4,128,512]{2,3,0,1:T(8,128)S(1)} %convolution_bitcast_fusion.1, f32[8,4,128,128]{2,3,0,1:T(8,128)} %copy.271, f32[8,4,128,128]{2,3,0,1:T(8,128)} %copy.270, f32[1024]{0:T(1024)S(1)} %copy-done.60, pred[8,1024]{1,0:T(8,128)(4,1)S(1)} %concatenate.82, ...), kind=kOutput, calls=%fused_computation.180 | output fusion | flops 33555456 | bytes 33583104 | tf_op jit(solution)/shard_map/sub | solution.py:243
  207.7 4.6 copy.395
  216.2 5.4 %fusion.25 = bf16[1024,512]{0,1:T(8,128)(2,1)} fusion(f32[64,8,8,128]{3,2,1,0:T(8,128)} %bitcast.343, f32[1024,512]{0,1:T(8,128)} %reshape.434, f32[1024,512]{0,1:T(8,128)} %reshape.433, f32[64,8,8,128]{3,2,1,0:T(8,128)} %bitcast.344), kind=kLoop, calls=%fused_computation.53 | loop fusion | flops 2097152 | bytes 9437184 | tf_op jit(solution)/shard_map/convert_element_type | solution.py:247
  226.7 5.0 gather_fusion
  231.8 6.2 %copy.291 = bf16[512,4,1024]{0,2,1:T(8,128)(2,1)} copy(bf16[512,4,1024]{2,0,1:T(8,128)(2,1)} %bitcast.325) | data formatting | bytes 8388608 | tf_op jit(solution)/shard_map/transpose | solution.py:65
  243.8 9.2 %fusion.48 = bf16[1024,512]{1,0:T(8,128)(2,1)S(1)} fusion(bf16[512,4096]{1,0:T(8,128)(2,1)} %param.9, bf16[512,4096]{0,1:T(8,128)(2,1)} %bitcast.351, bf16[512,4096]{0,1:T(8,128)(2,1)} %all-gather.2.cloned.1.call-done), kind=kOutput, calls=%fused_computation.87 | convolution fusion | flops 4312268800 | bytes 13631488 | tf_op jit(solution)/shard_map/dot_general | solution.py:257
  270.8 4.7 fusion.16
  278.2 5.5 %convolution_bitcast_fusion = f32[8,4,128,512]{2,3,0,1:T(8,128)} fusion(bf16[512,4,128,1]{0,2,3,1:T(8,128)(2,1)S(1)} %bitcast.338, bf16[8,128,4,128]{1,3,0,2:T(8,128)(2,1)S(1)} %copy.305), kind=kOutput, calls=%fused_computation.35 | convolution fusion | flops 536870912 | bytes 9961472 | tf_op jit(solution)/shard_map/gfqhd,gkhd->gfhqk/dot_general | solution.py:190
  284.5 8.3 %fusion.7 = f32[4096,512]{1,0:T(8,128)} fusion(bf16[1024,512]{0,1:T(8,128)(2,1)} %fusion.25, bf16[512,4096]{0,1:T(8,128)(2,1)S(1)} %bitcast.352, bf16[512,4096]{0,1:T(8,128)(2,1)S(1)} %copy-done.59), kind=kOutput, calls=%fused_computation.15 | convolution fusion | flops 4311744512 | bytes 17825792 | tf_op jit(solution)/shard_map/dot_general | solution.py:263
  303.0 28.8 %multiply_convert_fusion = bf16[8,4,128,1024]{2,3,0,1:T(8,128)(2,1)} fusion(f32[8,4,128,512]{2,3,0,1:T(8,128)} %convolution_bitcast_fusion, f32[8,4,128,128]{2,3,0,1:T(8,128)} %bitcast.363, f32[8,4,128,128]{2,3,0,1:T(8,128)} %bitcast.362, f32[8,4,128,256]{2,3,0,1:T(8,128)} %convolution_bitcast_fusion.2, f32[8,4,128,1024]{2,3,0,1:T(8,128)} %copy-done.4, ...), kind=kOutput, calls=%fused_computation.7 | output fusion | flops 50336768 | bytes 41959424 | tf_op jit(solution)/shard_map/sub | solution.py:273
  373.3 6.4 %collective-permute-done.20 = f32[2,128,512]{2,1,0:T(8,128)S(1)} collective-permute-done((f32[2,128,512]{2,1,0:T(8,128)S(1)}, f32[2,128,512]{2,1,0:T(8,128)S(1)}, u32[]{:S(2)}, u32[]{:S(2)}) %collective-permute-start.20) | collective-permute-done | bytes 524320 | tf_op jit(solution)/shard_map/ppermute | solution.py:18
  386.3 14.7 %collective-permute-done.21 = f32[2,128,512]{2,1,0:T(8,128)S(1)} collective-permute-done((f32[2,128,512]{2,1,0:T(8,128)S(1)}, f32[2,128,512]{2,1,0:T(8,128)S(1)}, u32[]{:S(2)}, u32[]{:S(2)}) %collective-permute-start.21) | collective-permute-done | bytes 524320 | tf_op jit(solution)/shard_map/ppermute | solution.py:18
  402.2 14.3 %collective-permute-done.16 = bf16[1024,1024]{0,1:T(8,128)(2,1)S(1)} collective-permute-done((bf16[1024,1024]{0,1:T(8,128)(2,1)S(1)}, bf16[1024,1024]{0,1:T(8,128)(2,1)S(1)}, u32[]{:S(2)}, u32[]{:S(2)}) %collective-permute-start.16) | collective-permute-done | bytes 2097184 | tf_op jit(solution)/shard_map/ppermute | solution.py:48
  431.2 5.8 %copy.334 = f32[2,8,128,512]{3,2,1,0:T(8,128)} copy(f32[2,8,128,512]{2,3,1,0:T(8,128)} %get-tuple-element.44) | data formatting | bytes 8388608 | tf_op jit(solution)/shard_map/slice | solution.py:286
  437.0 5.3 %copy.335 = f32[2,4,2,128,512]{4,3,2,1,0:T(8,128)} copy(f32[2,4,2,128,512]{3,4,2,1,0:T(8,128)} %bitcast.328) | data formatting | bytes 8388608 | tf_op jit(solution)/shard_map/reshape | solution.py:294
  442.4 4.8 rev.15
  447.2 4.7 copy.410
  463.1 6.0 %fusion.23 = bf16[1024,512]{0,1:T(8,128)(2,1)} fusion(f32[64,8,8,128]{3,2,1,0:T(8,128)} %bitcast.342, f32[1024,512]{0,1:T(8,128)} %reshape.436, f32[1024,512]{0,1:T(8,128)} %reshape.435, f32[64,8,8,128]{3,2,1,0:T(8,128)} %bitcast.341), kind=kLoop, calls=%fused_computation.49 | loop fusion | flops 2621440 | bytes 9437184 | tf_op jit(solution)/shard_map/convert_element_type | solution.py:275
  492.5 6.1 %reshape.406 = f32[2,1024,512]{2,1,0:T(8,128)} reshape(f32[2,512,2,512]{3,2,1,0:T(2,128)} %broadcast_in_dim.34) | data formatting | bytes 8388608 | tf_op jit(solution)/shard_map/reshape | solution.py:32
  498.6 5.9 %fusion.11 = bf16[2,1024,512]{2,1,0:T(8,128)(2,1)S(1)} fusion(f32[2,1024,512]{2,1,0:T(8,128)} %reshape.406, f32[2,4,2,128,512]{4,3,2,1,0:T(8,128)} %rev.15, f32[2,8,128,512]{3,2,1,0:T(8,128)} %copy.334), kind=kLoop, calls=%fused_computation.23 | loop fusion | flops 3145728 | bytes 14680064 | tf_op jit(solution)/shard_map/convert.1
  (341 shorter events, 324.2 us)
Async XLA Ops:
  7.2 236.6 %all-gather.2.cloned.1.call-start = ((), (), s32[]{:S(2)}) async-start(), calls=%async_computation.1 | async-start | bytes 4718592 | tf_op jit(solution)/shard_map/all_gather | solution.py:252
  9.1 85.6 %collective-permute-start.9 = (bf16[512,512]{1,0:T(8,128)(2,1)}, bf16[512,512]{1,0:T(8,128)(2,1)}, u32[]{:S(2)}, u32[]{:S(2)}) collective-permute-start(bf16[512,512]{1,0:T(8,128)(2,1)} %slice.197), channel_id=1, source_target_pairs={{0,1},{1,0},{2,3},{3,2},{4,5},{5,4},{6,7},{7,6},{8,9},{9,8},{10,11... | collective-permute-start | bytes 1572872 | tf_op jit(solution)/shard_map/ppermute | solution.py:41
  14.5 56.5 %collective-permute-start = (f32[2,128,512]{2,1,0:T(8,128)}, f32[2,128,512]{2,1,0:T(8,128)}, u32[]{:S(2)}, u32[]{:S(2)}) collective-permute-start(f32[2,128,512]{2,1,0:T(8,128)} %broadcast_multiply_fusion.2), channel_id=1, source_target_pairs={{0,8},{8,0},{16,24},{24,16},{32,40},{40,32},{48,56},{56,48},{64,72... | collective-permute-start | bytes 1572872 | tf_op jit(solution)/shard_map/ppermute | solution.py:18
  18.4 111.7 %collective-permute-start.7 = (bf16[512,512]{0,1:T(8,128)(2,1)}, bf16[512,512]{0,1:T(8,128)(2,1)}, u32[]{:S(2)}, u32[]{:S(2)}) collective-permute-start(bf16[512,512]{0,1:T(8,128)(2,1)} %copy.429), channel_id=1, source_target_pairs={{0,7},{1,0},{2,1},{3,2},{4,3},{5,4},{6,5},{7,6},{16,23},{17,16},{1... | collective-permute-start | bytes 1572872 | tf_op jit(solution)/shard_map/ppermute | solution.py:90
  24.3 110.8 %collective-permute-start.4 = (bf16[512,512]{0,1:T(8,128)(2,1)}, bf16[512,512]{0,1:T(8,128)(2,1)}, u32[]{:S(2)}, u32[]{:S(2)}) collective-permute-start(bf16[512,512]{0,1:T(8,128)(2,1)} %copy.426), channel_id=1, source_target_pairs={{0,1},{1,2},{2,3},{3,4},{4,5},{5,6},{6,7},{7,0},{8,10},{9,11},{10,... | collective-permute-start | bytes 1572872 | tf_op jit(solution)/shard_map/ppermute | solution.py:90
  74.9 14.0 %collective-permute-start.1 = (f32[2,128,512]{2,1,0:T(8,128)}, f32[2,128,512]{2,1,0:T(8,128)}, u32[]{:S(2)}, u32[]{:S(2)}) collective-permute-start(f32[2,128,512]{2,1,0:T(8,128)} %copy_multiply_fusion.2), channel_id=1, source_target_pairs={{0,16},{8,24},{16,0},{24,8},{32,48},{40,56},{48,32},{56,40},{64,80... | collective-permute-start | bytes 1572872 | tf_op jit(solution)/shard_map/ppermute | solution.py:18
  92.8 34.0 %collective-permute-start.2 = (f32[2,128,512]{2,1,0:T(8,128)}, f32[2,128,512]{2,1,0:T(8,128)}, u32[]{:S(2)}, u32[]{:S(2)}) collective-permute-start(f32[2,128,512]{2,1,0:T(8,128)} %copy_multiply_fusion.1), channel_id=1, source_target_pairs={{0,32},{8,40},{16,48},{24,56},{32,0},{40,8},{48,16},{56,24},{64,96... | collective-permute-start | bytes 1572872 | tf_op jit(solution)/shard_map/ppermute | solution.py:18
  98.3 57.2 %collective-permute-start.10 = (bf16[512,1024]{1,0:T(8,128)(2,1)}, bf16[512,1024]{1,0:T(8,128)(2,1)S(1)}, u32[]{:S(2)}, u32[]{:S(2)}) collective-permute-start(bf16[512,1024]{1,0:T(8,128)(2,1)} %get-tuple-element.80), channel_id=1, source_target_pairs={{0,6},{1,7},{2,0},{3,1},{4,2},{5,3},{6,4},{7,5},{8,14},{9,15},{10,... | collective-permute-start | bytes 3145736 | tf_op jit(solution)/shard_map/ppermute | solution.py:49
  100.0 59.0 %collective-permute-start.11 = (bf16[512,1024]{1,0:T(8,128)(2,1)}, bf16[512,1024]{1,0:T(8,128)(2,1)}, u32[]{:S(2)}, u32[]{:S(2)}) collective-permute-start(bf16[512,1024]{1,0:T(8,128)(2,1)} %get-tuple-element.80), channel_id=1, source_target_pairs={{0,2},{1,3},{2,4},{3,5},{4,6},{5,7},{6,0},{7,1},{8,10},{9,11},{10,... | collective-permute-start | bytes 3145736 | tf_op jit(solution)/shard_map/ppermute | solution.py:48
  126.8 14.4 %collective-permute-start.5 = (bf16[512,512]{0,1:T(8,128)(2,1)}, bf16[512,512]{0,1:T(8,128)(2,1)}, u32[]{:S(2)}, u32[]{:S(2)}) collective-permute-start(bf16[512,512]{0,1:T(8,128)(2,1)} %copy.427), channel_id=1, source_target_pairs={{0,3},{1,4},{2,5},{3,6},{4,7},{5,0},{6,1},{7,2},{8,12},{9,13},{10,... | collective-permute-start | bytes 1572872 | tf_op jit(solution)/shard_map/ppermute | solution.py:90
  130.2 14.6 %collective-permute-start.6 = (bf16[512,512]{0,1:T(8,128)(2,1)}, bf16[512,512]{0,1:T(8,128)(2,1)}, u32[]{:S(2)}, u32[]{:S(2)}) collective-permute-start(bf16[512,512]{0,1:T(8,128)(2,1)} %copy.428), channel_id=1, source_target_pairs={{0,5},{1,6},{2,7},{3,0},{4,1},{5,2},{6,3},{7,4},{8,14},{9,15},{10,... | collective-permute-start | bytes 1572872 | tf_op jit(solution)/shard_map/ppermute | solution.py:90
  135.1 27.1 %collective-permute-start.3 = (bf16[2,128,512]{2,1,0:T(8,128)(2,1)}, bf16[2,128,512]{2,1,0:T(8,128)(2,1)}, u32[]{:S(2)}, u32[]{:S(2)}) collective-permute-start(bf16[2,128,512]{2,1,0:T(8,128)(2,1)} %copy_multiply_fusion), channel_id=1, source_target_pairs={{0,64},{8,72},{16,80},{24,88},{32,96},{40,104},{48,112},{56,120},{... | collective-permute-start | bytes 786440 | tf_op jit(solution)/shard_map/ppermute | solution.py:18
  141.1 373.9 %reduce-scatter.2.cloned.1.call-start = ((), (), s32[]{:S(2)}) async-start(), calls=%async_computation.2 | async-start | bytes 8912896 | tf_op jit(solution)/shard_map/reduce_scatter | solution.py:262
  147.9 90.1 %collective-permute-start.8 = (bf16[4,512,512]{1,2,0:T(8,128)(2,1)}, bf16[4,512,512]{1,2,0:T(8,128)(2,1)}, u32[]{:S(2)}, u32[]{:S(2)}) collective-permute-start(bf16[4,512,512]{1,2,0:T(8,128)(2,1)} %pad_maximum_fusion.9), channel_id=1, source_target_pairs={{0,8},{8,0},{16,24},{24,16},{32,40},{40,32},{48,56},{56,48},{64,72... | collective-permute-start | bytes 6291464 | tf_op jit(solution)/shard_map/ppermute | solution.py:92
  156.4 65.2 %collective-permute-start.13 = (bf16[512,512]{1,0:T(8,128)(2,1)}, bf16[512,512]{1,0:T(8,128)(2,1)}, u32[]{:S(2)}, u32[]{:S(2)}) collective-permute-start(bf16[512,512]{1,0:T(8,128)(2,1)} %slice.242), channel_id=1, source_target_pairs={{0,6},{1,7},{2,0},{3,1},{4,2},{5,3},{6,4},{7,5},{8,14},{9,15},{10,... | collective-permute-start | bytes 1572872 | tf_op jit(solution)/shard_map/ppermute | solution.py:55
  160.9 60.7 %collective-permute-start.12 = (bf16[512,512]{1,0:T(8,128)(2,1)}, bf16[512,512]{1,0:T(8,128)(2,1)}, u32[]{:S(2)}, u32[]{:S(2)}) collective-permute-start(bf16[512,512]{1,0:T(8,128)(2,1)} %slice.241), channel_id=1, source_target_pairs={{0,2},{1,3},{2,4},{3,5},{4,6},{5,7},{6,0},{7,1},{8,10},{9,11},{10,... | collective-permute-start | bytes 1572872 | tf_op jit(solution)/shard_map/ppermute | solution.py:54
  303.0 63.3 %collective-permute-start.14 = (bf16[1024,512]{0,1:T(8,128)(2,1)}, bf16[1024,512]{0,1:T(8,128)(2,1)}, u32[]{:S(2)}, u32[]{:S(2)}) collective-permute-start(bf16[1024,512]{0,1:T(8,128)(2,1)} %fusion.25), channel_id=1, source_target_pairs={{0,1},{1,0},{2,3},{3,2},{4,5},{5,4},{6,7},{7,6},{8,9},{9,8},{10,11... | collective-permute-start | bytes 3145736 | tf_op jit(solution)/shard_map/ppermute | solution.py:41
  336.7 27.1 %collective-permute-start.19 = (f32[2,128,512]{2,1,0:T(8,128)}, f32[2,128,512]{2,1,0:T(8,128)}, u32[]{:S(2)}, u32[]{:S(2)}) collective-permute-start(f32[2,128,512]{2,1,0:T(8,128)} %fusion.70), channel_id=1, source_target_pairs={{0,64},{8,72},{16,80},{24,88},{32,96},{40,104},{48,112},{56,120},{... | collective-permute-start | bytes 1572872 | tf_op jit(solution)/shard_map/ppermute | solution.py:18
  368.2 48.4 %collective-permute-start.16 = (bf16[1024,1024]{0,1:T(8,128)(2,1)S(1)}, bf16[1024,1024]{0,1:T(8,128)(2,1)S(1)}, u32[]{:S(2)}, u32[]{:S(2)}) collective-permute-start(bf16[1024,1024]{0,1:T(8,128)(2,1)S(1)} %pad_maximum_fusion.10), channel_id=1, source_target_pairs={{0,2},{1,3},{2,4},{3,5},{4,6},{5,7},{6,0},{7,1},{8,10},{9,11},{10,... | collective-permute-start | bytes 6291464 | tf_op jit(solution)/shard_map/ppermute | solution.py:48
  370.3 47.8 %collective-permute-start.15 = (bf16[1024,1024]{0,1:T(8,128)(2,1)S(1)}, bf16[1024,1024]{0,1:T(8,128)(2,1)S(1)}, u32[]{:S(2)}, u32[]{:S(2)}) collective-permute-start(bf16[1024,1024]{0,1:T(8,128)(2,1)S(1)} %pad_maximum_fusion.10), channel_id=1, source_target_pairs={{0,6},{1,7},{2,0},{3,1},{4,2},{5,3},{6,4},{7,5},{8,14},{9,15},{10,... | collective-permute-start | bytes 6291464 | tf_op jit(solution)/shard_map/ppermute | solution.py:49
  381.2 19.7 %collective-permute-start.21 = (f32[2,128,512]{2,1,0:T(8,128)S(1)}, f32[2,128,512]{2,1,0:T(8,128)S(1)}, u32[]{:S(2)}, u32[]{:S(2)}) collective-permute-start(f32[2,128,512]{2,1,0:T(8,128)S(1)} %fusion.69), channel_id=1, source_target_pairs={{0,16},{8,24},{16,0},{24,8},{32,48},{40,56},{48,32},{56,40},{64,80... | collective-permute-start | bytes 1572872 | tf_op jit(solution)/shard_map/ppermute | solution.py:18
  417.7 54.9 %collective-permute-start.17 = (bf16[1024,512]{0,1:T(8,128)(2,1)}, bf16[1024,512]{0,1:T(8,128)(2,1)}, u32[]{:S(2)}, u32[]{:S(2)}) collective-permute-start(bf16[1024,512]{0,1:T(8,128)(2,1)} %slice.243), channel_id=1, source_target_pairs={{0,2},{1,3},{2,4},{3,5},{4,6},{5,7},{6,0},{7,1},{8,10},{9,11},{10,... | collective-permute-start | bytes 3145736 | tf_op jit(solution)/shard_map/ppermute | solution.py:54
  419.3 53.3 %collective-permute-start.18 = (bf16[1024,512]{0,1:T(8,128)(2,1)}, bf16[1024,512]{0,1:T(8,128)(2,1)}, u32[]{:S(2)}, u32[]{:S(2)}) collective-permute-start(bf16[1024,512]{0,1:T(8,128)(2,1)} %slice.244), channel_id=1, source_target_pairs={{0,6},{1,7},{2,0},{3,1},{4,2},{5,3},{6,4},{7,5},{8,14},{9,15},{10,... | collective-permute-start | bytes 3145736 | tf_op jit(solution)/shard_map/ppermute | solution.py:55
  423.1 48.2 %collective-permute-start.22 = (f32[2,128,512]{2,1,0:T(8,128)}, f32[2,128,512]{2,1,0:T(8,128)}, u32[]{:S(2)}, u32[]{:S(2)}) collective-permute-start(f32[2,128,512]{2,1,0:T(8,128)} %fusion.73), channel_id=1, source_target_pairs={{0,8},{8,0},{16,24},{24,16},{32,40},{40,32},{48,56},{56,48},{64,72... | collective-permute-start | bytes 1572872 | tf_op jit(solution)/shard_map/ppermute | solution.py:18
  (64 other events, 312.7 us)
Sparse Core Ops, SparseCore 0:
  141.3 89.1 all-gather.1
  293.0 113.5 reduce-scatter.1

commit v9 on v7

--- a/solution.py
+++ b/solution.py
@@ -316,10 +316,12 @@
             attended_blocks[dist], weight_cols[dist], preferred_element_type=jnp.float32
         )
     output = output_sum.astype(jnp.bfloat16)
-    pooled_grad = carried
-    for level_idx in reversed(range(local_levels)):
-        pooled_grad = level_grads[level_idx] + spread_rows(pooled_grad, 2)
-    token_grad = token_grad + pooled_grad
+    if local_levels:
+        pooled_grad = level_grads[-1]
+        for level_idx in reversed(range(local_levels - 1)):
+            pooled_grad = level_grads[level_idx] + spread_rows(pooled_grad, 2)
+        token_grad = token_grad + pooled_grad
+    token_grad = token_grad + spread_rows(carried, 2**local_levels)
     grad_keys = token_grad[0].astype(jnp.bfloat16)
     grad_values = token_grad[1].astype(jnp.bfloat16)
     return (output, grad_query, grad_keys, grad_values, grad_weight)

time: 473 us -> 458 us (0.968)
  local copies, waits for them, and re-layouts: 137 us -> 127 us
    another operation x2 -> x0, local copies, waits for them, and re-layouts: 4.79 us -> none
    reshape x3 -> x2, local copies, waits for them, and re-layouts: 12.9 us -> 10.1 us  [spread_rows(): return wide.reshape(shape_in[:-2] + (shape_in[-2] * factor, shape_in[-1]))]
    unnamed x99 -> x91, local copies, waits for them, and re-layouts: 24.8 us -> 22.8 us
  transfers between devices with their start and end apart: 25 -> 25, of which waited for: 6 -> 7; matrix products, arithmetic and copies ran while one was open for 62% -> 60% of each run, Pallas kernels for 0% -> 0%
where the time goes in v9:
time: 458 us; the launch traced here: 453 us
  local copies, waits for them, and re-layouts  127 us (28%)
  other arithmetic  119 us (26%)
  matrix products  73.7 us (16%)
  waiting for transfers between devices  66.5 us (15%)
  starting transfers between devices  51.9 us (11%)
  between operations  15.2 us (3%)
    ppermute x8, waiting for transfers between devices, swapped(): return lax.ppermute(value, axis, pairs)  32.6 us
    sub x1, other arithmetic, body(): grad_score = (attn_prob * (grad_prob - row_delta)).astype(jnp.bfloat16)  29.8 us
    unnamed x91, local copies, waits for them, and re-layouts  22.8 us
    ppermute x2, waiting for transfers between devices, head_ring_gather(): from_below = lax.ppermute(pair_block, 'head', upward)  18.5 us
    ppermute x8, starting transfers between devices, swapped(): return lax.ppermute(value, axis, pairs)  16.5 us
    ppermute x1, starting transfers between devices, weight_columns(): lax.ppermute(mine, 'seq', [(src, src ^ 1) for src in range(seq_count)])  13.2 us
    reduce_sum x2, other arithmetic, body(): pooled = stacked.reshape(2, row_count // factor, factor, features).astype...  12.1 us
    all_gather x1, waiting for transfers between devices, body(): lax.all_gather(cotangent[:half_rows], 'head', axis=1, tiled=True)  10.9 us
  transfers between devices with their start and end apart: 25, of which 7 were waited for; matrix products, arithmetic and copies ran while one was open for 60% of the time, Pallas kernels for 0%

profile of v9, /device:TPU:0, one launch (start us, length us, event | category | flops | bytes accessed | tf_op | source)
XLA Modules:
  0.0 453.2 jit_solution(16630629014670095088)
XLA Ops:
  18.4 4.9 %collective-permute-start.7 = (bf16[512,512]{0,1:T(8,128)(2,1)}, bf16[512,512]{0,1:T(8,128)(2,1)}, u32[]{:S(2)}, u32[]{:S(2)}) collective-permute-start(bf16[512,512]{0,1:T(8,128)(2,1)} %copy.282), channel_id=1, source_target_pairs={{0,7},{1,0},{2,1},{3,2},{4,3},{5,4},{6,5},{7,6},{16,23},{17,16},{1... | collective-permute-start | bytes 1572872 | tf_op jit(solution)/shard_map/ppermute | solution.py:90
  32.1 7.6 %convert_reduce_fusion.2 = f32[2,512,512]{2,1,0:T(8,128)S(1)} fusion(bf16[1,512,2,512]{3,2,1,0:T(2,128)(2,1)} %stack.88, bf16[1,512,2,512]{3,2,1,0:T(2,128)(2,1)} %stack.87), kind=kLoop, calls=%fused_computation.41 | loop fusion | flops 2621440 | bytes 4194304 | tf_op jit(solution)/shard_map/reduce_sum | solution.py:152
  60.5 6.9 %copy.204 = bf16[1,8,512,512]{2,3,1,0:T(8,128)(2,1)} copy(bf16[1,8,512,512]{3,2,1,0:T(8,128)(2,1)} %get-tuple-element.54) | data formatting | bytes 8388608 | tf_op jit(solution)/shard_map/slice | solution.py:184
  78.4 6.1 %collective-permute-done.1 = f32[2,128,512]{2,1,0:T(8,128)S(1)} collective-permute-done((f32[2,128,512]{2,1,0:T(8,128)S(1)}, f32[2,128,512]{2,1,0:T(8,128)S(1)}, u32[]{:S(2)}, u32[]{:S(2)}) %collective-permute-start.1) | collective-permute-done | bytes 524320 | tf_op jit(solution)/shard_map/ppermute | solution.py:18
  94.3 6.5 %copy.202 = bf16[1,8,512,512]{2,3,1,0:T(8,128)(2,1)} copy(bf16[1,8,512,512]{3,2,1,0:T(8,128)(2,1)} %get-tuple-element.53) | data formatting | bytes 8388608 | tf_op jit(solution)/shard_map/slice | solution.py:185
  128.1 13.2 %collective-permute-start.8 = (bf16[4,512,512]{1,2,0:T(8,128)(2,1)}, bf16[4,512,512]{1,2,0:T(8,128)(2,1)}, u32[]{:S(2)}, u32[]{:S(2)}) collective-permute-start(bf16[4,512,512]{1,2,0:T(8,128)(2,1)} %pad_maximum_fusion.9), channel_id=1, source_target_pairs={{0,8},{8,0},{16,24},{24,16},{32,40},{40,32},{48,56},{56,48},{64,72... | collective-permute-start | bytes 6291464 | tf_op jit(solution)/shard_map/ppermute | solution.py:92
  152.2 7.8 %fusion.74 = (f32[8,4,128]{2,1,0:T(4,128)S(1)}, f32[8,4,128,1024]{2,3,1,0:T(8,128)S(1)}) fusion(f32[8,4,128,512]{2,3,1,0:T(8,128)S(1)} %convolution_bitcast_fusion.1, f32[8,4,128,512]{2,3,1,0:T(8,128)} %convolution_bitcast_fusion.2, f32[1024]{0:T(1024)S(1)} %copy-done.38, pred[8,1024]{1,0:T(8,128)(4,1)S(1)} %concatenate.80), kind=kOutput, calls=%fused_computation.157 | output fusion | flops 25166848 | bytes 33583104 | tf_op jit(solution)/shard_map/sub | solution.py:205
  181.4 5.0 %gather_fusion = bf16[4,512,1024]{2,1,0:T(8,128)(2,1)} fusion(bf16[4,512,1024]{2,1,0:T(8,128)(2,1)} %pad_maximum_fusion.7, s32[1024]{0:T(1024)S(1)} %pad_clamp_fusion), kind=kCustom, calls=%fused_computation | custom fusion | bytes 8388624 | tf_op jit(solution)/shard_map/gather | solution.py:64
  186.4 6.2 %copy.226 = bf16[512,4,1024]{0,2,1:T(8,128)(2,1)} copy(bf16[512,4,1024]{2,0,1:T(8,128)(2,1)} %bitcast.178) | data formatting | bytes 8388608 | tf_op jit(solution)/shard_map/transpose | solution.py:65
  198.8 10.9 %all-gather.2.cloned.1.call-done = bf16[512,4096]{0,1:T(8,128)(2,1)} async-done(((bf16[512,512]{0,1:T(8,128)(2,1)}), bf16[512,4096]{0,1:T(8,128)(2,1)}) %all-gather.2.cloned.1.call-update) | async-done | bytes 4194320 | tf_op jit(solution)/shard_map/all_gather | solution.py:217
  209.7 9.2 %fusion.44 = bf16[1024,512]{1,0:T(8,128)(2,1)S(1)} fusion(bf16[512,4096]{1,0:T(8,128)(2,1)} %param.9, bf16[512,4096]{0,1:T(8,128)(2,1)} %bitcast.193, bf16[512,4096]{0,1:T(8,128)(2,1)} %all-gather.2.cloned.1.call-done), kind=kOutput, calls=%fused_computation.78 | convolution fusion | flops 4312268800 | bytes 13631488 | tf_op jit(solution)/shard_map/dot_general | solution.py:222
  221.7 5.4 %fusion.20 = f32[4,128,512,1]{2,1,3,0:T(8,128)} fusion(bf16[8,128,4,128]{3,2,1,0:T(4,128)(2,1)} %reshape.232, bf16[8,4,128,1024]{2,3,1,0:T(8,128)(2,1)} %fusion.68), kind=kOutput, calls=%fused_computation.36 | convolution fusion | flops 536870912 | bytes 6291456 | tf_op jit(solution)/shard_map/bhqk,bqhd->khd/dot_general | solution.py:277
  231.7 5.5 %convolution_bitcast_fusion = f32[8,4,128,512]{2,3,1,0:T(8,128)} fusion(bf16[512,4,128,1]{0,2,1,3:T(8,128)(2,1)S(1)} %bitcast.187, bf16[8,128,4,128]{1,3,2,0:T(8,128)(2,1)S(1)} %copy.252), kind=kOutput, calls=%fused_computation.54 | convolution fusion | flops 536870912 | bytes 9961472 | tf_op jit(solution)/shard_map/bqhd,khd->bhqk/dot_general | solution.py:241
  238.0 8.3 %fusion.13 = f32[4096,512]{1,0:T(8,128)} fusion(bf16[1024,512]{0,1:T(8,128)(2,1)} %bitcast.163, bf16[512,4096]{0,1:T(8,128)(2,1)S(1)} %bitcast.194, bf16[512,4096]{0,1:T(8,128)(2,1)S(1)} %copy-done.37), kind=kOutput, calls=%fused_computation.25 | convolution fusion | flops 4311744512 | bytes 17825792 | tf_op jit(solution)/shard_map/dot_general | solution.py:228
  248.3 29.8 %multiply_convert_fusion = bf16[8,4,128,1024]{2,3,1,0:T(8,128)(2,1)} fusion(f32[8,4,128,512]{2,3,1,0:T(8,128)} %convolution_bitcast_fusion, f32[8,4,128,512]{2,3,1,0:T(8,128)} %fusion.75, f32[8,4,128,1024]{2,3,1,0:T(8,128)} %copy-done.7, f32[8,4,128]{2,1,0:T(4,128)S(1)} %get-tuple-element.90), kind=kOutput, calls=%fused_computation.13 | output fusion | flops 33559552 | bytes 41959424 | tf_op jit(solution)/shard_map/sub | solution.py:248
  287.9 6.1 %fusion.24 = f32[8,4,128,128]{3,2,1,0:T(8,128)} fusion(bf16[8,512,4,128]{1,3,2,0:T(8,128)(2,1)} %bitcast.164, bf16[8,4,128,1024]{2,3,1,0:T(8,128)(2,1)} %multiply_convert_fusion), kind=kOutput, calls=%fused_computation.44 | convolution fusion | flops 536870912 | bytes 10485760 | tf_op jit(solution)/shard_map/bhqk,bkhd->bqhd/dot_general | solution.py:253
  295.2 16.5 %collective-permute-done.19 = f32[2,128,512]{2,1,0:T(8,128)S(1)} collective-permute-done((f32[2,128,512]{2,1,0:T(8,128)S(1)}, f32[2,128,512]{2,1,0:T(8,128)S(1)}, u32[]{:S(2)}, u32[]{:S(2)}) %collective-permute-start.19) | collective-permute-done | bytes 524320 | tf_op jit(solution)/shard_map/ppermute | solution.py:18
  331.0 7.1 %fusion.16 = (f32[2,8,128,512]{2,3,1,0:T(8,128)}, f32[2,8,128,512]{2,3,1,0:T(8,128)}, f32[2,8,128,512]{2,3,1,0:T(8,128)}, f32[2,8,128,512]{2,3,1,0:T(8,128)}) fusion(f32[1,8,512,512]{2,3,1,0:T(8,128)S(1)} %bitcast.171, f32[1,8,512,512]{2,3,1,0:T(8,128)S(1)} %bitcast.170), kind=kLoop, calls=%fused_computation.28 | loop fusion | flops 4194304 | bytes 33554432 | tf_op jit(solution)/shard_map/stack | solution.py:272
  338.1 8.9 %collective-permute-done.21 = f32[2,128,512]{2,1,0:T(8,128)} collective-permute-done((f32[2,128,512]{2,1,0:T(8,128)}, f32[2,128,512]{2,1,0:T(8,128)}, u32[]{:S(2)}, u32[]{:S(2)}) %collective-permute-start.21) | collective-permute-done | bytes 524320 | tf_op jit(solution)/shard_map/ppermute | solution.py:18
  350.5 18.5 %collective-permute-done.16 = bf16[1024,1024]{0,1:T(8,128)(2,1)S(1)} collective-permute-done((bf16[1024,1024]{0,1:T(8,128)(2,1)}, bf16[1024,1024]{0,1:T(8,128)(2,1)S(1)}, u32[]{:S(2)}, u32[]{:S(2)}) %collective-permute-start.16) | collective-permute-done | bytes 2097184 | tf_op jit(solution)/shard_map/ppermute | solution.py:48
  381.8 5.3 %copy.254 = f32[2,8,128,512]{3,2,1,0:T(8,128)} copy(f32[2,8,128,512]{2,3,1,0:T(8,128)} %get-tuple-element.49) | data formatting | bytes 8388608 | tf_op jit(solution)/shard_map/slice | solution.py:281
  387.2 5.3 %copy.255 = f32[2,4,2,128,512]{4,3,2,1,0:T(8,128)} copy(f32[2,4,2,128,512]{3,4,2,1,0:T(8,128)} %bitcast.181) | data formatting | bytes 8388608 | tf_op jit(solution)/shard_map/reshape | solution.py:292
  419.8 6.4 %reshape.245 = f32[2,1024,512]{2,1,0:T(8,128)} reshape(f32[2,512,2,512]{3,2,1,0:T(2,128)} %broadcast_in_dim.45) | data formatting | bytes 8388608 | tf_op jit(solution)/shard_map/reshape | solution.py:32
  429.5 4.9 %fusion.18 = bf16[2,1024,512]{2,1,0:T(8,128)(2,1)S(1)} fusion(f32[2,1024,512]{2,1,0:T(8,128)} %reshape.245, f32[2,4,2,128,512]{4,3,2,1,0:T(8,128)} %rev.19, f32[2,8,128,512]{3,2,1,0:T(8,128)S(1)} %copy-done.8, f32[2,128,512]{2,1,0:T(8,128)S(1)} %broadcast_multiply_fusion.2), kind=kLoop, calls=%fused_computation.33 | loop fusion | flops 4194304 | bytes 15204352 | tf_op jit(solution)/shard_map/convert.1
  (244 shorter events, 225.6 us)
Async XLA Ops:
  7.2 202.6 %all-gather.2.cloned.1.call-start = ((), (), s32[]{:S(2)}) async-start(), calls=%async_computation.1 | async-start | bytes 4718592 | tf_op jit(solution)/shard_map/all_gather | solution.py:217
  9.1 79.5 %collective-permute-start.9 = (bf16[512,512]{1,0:T(8,128)(2,1)}, bf16[512,512]{1,0:T(8,128)(2,1)}, u32[]{:S(2)}, u32[]{:S(2)}) collective-permute-start(bf16[512,512]{1,0:T(8,128)(2,1)} %slice.127), channel_id=1, source_target_pairs={{0,1},{1,0},{2,3},{3,2},{4,5},{5,4},{6,7},{7,6},{8,9},{9,8},{10,11... | collective-permute-start | bytes 1572872 | tf_op jit(solution)/shard_map/ppermute | solution.py:41
  14.5 52.9 %collective-permute-start = (f32[2,128,512]{2,1,0:T(8,128)}, f32[2,128,512]{2,1,0:T(8,128)}, u32[]{:S(2)}, u32[]{:S(2)}) collective-permute-start(f32[2,128,512]{2,1,0:T(8,128)} %broadcast_multiply_fusion.3), channel_id=1, source_target_pairs={{0,8},{8,0},{16,24},{24,16},{32,40},{40,32},{48,56},{56,48},{64,72... | collective-permute-start | bytes 1572872 | tf_op jit(solution)/shard_map/ppermute | solution.py:18
  18.4 91.9 %collective-permute-start.7 = (bf16[512,512]{0,1:T(8,128)(2,1)}, bf16[512,512]{0,1:T(8,128)(2,1)}, u32[]{:S(2)}, u32[]{:S(2)}) collective-permute-start(bf16[512,512]{0,1:T(8,128)(2,1)} %copy.282), channel_id=1, source_target_pairs={{0,7},{1,0},{2,1},{3,2},{4,3},{5,4},{6,5},{7,6},{16,23},{17,16},{1... | collective-permute-start | bytes 1572872 | tf_op jit(solution)/shard_map/ppermute | solution.py:90
  24.3 90.4 %collective-permute-start.4 = (bf16[512,512]{0,1:T(8,128)(2,1)}, bf16[512,512]{0,1:T(8,128)(2,1)}, u32[]{:S(2)}, u32[]{:S(2)}) collective-permute-start(bf16[512,512]{0,1:T(8,128)(2,1)} %copy.279), channel_id=1, source_target_pairs={{0,1},{1,2},{2,3},{3,4},{4,5},{5,6},{6,7},{7,0},{8,10},{9,11},{10,... | collective-permute-start | bytes 1572872 | tf_op jit(solution)/shard_map/ppermute | solution.py:90
  70.7 13.8 %collective-permute-start.1 = (f32[2,128,512]{2,1,0:T(8,128)S(1)}, f32[2,128,512]{2,1,0:T(8,128)S(1)}, u32[]{:S(2)}, u32[]{:S(2)}) collective-permute-start(f32[2,128,512]{2,1,0:T(8,128)S(1)} %copy_multiply_fusion.2), channel_id=1, source_target_pairs={{0,16},{8,24},{16,0},{24,8},{32,48},{40,56},{48,32},{56,40},{64,80... | collective-permute-start | bytes 1572872 | tf_op jit(solution)/shard_map/ppermute | solution.py:18
  86.7 20.3 %collective-permute-start.2 = (f32[2,128,512]{2,1,0:T(8,128)}, f32[2,128,512]{2,1,0:T(8,128)}, u32[]{:S(2)}, u32[]{:S(2)}) collective-permute-start(f32[2,128,512]{2,1,0:T(8,128)} %copy_multiply_fusion.1), channel_id=1, source_target_pairs={{0,32},{8,40},{16,48},{24,56},{32,0},{40,8},{48,16},{56,24},{64,96... | collective-permute-start | bytes 1572872 | tf_op jit(solution)/shard_map/ppermute | solution.py:18
  92.2 50.2 %collective-permute-start.10 = (bf16[512,1024]{1,0:T(8,128)(2,1)}, bf16[512,1024]{1,0:T(8,128)(2,1)S(1)}, u32[]{:S(2)}, u32[]{:S(2)}) collective-permute-start(bf16[512,1024]{1,0:T(8,128)(2,1)} %get-tuple-element.83), channel_id=1, source_target_pairs={{0,6},{1,7},{2,0},{3,1},{4,2},{5,3},{6,4},{7,5},{8,14},{9,15},{10,... | collective-permute-start | bytes 3145736 | tf_op jit(solution)/shard_map/ppermute | solution.py:49
  94.0 51.3 %collective-permute-start.11 = (bf16[512,1024]{1,0:T(8,128)(2,1)}, bf16[512,1024]{1,0:T(8,128)(2,1)S(1)}, u32[]{:S(2)}, u32[]{:S(2)}) collective-permute-start(bf16[512,1024]{1,0:T(8,128)(2,1)} %get-tuple-element.83), channel_id=1, source_target_pairs={{0,2},{1,3},{2,4},{3,5},{4,6},{5,7},{6,0},{7,1},{8,10},{9,11},{10,... | collective-permute-start | bytes 3145736 | tf_op jit(solution)/shard_map/ppermute | solution.py:48
  107.0 13.5 %collective-permute-start.5 = (bf16[512,512]{0,1:T(8,128)(2,1)}, bf16[512,512]{0,1:T(8,128)(2,1)}, u32[]{:S(2)}, u32[]{:S(2)}) collective-permute-start(bf16[512,512]{0,1:T(8,128)(2,1)} %copy.280), channel_id=1, source_target_pairs={{0,3},{1,4},{2,5},{3,6},{4,7},{5,0},{6,1},{7,2},{8,12},{9,13},{10,... | collective-permute-start | bytes 1572872 | tf_op jit(solution)/shard_map/ppermute | solution.py:90
  110.4 14.6 %collective-permute-start.6 = (bf16[512,512]{0,1:T(8,128)(2,1)}, bf16[512,512]{0,1:T(8,128)(2,1)}, u32[]{:S(2)}, u32[]{:S(2)}) collective-permute-start(bf16[512,512]{0,1:T(8,128)(2,1)} %copy.281), channel_id=1, source_target_pairs={{0,5},{1,6},{2,7},{3,0},{4,1},{5,2},{6,3},{7,4},{8,14},{9,15},{10,... | collective-permute-start | bytes 1572872 | tf_op jit(solution)/shard_map/ppermute | solution.py:90
  114.7 32.9 %collective-permute-start.3 = (bf16[2,128,512]{2,1,0:T(8,128)(2,1)S(1)}, bf16[2,128,512]{2,1,0:T(8,128)(2,1)}, u32[]{:S(2)}, u32[]{:S(2)}) collective-permute-start(bf16[2,128,512]{2,1,0:T(8,128)(2,1)S(1)} %copy_multiply_fusion), channel_id=1, source_target_pairs={{0,64},{8,72},{16,80},{24,88},{32,96},{40,104},{48,112},{56,120},{... | collective-permute-start | bytes 786440 | tf_op jit(solution)/shard_map/ppermute | solution.py:18
  120.5 325.7 %reduce-scatter.2.cloned.1.call-start = ((), (), s32[]{:S(2)}) async-start(), calls=%async_computation.2 | async-start | bytes 8912896 | tf_op jit(solution)/shard_map/reduce_scatter | solution.py:227
  128.1 64.6 %collective-permute-start.8 = (bf16[4,512,512]{1,2,0:T(8,128)(2,1)}, bf16[4,512,512]{1,2,0:T(8,128)(2,1)}, u32[]{:S(2)}, u32[]{:S(2)}) collective-permute-start(bf16[4,512,512]{1,2,0:T(8,128)(2,1)} %pad_maximum_fusion.9), channel_id=1, source_target_pairs={{0,8},{8,0},{16,24},{24,16},{32,40},{40,32},{48,56},{56,48},{64,72... | collective-permute-start | bytes 6291464 | tf_op jit(solution)/shard_map/ppermute | solution.py:92
  143.4 34.2 %collective-permute-start.13 = (bf16[512,512]{1,0:T(8,128)(2,1)}, bf16[512,512]{1,0:T(8,128)(2,1)}, u32[]{:S(2)}, u32[]{:S(2)}) collective-permute-start(bf16[512,512]{1,0:T(8,128)(2,1)} %slice.166), channel_id=1, source_target_pairs={{0,6},{1,7},{2,0},{3,1},{4,2},{5,3},{6,4},{7,5},{8,14},{9,15},{10,... | collective-permute-start | bytes 1572872 | tf_op jit(solution)/shard_map/ppermute | solution.py:55
  146.2 31.5 %collective-permute-start.12 = (bf16[512,512]{1,0:T(8,128)(2,1)}, bf16[512,512]{1,0:T(8,128)(2,1)}, u32[]{:S(2)}, u32[]{:S(2)}) collective-permute-start(bf16[512,512]{1,0:T(8,128)(2,1)} %slice.165), channel_id=1, source_target_pairs={{0,2},{1,3},{2,4},{3,5},{4,6},{5,7},{6,0},{7,1},{8,10},{9,11},{10,... | collective-permute-start | bytes 1572872 | tf_op jit(solution)/shard_map/ppermute | solution.py:54
  247.9 70.4 %collective-permute-start.14 = (bf16[1024,512]{0,1:T(8,128)(2,1)}, bf16[1024,512]{0,1:T(8,128)(2,1)}, u32[]{:S(2)}, u32[]{:S(2)}) collective-permute-start(bf16[1024,512]{0,1:T(8,128)(2,1)} %bitcast.163), channel_id=1, source_target_pairs={{0,1},{1,0},{2,3},{3,2},{4,5},{5,4},{6,7},{7,6},{8,9},{9,8},{10,11... | collective-permute-start | bytes 3145736 | tf_op jit(solution)/shard_map/ppermute | solution.py:41
  284.6 27.2 %collective-permute-start.19 = (f32[2,128,512]{2,1,0:T(8,128)S(1)}, f32[2,128,512]{2,1,0:T(8,128)S(1)}, u32[]{:S(2)}, u32[]{:S(2)}) collective-permute-start(f32[2,128,512]{2,1,0:T(8,128)S(1)} %fusion.54), channel_id=1, source_target_pairs={{0,64},{8,72},{16,80},{24,88},{32,96},{40,104},{48,112},{56,120},{... | collective-permute-start | bytes 1572872 | tf_op jit(solution)/shard_map/ppermute | solution.py:18
  321.5 47.4 %collective-permute-start.16 = (bf16[1024,1024]{0,1:T(8,128)(2,1)}, bf16[1024,1024]{0,1:T(8,128)(2,1)S(1)}, u32[]{:S(2)}, u32[]{:S(2)}) collective-permute-start(bf16[1024,1024]{0,1:T(8,128)(2,1)} %pad_maximum_fusion.10), channel_id=1, source_target_pairs={{0,2},{1,3},{2,4},{3,5},{4,6},{5,7},{6,0},{7,1},{8,10},{9,11},{10,... | collective-permute-start | bytes 6291464 | tf_op jit(solution)/shard_map/ppermute | solution.py:48
  323.0 48.5 %collective-permute-start.15 = (bf16[1024,1024]{0,1:T(8,128)(2,1)}, bf16[1024,1024]{0,1:T(8,128)(2,1)}, u32[]{:S(2)}, u32[]{:S(2)}) collective-permute-start(bf16[1024,1024]{0,1:T(8,128)(2,1)} %pad_maximum_fusion.10), channel_id=1, source_target_pairs={{0,6},{1,7},{2,0},{3,1},{4,2},{5,3},{6,4},{7,5},{8,14},{9,15},{10,... | collective-permute-start | bytes 6291464 | tf_op jit(solution)/shard_map/ppermute | solution.py:49
  328.2 18.9 %collective-permute-start.21 = (f32[2,128,512]{2,1,0:T(8,128)}, f32[2,128,512]{2,1,0:T(8,128)}, u32[]{:S(2)}, u32[]{:S(2)}) collective-permute-start(f32[2,128,512]{2,1,0:T(8,128)} %fusion.53), channel_id=1, source_target_pairs={{0,16},{8,24},{16,0},{24,8},{32,48},{40,56},{48,32},{56,40},{64,80... | collective-permute-start | bytes 1572872 | tf_op jit(solution)/shard_map/ppermute | solution.py:18
  350.5 75.8 %collective-permute-start.22 = (f32[2,128,512]{2,1,0:T(8,128)}, f32[2,128,512]{2,1,0:T(8,128)}, u32[]{:S(2)}, u32[]{:S(2)}) collective-permute-start(f32[2,128,512]{2,1,0:T(8,128)} %fusion.57), channel_id=1, source_target_pairs={{0,8},{8,0},{16,24},{24,16},{32,40},{40,32},{48,56},{56,48},{64,72... | collective-permute-start | bytes 1572872 | tf_op jit(solution)/shard_map/ppermute | solution.py:18
  371.3 56.4 %collective-permute-start.17 = (bf16[1024,512]{0,1:T(8,128)(2,1)}, bf16[1024,512]{0,1:T(8,128)(2,1)}, u32[]{:S(2)}, u32[]{:S(2)}) collective-permute-start(bf16[1024,512]{0,1:T(8,128)(2,1)} %slice.167), channel_id=1, source_target_pairs={{0,2},{1,3},{2,4},{3,5},{4,6},{5,7},{6,0},{7,1},{8,10},{9,11},{10,... | collective-permute-start | bytes 3145736 | tf_op jit(solution)/shard_map/ppermute | solution.py:54
  373.8 53.9 %collective-permute-start.18 = (bf16[1024,512]{0,1:T(8,128)(2,1)}, bf16[1024,512]{0,1:T(8,128)(2,1)}, u32[]{:S(2)}, u32[]{:S(2)}) collective-permute-start(bf16[1024,512]{0,1:T(8,128)(2,1)} %slice.168), channel_id=1, source_target_pairs={{0,6},{1,7},{2,0},{3,1},{4,2},{5,3},{6,4},{7,5},{8,14},{9,15},{10,... | collective-permute-start | bytes 3145736 | tf_op jit(solution)/shard_map/ppermute | solution.py:55
  (42 other events, 332.5 us)
Sparse Core Ops, SparseCore 0:
  120.6 89.1 all-gather.1
  246.5 110.2 reduce-scatter.1

commit v10 on v9

--- a/solution.py
+++ b/solution.py
@@ -152,7 +152,8 @@
                 .mean(axis=2)
                 .astype(jnp.bfloat16)
             )
-        sibling = pooled.reshape(2, group_count // 2, 2, BLK, features)[:, :, ::-1].reshape(
+        paired = pooled.reshape(2, group_count // 2, 2, BLK, features)
+        sibling = jnp.concatenate([paired[:, :, 1:], paired[:, :, :1]], axis=2).reshape(
             2, group_count, BLK, features
         )
         segments.append(
@@ -289,7 +290,8 @@
             .reshape(2, group_count, factor, BLK, features)
             .sum(axis=2)
         )
-        restored = segment.reshape(2, group_count // 2, 2, BLK, features)[:, :, ::-1].reshape(
+        paired = segment.reshape(2, group_count // 2, 2, BLK, features)
+        restored = jnp.concatenate([paired[:, :, 1:], paired[:, :, :1]], axis=2).reshape(
             2, group_count * BLK, features
         )
         level_grads.append(restored)

time: 458 us -> 423 us (0.924)
  waiting for transfers between devices: 66.5 us -> 31.7 us
    ppermute x8, waiting for transfers between devices: 32.6 us -> 11.6 us  [swapped(): return lax.ppermute(value, axis, pairs)]
    ppermute x2, waiting for transfers between devices: 18.5 us -> 0.01 us  [head_ring_gather(): from_below = lax.ppermute(pair_block, 'head', upward)]
    unnamed x91 -> x105, local copies, waits for them, and re-layouts: 22.8 us -> 35.2 us
    rev x4 -> x0, local copies, waits for them, and re-layouts: 12 us -> none  [the longest x2 6.67 us: body(): segment.reshape(2, group_count // 2, 2, BLK, features)[:, :, ::-1]]
    slice x0 -> x5, local copies, waits for them, and re-layouts: none -> 8.05 us  [body(): paired[:, :, 1:]]
    reshape x2 -> x0, local copies, waits for them, and re-layouts: 7.12 us -> none  [body(): segment.reshape(2, group_count // 2, 2, BLK, features)[:, :, ::-1]]
    concatenate x0 -> x4, other arithmetic: none -> 4.94 us  [body(): jnp.concatenate([paired[:, :, 1:], paired[:, :, :1]], axis=2)]
  transfers between devices with their start and end apart: 25 -> 25, of which waited for: 7 -> 6; matrix products, arithmetic and copies ran while one was open for 60% -> 66% of each run, Pallas kernels for 0% -> 0%
where the time goes in v10:
time: 423 us; the launch traced here: 417 us
  local copies, waits for them, and re-layouts  127 us (30%)
  other arithmetic  116 us (27%)
  matrix products  76 us (18%)
  starting transfers between devices  51.6 us (12%)
  waiting for transfers between devices  31.7 us (7%)
  between operations  15.5 us (4%)
    unnamed x105, local copies, waits for them, and re-layouts  35.2 us
    sub x1, other arithmetic, body(): grad_score = (attn_prob * (grad_prob - row_delta)).astype(jnp.bfloat16)  29.6 us
    ppermute x8, starting transfers between devices, swapped(): return lax.ppermute(value, axis, pairs)  15.9 us
    ppermute x1, starting transfers between devices, weight_columns(): lax.ppermute(mine, 'seq', [(src, src ^ 1) for src in range(seq_count)])  13.3 us
    ppermute x8, waiting for transfers between devices, swapped(): return lax.ppermute(value, axis, pairs)  11.6 us
    all_gather x1, waiting for transfers between devices, body(): lax.all_gather(cotangent[:half_rows], 'head', axis=1, tiled=True)  10.7 us
    slice x2, local copies, waits for them, and re-layouts, body(): value_heads = key_set[1].reshape(blocks, near_keys, head_count, DH)  10 us
    reshape x2, local copies, waits for them, and re-layouts, spread_rows(): return wide.reshape(shape_in[:-2] + (shape_in[-2] * factor, shape_in[-1]))  9.92 us
  transfers between devices with their start and end apart: 25, of which 6 were waited for; matrix products, arithmetic and copies ran while one was open for 66% of the time, Pallas kernels for 0%

profile of v10, /device:TPU:0, one launch (start us, length us, event | category | flops | bytes accessed | tf_op | source)
XLA Modules:
  0.0 417.3 jit_solution(2353779151247351865)
XLA Ops:
  18.4 4.9 %collective-permute-start.7 = (bf16[512,512]{0,1:T(8,128)(2,1)}, bf16[512,512]{0,1:T(8,128)(2,1)}, u32[]{:S(2)}, u32[]{:S(2)}) collective-permute-start(bf16[512,512]{0,1:T(8,128)(2,1)} %copy.289), channel_id=1, source_target_pairs={{0,7},{1,0},{2,1},{3,2},{4,3},{5,4},{6,5},{7,6},{16,23},{17,16},{1... | collective-permute-start | bytes 1572872 | tf_op jit(solution)/shard_map/ppermute | solution.py:90
  34.2 5.8 %convert_reduce_fusion.2 = f32[2,512,512]{2,1,0:T(8,128)S(1)} fusion(bf16[1,512,2,512]{3,2,1,0:T(2,128)(2,1)S(1)} %copy-done.27, bf16[1,512,2,512]{3,2,1,0:T(2,128)(2,1)S(1)} %copy-done.26), kind=kLoop, calls=%fused_computation.42 | loop fusion | flops 2621440 | bytes 4194304 | tf_op jit(solution)/shard_map/reduce_sum | solution.py:152
  48.3 6.6 %copy.209 = bf16[1,8,512,512]{2,3,1,0:T(8,128)(2,1)} copy(bf16[1,8,512,512]{3,2,1,0:T(8,128)(2,1)} %get-tuple-element.54) | data formatting | bytes 8388608 | tf_op jit(solution)/shard_map/slice | solution.py:185
  61.3 4.6 %convolution_bitcast_fusion.2 = f32[8,4,128,512]{2,3,1,0:T(8,128)} fusion(bf16[8,512,4,128]{1,3,2,0:T(8,128)(2,1)S(1)} %bitcast.165, bf16[8,128,4,128]{1,3,2,0:T(8,128)(2,1)S(1)} %copy.238), kind=kOutput, calls=%fused_computation.57 | convolution fusion | flops 536870912 | bytes 13631488 | tf_op jit(solution)/shard_map/bqhd,bkhd->bhqk/dot_general | solution.py:192
  65.9 6.1 %collective-permute-done.1 = f32[2,128,512]{2,1,0:T(8,128)S(1)} collective-permute-done((f32[2,128,512]{2,1,0:T(8,128)S(1)}, f32[2,128,512]{2,1,0:T(8,128)S(1)}, u32[]{:S(2)}, u32[]{:S(2)}) %collective-permute-start.1) | collective-permute-done | bytes 524320 | tf_op jit(solution)/shard_map/ppermute | solution.py:18
  81.8 6.5 %copy.207 = bf16[1,8,512,512]{2,3,1,0:T(8,128)(2,1)} copy(bf16[1,8,512,512]{3,2,1,0:T(8,128)(2,1)} %get-tuple-element.53) | data formatting | bytes 8388608 | tf_op jit(solution)/shard_map/slice | solution.py:186
  107.9 4.4 %collective-permute-done.6 = bf16[512,512]{0,1:T(8,128)(2,1)} collective-permute-done((bf16[512,512]{0,1:T(8,128)(2,1)}, bf16[512,512]{0,1:T(8,128)(2,1)}, u32[]{:S(2)}, u32[]{:S(2)}) %collective-permute-start.6) | collective-permute-done | bytes 524320 | tf_op jit(solution)/shard_map/ppermute | solution.py:90
  115.5 13.3 %collective-permute-start.8 = (bf16[4,512,512]{1,2,0:T(8,128)(2,1)}, bf16[4,512,512]{1,2,0:T(8,128)(2,1)}, u32[]{:S(2)}, u32[]{:S(2)}) collective-permute-start(bf16[4,512,512]{1,2,0:T(8,128)(2,1)} %pad_maximum_fusion.10), channel_id=1, source_target_pairs={{0,8},{8,0},{16,24},{24,16},{32,40},{40,32},{48,56},{56,48},{64,72... | collective-permute-start | bytes 6291464 | tf_op jit(solution)/shard_map/ppermute | solution.py:92
  139.7 7.8 %fusion.81 = (f32[8,4,128]{2,1,0:T(4,128)S(1)}, f32[8,4,128,1024]{2,3,1,0:T(8,128)S(1)}) fusion(f32[8,4,128,512]{2,3,1,0:T(8,128)S(1)} %convolution_bitcast_fusion.1, f32[8,4,128,512]{2,3,1,0:T(8,128)} %convolution_bitcast_fusion.2, f32[1024]{0:T(1024)S(1)} %copy-done.45, pred[8,1024]{1,0:T(8,128)(4,1)S(1)} %concatenate.101), kind=kOutput, calls=%fused_computation.169 | output fusion | flops 25166848 | bytes 33583104 | tf_op jit(solution)/shard_map/sub | solution.py:206
  168.8 5.0 %gather_fusion = bf16[4,512,1024]{2,1,0:T(8,128)(2,1)} fusion(bf16[4,512,1024]{2,1,0:T(8,128)(2,1)} %pad_maximum_fusion.7, s32[1024]{0:T(1024)S(1)} %pad_clamp_fusion), kind=kCustom, calls=%fused_computation | custom fusion | bytes 8388624 | tf_op jit(solution)/shard_map/gather | solution.py:64
  173.9 6.3 %copy.231 = bf16[512,4,1024]{0,2,1:T(8,128)(2,1)} copy(bf16[512,4,1024]{2,0,1:T(8,128)(2,1)} %bitcast.179) | data formatting | bytes 8388608 | tf_op jit(solution)/shard_map/transpose | solution.py:65
  186.4 10.7 %all-gather.2.cloned.1.call-done = bf16[512,4096]{0,1:T(8,128)(2,1)} async-done(((bf16[512,512]{0,1:T(8,128)(2,1)}), bf16[512,4096]{0,1:T(8,128)(2,1)}) %all-gather.2.cloned.1.call-update) | async-done | bytes 4194320 | tf_op jit(solution)/shard_map/all_gather | solution.py:218
  197.2 9.2 %fusion.45 = bf16[1024,512]{1,0:T(8,128)(2,1)S(1)} fusion(bf16[512,4096]{1,0:T(8,128)(2,1)} %param.9, bf16[512,4096]{0,1:T(8,128)(2,1)} %bitcast.194, bf16[512,4096]{0,1:T(8,128)(2,1)} %all-gather.2.cloned.1.call-done), kind=kOutput, calls=%fused_computation.83 | convolution fusion | flops 4312268800 | bytes 13631488 | tf_op jit(solution)/shard_map/dot_general | solution.py:223
  207.4 5.1 %fusion.20 = f32[4,128,512,1]{2,1,3,0:T(8,128)} fusion(bf16[8,128,4,128]{3,2,1,0:T(4,128)(2,1)S(1)} %reshape.232, bf16[8,4,128,1024]{2,3,1,0:T(8,128)(2,1)} %fusion.70), kind=kOutput, calls=%fused_computation.37 | convolution fusion | flops 536870912 | bytes 6291456 | tf_op jit(solution)/shard_map/bhqk,bqhd->khd/dot_general | solution.py:278
  212.5 4.6 %fusion.82 = f32[8,4,128,512]{2,3,1,0:T(8,128)} fusion(bf16[8,128,4,128]{1,3,2,0:T(8,128)(2,1)S(1)} %copy.257, bf16[8,512,4,128]{1,3,2,0:T(8,128)(2,1)S(1)} %bitcast.176), kind=kOutput, calls=%fused_computation.170 | convolution fusion | flops 536870912 | bytes 13631488 | tf_op jit(solution)/shard_map/bqhd,bkhd->bhqk/dot_general | solution.py:239
  217.1 5.5 %convolution_bitcast_fusion = f32[8,4,128,512]{2,3,1,0:T(8,128)} fusion(bf16[512,4,128,1]{0,2,1,3:T(8,128)(2,1)S(1)} %bitcast.188, bf16[8,128,4,128]{1,3,2,0:T(8,128)(2,1)S(1)} %copy.257), kind=kOutput, calls=%fused_computation.55 | convolution fusion | flops 536870912 | bytes 9961472 | tf_op jit(solution)/shard_map/bqhd,khd->bhqk/dot_general | solution.py:242
  223.4 8.3 %fusion.13 = f32[4096,512]{1,0:T(8,128)} fusion(bf16[1024,512]{0,1:T(8,128)(2,1)} %bitcast.164, bf16[512,4096]{0,1:T(8,128)(2,1)S(1)} %bitcast.195, bf16[512,4096]{0,1:T(8,128)(2,1)S(1)} %copy-done.44), kind=kOutput, calls=%fused_computation.25 | convolution fusion | flops 4311744512 | bytes 17825792 | tf_op jit(solution)/shard_map/dot_general | solution.py:229
  233.7 29.6 %multiply_convert_fusion = bf16[8,4,128,1024]{2,3,1,0:T(8,128)(2,1)} fusion(f32[8,4,128,512]{2,3,1,0:T(8,128)} %convolution_bitcast_fusion, f32[8,4,128,512]{2,3,1,0:T(8,128)} %fusion.82, f32[8,4,128,1024]{2,3,1,0:T(8,128)} %copy-done.12, f32[8,4,128]{2,1,0:T(4,128)S(1)} %get-tuple-element.100), kind=kOutput, calls=%fused_computation.13 | output fusion | flops 33559552 | bytes 41959424 | tf_op jit(solution)/shard_map/sub | solution.py:249
  263.3 4.7 %fusion.49 = f32[4,512,128]{1,2,0:T(8,128)} fusion(bf16[8,128,4,128]{1,3,2,0:T(8,128)(2,1)S(1)} %copy-done.9, bf16[8,4,128,1024]{2,3,1,0:T(8,128)(2,1)} %multiply_convert_fusion), kind=kOutput, calls=%fused_computation.85 | convolution fusion | flops 537133056 | bytes 6291456 | tf_op jit(solution)/shard_map/bhqk,bqhd->khd/dot_general | solution.py:275
  280.4 7.0 %fusion.16 = (f32[2,8,128,512]{2,3,1,0:T(8,128)}, f32[2,8,128,512]{2,3,1,0:T(8,128)}, f32[2,8,128,512]{2,3,1,0:T(8,128)}, f32[2,8,128,512]{2,3,1,0:T(8,128)}) fusion(f32[1,8,512,512]{2,3,1,0:T(8,128)S(1)} %bitcast.178, f32[1,8,512,512]{2,3,1,0:T(8,128)S(1)} %bitcast.177), kind=kLoop, calls=%fused_computation.28 | loop fusion | flops 4194304 | bytes 33554432 | tf_op jit(solution)/shard_map/stack | solution.py:273
  298.8 4.8 %fusion.72 = (f32[2,4,1,128,512]{3,4,2,1,0:T(8,128)}, f32[2,4,1,128,512]{3,4,2,1,0:T(8,128)}) fusion(f32[2,4,2,128,512]{3,4,2,1,0:T(8,128)} %bitcast.181), kind=kLoop, calls=%fused_computation.160 | loop fusion | bytes 8388608 | tf_op jit(solution)/shard_map/slice | solution.py:294
  313.5 5.5 %collective-permute-done.20 = f32[2,128,512]{2,1,0:T(8,128)S(1)} collective-permute-done((f32[2,128,512]{2,1,0:T(8,128)S(1)}, f32[2,128,512]{2,1,0:T(8,128)S(1)}, u32[]{:S(2)}, u32[]{:S(2)}) %collective-permute-start.20) | collective-permute-done | bytes 524320 | tf_op jit(solution)/shard_map/ppermute | solution.py:18
  330.1 5.4 %copy.259 = f32[2,8,128,512]{3,2,1,0:T(8,128)} copy(f32[2,8,128,512]{2,3,1,0:T(8,128)} %get-tuple-element.49) | data formatting | bytes 8388608 | tf_op jit(solution)/shard_map/slice | solution.py:282
  377.4 6.3 %reshape.246 = f32[2,1024,512]{2,1,0:T(8,128)} reshape(f32[2,512,2,512]{3,2,1,0:T(2,128)} %broadcast_in_dim.45) | data formatting | bytes 8388608 | tf_op jit(solution)/shard_map/reshape | solution.py:32
  (260 shorter events, 223.9 us)
Async XLA Ops:
  7.2 190.0 %all-gather.2.cloned.1.call-start = ((), (), s32[]{:S(2)}) async-start(), calls=%async_computation.1 | async-start | bytes 4718592 | tf_op jit(solution)/shard_map/all_gather | solution.py:218
  9.1 67.1 %collective-permute-start.9 = (bf16[512,512]{1,0:T(8,128)(2,1)}, bf16[512,512]{1,0:T(8,128)(2,1)}, u32[]{:S(2)}, u32[]{:S(2)}) collective-permute-start(bf16[512,512]{1,0:T(8,128)(2,1)} %slice.169), channel_id=1, source_target_pairs={{0,1},{1,0},{2,3},{3,2},{4,5},{5,4},{6,7},{7,6},{8,9},{9,8},{10,11... | collective-permute-start | bytes 1572872 | tf_op jit(solution)/shard_map/ppermute | solution.py:41
  14.5 40.4 %collective-permute-start = (f32[2,128,512]{2,1,0:T(8,128)}, f32[2,128,512]{2,1,0:T(8,128)}, u32[]{:S(2)}, u32[]{:S(2)}) collective-permute-start(f32[2,128,512]{2,1,0:T(8,128)} %broadcast_multiply_fusion.3), channel_id=1, source_target_pairs={{0,8},{8,0},{16,24},{24,16},{32,40},{40,32},{48,56},{56,48},{64,72... | collective-permute-start | bytes 1572872 | tf_op jit(solution)/shard_map/ppermute | solution.py:18
  18.4 79.4 %collective-permute-start.7 = (bf16[512,512]{0,1:T(8,128)(2,1)}, bf16[512,512]{0,1:T(8,128)(2,1)}, u32[]{:S(2)}, u32[]{:S(2)}) collective-permute-start(bf16[512,512]{0,1:T(8,128)(2,1)} %copy.289), channel_id=1, source_target_pairs={{0,7},{1,0},{2,1},{3,2},{4,3},{5,4},{6,5},{7,6},{16,23},{17,16},{1... | collective-permute-start | bytes 1572872 | tf_op jit(solution)/shard_map/ppermute | solution.py:90
  24.3 77.8 %collective-permute-start.4 = (bf16[512,512]{0,1:T(8,128)(2,1)}, bf16[512,512]{0,1:T(8,128)(2,1)}, u32[]{:S(2)}, u32[]{:S(2)}) collective-permute-start(bf16[512,512]{0,1:T(8,128)(2,1)} %copy.286), channel_id=1, source_target_pairs={{0,1},{1,2},{2,3},{3,4},{4,5},{5,6},{6,7},{7,0},{8,10},{9,11},{10,... | collective-permute-start | bytes 1572872 | tf_op jit(solution)/shard_map/ppermute | solution.py:90
  58.1 13.8 %collective-permute-start.1 = (f32[2,128,512]{2,1,0:T(8,128)S(1)}, f32[2,128,512]{2,1,0:T(8,128)S(1)}, u32[]{:S(2)}, u32[]{:S(2)}) collective-permute-start(f32[2,128,512]{2,1,0:T(8,128)S(1)} %copy_multiply_fusion.2), channel_id=1, source_target_pairs={{0,16},{8,24},{16,0},{24,8},{32,48},{40,56},{48,32},{56,40},{64,80... | collective-permute-start | bytes 1572872 | tf_op jit(solution)/shard_map/ppermute | solution.py:18
  74.2 20.2 %collective-permute-start.2 = (f32[2,128,512]{2,1,0:T(8,128)}, f32[2,128,512]{2,1,0:T(8,128)}, u32[]{:S(2)}, u32[]{:S(2)}) collective-permute-start(f32[2,128,512]{2,1,0:T(8,128)} %copy_multiply_fusion.1), channel_id=1, source_target_pairs={{0,32},{8,40},{16,48},{24,56},{32,0},{40,8},{48,16},{56,24},{64,96... | collective-permute-start | bytes 1572872 | tf_op jit(solution)/shard_map/ppermute | solution.py:18
  79.7 50.2 %collective-permute-start.10 = (bf16[512,1024]{1,0:T(8,128)(2,1)}, bf16[512,1024]{1,0:T(8,128)(2,1)S(1)}, u32[]{:S(2)}, u32[]{:S(2)}) collective-permute-start(bf16[512,1024]{1,0:T(8,128)(2,1)} %get-tuple-element.89), channel_id=1, source_target_pairs={{0,6},{1,7},{2,0},{3,1},{4,2},{5,3},{6,4},{7,5},{8,14},{9,15},{10,... | collective-permute-start | bytes 3145736 | tf_op jit(solution)/shard_map/ppermute | solution.py:49
  81.4 51.3 %collective-permute-start.11 = (bf16[512,1024]{1,0:T(8,128)(2,1)}, bf16[512,1024]{1,0:T(8,128)(2,1)S(1)}, u32[]{:S(2)}, u32[]{:S(2)}) collective-permute-start(bf16[512,1024]{1,0:T(8,128)(2,1)} %get-tuple-element.89), channel_id=1, source_target_pairs={{0,2},{1,3},{2,4},{3,5},{4,6},{5,7},{6,0},{7,1},{8,10},{9,11},{10,... | collective-permute-start | bytes 3145736 | tf_op jit(solution)/shard_map/ppermute | solution.py:48
  94.4 13.5 %collective-permute-start.5 = (bf16[512,512]{0,1:T(8,128)(2,1)}, bf16[512,512]{0,1:T(8,128)(2,1)}, u32[]{:S(2)}, u32[]{:S(2)}) collective-permute-start(bf16[512,512]{0,1:T(8,128)(2,1)} %copy.287), channel_id=1, source_target_pairs={{0,3},{1,4},{2,5},{3,6},{4,7},{5,0},{6,1},{7,2},{8,12},{9,13},{10,... | collective-permute-start | bytes 1572872 | tf_op jit(solution)/shard_map/ppermute | solution.py:90
  97.8 14.6 %collective-permute-start.6 = (bf16[512,512]{0,1:T(8,128)(2,1)}, bf16[512,512]{0,1:T(8,128)(2,1)}, u32[]{:S(2)}, u32[]{:S(2)}) collective-permute-start(bf16[512,512]{0,1:T(8,128)(2,1)} %copy.288), channel_id=1, source_target_pairs={{0,5},{1,6},{2,7},{3,0},{4,1},{5,2},{6,3},{7,4},{8,14},{9,15},{10,... | collective-permute-start | bytes 1572872 | tf_op jit(solution)/shard_map/ppermute | solution.py:90
  102.1 32.9 %collective-permute-start.3 = (bf16[2,128,512]{2,1,0:T(8,128)(2,1)S(1)}, bf16[2,128,512]{2,1,0:T(8,128)(2,1)}, u32[]{:S(2)}, u32[]{:S(2)}) collective-permute-start(bf16[2,128,512]{2,1,0:T(8,128)(2,1)S(1)} %copy_multiply_fusion), channel_id=1, source_target_pairs={{0,64},{8,72},{16,80},{24,88},{32,96},{40,104},{48,112},{56,120},{... | collective-permute-start | bytes 786440 | tf_op jit(solution)/shard_map/ppermute | solution.py:18
  107.9 302.2 %reduce-scatter.2.cloned.1.call-start = ((), (), s32[]{:S(2)}) async-start(), calls=%async_computation.2 | async-start | bytes 8912896 | tf_op jit(solution)/shard_map/reduce_scatter | solution.py:228
  115.5 64.6 %collective-permute-start.8 = (bf16[4,512,512]{1,2,0:T(8,128)(2,1)}, bf16[4,512,512]{1,2,0:T(8,128)(2,1)}, u32[]{:S(2)}, u32[]{:S(2)}) collective-permute-start(bf16[4,512,512]{1,2,0:T(8,128)(2,1)} %pad_maximum_fusion.10), channel_id=1, source_target_pairs={{0,8},{8,0},{16,24},{24,16},{32,40},{40,32},{48,56},{56,48},{64,72... | collective-permute-start | bytes 6291464 | tf_op jit(solution)/shard_map/ppermute | solution.py:92
  130.8 34.3 %collective-permute-start.13 = (bf16[512,512]{1,0:T(8,128)(2,1)}, bf16[512,512]{1,0:T(8,128)(2,1)}, u32[]{:S(2)}, u32[]{:S(2)}) collective-permute-start(bf16[512,512]{1,0:T(8,128)(2,1)} %slice.220), channel_id=1, source_target_pairs={{0,6},{1,7},{2,0},{3,1},{4,2},{5,3},{6,4},{7,5},{8,14},{9,15},{10,... | collective-permute-start | bytes 1572872 | tf_op jit(solution)/shard_map/ppermute | solution.py:55
  133.6 31.5 %collective-permute-start.12 = (bf16[512,512]{1,0:T(8,128)(2,1)}, bf16[512,512]{1,0:T(8,128)(2,1)}, u32[]{:S(2)}, u32[]{:S(2)}) collective-permute-start(bf16[512,512]{1,0:T(8,128)(2,1)} %slice.219), channel_id=1, source_target_pairs={{0,2},{1,3},{2,4},{3,5},{4,6},{5,7},{6,0},{7,1},{8,10},{9,11},{10,... | collective-permute-start | bytes 1572872 | tf_op jit(solution)/shard_map/ppermute | solution.py:54
  233.3 73.5 %collective-permute-start.14 = (bf16[1024,512]{0,1:T(8,128)(2,1)}, bf16[1024,512]{0,1:T(8,128)(2,1)}, u32[]{:S(2)}, u32[]{:S(2)}) collective-permute-start(bf16[1024,512]{0,1:T(8,128)(2,1)} %bitcast.164), channel_id=1, source_target_pairs={{0,1},{1,0},{2,3},{3,2},{4,5},{5,4},{6,7},{7,6},{8,9},{9,8},{10,11... | collective-permute-start | bytes 3145736 | tf_op jit(solution)/shard_map/ppermute | solution.py:41
  269.8 33.8 %collective-permute-start.19 = (f32[2,128,512]{2,1,0:T(8,128)S(1)}, f32[2,128,512]{2,1,0:T(8,128)}, u32[]{:S(2)}, u32[]{:S(2)}) collective-permute-start(f32[2,128,512]{2,1,0:T(8,128)S(1)} %fusion.56), channel_id=1, source_target_pairs={{0,64},{8,72},{16,80},{24,88},{32,96},{40,104},{48,112},{56,120},{... | collective-permute-start | bytes 1572872 | tf_op jit(solution)/shard_map/ppermute | solution.py:18
  310.0 54.2 %collective-permute-start.16 = (bf16[1024,1024]{0,1:T(8,128)(2,1)}, bf16[1024,1024]{0,1:T(8,128)(2,1)}, u32[]{:S(2)}, u32[]{:S(2)}) collective-permute-start(bf16[1024,1024]{0,1:T(8,128)(2,1)} %pad_maximum_fusion.11), channel_id=1, source_target_pairs={{0,2},{1,3},{2,4},{3,5},{4,6},{5,7},{6,0},{7,1},{8,10},{9,11},{10,... | collective-permute-start | bytes 6291464 | tf_op jit(solution)/shard_map/ppermute | solution.py:48
  311.5 56.7 %collective-permute-start.15 = (bf16[1024,1024]{0,1:T(8,128)(2,1)}, bf16[1024,1024]{0,1:T(8,128)(2,1)}, u32[]{:S(2)}, u32[]{:S(2)}) collective-permute-start(bf16[1024,1024]{0,1:T(8,128)(2,1)} %pad_maximum_fusion.11), channel_id=1, source_target_pairs={{0,6},{1,7},{2,0},{3,1},{4,2},{5,3},{6,4},{7,5},{8,14},{9,15},{10,... | collective-permute-start | bytes 6291464 | tf_op jit(solution)/shard_map/ppermute | solution.py:49
  321.4 40.4 %collective-permute-start.21 = (f32[2,128,512]{2,1,0:T(8,128)}, f32[2,128,512]{2,1,0:T(8,128)}, u32[]{:S(2)}, u32[]{:S(2)}) collective-permute-start(f32[2,128,512]{2,1,0:T(8,128)} %fusion.55), channel_id=1, source_target_pairs={{0,16},{8,24},{16,0},{24,8},{32,48},{40,56},{48,32},{56,40},{64,80... | collective-permute-start | bytes 1572872 | tf_op jit(solution)/shard_map/ppermute | solution.py:18
  366.6 24.6 %collective-permute-start.17 = (bf16[1024,512]{0,1:T(8,128)(2,1)}, bf16[1024,512]{0,1:T(8,128)(2,1)}, u32[]{:S(2)}, u32[]{:S(2)}) collective-permute-start(bf16[1024,512]{0,1:T(8,128)(2,1)} %slice.221), channel_id=1, source_target_pairs={{0,2},{1,3},{2,4},{3,5},{4,6},{5,7},{6,0},{7,1},{8,10},{9,11},{10,... | collective-permute-start | bytes 3145736 | tf_op jit(solution)/shard_map/ppermute | solution.py:54
  370.4 23.1 %collective-permute-start.18 = (bf16[1024,512]{0,1:T(8,128)(2,1)}, bf16[1024,512]{0,1:T(8,128)(2,1)}, u32[]{:S(2)}, u32[]{:S(2)}) collective-permute-start(bf16[1024,512]{0,1:T(8,128)(2,1)} %slice.222), channel_id=1, source_target_pairs={{0,6},{1,7},{2,0},{3,1},{4,2},{5,3},{6,4},{7,5},{8,14},{9,15},{10,... | collective-permute-start | bytes 3145736 | tf_op jit(solution)/shard_map/ppermute | solution.py:55
  373.2 15.3 %collective-permute-start.22 = (f32[2,128,512]{2,1,0:T(8,128)}, f32[2,128,512]{2,1,0:T(8,128)S(1)}, u32[]{:S(2)}, u32[]{:S(2)}) collective-permute-start(f32[2,128,512]{2,1,0:T(8,128)} %fusion.59), channel_id=1, source_target_pairs={{0,8},{8,0},{16,24},{24,16},{32,40},{40,32},{48,56},{56,48},{64,72... | collective-permute-start | bytes 1572872 | tf_op jit(solution)/shard_map/ppermute | solution.py:18
  (47 other events, 411.5 us)
Sparse Core Ops, SparseCore 0:
  108.0 89.1 all-gather.1
  231.8 113.9 reduce-scatter.1

commit v11 on v10

--- a/solution.py
+++ b/solution.py
@@ -212,7 +212,7 @@
     ) + jnp.einsum("bhqk,khd->bqhd", far_prob, far_value_heads, preferred_element_type=jnp.float32)
     attended = mixed.astype(jnp.bfloat16).reshape(row_count, features)
     attended, weight_cols = lax.optimization_barrier((attended, weight_columns(out_weight)))
-    half_rows = row_count // 2
+    half_rows = row_count // 4
     grads_full = jnp.concatenate(
         [
             lax.all_gather(cotangent[:half_rows], "head", axis=1, tiled=True),

time: 423 us -> 425 us (level)
  waiting for transfers between devices: 31.7 us -> 50.5 us
  starting transfers between devices: 51.6 us -> 36.9 us
    ppermute x8, waiting for transfers between devices: 11.6 us -> 29.5 us  [swapped(): return lax.ppermute(value, axis, pairs)]
    ppermute x1, starting transfers between devices: 13.3 us -> 0.01 us  [weight_columns(): lax.ppermute(mine, 'seq', [(src, src ^ 1) for src in range(seq_count)])]
    all_gather x1, waiting for transfers between devices: 10.7 us -> 0.01 us  [body(): lax.all_gather(cotangent[:half_rows], 'head', axis=1, tiled=True)]
    ppermute x2, waiting for transfers between devices: 2.28 us -> 10.5 us  [head_ring_gather(): lax.ppermute(from_above[..., width:], 'head', downward)]
    ppermute x8, starting transfers between devices: 15.9 us -> 10.2 us  [swapped(): return lax.ppermute(value, axis, pairs)]
    ppermute x4, waiting for transfers between devices: 4.43 us -> 0.01 us  [weight_columns(): fetched.append(lax.ppermute(outgoing, ('seq', 'head'), pairs))]
    unnamed x105 -> x101, local copies, waits for them, and re-layouts: 35.2 us -> 32.2 us
  transfers between devices with their start and end apart: 25 -> 25, of which waited for: 6 -> 8; matrix products, arithmetic and copies ran while one was open for 66% -> 65% of each run, Pallas kernels for 0% -> 0%
where the time goes in v11:
time: 425 us; the launch traced here: 418 us
  local copies, waits for them, and re-layouts  128 us (30%)
  other arithmetic  112 us (26%)
  matrix products  75.4 us (18%)
  waiting for transfers between devices  50.5 us (12%)
  starting transfers between devices  36.9 us (9%)
  between operations  15.2 us (4%)
    unnamed x101, local copies, waits for them, and re-layouts  32.2 us
    ppermute x8, waiting for transfers between devices, swapped(): return lax.ppermute(value, axis, pairs)  29.5 us
    sub x1, other arithmetic, body(): grad_score = (attn_prob * (grad_prob - row_delta)).astype(jnp.bfloat16)  29 us
    ppermute x2, waiting for transfers between devices, head_ring_gather(): lax.ppermute(from_above[..., width:], 'head', downward)  10.5 us
    ppermute x4, starting transfers between devices, weight_columns(): fetched.append(lax.ppermute(outgoing, ('seq', 'head'), pairs))  10.4 us
    ppermute x8, starting transfers between devices, swapped(): return lax.ppermute(value, axis, pairs)  10.2 us
    slice x2, local copies, waits for them, and re-layouts, body(): value_heads = key_set[1].reshape(blocks, near_keys, head_count, DH)  10.2 us
    reshape x2, local copies, waits for them, and re-layouts, spread_rows(): return wide.reshape(shape_in[:-2] + (shape_in[-2] * factor, shape_in[-1]))  10.1 us
  transfers between devices with their start and end apart: 25, of which 8 were waited for; matrix products, arithmetic and copies ran while one was open for 65% of the time, Pallas kernels for 0%

profile of v11, /device:TPU:0, one launch (start us, length us, event | category | flops | bytes accessed | tf_op | source)
XLA Modules:
  0.0 418.4 jit_solution(16845849462348341462)
XLA Ops:
  16.9 6.0 %collective-permute-start.7 = (bf16[512,512]{0,1:T(8,128)(2,1)}, bf16[512,512]{0,1:T(8,128)(2,1)}, u32[]{:S(2)}, u32[]{:S(2)}) collective-permute-start(bf16[512,512]{0,1:T(8,128)(2,1)} %copy.289), channel_id=1, source_target_pairs={{0,7},{1,0},{2,1},{3,2},{4,3},{5,4},{6,5},{7,6},{16,23},{17,16},{1... | collective-permute-start | bytes 1572872 | tf_op jit(solution)/shard_map/ppermute | solution.py:90
  43.1 5.8 %convert_reduce_fusion.2 = f32[2,512,512]{2,1,0:T(8,128)S(1)} fusion(bf16[1,512,2,512]{3,2,1,0:T(2,128)(2,1)S(1)} %copy-done.26, bf16[1,512,2,512]{3,2,1,0:T(2,128)(2,1)S(1)} %copy-done.25), kind=kLoop, calls=%fused_computation.42 | loop fusion | flops 2621440 | bytes 4194304 | tf_op jit(solution)/shard_map/reduce_sum | solution.py:152
  57.3 6.7 %copy.209 = bf16[1,8,512,512]{2,3,1,0:T(8,128)(2,1)} copy(bf16[1,8,512,512]{3,2,1,0:T(8,128)(2,1)} %get-tuple-element.54) | data formatting | bytes 8388608 | tf_op jit(solution)/shard_map/slice | solution.py:185
  70.1 4.6 %convolution_bitcast_fusion.2 = f32[8,4,128,512]{2,3,1,0:T(8,128)} fusion(bf16[8,512,4,128]{1,3,2,0:T(8,128)(2,1)S(1)} %bitcast.165, bf16[8,128,4,128]{1,3,2,0:T(8,128)(2,1)S(1)} %copy.238), kind=kOutput, calls=%fused_computation.57 | convolution fusion | flops 536870912 | bytes 13631488 | tf_op jit(solution)/shard_map/bqhd,bkhd->bhqk/dot_general | solution.py:192
  74.7 23.1 %collective-permute-done.1 = f32[2,128,512]{2,1,0:T(8,128)S(1)} collective-permute-done((f32[2,128,512]{2,1,0:T(8,128)S(1)}, f32[2,128,512]{2,1,0:T(8,128)S(1)}, u32[]{:S(2)}, u32[]{:S(2)}) %collective-permute-start.1) | collective-permute-done | bytes 524320 | tf_op jit(solution)/shard_map/ppermute | solution.py:18
  103.6 6.5 %copy.207 = bf16[1,8,512,512]{2,3,1,0:T(8,128)(2,1)} copy(bf16[1,8,512,512]{3,2,1,0:T(8,128)(2,1)} %get-tuple-element.53) | data formatting | bytes 8388608 | tf_op jit(solution)/shard_map/slice | solution.py:186
  130.9 8.3 %fusion.81 = (f32[8,4,128]{2,1,0:T(4,128)S(1)}, f32[8,4,128,1024]{2,3,1,0:T(8,128)S(1)}) fusion(f32[8,4,128,512]{2,3,1,0:T(8,128)S(1)} %convolution_bitcast_fusion.1, f32[8,4,128,512]{2,3,1,0:T(8,128)} %convolution_bitcast_fusion.2, f32[1024]{0:T(1024)S(1)} %copy-done.41, pred[8,1024]{1,0:T(8,128)(4,1)S(1)} %concatenate.101), kind=kOutput, calls=%fused_computation.169 | output fusion | flops 25166848 | bytes 33583104 | tf_op jit(solution)/shard_map/sub | solution.py:206
  172.8 9.0 %collective-permute-done.13 = bf16[768,512]{1,0:T(8,128)(2,1)S(1)} collective-permute-done((bf16[768,512]{1,0:T(8,128)(2,1)S(1)}, bf16[768,512]{1,0:T(8,128)(2,1)S(1)}, u32[]{:S(2)}, u32[]{:S(2)}) %collective-permute-start.13) | collective-permute-done | bytes 786464 | tf_op jit(solution)/shard_map/ppermute | solution.py:55
  181.8 4.7 %collective-permute-done.12 = bf16[768,512]{1,0:T(8,128)(2,1)S(1)} collective-permute-done((bf16[768,512]{1,0:T(8,128)(2,1)S(1)}, bf16[768,512]{1,0:T(8,128)(2,1)S(1)}, u32[]{:S(2)}, u32[]{:S(2)}) %collective-permute-start.12) | collective-permute-done | bytes 786464 | tf_op jit(solution)/shard_map/ppermute | solution.py:54
  186.6 5.1 %pad_maximum_fusion.4 = bf16[4,768,1024]{2,1,0:T(8,128)(2,1)} fusion(bf16[1,768,1024]{2,1,0:T(8,128)(2,1)} %bitcast.41, bf16[1,768,1024]{2,1,0:T(8,128)(2,1)S(1)} %maximum_bitcast_fusion, bf16[1,768,1024]{2,1,0:T(8,128)(2,1)} %bitcast.39, bf16[1,768,1024]{2,1,0:T(8,128)(2,1)S(1)} %get-tuple-element.79), kind=kLoop, calls=%fused_computation.25 | loop fusion | flops 9437184 | bytes 12582912 | tf_op jit(solution)/shard_map/stack | solution.py:62
  191.7 6.4 %gather_fusion = bf16[4,768,1024]{2,1,0:T(8,128)(2,1)} fusion(bf16[4,768,1024]{2,1,0:T(8,128)(2,1)} %pad_maximum_fusion.4, s32[1024]{0:T(1024)S(1)} %pad_clamp_fusion), kind=kCustom, calls=%fused_computation | custom fusion | bytes 12582928 | tf_op jit(solution)/shard_map/gather | solution.py:64
  198.0 8.6 %copy.231 = bf16[768,4,1024]{0,2,1:T(8,128)(2,1)} copy(bf16[768,4,1024]{2,0,1:T(8,128)(2,1)} %bitcast.179) | data formatting | bytes 12582912 | tf_op jit(solution)/shard_map/transpose | solution.py:65
  206.7 9.2 %fusion.45 = bf16[1024,512]{1,0:T(8,128)(2,1)S(1)} fusion(bf16[512,4096]{1,0:T(8,128)(2,1)} %param.9, bf16[768,4096]{0,1:T(8,128)(2,1)} %bitcast.187, bf16[256,4096]{0,1:T(8,128)(2,1)} %all-gather.2.cloned.1.call-done), kind=kOutput, calls=%fused_computation.85 | convolution fusion | flops 4312268800 | bytes 13631488 | tf_op jit(solution)/shard_map/dot_general | solution.py:223
  216.9 5.1 %fusion.20 = f32[4,128,512,1]{2,1,3,0:T(8,128)} fusion(bf16[8,128,4,128]{3,2,1,0:T(4,128)(2,1)S(1)} %reshape.232, bf16[8,4,128,1024]{2,3,1,0:T(8,128)(2,1)} %fusion.70), kind=kOutput, calls=%fused_computation.37 | convolution fusion | flops 536870912 | bytes 6291456 | tf_op jit(solution)/shard_map/bhqk,bqhd->khd/dot_general | solution.py:278
  222.0 4.6 %fusion.82 = f32[8,4,128,512]{2,3,1,0:T(8,128)} fusion(bf16[8,128,4,128]{1,3,2,0:T(8,128)(2,1)S(1)} %copy.257, bf16[8,512,4,128]{1,3,2,0:T(8,128)(2,1)S(1)} %bitcast.176), kind=kOutput, calls=%fused_computation.170 | convolution fusion | flops 536870912 | bytes 13631488 | tf_op jit(solution)/shard_map/bqhd,bkhd->bhqk/dot_general | solution.py:239
  226.6 4.6 %convolution_bitcast_fusion = f32[8,4,128,512]{2,3,1,0:T(8,128)} fusion(bf16[512,4,128,1]{0,2,1,3:T(8,128)(2,1)S(1)} %bitcast.192, bf16[8,128,4,128]{1,3,2,0:T(8,128)(2,1)S(1)} %copy.257), kind=kOutput, calls=%fused_computation.55 | convolution fusion | flops 536870912 | bytes 9961472 | tf_op jit(solution)/shard_map/bqhd,khd->bhqk/dot_general | solution.py:242
  231.1 8.3 %fusion.13 = f32[4096,512]{1,0:T(8,128)} fusion(bf16[1024,512]{0,1:T(8,128)(2,1)} %bitcast.164, bf16[768,4096]{0,1:T(8,128)(2,1)S(1)} %bitcast.190, bf16[256,4096]{0,1:T(8,128)(2,1)S(1)} %copy-done.40), kind=kOutput, calls=%fused_computation.26 | convolution fusion | flops 4311744512 | bytes 17825792 | tf_op jit(solution)/shard_map/dot_general | solution.py:229
  241.7 29.0 %multiply_convert_fusion = bf16[8,4,128,1024]{2,3,1,0:T(8,128)(2,1)} fusion(f32[8,4,128,512]{2,3,1,0:T(8,128)} %convolution_bitcast_fusion, f32[8,4,128,512]{2,3,1,0:T(8,128)} %fusion.82, f32[8,4,128,1024]{2,3,1,0:T(8,128)} %copy-done.12, f32[8,4,128]{2,1,0:T(4,128)S(1)} %get-tuple-element.99), kind=kOutput, calls=%fused_computation.13 | output fusion | flops 33559552 | bytes 41959424 | tf_op jit(solution)/shard_map/sub | solution.py:249
  270.7 5.1 %fusion.49 = f32[4,512,128]{1,2,0:T(8,128)} fusion(bf16[8,128,4,128]{1,3,2,0:T(8,128)(2,1)S(1)} %copy-done.9, bf16[8,4,128,1024]{2,3,1,0:T(8,128)(2,1)} %multiply_convert_fusion), kind=kOutput, calls=%fused_computation.87 | convolution fusion | flops 537133056 | bytes 6291456 | tf_op jit(solution)/shard_map/bhqk,bqhd->khd/dot_general | solution.py:275
  285.4 7.4 %fusion.16 = (f32[2,8,128,512]{2,3,1,0:T(8,128)}, f32[2,8,128,512]{2,3,1,0:T(8,128)}, f32[2,8,128,512]{2,3,1,0:T(8,128)}, f32[2,8,128,512]{2,3,1,0:T(8,128)}) fusion(f32[1,8,512,512]{2,3,1,0:T(8,128)S(1)} %bitcast.178, f32[1,8,512,512]{2,3,1,0:T(8,128)S(1)} %bitcast.177), kind=kLoop, calls=%fused_computation.29 | loop fusion | flops 4194304 | bytes 33554432 | tf_op jit(solution)/shard_map/stack | solution.py:273
  304.1 4.6 %fusion.72 = (f32[2,4,1,128,512]{3,4,2,1,0:T(8,128)}, f32[2,4,1,128,512]{3,4,2,1,0:T(8,128)}) fusion(f32[2,4,2,128,512]{3,4,2,1,0:T(8,128)} %bitcast.181), kind=kLoop, calls=%fused_computation.160 | loop fusion | bytes 8388608 | tf_op jit(solution)/shard_map/slice | solution.py:294
  318.0 5.4 %collective-permute-done.20 = f32[2,128,512]{2,1,0:T(8,128)S(1)} collective-permute-done((f32[2,128,512]{2,1,0:T(8,128)S(1)}, f32[2,128,512]{2,1,0:T(8,128)S(1)}, u32[]{:S(2)}, u32[]{:S(2)}) %collective-permute-start.20) | collective-permute-done | bytes 524320 | tf_op jit(solution)/shard_map/ppermute | solution.py:18
  333.0 5.4 %copy.259 = f32[2,8,128,512]{3,2,1,0:T(8,128)} copy(f32[2,8,128,512]{2,3,1,0:T(8,128)} %get-tuple-element.49) | data formatting | bytes 8388608 | tf_op jit(solution)/shard_map/slice | solution.py:282
  380.0 6.4 %reshape.246 = f32[2,1024,512]{2,1,0:T(8,128)} reshape(f32[2,512,2,512]{3,2,1,0:T(2,128)} %broadcast_in_dim.45) | data formatting | bytes 8388608 | tf_op jit(solution)/shard_map/reshape | solution.py:32
  (258 shorter events, 213.3 us)
Async XLA Ops:
  7.2 199.5 %all-gather.2.cloned.1.call-start = ((), (), s32[]{:S(2)}) async-start(), calls=%async_computation.1 | async-start | bytes 2359296 | tf_op jit(solution)/shard_map/all_gather | solution.py:218
  9.0 402.3 %reduce-scatter.2.cloned.1.call-start = ((), (), s32[]{:S(2)}) async-start(), calls=%async_computation.2 | async-start | bytes 8912896 | tf_op jit(solution)/shard_map/reduce_scatter | solution.py:228
  12.9 51.1 %collective-permute-start = (f32[2,128,512]{2,1,0:T(8,128)}, f32[2,128,512]{2,1,0:T(8,128)}, u32[]{:S(2)}, u32[]{:S(2)}) collective-permute-start(f32[2,128,512]{2,1,0:T(8,128)} %broadcast_multiply_fusion.3), channel_id=1, source_target_pairs={{0,8},{8,0},{16,24},{24,16},{32,40},{40,32},{48,56},{56,48},{64,72... | collective-permute-start | bytes 1572872 | tf_op jit(solution)/shard_map/ppermute | solution.py:18
  16.9 85.1 %collective-permute-start.7 = (bf16[512,512]{0,1:T(8,128)(2,1)}, bf16[512,512]{0,1:T(8,128)(2,1)}, u32[]{:S(2)}, u32[]{:S(2)}) collective-permute-start(bf16[512,512]{0,1:T(8,128)(2,1)} %copy.289), channel_id=1, source_target_pairs={{0,7},{1,0},{2,1},{3,2},{4,3},{5,4},{6,5},{7,6},{16,23},{17,16},{1... | collective-permute-start | bytes 1572872 | tf_op jit(solution)/shard_map/ppermute | solution.py:90
  23.8 87.3 %collective-permute-start.4 = (bf16[512,512]{0,1:T(8,128)(2,1)}, bf16[512,512]{0,1:T(8,128)(2,1)}, u32[]{:S(2)}, u32[]{:S(2)}) collective-permute-start(bf16[512,512]{0,1:T(8,128)(2,1)} %copy.286), channel_id=1, source_target_pairs={{0,1},{1,2},{2,3},{3,4},{4,5},{5,6},{6,7},{7,0},{8,10},{9,11},{10,... | collective-permute-start | bytes 1572872 | tf_op jit(solution)/shard_map/ppermute | solution.py:90
  26.0 85.2 %collective-permute-start.5 = (bf16[512,512]{0,1:T(8,128)(2,1)}, bf16[512,512]{0,1:T(8,128)(2,1)}, u32[]{:S(2)}, u32[]{:S(2)}) collective-permute-start(bf16[512,512]{0,1:T(8,128)(2,1)} %copy.287), channel_id=1, source_target_pairs={{0,3},{1,4},{2,5},{3,6},{4,7},{5,0},{6,1},{7,2},{8,12},{9,13},{10,... | collective-permute-start | bytes 1572872 | tf_op jit(solution)/shard_map/ppermute | solution.py:90
  29.4 81.7 %collective-permute-start.6 = (bf16[512,512]{0,1:T(8,128)(2,1)}, bf16[512,512]{0,1:T(8,128)(2,1)}, u32[]{:S(2)}, u32[]{:S(2)}) collective-permute-start(bf16[512,512]{0,1:T(8,128)(2,1)} %copy.288), channel_id=1, source_target_pairs={{0,5},{1,6},{2,7},{3,0},{4,1},{5,2},{6,3},{7,4},{8,14},{9,15},{10,... | collective-permute-start | bytes 1572872 | tf_op jit(solution)/shard_map/ppermute | solution.py:90
  67.2 30.6 %collective-permute-start.1 = (f32[2,128,512]{2,1,0:T(8,128)S(1)}, f32[2,128,512]{2,1,0:T(8,128)S(1)}, u32[]{:S(2)}, u32[]{:S(2)}) collective-permute-start(f32[2,128,512]{2,1,0:T(8,128)S(1)} %copy_multiply_fusion.2), channel_id=1, source_target_pairs={{0,16},{8,24},{16,0},{24,8},{32,48},{40,56},{48,32},{56,40},{64,80... | collective-permute-start | bytes 1572872 | tf_op jit(solution)/shard_map/ppermute | solution.py:18
  99.3 16.2 %collective-permute-start.2 = (f32[2,128,512]{2,1,0:T(8,128)S(1)}, f32[2,128,512]{2,1,0:T(8,128)S(1)}, u32[]{:S(2)}, u32[]{:S(2)}) collective-permute-start(f32[2,128,512]{2,1,0:T(8,128)S(1)} %copy_multiply_fusion.1), channel_id=1, source_target_pairs={{0,32},{8,40},{16,48},{24,56},{32,0},{40,8},{48,16},{56,24},{64,96... | collective-permute-start | bytes 1572872 | tf_op jit(solution)/shard_map/ppermute | solution.py:18
  102.0 17.5 %collective-permute-start.9 = (bf16[768,512]{1,0:T(8,128)(2,1)}, bf16[768,512]{1,0:T(8,128)(2,1)}, u32[]{:S(2)}, u32[]{:S(2)}) collective-permute-start(bf16[768,512]{1,0:T(8,128)(2,1)} %slice.169), channel_id=1, source_target_pairs={{0,1},{1,0},{2,3},{3,2},{4,5},{5,4},{6,7},{7,6},{8,9},{9,8},{10,11... | collective-permute-start | bytes 2359304 | tf_op jit(solution)/shard_map/ppermute | solution.py:41
  114.4 52.3 %collective-permute-start.8 = (bf16[4,512,512]{1,2,0:T(8,128)(2,1)}, bf16[4,512,512]{1,2,0:T(8,128)(2,1)}, u32[]{:S(2)}, u32[]{:S(2)}) collective-permute-start(bf16[4,512,512]{1,2,0:T(8,128)(2,1)} %pad_maximum_fusion.10), channel_id=1, source_target_pairs={{0,8},{8,0},{16,24},{24,16},{32,40},{40,32},{48,56},{56,48},{64,72... | collective-permute-start | bytes 6291464 | tf_op jit(solution)/shard_map/ppermute | solution.py:92
  122.4 38.0 %collective-permute-start.10 = (bf16[768,1024]{1,0:T(8,128)(2,1)}, bf16[768,1024]{1,0:T(8,128)(2,1)}, u32[]{:S(2)}, u32[]{:S(2)}) collective-permute-start(bf16[768,1024]{1,0:T(8,128)(2,1)} %get-tuple-element.80), channel_id=1, source_target_pairs={{0,6},{1,7},{2,0},{3,1},{4,2},{5,3},{6,4},{7,5},{8,14},{9,15},{10,... | collective-permute-start | bytes 4718600 | tf_op jit(solution)/shard_map/ppermute | solution.py:49
  126.1 39.3 %collective-permute-start.11 = (bf16[768,1024]{1,0:T(8,128)(2,1)}, bf16[768,1024]{1,0:T(8,128)(2,1)}, u32[]{:S(2)}, u32[]{:S(2)}) collective-permute-start(bf16[768,1024]{1,0:T(8,128)(2,1)} %get-tuple-element.80), channel_id=1, source_target_pairs={{0,2},{1,3},{2,4},{3,5},{4,6},{5,7},{6,0},{7,1},{8,10},{9,11},{10,... | collective-permute-start | bytes 4718600 | tf_op jit(solution)/shard_map/ppermute | solution.py:48
  161.7 20.1 %collective-permute-start.13 = (bf16[768,512]{1,0:T(8,128)(2,1)S(1)}, bf16[768,512]{1,0:T(8,128)(2,1)S(1)}, u32[]{:S(2)}, u32[]{:S(2)}) collective-permute-start(bf16[768,512]{1,0:T(8,128)(2,1)S(1)} %slice.220), channel_id=1, source_target_pairs={{0,6},{1,7},{2,0},{3,1},{4,2},{5,3},{6,4},{7,5},{8,14},{9,15},{10,... | collective-permute-start | bytes 2359304 | tf_op jit(solution)/shard_map/ppermute | solution.py:55
  166.6 19.8 %collective-permute-start.12 = (bf16[768,512]{1,0:T(8,128)(2,1)S(1)}, bf16[768,512]{1,0:T(8,128)(2,1)S(1)}, u32[]{:S(2)}, u32[]{:S(2)}) collective-permute-start(bf16[768,512]{1,0:T(8,128)(2,1)S(1)} %slice.219), channel_id=1, source_target_pairs={{0,2},{1,3},{2,4},{3,5},{4,6},{5,7},{6,0},{7,1},{8,10},{9,11},{10,... | collective-permute-start | bytes 2359304 | tf_op jit(solution)/shard_map/ppermute | solution.py:54
  241.0 70.4 %collective-permute-start.14 = (bf16[1024,512]{0,1:T(8,128)(2,1)}, bf16[1024,512]{0,1:T(8,128)(2,1)}, u32[]{:S(2)}, u32[]{:S(2)}) collective-permute-start(bf16[1024,512]{0,1:T(8,128)(2,1)} %bitcast.164), channel_id=1, source_target_pairs={{0,1},{1,0},{2,3},{3,2},{4,5},{5,4},{6,7},{7,6},{8,9},{9,8},{10,11... | collective-permute-start | bytes 3145736 | tf_op jit(solution)/shard_map/ppermute | solution.py:41
  277.3 31.4 %collective-permute-start.19 = (f32[2,128,512]{2,1,0:T(8,128)S(1)}, f32[2,128,512]{2,1,0:T(8,128)}, u32[]{:S(2)}, u32[]{:S(2)}) collective-permute-start(f32[2,128,512]{2,1,0:T(8,128)S(1)} %fusion.56), channel_id=1, source_target_pairs={{0,64},{8,72},{16,80},{24,88},{32,96},{40,104},{48,112},{56,120},{... | collective-permute-start | bytes 1572872 | tf_op jit(solution)/shard_map/ppermute | solution.py:18
  311.2 12.2 %collective-permute-start.20 = (f32[2,128,512]{2,1,0:T(8,128)S(1)}, f32[2,128,512]{2,1,0:T(8,128)S(1)}, u32[]{:S(2)}, u32[]{:S(2)}) collective-permute-start(f32[2,128,512]{2,1,0:T(8,128)S(1)} %fusion.58), channel_id=1, source_target_pairs={{0,32},{8,40},{16,48},{24,56},{32,0},{40,8},{48,16},{56,24},{64,96... | collective-permute-start | bytes 1572872 | tf_op jit(solution)/shard_map/ppermute | solution.py:18
  314.7 52.3 %collective-permute-start.16 = (bf16[1024,1024]{0,1:T(8,128)(2,1)}, bf16[1024,1024]{0,1:T(8,128)(2,1)}, u32[]{:S(2)}, u32[]{:S(2)}) collective-permute-start(bf16[1024,1024]{0,1:T(8,128)(2,1)} %pad_maximum_fusion.11), channel_id=1, source_target_pairs={{0,2},{1,3},{2,4},{3,5},{4,6},{5,7},{6,0},{7,1},{8,10},{9,11},{10,... | collective-permute-start | bytes 6291464 | tf_op jit(solution)/shard_map/ppermute | solution.py:48
  314.7 54.8 %collective-permute-start.15 = (bf16[1024,1024]{0,1:T(8,128)(2,1)}, bf16[1024,1024]{0,1:T(8,128)(2,1)}, u32[]{:S(2)}, u32[]{:S(2)}) collective-permute-start(bf16[1024,1024]{0,1:T(8,128)(2,1)} %pad_maximum_fusion.11), channel_id=1, source_target_pairs={{0,6},{1,7},{2,0},{3,1},{4,2},{5,3},{6,4},{7,5},{8,14},{9,15},{10,... | collective-permute-start | bytes 6291464 | tf_op jit(solution)/shard_map/ppermute | solution.py:49
  325.8 38.9 %collective-permute-start.21 = (f32[2,128,512]{2,1,0:T(8,128)}, f32[2,128,512]{2,1,0:T(8,128)}, u32[]{:S(2)}, u32[]{:S(2)}) collective-permute-start(f32[2,128,512]{2,1,0:T(8,128)} %fusion.55), channel_id=1, source_target_pairs={{0,16},{8,24},{16,0},{24,8},{32,48},{40,56},{48,32},{56,40},{64,80... | collective-permute-start | bytes 1572872 | tf_op jit(solution)/shard_map/ppermute | solution.py:18
  369.5 23.8 %collective-permute-start.17 = (bf16[1024,512]{0,1:T(8,128)(2,1)}, bf16[1024,512]{0,1:T(8,128)(2,1)}, u32[]{:S(2)}, u32[]{:S(2)}) collective-permute-start(bf16[1024,512]{0,1:T(8,128)(2,1)} %slice.221), channel_id=1, source_target_pairs={{0,2},{1,3},{2,4},{3,5},{4,6},{5,7},{6,0},{7,1},{8,10},{9,11},{10,... | collective-permute-start | bytes 3145736 | tf_op jit(solution)/shard_map/ppermute | solution.py:54
  371.8 23.0 %collective-permute-start.18 = (bf16[1024,512]{0,1:T(8,128)(2,1)}, bf16[1024,512]{0,1:T(8,128)(2,1)}, u32[]{:S(2)}, u32[]{:S(2)}) collective-permute-start(bf16[1024,512]{0,1:T(8,128)(2,1)} %slice.222), channel_id=1, source_target_pairs={{0,6},{1,7},{2,0},{3,1},{4,2},{5,3},{6,4},{7,5},{8,14},{9,15},{10,... | collective-permute-start | bytes 3145736 | tf_op jit(solution)/shard_map/ppermute | solution.py:55
  376.0 15.2 %collective-permute-start.22 = (f32[2,128,512]{2,1,0:T(8,128)}, f32[2,128,512]{2,1,0:T(8,128)S(1)}, u32[]{:S(2)}, u32[]{:S(2)}) collective-permute-start(f32[2,128,512]{2,1,0:T(8,128)} %fusion.59), channel_id=1, source_target_pairs={{0,8},{8,0},{16,24},{24,16},{32,40},{40,32},{48,56},{56,48},{64,72... | collective-permute-start | bytes 1572872 | tf_op jit(solution)/shard_map/ppermute | solution.py:18
  (45 other events, 382.6 us)
Sparse Core Ops, SparseCore 0:
  9.6 78.9 all-gather.1
  239.6 108.8 reduce-scatter.1

commit v12 on v10

--- a/solution.py
+++ b/solution.py
@@ -40,9 +40,12 @@
     ring_pos = where_head // 2
     partner = lax.ppermute(value, "head", [(src, src ^ 1) for src in range(count)])
     low_first = where_head % 2 == 0
-    pair_block = jnp.concatenate(
-        [jnp.where(low_first, value, partner), jnp.where(low_first, partner, value)], axis=-1
-    )
+    if relative:
+        pair_block = jnp.concatenate([value, partner], axis=-1)
+    else:
+        pair_block = jnp.concatenate(
+            [jnp.where(low_first, value, partner), jnp.where(low_first, partner, value)], axis=-1
+        )
     upward = [(src, ((src // 2 + 1) % rings) * 2 + src % 2) for src in range(count)]
     downward = [(src, ((src // 2 - 1) % rings) * 2 + src % 2) for src in range(count)]
     from_below = lax.ppermute(pair_block, "head", upward)
@@ -99,14 +102,16 @@
     ring_blocks = []
     for dist in range(count // 2):
         ring_blocks.append(
-            jnp.where(
-                low_first,
-                jnp.concatenate(
-                    [by_shift[(-2 * dist) % count], by_shift[(-1 - 2 * dist) % count]], axis=0
-                ),
-                jnp.concatenate(
-                    [by_shift[(1 - 2 * dist) % count], by_shift[(-2 * dist) % count]], axis=0
-                ),
+            jnp.concatenate(
+                [
+                    by_shift[(-2 * dist) % count],
+                    jnp.where(
+                        low_first,
+                        by_shift[(-1 - 2 * dist) % count],
+                        by_shift[(1 - 2 * dist) % count],
+                    ),
+                ],
+                axis=0,
             )
         )
     return ring_blocks

time: 423 us -> 413 us (0.976)
  local copies, waits for them, and re-layouts: 127 us -> 120 us
  waiting for transfers between devices: 31.7 us -> 26.5 us
    unnamed x105 -> x103, local copies, waits for them, and re-layouts: 35.2 us -> 28.6 us
  transfers between devices with their start and end apart: 25 -> 25, of which waited for: 6 -> 6; matrix products, arithmetic and copies ran while one was open for 66% -> 65% of each run, Pallas kernels for 0% -> 0%
where the time goes in v12:
time: 413 us; the launch traced here: 408 us
  local copies, waits for them, and re-layouts  120 us (29%)
  other arithmetic  115 us (28%)
  matrix products  76 us (18%)
  starting transfers between devices  55.8 us (14%)
  waiting for transfers between devices  26.5 us (6%)
  between operations  15.2 us (4%)
    sub x1, other arithmetic, body(): grad_score = (attn_prob * (grad_prob - row_delta)).astype(jnp.bfloat16)  29.7 us
    unnamed x103, local copies, waits for them, and re-layouts  28.6 us
    ppermute x1, starting transfers between devices, weight_columns(): lax.ppermute(mine, 'seq', [(src, src ^ 1) for src in range(seq_count)])  17.4 us
    ppermute x8, starting transfers between devices, swapped(): return lax.ppermute(value, axis, pairs)  15.8 us
    ppermute x8, waiting for transfers between devices, swapped(): return lax.ppermute(value, axis, pairs)  12.3 us
    slice x2, local copies, waits for them, and re-layouts, body(): value_heads = key_set[1].reshape(blocks, near_keys, head_count, DH)  10 us
    reshape x2, local copies, waits for them, and re-layouts, spread_rows(): return wide.reshape(shape_in[:-2] + (shape_in[-2] * factor, shape_in[-1]))  9.9 us
    ppermute x4, starting transfers between devices, weight_columns(): fetched.append(lax.ppermute(outgoing, ('seq', 'head'), pairs))  9.28 us
  transfers between devices with their start and end apart: 25, of which 6 were waited for; matrix products, arithmetic and copies ran while one was open for 65% of the time, Pallas kernels for 0%

profile of v12, /device:TPU:0, one launch (start us, length us, event | category | flops | bytes accessed | tf_op | source)
XLA Modules:
  0.0 408.2 jit_solution(15762008881767522509)
XLA Ops:
  30.6 5.8 %convert_reduce_fusion.2 = f32[2,512,512]{2,1,0:T(8,128)S(1)} fusion(bf16[1,512,2,512]{3,2,1,0:T(2,128)(2,1)S(1)} %copy-done.28, bf16[1,512,2,512]{3,2,1,0:T(2,128)(2,1)S(1)} %copy-done.27), kind=kLoop, calls=%fused_computation.42 | loop fusion | flops 2621440 | bytes 4194304 | tf_op jit(solution)/shard_map/reduce_sum | solution.py:157
  44.7 6.7 %copy.194 = bf16[1,8,512,512]{2,3,1,0:T(8,128)(2,1)} copy(bf16[1,8,512,512]{3,2,1,0:T(8,128)(2,1)} %get-tuple-element.54) | data formatting | bytes 8388608 | tf_op jit(solution)/shard_map/slice | solution.py:190
  57.8 4.6 %convolution_bitcast_fusion.2 = f32[8,4,128,512]{2,3,1,0:T(8,128)} fusion(bf16[8,512,4,128]{1,3,2,0:T(8,128)(2,1)S(1)} %bitcast.165, bf16[8,128,4,128]{1,3,2,0:T(8,128)(2,1)S(1)} %copy.218), kind=kOutput, calls=%fused_computation.57 | convolution fusion | flops 536870912 | bytes 13631488 | tf_op jit(solution)/shard_map/bqhd,bkhd->bhqk/dot_general | solution.py:197
  62.4 8.1 %collective-permute-done.1 = f32[2,128,512]{2,1,0:T(8,128)S(1)} collective-permute-done((f32[2,128,512]{2,1,0:T(8,128)S(1)}, f32[2,128,512]{2,1,0:T(8,128)S(1)}, u32[]{:S(2)}, u32[]{:S(2)}) %collective-permute-start.1) | collective-permute-done | bytes 524320 | tf_op jit(solution)/shard_map/ppermute | solution.py:18
  80.3 6.5 %copy.192 = bf16[1,8,512,512]{2,3,1,0:T(8,128)(2,1)} copy(bf16[1,8,512,512]{3,2,1,0:T(8,128)(2,1)} %get-tuple-element.53) | data formatting | bytes 8388608 | tf_op jit(solution)/shard_map/slice | solution.py:191
  89.3 5.5 %collective-permute-start.7 = (bf16[512,512]{1,0:T(8,128)(2,1)}, bf16[512,512]{1,0:T(8,128)(2,1)}, u32[]{:S(2)}, u32[]{:S(2)}) collective-permute-start(bf16[512,512]{1,0:T(8,128)(2,1)} %get-tuple-element.63), channel_id=1, source_target_pairs={{0,7},{1,0},{2,1},{3,2},{4,3},{5,4},{6,5},{7,6},{16,23},{17,16},{1... | collective-permute-start | bytes 1572872 | tf_op jit(solution)/shard_map/ppermute | solution.py:93
  105.6 17.4 %collective-permute-start.8 = (bf16[4,512,512]{2,1,0:T(8,128)(2,1)}, bf16[4,512,512]{2,1,0:T(8,128)(2,1)}, u32[]{:S(2)}, u32[]{:S(2)}) collective-permute-start(bf16[4,512,512]{2,1,0:T(8,128)(2,1)} %pad_maximum_fusion.10), channel_id=1, source_target_pairs={{0,8},{8,0},{16,24},{24,16},{32,40},{40,32},{48,56},{56,48},{64,72... | collective-permute-start | bytes 6291464 | tf_op jit(solution)/shard_map/ppermute | solution.py:95
  134.2 7.8 %fusion.81 = (f32[8,4,128]{2,1,0:T(4,128)S(1)}, f32[8,4,128,1024]{2,3,1,0:T(8,128)S(1)}) fusion(f32[8,4,128,512]{2,3,1,0:T(8,128)S(1)} %convolution_bitcast_fusion.1, f32[8,4,128,512]{2,3,1,0:T(8,128)} %convolution_bitcast_fusion.2, f32[1024]{0:T(1024)S(1)} %copy-done.46, pred[8,1024]{1,0:T(8,128)(4,1)S(1)} %concatenate.89), kind=kOutput, calls=%fused_computation.168 | output fusion | flops 25166848 | bytes 33583104 | tf_op jit(solution)/shard_map/sub | solution.py:211
  146.2 4.2 %copy-done.12 = f32[8,4,128,1024]{2,3,1,0:T(8,128)} copy-done((f32[8,4,128,1024]{2,3,1,0:T(8,128)}, f32[8,4,128,1024]{2,3,1,0:T(8,128)S(1)}, u32[]{:S(2)}) %copy-start.12) | copy-done | bytes 16777240
  163.3 5.0 %gather_fusion = bf16[4,512,1024]{2,1,0:T(8,128)(2,1)} fusion(bf16[4,512,1024]{2,1,0:T(8,128)(2,1)} %pad_maximum_fusion.7, s32[1024]{0:T(1024)S(1)} %pad_clamp_fusion), kind=kCustom, calls=%fused_computation | custom fusion | bytes 8388624 | tf_op jit(solution)/shard_map/gather | solution.py:67
  168.3 6.2 %copy.211 = bf16[512,4,1024]{0,2,1:T(8,128)(2,1)} copy(bf16[512,4,1024]{2,0,1:T(8,128)(2,1)} %bitcast.179) | data formatting | bytes 8388608 | tf_op jit(solution)/shard_map/transpose | solution.py:68
  181.6 8.7 %all-gather.2.cloned.1.call-done = bf16[512,4096]{0,1:T(8,128)(2,1)} async-done(((bf16[512,512]{0,1:T(8,128)(2,1)}), bf16[512,4096]{0,1:T(8,128)(2,1)}) %all-gather.2.cloned.1.call-update) | async-done | bytes 4194320 | tf_op jit(solution)/shard_map/all_gather | solution.py:223
  190.3 9.2 %fusion.45 = bf16[1024,512]{1,0:T(8,128)(2,1)S(1)} fusion(bf16[512,4096]{1,0:T(8,128)(2,1)} %param.9, bf16[512,4096]{0,1:T(8,128)(2,1)} %bitcast.194, bf16[512,4096]{0,1:T(8,128)(2,1)} %all-gather.2.cloned.1.call-done), kind=kOutput, calls=%fused_computation.82 | convolution fusion | flops 4312268800 | bytes 13631488 | tf_op jit(solution)/shard_map/dot_general | solution.py:228
  200.5 5.1 %fusion.20 = f32[4,128,512,1]{2,1,3,0:T(8,128)} fusion(bf16[8,128,4,128]{3,2,1,0:T(4,128)(2,1)S(1)} %reshape.240, bf16[8,4,128,1024]{2,3,1,0:T(8,128)(2,1)} %fusion.70), kind=kOutput, calls=%fused_computation.37 | convolution fusion | flops 536870912 | bytes 6291456 | tf_op jit(solution)/shard_map/bhqk,bqhd->khd/dot_general | solution.py:283
  205.6 4.6 %fusion.82 = f32[8,4,128,512]{2,3,1,0:T(8,128)} fusion(bf16[8,128,4,128]{1,3,2,0:T(8,128)(2,1)S(1)} %copy.237, bf16[8,512,4,128]{1,3,2,0:T(8,128)(2,1)S(1)} %bitcast.176), kind=kOutput, calls=%fused_computation.169 | convolution fusion | flops 536870912 | bytes 13631488 | tf_op jit(solution)/shard_map/bqhd,bkhd->bhqk/dot_general | solution.py:244
  210.2 5.5 %convolution_bitcast_fusion = f32[8,4,128,512]{2,3,1,0:T(8,128)} fusion(bf16[512,4,128,1]{0,2,1,3:T(8,128)(2,1)S(1)} %bitcast.188, bf16[8,128,4,128]{1,3,2,0:T(8,128)(2,1)S(1)} %copy.237), kind=kOutput, calls=%fused_computation.55 | convolution fusion | flops 536870912 | bytes 9961472 | tf_op jit(solution)/shard_map/bqhd,khd->bhqk/dot_general | solution.py:247
  216.5 8.3 %fusion.13 = f32[4096,512]{1,0:T(8,128)} fusion(bf16[1024,512]{0,1:T(8,128)(2,1)} %bitcast.164, bf16[512,4096]{0,1:T(8,128)(2,1)S(1)} %bitcast.195, bf16[512,4096]{0,1:T(8,128)(2,1)S(1)} %copy-done.45), kind=kOutput, calls=%fused_computation.25 | convolution fusion | flops 4311744512 | bytes 17825792 | tf_op jit(solution)/shard_map/dot_general | solution.py:234
  226.8 29.7 %multiply_convert_fusion = bf16[8,4,128,1024]{2,3,1,0:T(8,128)(2,1)} fusion(f32[8,4,128,512]{2,3,1,0:T(8,128)} %convolution_bitcast_fusion, f32[8,4,128,512]{2,3,1,0:T(8,128)} %fusion.82, f32[8,4,128,1024]{2,3,1,0:T(8,128)} %copy-done.12, f32[8,4,128]{2,1,0:T(4,128)S(1)} %get-tuple-element.94), kind=kOutput, calls=%fused_computation.13 | output fusion | flops 33559552 | bytes 41959424 | tf_op jit(solution)/shard_map/sub | solution.py:254
  256.4 4.6 %fusion.49 = f32[4,512,128]{1,2,0:T(8,128)} fusion(bf16[8,128,4,128]{1,3,2,0:T(8,128)(2,1)S(1)} %copy-done.9, bf16[8,4,128,1024]{2,3,1,0:T(8,128)(2,1)} %multiply_convert_fusion), kind=kOutput, calls=%fused_computation.84 | convolution fusion | flops 537133056 | bytes 6291456 | tf_op jit(solution)/shard_map/bhqk,bqhd->khd/dot_general | solution.py:280
  273.5 7.0 %fusion.16 = (f32[2,8,128,512]{2,3,1,0:T(8,128)}, f32[2,8,128,512]{2,3,1,0:T(8,128)}, f32[2,8,128,512]{2,3,1,0:T(8,128)}, f32[2,8,128,512]{2,3,1,0:T(8,128)}) fusion(f32[1,8,512,512]{2,3,1,0:T(8,128)S(1)} %bitcast.178, f32[1,8,512,512]{2,3,1,0:T(8,128)S(1)} %bitcast.177), kind=kLoop, calls=%fused_computation.28 | loop fusion | flops 4194304 | bytes 33554432 | tf_op jit(solution)/shard_map/stack | solution.py:278
  284.2 4.2 %fusion.39 = bf16[8,128,4,128]{1,3,2,0:T(8,128)(2,1)} fusion(f32[8,4,128,128]{3,2,1,0:T(8,128)S(1)} %fusion.24, bf16[512,4,128,1]{0,2,1,3:T(8,128)(2,1)S(1)} %bitcast.190, bf16[8,4,128,1024]{2,3,1,0:T(8,128)(2,1)} %multiply_convert_fusion), kind=kOutput, calls=%fused_computation.75 | convolution fusion | flops 538443776 | bytes 7864320 | tf_op jit(solution)/shard_map/bhqk,khd->bqhd/dot_general | solution.py:262
  305.9 4.2 %collective-permute-done.20 = f32[2,128,512]{2,1,0:T(8,128)S(1)} collective-permute-done((f32[2,128,512]{2,1,0:T(8,128)S(1)}, f32[2,128,512]{2,1,0:T(8,128)S(1)}, u32[]{:S(2)}, u32[]{:S(2)}) %collective-permute-start.20) | collective-permute-done | bytes 524320 | tf_op jit(solution)/shard_map/ppermute | solution.py:18
  321.2 5.4 %copy.239 = f32[2,8,128,512]{3,2,1,0:T(8,128)} copy(f32[2,8,128,512]{2,3,1,0:T(8,128)} %get-tuple-element.49) | data formatting | bytes 8388608 | tf_op jit(solution)/shard_map/slice | solution.py:287
  368.5 6.3 %reshape.254 = f32[2,1024,512]{2,1,0:T(8,128)} reshape(f32[2,512,2,512]{3,2,1,0:T(2,128)} %broadcast_in_dim.45) | data formatting | bytes 8388608 | tf_op jit(solution)/shard_map/reshape | solution.py:32
  (260 shorter events, 212.3 us)
Async XLA Ops:
  7.2 183.1 %all-gather.2.cloned.1.call-start = ((), (), s32[]{:S(2)}) async-start(), calls=%async_computation.1 | async-start | bytes 4718592 | tf_op jit(solution)/shard_map/all_gather | solution.py:223
  9.1 65.5 %collective-permute-start.9 = (bf16[512,512]{1,0:T(8,128)(2,1)}, bf16[512,512]{1,0:T(8,128)(2,1)}, u32[]{:S(2)}, u32[]{:S(2)}) collective-permute-start(bf16[512,512]{1,0:T(8,128)(2,1)} %slice.169), channel_id=1, source_target_pairs={{0,1},{1,0},{2,3},{3,2},{4,5},{5,4},{6,7},{7,6},{8,9},{9,8},{10,11... | collective-permute-start | bytes 1572872 | tf_op jit(solution)/shard_map/ppermute | solution.py:41
  14.6 36.8 %collective-permute-start = (f32[2,128,512]{2,1,0:T(8,128)}, f32[2,128,512]{2,1,0:T(8,128)}, u32[]{:S(2)}, u32[]{:S(2)}) collective-permute-start(f32[2,128,512]{2,1,0:T(8,128)} %broadcast_multiply_fusion.3), channel_id=1, source_target_pairs={{0,8},{8,0},{16,24},{24,16},{32,40},{40,32},{48,56},{56,48},{64,72... | collective-permute-start | bytes 1572872 | tf_op jit(solution)/shard_map/ppermute | solution.py:18
  17.9 71.4 %collective-permute-start.6 = (bf16[512,512]{1,0:T(8,128)(2,1)}, bf16[512,512]{1,0:T(8,128)(2,1)}, u32[]{:S(2)}, u32[]{:S(2)}) collective-permute-start(bf16[512,512]{1,0:T(8,128)(2,1)} %get-tuple-element.60), channel_id=1, source_target_pairs={{0,5},{1,6},{2,7},{3,0},{4,1},{5,2},{6,3},{7,4},{8,14},{9,15},{10,... | collective-permute-start | bytes 1572872 | tf_op jit(solution)/shard_map/ppermute | solution.py:93
  21.1 75.1 %collective-permute-start.5 = (bf16[512,512]{1,0:T(8,128)(2,1)}, bf16[512,512]{1,0:T(8,128)(2,1)}, u32[]{:S(2)}, u32[]{:S(2)}) collective-permute-start(bf16[512,512]{1,0:T(8,128)(2,1)} %get-tuple-element.61), channel_id=1, source_target_pairs={{0,3},{1,4},{2,5},{3,6},{4,7},{5,0},{6,1},{7,2},{8,12},{9,13},{10,... | collective-permute-start | bytes 1572872 | tf_op jit(solution)/shard_map/ppermute | solution.py:93
  54.7 15.8 %collective-permute-start.1 = (f32[2,128,512]{2,1,0:T(8,128)S(1)}, f32[2,128,512]{2,1,0:T(8,128)S(1)}, u32[]{:S(2)}, u32[]{:S(2)}) collective-permute-start(f32[2,128,512]{2,1,0:T(8,128)S(1)} %copy_multiply_fusion.2), channel_id=1, source_target_pairs={{0,16},{8,24},{16,0},{24,8},{32,48},{40,56},{48,32},{56,40},{64,80... | collective-permute-start | bytes 1572872 | tf_op jit(solution)/shard_map/ppermute | solution.py:18
  72.7 14.0 %collective-permute-start.2 = (f32[2,128,512]{2,1,0:T(8,128)}, f32[2,128,512]{2,1,0:T(8,128)}, u32[]{:S(2)}, u32[]{:S(2)}) collective-permute-start(f32[2,128,512]{2,1,0:T(8,128)} %copy_multiply_fusion.1), channel_id=1, source_target_pairs={{0,32},{8,40},{16,48},{24,56},{32,0},{40,8},{48,16},{56,24},{64,96... | collective-permute-start | bytes 1572872 | tf_op jit(solution)/shard_map/ppermute | solution.py:18
  78.2 45.9 %collective-permute-start.10 = (bf16[512,1024]{1,0:T(8,128)(2,1)}, bf16[512,1024]{1,0:T(8,128)(2,1)S(1)}, u32[]{:S(2)}, u32[]{:S(2)}) collective-permute-start(bf16[512,1024]{1,0:T(8,128)(2,1)} %get-tuple-element.87), channel_id=1, source_target_pairs={{0,6},{1,7},{2,0},{3,1},{4,2},{5,3},{6,4},{7,5},{8,14},{9,15},{10,... | collective-permute-start | bytes 3145736 | tf_op jit(solution)/shard_map/ppermute | solution.py:52
  79.2 47.8 %collective-permute-start.11 = (bf16[512,1024]{1,0:T(8,128)(2,1)}, bf16[512,1024]{1,0:T(8,128)(2,1)S(1)}, u32[]{:S(2)}, u32[]{:S(2)}) collective-permute-start(bf16[512,1024]{1,0:T(8,128)(2,1)} %get-tuple-element.87), channel_id=1, source_target_pairs={{0,2},{1,3},{2,4},{3,5},{4,6},{5,7},{6,0},{7,1},{8,10},{9,11},{10,... | collective-permute-start | bytes 3145736 | tf_op jit(solution)/shard_map/ppermute | solution.py:51
  86.8 15.2 %collective-permute-start.4 = (bf16[512,512]{1,0:T(8,128)(2,1)}, bf16[512,512]{1,0:T(8,128)(2,1)}, u32[]{:S(2)}, u32[]{:S(2)}) collective-permute-start(bf16[512,512]{1,0:T(8,128)(2,1)} %get-tuple-element.62), channel_id=1, source_target_pairs={{0,1},{1,2},{2,3},{3,4},{4,5},{5,6},{6,7},{7,0},{8,10},{9,11},{10,... | collective-permute-start | bytes 1572872 | tf_op jit(solution)/shard_map/ppermute | solution.py:93
  96.2 33.3 %collective-permute-start.3 = (bf16[2,128,512]{2,1,0:T(8,128)(2,1)S(1)}, bf16[2,128,512]{2,1,0:T(8,128)(2,1)}, u32[]{:S(2)}, u32[]{:S(2)}) collective-permute-start(bf16[2,128,512]{2,1,0:T(8,128)(2,1)S(1)} %copy_multiply_fusion), channel_id=1, source_target_pairs={{0,64},{8,72},{16,80},{24,88},{32,96},{40,104},{48,112},{56,120},{... | collective-permute-start | bytes 786440 | tf_op jit(solution)/shard_map/ppermute | solution.py:18
  101.9 299.3 %reduce-scatter.2.cloned.1.call-start = ((), (), s32[]{:S(2)}) async-start(), calls=%async_computation.2 | async-start | bytes 8912896 | tf_op jit(solution)/shard_map/reduce_scatter | solution.py:233
  105.6 69.0 %collective-permute-start.8 = (bf16[4,512,512]{2,1,0:T(8,128)(2,1)}, bf16[4,512,512]{2,1,0:T(8,128)(2,1)}, u32[]{:S(2)}, u32[]{:S(2)}) collective-permute-start(bf16[4,512,512]{2,1,0:T(8,128)(2,1)} %pad_maximum_fusion.10), channel_id=1, source_target_pairs={{0,8},{8,0},{16,24},{24,16},{32,40},{40,32},{48,56},{56,48},{64,72... | collective-permute-start | bytes 6291464 | tf_op jit(solution)/shard_map/ppermute | solution.py:95
  125.1 34.5 %collective-permute-start.13 = (bf16[512,512]{1,0:T(8,128)(2,1)}, bf16[512,512]{1,0:T(8,128)(2,1)}, u32[]{:S(2)}, u32[]{:S(2)}) collective-permute-start(bf16[512,512]{1,0:T(8,128)(2,1)} %slice.220), channel_id=1, source_target_pairs={{0,6},{1,7},{2,0},{3,1},{4,2},{5,3},{6,4},{7,5},{8,14},{9,15},{10,... | collective-permute-start | bytes 1572872 | tf_op jit(solution)/shard_map/ppermute | solution.py:58
  127.9 31.6 %collective-permute-start.12 = (bf16[512,512]{1,0:T(8,128)(2,1)}, bf16[512,512]{1,0:T(8,128)(2,1)}, u32[]{:S(2)}, u32[]{:S(2)}) collective-permute-start(bf16[512,512]{1,0:T(8,128)(2,1)} %slice.219), channel_id=1, source_target_pairs={{0,2},{1,3},{2,4},{3,5},{4,6},{5,7},{6,0},{7,1},{8,10},{9,11},{10,... | collective-permute-start | bytes 1572872 | tf_op jit(solution)/shard_map/ppermute | solution.py:57
  226.4 73.5 %collective-permute-start.14 = (bf16[1024,512]{0,1:T(8,128)(2,1)}, bf16[1024,512]{0,1:T(8,128)(2,1)}, u32[]{:S(2)}, u32[]{:S(2)}) collective-permute-start(bf16[1024,512]{0,1:T(8,128)(2,1)} %bitcast.164), channel_id=1, source_target_pairs={{0,1},{1,0},{2,3},{3,2},{4,5},{5,4},{6,7},{7,6},{8,9},{9,8},{10,11... | collective-permute-start | bytes 3145736 | tf_op jit(solution)/shard_map/ppermute | solution.py:41
  262.9 31.5 %collective-permute-start.19 = (f32[2,128,512]{2,1,0:T(8,128)S(1)}, f32[2,128,512]{2,1,0:T(8,128)}, u32[]{:S(2)}, u32[]{:S(2)}) collective-permute-start(f32[2,128,512]{2,1,0:T(8,128)S(1)} %fusion.56), channel_id=1, source_target_pairs={{0,64},{8,72},{16,80},{24,88},{32,96},{40,104},{48,112},{56,120},{... | collective-permute-start | bytes 1572872 | tf_op jit(solution)/shard_map/ppermute | solution.py:18
  296.9 13.1 %collective-permute-start.20 = (f32[2,128,512]{2,1,0:T(8,128)S(1)}, f32[2,128,512]{2,1,0:T(8,128)S(1)}, u32[]{:S(2)}, u32[]{:S(2)}) collective-permute-start(f32[2,128,512]{2,1,0:T(8,128)S(1)} %fusion.58), channel_id=1, source_target_pairs={{0,32},{8,40},{16,48},{24,56},{32,0},{40,8},{48,16},{56,24},{64,96... | collective-permute-start | bytes 1572872 | tf_op jit(solution)/shard_map/ppermute | solution.py:18
  302.2 53.1 %collective-permute-start.16 = (bf16[1024,1024]{0,1:T(8,128)(2,1)}, bf16[1024,1024]{0,1:T(8,128)(2,1)}, u32[]{:S(2)}, u32[]{:S(2)}) collective-permute-start(bf16[1024,1024]{0,1:T(8,128)(2,1)} %constant_dynamic-update-slice_fusion), channel_id=1, source_target_pairs={{0,2},{1,3},{2,4},{3,5},{4,6},{5,7},{6,0},{7,1},{8,10},{9,11},{10,... | collective-permute-start | bytes 6291464 | tf_op jit(solution)/shard_map/ppermute | solution.py:51
  303.6 55.6 %collective-permute-start.15 = (bf16[1024,1024]{0,1:T(8,128)(2,1)}, bf16[1024,1024]{0,1:T(8,128)(2,1)}, u32[]{:S(2)}, u32[]{:S(2)}) collective-permute-start(bf16[1024,1024]{0,1:T(8,128)(2,1)} %constant_dynamic-update-slice_fusion), channel_id=1, source_target_pairs={{0,6},{1,7},{2,0},{3,1},{4,2},{5,3},{6,4},{7,5},{8,14},{9,15},{10,... | collective-permute-start | bytes 6291464 | tf_op jit(solution)/shard_map/ppermute | solution.py:52
  312.4 40.5 %collective-permute-start.21 = (f32[2,128,512]{2,1,0:T(8,128)}, f32[2,128,512]{2,1,0:T(8,128)}, u32[]{:S(2)}, u32[]{:S(2)}) collective-permute-start(f32[2,128,512]{2,1,0:T(8,128)} %fusion.55), channel_id=1, source_target_pairs={{0,16},{8,24},{16,0},{24,8},{32,48},{40,56},{48,32},{56,40},{64,80... | collective-permute-start | bytes 1572872 | tf_op jit(solution)/shard_map/ppermute | solution.py:18
  357.8 24.7 %collective-permute-start.17 = (bf16[1024,512]{0,1:T(8,128)(2,1)}, bf16[1024,512]{0,1:T(8,128)(2,1)}, u32[]{:S(2)}, u32[]{:S(2)}) collective-permute-start(bf16[1024,512]{0,1:T(8,128)(2,1)} %slice.221), channel_id=1, source_target_pairs={{0,2},{1,3},{2,4},{3,5},{4,6},{5,7},{6,0},{7,1},{8,10},{9,11},{10,... | collective-permute-start | bytes 3145736 | tf_op jit(solution)/shard_map/ppermute | solution.py:57
  361.5 23.2 %collective-permute-start.18 = (bf16[1024,512]{0,1:T(8,128)(2,1)}, bf16[1024,512]{0,1:T(8,128)(2,1)}, u32[]{:S(2)}, u32[]{:S(2)}) collective-permute-start(bf16[1024,512]{0,1:T(8,128)(2,1)} %slice.222), channel_id=1, source_target_pairs={{0,6},{1,7},{2,0},{3,1},{4,2},{5,3},{6,4},{7,5},{8,14},{9,15},{10,... | collective-permute-start | bytes 3145736 | tf_op jit(solution)/shard_map/ppermute | solution.py:58
  364.3 15.2 %collective-permute-start.22 = (f32[2,128,512]{2,1,0:T(8,128)}, f32[2,128,512]{2,1,0:T(8,128)S(1)}, u32[]{:S(2)}, u32[]{:S(2)}) collective-permute-start(f32[2,128,512]{2,1,0:T(8,128)} %fusion.59), channel_id=1, source_target_pairs={{0,8},{8,0},{16,24},{24,16},{32,40},{40,32},{48,56},{56,48},{64,72... | collective-permute-start | bytes 1572872 | tf_op jit(solution)/shard_map/ppermute | solution.py:18
  (48 other events, 417.2 us)
Sparse Core Ops, SparseCore 0:
  102.0 88.2 all-gather.1
  225.0 113.2 reduce-scatter.1
